TPU v7x, 32 devices: a whole 2x2x4 slice. The times are simulated.
32 devices in a mesh: row: 2 (over y), col: 4 (over z), chan: 4 (over x, core).
Axes of the slice: x: 2, y: 2, z: 4, core: 2. Of those that a mesh axis runs over, the one named last changes fastest.
Arguments:
- feature: bfloat16 [192, 16, 512], P(None, 'row', 'col'), may hold values from -6 to 6
- kernel: float32 [7, 7, 192], replicated, may hold values from -0.875 to 0.875
- conv_bias: float32 [192], replicated, may hold values from -3 to 3
- norm_gain: float32 [192], replicated, may hold values from 0.5 to 1.5
- norm_bias: float32 [192], replicated, may hold values from -3 to 3
- w_in: bfloat16 [192, 768], P(None, 'chan'), may hold values from -0.4375 to 0.4375
- b_in: float32 [768], P('chan'), may hold values from -3 to 3
- w_out: bfloat16 [768, 192], P('chan'), may hold values from -0.21875 to 0.21875
- b_out: float32 [192], replicated, may hold values from -3 to 3
- layer_scale: float32 [192], replicated, may hold values from 0.3 to 1.5
- cotangent: bfloat16 [192, 16, 512], P(None, 'row', 'col'), may hold values from -6 to 6
Outputs:
- result: bfloat16 [192, 16, 512], P(None, 'row', 'col')
- grad_feature: bfloat16 [192, 16, 512], P(None, 'row', 'col')
- grad_kernel: float32 [7, 7, 192], replicated
- grad_conv_bias: float32 [192], replicated
- norm_gain_gradient: float32 [192], replicated
- grad_ln_bias: float32 [192], replicated
- grad_w_in: float32 [192, 768], P(None, 'chan')
- grad_b_in: float32 [768], P('chan')
- grad_w_out: float32 [768, 192], P('chan')
- grad_b_out: float32 [192], replicated
- grad_layer_scale: float32 [192], replicated
All inputs are finite; a program needn't handle non-finite values.
Results may differ from a plain program's by a relative error of at most 0.009.
Values may be sent and summed in bfloat16 or wider, within the bound.
No kernel may reach another device: no remote copies, remote signals or barrier semaphores. Data moves between devices by JAX's collectives and lax.ppermute only.
A program may use at most 64 MiB of HBM per device.

v0:
```python
import jax
import jax.numpy as jnp
from jax import lax
from jax.experimental import pallas as pl
from jax.sharding import PartitionSpec as P


def extended(x, sides, width):
    for axis, dim in sides:
        devices, length = (lax.axis_size(axis), x.shape[dim])
        up = [(i, (i + 1) % devices) for i in range(devices - 1)]
        down = [(j, i) for i, j in up]
        last = lax.slice_in_dim(x, length - width, length, axis=dim)
        leading = lax.slice_in_dim(x, 0, width, axis=dim)
        before = lax.ppermute(last, axis, up)
        after = lax.ppermute(leading, axis, down)
        x = jnp.concatenate([before, x, after], axis=dim)
    return x


def shortened(x):
    return jax.tree.map(lambda a: a.astype(jnp.bfloat16) if a.dtype == jnp.float32 else a, x)


def depthwise(padded, kernel):
    channel_count = padded.shape[0]
    return lax.conv_general_dilated(
        padded[None],
        kernel[:, :, None, :],
        (1, 1),
        "VALID",
        dimension_numbers=("NCHW", "HWIO", "NCHW"),
        feature_group_count=channel_count,
        precision=lax.Precision.HIGHEST,
    )[0]


def gelu_parts(pre_act):
    cdf_val = 0.5 * (1.0 + lax.erf(pre_act * 0.7071067811865476))
    density = jnp.exp(-0.5 * pre_act * pre_act) * 0.3989422804014327
    return (pre_act * cdf_val, cdf_val + pre_act * density)


def contract(left, right, dim_left, dim_right):
    return lax.dot_general(
        left, right, (((dim_left,), (dim_right,)), ((), ())), preferred_element_type=jnp.float32
    )


def layer_norm_forward(conv_flat, norm_gain, norm_bias):
    mean_val = jnp.mean(conv_flat, axis=0)
    centered_values = conv_flat - mean_val
    variance = jnp.mean(centered_values * centered_values, axis=0)
    inverse_deviation = lax.rsqrt(variance + 1e-06)
    standardized_input = centered_values * inverse_deviation
    normalized_output = (standardized_input * norm_gain[:, None] + norm_bias[:, None]).astype(
        jnp.bfloat16
    )
    return (standardized_input, inverse_deviation, normalized_output)


def layer_norm_backward(normalized_gradient, standardized_input, inverse_deviation, norm_gain):
    standardized_gradient = normalized_gradient * norm_gain[:, None]
    initial_mean = jnp.mean(standardized_gradient, axis=0)
    product_mean = jnp.mean(standardized_gradient * standardized_input, axis=0)
    convolved_gradient = inverse_deviation * (
        standardized_gradient - initial_mean - standardized_input * product_mean
    )
    return (
        convolved_gradient,
        jnp.sum(normalized_gradient * standardized_input, axis=1),
        jnp.sum(normalized_gradient, axis=1),
    )


def kernel_grad_body(d_ref, p_ref, o_ref):
    rows, cols, _ = d_ref.shape
    taps = o_ref.shape[0]
    side = int(round(taps ** 0.5))
    o_ref[...] = jnp.zeros(o_ref.shape, o_ref.dtype)

    def row_step(h, carry):
        d_row = d_ref[h]
        for i in range(side):
            for j in range(side):
                prod = d_row * p_ref[h + i, j : j + cols, :]
                part = jnp.sum(prod.reshape(cols // 8, 8, prod.shape[-1]), axis=0)
                o_ref[i * side + j] += part
        return carry

    lax.fori_loop(0, rows, row_step, 0)


def kernel_grad(d_grid, padded):
    d_t = jnp.transpose(d_grid, (1, 2, 0))
    p_t = jnp.transpose(padded, (1, 2, 0))
    side = padded.shape[1] - d_grid.shape[1] + 1
    channel_count = d_grid.shape[0]
    partial = pl.pallas_call(
        kernel_grad_body,
        out_shape=jax.ShapeDtypeStruct((side * side, 8, channel_count), jnp.float32),
    )(d_t, p_t)
    return jnp.sum(partial, axis=1).reshape(side, side, channel_count)


def shards(
    feature,
    kernel,
    conv_bias,
    norm_gain,
    norm_bias,
    w_in,
    b_in,
    w_out,
    b_out,
    layer_scale,
    cotangent,
):
    channel_count, tile_rows, tile_cols = feature.shape
    pixel_count = tile_rows * tile_cols
    blocks = lax.axis_size("chan")
    share = w_in.shape[1]
    own = lax.axis_index("chan")
    w_in_all = lax.all_gather(w_in, "chan", axis=1, tiled=True)
    b_in_all = lax.all_gather(b_in, "chan", axis=0, tiled=True)
    w_out_all = lax.all_gather(w_out, "chan", axis=0, tiled=True)
    padded_bf = extended(feature, (("row", 1), ("col", 2)), 3)
    padded = padded_bf.astype(jnp.float32)
    total_pixels = pixel_count * lax.axis_size("row") * lax.axis_size("col")
    norm_factor = 1.0 / jnp.sqrt(jnp.float32(total_pixels))
    convolved_output = depthwise(padded, kernel) + conv_bias[:, None, None]
    standardized_input, inverse_deviation, normalized_output = layer_norm_forward(
        convolved_output.reshape(channel_count, pixel_count), norm_gain, norm_bias
    )
    pre_act = contract(w_in_all, normalized_output, 0, 0) + b_in_all[:, None]
    gelu_val, gelu_slope = gelu_parts(pre_act)
    hidden = gelu_val.astype(jnp.bfloat16)
    w_out_blocks = w_out_all.reshape(blocks, share, channel_count)
    hidden_blocks = hidden.reshape(blocks, share, pixel_count)
    out_partials = lax.dot_general(
        w_out_blocks,
        hidden_blocks,
        (((1,), (1,)), ((0,), (0,))),
        preferred_element_type=jnp.float32,
    )
    mixed_sum = jnp.sum(out_partials.astype(jnp.bfloat16).astype(jnp.float32), axis=0)
    branch = mixed_sum + b_out[:, None]
    feature_flat = feature.reshape(channel_count, pixel_count)
    result = (
        (feature_flat.astype(jnp.float32) + layer_scale[:, None] * branch)
        .astype(jnp.bfloat16)
        .reshape(channel_count, tile_rows, tile_cols)
    )
    grad_out = cotangent.reshape(channel_count, pixel_count).astype(jnp.float32)
    g_branch = grad_out * layer_scale[:, None]
    grad_layer_scale = jnp.sum(grad_out * branch, axis=1)
    grad_b_out = jnp.sum(g_branch, axis=1)
    g_out = g_branch.astype(jnp.bfloat16)
    d_pre = contract(w_out_all, g_out, 1, 0) * gelu_slope
    g_pre = d_pre.astype(jnp.bfloat16)
    hidden_own = lax.dynamic_slice_in_dim(hidden, own * share, share, axis=0)
    g_pre_own = lax.dynamic_slice_in_dim(g_pre, own * share, share, axis=0)
    d_pre_own = lax.dynamic_slice_in_dim(d_pre, own * share, share, axis=0)
    grad_w_out = contract(hidden_own, g_out, 1, 1)
    grad_b_in = jnp.sum(d_pre_own, axis=1)
    grad_w_in = contract(normalized_output, g_pre_own, 1, 1)
    (grad_w_in, grad_b_in, grad_w_out, grad_b_out, grad_layer_scale) = lax.psum(
        (grad_w_in, grad_b_in, grad_w_out, grad_b_out, grad_layer_scale), ("row", "col")
    )
    w_in_blocks = jnp.transpose(w_in_all.reshape(channel_count, blocks, share), (1, 0, 2))
    g_pre_blocks = g_pre.reshape(blocks, share, pixel_count)
    dn_partials = lax.dot_general(
        w_in_blocks,
        g_pre_blocks,
        (((2,), (1,)), ((0,), (0,))),
        preferred_element_type=jnp.float32,
    )
    normalized_gradient = jnp.sum(dn_partials.astype(jnp.bfloat16).astype(jnp.float32), axis=0)
    convolved_gradient, gain_portion, bias_portion = layer_norm_backward(
        normalized_gradient, standardized_input, inverse_deviation, norm_gain
    )
    grad_conv_bias = jnp.sum(convolved_gradient, axis=1)
    d_grid = convolved_gradient.reshape(channel_count, tile_rows, tile_cols)
    grad_kernel = kernel_grad(d_grid, padded)
    (grad_kernel, grad_conv_bias, gain_portion, bias_portion) = lax.psum(
        (grad_kernel, grad_conv_bias, gain_portion, bias_portion), ("row", "col")
    )
    d_padded = extended(shortened(d_grid), (("row", 1), ("col", 2)), 3).astype(d_grid.dtype)
    grad_feature = (cotangent.astype(jnp.float32) + depthwise(d_padded, kernel[::-1, ::-1])).astype(
        jnp.bfloat16
    )
    return (
        result,
        grad_feature,
        grad_kernel * norm_factor,
        grad_conv_bias * norm_factor,
        gain_portion * norm_factor,
        bias_portion * norm_factor,
        grad_w_in * norm_factor,
        grad_b_in * norm_factor,
        grad_w_out * norm_factor,
        grad_b_out * norm_factor,
        grad_layer_scale * norm_factor,
    )


def solution(mesh):
    return jax.shard_map(
        shards,
        mesh=mesh,
        in_specs=(
            P(None, "row", "col"),
            P(),
            P(),
            P(),
            P(),
            P(None, "chan"),
            P("chan"),
            P("chan", None),
            P(),
            P(),
            P(None, "row", "col"),
        ),
        out_specs=(
            P(None, "row", "col"),
            P(None, "row", "col"),
            P(),
            P(),
            P(),
            P(),
            P(None, "chan"),
            P("chan"),
            P("chan", None),
            P(),
            P(),
        ),
        check_vma=False,
    )
```

profile of v0, /device:TPU:0, one launch (start us, length us, event | category | flops | bytes accessed | tf_op | source)
XLA Modules:
  0.0 183.6 jit_solution(2124809146027351504)
XLA Ops:
  7.2 1.3 copy.95
  8.6 4.9 %collective-permute-start = (bf16[192,3,128]{0,2,1:T(8,128)(2,1)S(1)}, bf16[192,3,128]{0,2,1:T(8,128)(2,1)S(1)}, u32[]{:S(2)}, u32[]{:S(2)}) collective-permute-start(bf16[192,3,128]{0,2,1:T(8,128)(2,1)S(1)} %get-tuple-element.48), channel_id=1, source_target_pairs={{0,16},{1,17},{2,18},{3,19},{4,20},{5,21},{6,22},{7,23},{8,24},{9,... | collective-permute-start | bytes 442376 | tf_op jit(solution)/shard_map/ppermute | solution.py:15
  15.8 6.6 %all_gather.9 = bf16[192,768]{0,1:T(8,128)(2,1)S(1)} all-gather(bf16[192,192]{0,1:T(8,128)(2,1)S(1)} %copy.102), channel_id=1, replica_groups=mesh['row'=2,'col'=4,'chan'=4] {'chan'}, dimensions={1}, use_global_device_ids=true | all-gather | bytes 368640 | tf_op jit(solution)/shard_map/all_gather | solution.py:124
  22.4 3.5 %collective-permute-start.2 = (bf16[192,14,3]{0,2,1:T(4,128)(2,1)S(1)}, bf16[192,14,3]{0,2,1:T(4,128)(2,1)S(1)}, u32[]{:S(2)}, u32[]{:S(2)}) collective-permute-start(bf16[192,14,3]{0,2,1:T(4,128)(2,1)S(1)} %get-tuple-element.43), channel_id=1, source_target_pairs={{0,4},{4,8},{8,12},{1,5},{5,9},{9,13},{2,6},{6,10},{10,14},{3,7},{... | collective-permute-start | bytes 48392 | tf_op jit(solution)/shard_map/ppermute | solution.py:15
  27.2 6.7 %all_gather.11 = bf16[768,192]{1,0:T(8,128)(2,1)} all-gather(bf16[192,192]{1,0:T(8,128)(2,1)S(1)} %copy-done.8), channel_id=1, replica_groups=mesh['row'=2,'col'=4,'chan'=4] {'chan'}, dimensions={0}, use_global_device_ids=true | all-gather | bytes 368640 | tf_op jit(solution)/shard_map/all_gather | solution.py:126
  36.7 6.8 %all-reduce = f32[768]{0:T(1024)S(1)} all-reduce(f32[768]{0:T(1024)S(1)} %dynamic-update-slice), channel_id=1, replica_groups=mesh['row'=2,'col'=4,'chan'=4] {'chan'}, use_global_device_ids=true, to_apply=%add | all-reduce | flops 768 | bytes 6144
  43.5 1.6 convert_bitcast_fusion
  45.1 8.4 %fusion.10 = f32[1,192,8,128]{1,0,3,2:T(1,128)S(1)} fusion(bf16[1,192,14,134]{1,3,2,0:T(8,128)(2,1)S(1)} %get-tuple-element.40, f32[7,7,1,192]{3,1,0,2:T(8,128)S(1)} %bitcast.145), kind=kOutput, calls=%fused_computation.18 | convolution fusion | flops 115605504 | bytes 1544448 | tf_op jit(solution)/shard_map/conv_general_dilated | solution.py:27
  55.4 2.2 %fusion.8 = (bf16[768,1024]{1,0:T(8,128)(2,1)}, f32[1024,768]{0,1:T(8,128)S(1)}) fusion(f32[768]{0:T(1024)S(1)} %all-reduce, bf16[192,768]{0,1:T(8,128)(2,1)S(1)} %all_gather.9, f32[24,8,8,128]{3,2,1,0:T(8,128)S(1)} %bitcast.131, f32[192]{0:T(256)S(1)} %copy-done.15, f32[192]{0:T(256)S(1)} %copy-done.11, f32[1024]{0:T(1024)S(1)} %get-tuple-element.52, ...), kind=kOutput, calls=%fused_computation.13 | convolution fusion | flops 307888128 | bytes 5813504 | tf_op jit(solution)/shard_map/dot_general | solution.py:45
  57.6 3.2 %fusion.60 = (bf16[768,1024]{1,0:T(8,128)(2,1)S(1)}, f32[768,1024]{1,0:T(8,128)}) fusion(f32[1024,768]{0,1:T(8,128)S(1)} %get-tuple-element.56, f32[768]{0:T(1024)S(1)} %all-reduce, bf16[768,192]{1,0:T(8,128)(2,1)S(1)} %copy-done.5, f32[24,8,8,128]{3,2,1,0:T(8,128)S(1)} %convert.2, f32[192]{0:T(256)S(1)} %copy-done.12), kind=kOutput, calls=%fused_computation.101 | convolution fusion | flops 311033856 | bytes 8949504 | tf_op jit(solution)/shard_map/dot_general | solution.py:45
  63.9 2.8 %fusion.50 = (f32[8,128,192]{2,1,0:T(8,128)}, bf16[192,8,128]{0,2,1:T(8,128)(2,1)S(1)}) fusion(f32[8,128]{1,0:T(8,128)S(1)} %broadcast_multiply_fusion.3, f32[8,128]{1,0:T(8,128)S(1)} %get-tuple-element.54, f32[192]{0:T(256)S(1)} %copy-done.10, f32[1,192,8,128]{1,0,3,2:T(1,128)} %copy-done, f32[8,128]{1,0:T(8,128)S(1)} %multiply_bitcast_fusion, ...), kind=kLoop, calls=%fused_computation.95 | loop fusion | flops 1769472 | bytes 2770432 | tf_op jit(solution)/shard_map/transpose | solution.py:95
  67.5 4.6 %collective-permute-start.4 = (bf16[192,3,128]{0,2,1:T(8,128)(2,1)}, bf16[192,3,128]{0,2,1:T(8,128)(2,1)S(1)}, u32[]{:S(2)}, u32[]{:S(2)}) collective-permute-start(bf16[192,3,128]{0,2,1:T(8,128)(2,1)} %get-tuple-element.46), channel_id=1, source_target_pairs={{0,16},{1,17},{2,18},{3,19},{4,20},{5,21},{6,22},{7,23},{8,24},{9,... | collective-permute-start | bytes 442376 | tf_op jit(solution)/shard_map/ppermute | solution.py:15
  73.4 2.1 %fusion.39 = f32[192,192]{1,0:T(8,128)} fusion(bf16[768,1024]{1,0:T(8,128)(2,1)} %copy-done.16, s32[]{:T(128)S(6)} %select_n.2, f32[24,8,8,128]{3,2,1,0:T(8,128)S(1)} %bitcast.132, f32[192]{0:T(256)S(1)} %copy-done.15, f32[192]{0:T(256)S(1)} %copy-done.11, f32[1024]{0:T(1024)S(1)} %get-tuple-element.52, f32[1024]{0:T(1024)S(1)} %get-tuple-element.53, ...), kind=kOutput, calls=%fused_computation.65 | convolution fusion | flops 76677120 | bytes 1337604 | tf_op jit(solution)/shard_map/dot_general | solution.py:45
  75.4 2.1 %fusion.37 = f32[192,192]{1,0:T(8,128)} fusion(bf16[768,1024]{1,0:T(8,128)(2,1)} %get-tuple-element.55, s32[]{:T(128)S(6)} %select_n.2, f32[24,8,8,128]{3,2,1,0:T(8,128)S(1)} %copy-done.2, f32[192]{0:T(256)S(1)} %copy-done.12), kind=kOutput, calls=%fused_computation.63 | convolution fusion | flops 75890688 | bytes 1327876 | tf_op jit(solution)/shard_map/dot_general | solution.py:45
  77.5 2.1 %convert_reduce_fusion.2 = f32[1024,192]{0,1:T(8,128)S(1)} fusion(bf16[4,192,192]{2,1,0:T(8,128)(2,1)S(1)} %bitcast.144, bf16[4,192,1024]{2,1,0:T(8,128)(2,1)} %bitcast.141), kind=kOutput, calls=%fused_computation.14 | convolution fusion | flops 304152576 | bytes 2654208 | tf_op jit(solution)/shard_map/dot_general | solution.py:140
  79.9 4.4 %collective-permute-start.6 = (bf16[192,14,3]{0,2,1:T(4,128)(2,1)S(1)}, bf16[192,14,3]{0,2,1:T(4,128)(2,1)S(1)}, u32[]{:S(2)}, u32[]{:S(2)}) collective-permute-start(bf16[192,14,3]{0,2,1:T(4,128)(2,1)S(1)} %get-tuple-element.41), channel_id=1, source_target_pairs={{0,4},{4,8},{8,12},{1,5},{5,9},{9,13},{2,6},{6,10},{10,14},{3,7},{... | collective-permute-start | bytes 48392 | tf_op jit(solution)/shard_map/ppermute | solution.py:15
  84.3 1.5 collective-permute-start.7
  85.8 3.7 %fusion.27 = (f32[192]{0:T(256)S(1)}, f32[192]{0:T(256)S(1)}) fusion(f32[1,192,8,128]{3,2,1,0:T(8,128)S(1)} %copy.100, f32[8,128]{1,0:T(8,128)S(1)} %get-tuple-element.51, f32[8,128]{1,0:T(8,128)S(1)} %get-tuple-element.54, f32[192]{0:T(256)S(1)} %copy-done.10, f32[8,128]{1,0:T(8,128)S(1)} %broadcast_multiply_fusion.3, ...), kind=kLoop, calls=%fused_computation.40 | loop fusion | flops 2162304 | bytes 1592320 | tf_op jit(solution)/shard_map/reduce_sum | solution.py:71
  89.6 10.0 %shard_map.194 = f32[49,8,192]{2,1,0:T(8,128)} custom-call(f32[8,128,192]{2,1,0:T(8,128)} %get-tuple-element.37.d_ref, f32[14,134,192]{2,1,0:T(8,128)} %get-tuple-element.39.p_ref), custom_call_target="tpu_custom_call" | custom-call | tf_op jit(solution)/shard_map/pallas_call | solution.py:99
  103.3 4.1 %fusion.19 = f32[8,8,17,192]{3,1,2,0:T(8,128)S(1)} fusion(bf16[192,14,1,7,6]{0,3,4,1,2:T(8,128)(2,1)S(1)} %slice.38, bf16[192,14,1,8,17]{0,3,4,1,2:T(8,128)(2,1)S(1)} %copy.112, pred[8,17]{0,1:T(8,128)(4,1)S(1)} %copy-done.18, f32[7,7,1,192]{3,1,0,2:T(8,128)S(1)} %bitcast.146), kind=kOutput, calls=%fused_computation.28 | convolution fusion | flops 126007296 | bytes 1830280 | tf_op jit(solution)/shard_map/conv_general_dilated | solution.py:27
  108.8 3.8 %multiply_reduce_fusion = (f32[192]{0:T(256)S(1)}, f32[192]{0:T(256)S(1)}, bf16[192,8,128]{2,1,0:T(8,128)(2,1)}, bf16[192,8,128]{2,1,0:T(8,128)(2,1)}) fusion(f32[24,8,8,128]{3,2,1,0:T(8,128)S(1)} %copy.126, bf16[192,8,128]{2,1,0:T(8,128)(2,1)S(1)} %copy-done.4, f32[192]{0:T(256)S(1)} %copy-done.13, f32[192]{0:T(256)S(1)} %copy-done.12, ...), kind=kLoop, calls=%fused_computation.51 | loop fusion | flops 2358912 | bytes 3148800 | tf_op jit(solution)/shard_map/reduce_sum | solution.py:156
  112.6 40.3 %all-reduce.1 = (f32[7,7,192]{2,1,0:T(8,128)S(1)}, f32[192]{0:T(256)S(1)}, f32[192]{0:T(256)S(1)}, f32[192]{0:T(256)S(1)}, f32[192]{0:T(256)S(1)}, /*index=5*/f32[192]{0:T(256)S(1)}, f32[192]{0:T(256)S(1)}) all-reduce(f32[7,7,192]{2,1,0:T(8,128)S(1)} %reshape.251, ...), channel_id=1, replica_groups=mesh['row'=2,'col'=4,'chan'=4] {'row','col'}, use_global_device_ids=true, to_apply=%region_7.0 | all-reduce | flops 10560 | bytes 84480 | tf_op jit(solution)/shard_map/psum | solution.py:185
  155.2 19.8 %all-reduce.5.cloned.1.call-done = (f32[192,192]{1,0:T(8,128)}, f32[192,192]{1,0:T(8,128)}) async-done(((f32[192,192]{1,0:T(8,128)}, f32[192,192]{1,0:T(8,128)}), (f32[192,192]{1,0:T(8,128)}, f32[192,192]{1,0:T(8,128)})) %all-reduce.5.cloned.1.call-update) | async-done | bytes 294928 | tf_op jit(solution)/shard_map/psum | solution.py:167
  175.0 1.8 broadcast_multiply_fusion
  (90 shorter events, 20.3 us)
Async XLA Ops:
  7.2 20.1 %copy-start.8 = (bf16[192,192]{1,0:T(8,128)(2,1)S(1)}, bf16[192,192]{1,0:T(8,128)(2,1)}, u32[]{:S(2)}) copy-start(bf16[192,192]{1,0:T(8,128)(2,1)} %param.18) | copy-start | bytes 221188
  7.2 26.8 %copy-start.4 = (bf16[192,8,128]{2,1,0:T(8,128)(2,1)S(1)}, bf16[192,8,128]{2,1,0:T(8,128)(2,1)}, u32[]{:S(2)}) copy-start(bf16[192,8,128]{2,1,0:T(8,128)(2,1)} %param.21) | copy-start | bytes 1179652
  7.2 167.8 %all-reduce.5.cloned.1.call-start = ((), (), s32[]{:S(2)}) async-start(), calls=%async_computation | async-start | bytes 786432 | tf_op jit(solution)/shard_map/psum | solution.py:167
  8.6 13.8 %collective-permute-start = (bf16[192,3,128]{0,2,1:T(8,128)(2,1)S(1)}, bf16[192,3,128]{0,2,1:T(8,128)(2,1)S(1)}, u32[]{:S(2)}, u32[]{:S(2)}) collective-permute-start(bf16[192,3,128]{0,2,1:T(8,128)(2,1)S(1)} %get-tuple-element.48), channel_id=1, source_target_pairs={{0,16},{1,17},{2,18},{3,19},{4,20},{5,21},{6,22},{7,23},{8,24},{9,... | collective-permute-start | bytes 442376 | tf_op jit(solution)/shard_map/ppermute | solution.py:15
  13.5 8.9 %collective-permute-start.1 = (bf16[192,3,128]{0,2,1:T(8,128)(2,1)S(1)}, bf16[192,3,128]{0,2,1:T(8,128)(2,1)S(1)}, u32[]{:S(2)}, u32[]{:S(2)}) collective-permute-start(bf16[192,3,128]{0,2,1:T(8,128)(2,1)S(1)} %get-tuple-element.49), channel_id=1, source_target_pairs={{16,0},{17,1},{18,2},{19,3},{20,4},{21,5},{22,6},{23,7},{24,8},{25... | collective-permute-start | bytes 442376 | tf_op jit(solution)/shard_map/ppermute | solution.py:16
  15.8 19.3 %copy-start.9 = (f32[7,7,192]{2,1,0:T(8,128)S(1)}, f32[7,7,192]{2,1,0:T(8,128)}, u32[]{:S(2)}) copy-start(f32[7,7,192]{2,1,0:T(8,128)} %param.12) | copy-start | bytes 112900
  15.8 19.4 %copy-start.17 = (u32[32]{0:T(128)S(1)}, u32[32]{0:T(128)}, u32[]{:S(2)}) copy-start(u32[32]{0:T(128)} %constant.45) | copy-start | bytes 388
  15.8 20.6 %copy-start.14 = (f32[192]{0:T(256)S(1)}, f32[192]{0:T(256)}, u32[]{:S(2)}) copy-start(f32[192]{0:T(256)} %param.17) | copy-start | bytes 2308
  22.4 21.0 %collective-permute-start.2 = (bf16[192,14,3]{0,2,1:T(4,128)(2,1)S(1)}, bf16[192,14,3]{0,2,1:T(4,128)(2,1)S(1)}, u32[]{:S(2)}, u32[]{:S(2)}) collective-permute-start(bf16[192,14,3]{0,2,1:T(4,128)(2,1)S(1)} %get-tuple-element.43), channel_id=1, source_target_pairs={{0,4},{4,8},{8,12},{1,5},{5,9},{9,13},{2,6},{6,10},{10,14},{3,7},{... | collective-permute-start | bytes 48392 | tf_op jit(solution)/shard_map/ppermute | solution.py:15
  25.9 17.5 %collective-permute-start.3 = (bf16[192,14,3]{0,2,1:T(4,128)(2,1)S(1)}, bf16[192,14,3]{0,2,1:T(4,128)(2,1)S(1)}, u32[]{:S(2)}, u32[]{:S(2)}) collective-permute-start(bf16[192,14,3]{0,2,1:T(4,128)(2,1)S(1)} %get-tuple-element.44), channel_id=1, source_target_pairs={{4,0},{8,4},{12,8},{5,1},{9,5},{13,9},{6,2},{10,6},{14,10},{7,3},{... | collective-permute-start | bytes 48392 | tf_op jit(solution)/shard_map/ppermute | solution.py:16
  34.1 23.5 %copy-start.1 = (f32[24,8,8,128]{3,2,1,0:T(8,128)}, f32[24,8,8,128]{3,2,1,0:T(8,128)S(1)}, u32[]{:S(2)}) copy-start(f32[24,8,8,128]{3,2,1,0:T(8,128)S(1)} %convert.2) | copy-start | bytes 2359300
  45.1 9.7 %copy-start.10 = (f32[192]{0:T(256)S(1)}, f32[192]{0:T(256)}, u32[]{:S(2)}) copy-start(f32[192]{0:T(256)} %param.13) | copy-start | bytes 2308
  53.5 4.1 %copy-start = (f32[1,192,8,128]{1,0,3,2:T(1,128)}, f32[1,192,8,128]{1,0,3,2:T(1,128)S(1)}, u32[]{:S(2)}) copy-start(f32[1,192,8,128]{1,0,3,2:T(1,128)S(1)} %fusion.10) | copy-start | bytes 2359300
  53.5 1.9 %copy-start.11 = (f32[192]{0:T(256)S(1)}, f32[192]{0:T(256)}, u32[]{:S(2)}) copy-start(f32[192]{0:T(256)} %param.14) | copy-start | bytes 2308
  53.5 1.9 %copy-start.15 = (f32[192]{0:T(256)S(1)}, f32[192]{0:T(256)}, u32[]{:S(2)}) copy-start(f32[192]{0:T(256)} %param.15) | copy-start | bytes 2308
  55.4 2.2 %copy-start.5 = (bf16[768,192]{1,0:T(8,128)(2,1)S(1)}, bf16[768,192]{1,0:T(8,128)(2,1)}, u32[]{:S(2)}) copy-start(bf16[768,192]{1,0:T(8,128)(2,1)} %all_gather.11) | copy-start | bytes 884740
  55.4 2.2 %copy-start.12 = (f32[192]{0:T(256)S(1)}, f32[192]{0:T(256)}, u32[]{:S(2)}) copy-start(f32[192]{0:T(256)} %param.20) | copy-start | bytes 2308
  57.6 3.3 %copy-start.7 = (bf16[192,4,192]{2,0,1:T(8,128)(2,1)S(1)}, bf16[192,4,192]{2,0,1:T(8,128)(2,1)}, u32[]{:S(2)}) copy-start(bf16[192,4,192]{2,0,1:T(8,128)(2,1)} %copy.106) | copy-start | bytes 884740
  66.7 8.7 %copy-start.2 = (f32[24,8,8,128]{3,2,1,0:T(8,128)S(1)}, f32[24,8,8,128]{3,2,1,0:T(8,128)}, u32[]{:S(2)}) copy-start(f32[24,8,8,128]{3,2,1,0:T(8,128)} %copy-done.1) | copy-start | bytes 2359300
  66.7 10.8 %copy-start.6 = (bf16[768,192]{1,0:T(8,128)(2,1)S(1)}, bf16[768,192]{1,0:T(8,128)(2,1)}, u32[]{:S(2)}) copy-start(bf16[768,192]{1,0:T(8,128)(2,1)} %all_gather.11) | copy-start | bytes 884740
  67.5 12.1 %collective-permute-start.4 = (bf16[192,3,128]{0,2,1:T(8,128)(2,1)}, bf16[192,3,128]{0,2,1:T(8,128)(2,1)S(1)}, u32[]{:S(2)}, u32[]{:S(2)}) collective-permute-start(bf16[192,3,128]{0,2,1:T(8,128)(2,1)} %get-tuple-element.46), channel_id=1, source_target_pairs={{0,16},{1,17},{2,18},{3,19},{4,20},{5,21},{6,22},{7,23},{8,24},{9,... | collective-permute-start | bytes 442376 | tf_op jit(solution)/shard_map/ppermute | solution.py:15
  72.1 7.8 %collective-permute-start.5 = (bf16[192,3,128]{0,2,1:T(8,128)(2,1)}, bf16[192,3,128]{0,2,1:T(8,128)(2,1)S(1)}, u32[]{:S(2)}, u32[]{:S(2)}) collective-permute-start(bf16[192,3,128]{0,2,1:T(8,128)(2,1)} %get-tuple-element.47), channel_id=1, source_target_pairs={{16,0},{17,1},{18,2},{19,3},{20,4},{21,5},{22,6},{23,7},{24,8},{25... | collective-permute-start | bytes 442376 | tf_op jit(solution)/shard_map/ppermute | solution.py:16
  79.9 22.1 %collective-permute-start.6 = (bf16[192,14,3]{0,2,1:T(4,128)(2,1)S(1)}, bf16[192,14,3]{0,2,1:T(4,128)(2,1)S(1)}, u32[]{:S(2)}, u32[]{:S(2)}) collective-permute-start(bf16[192,14,3]{0,2,1:T(4,128)(2,1)S(1)} %get-tuple-element.41), channel_id=1, source_target_pairs={{0,4},{4,8},{8,12},{1,5},{5,9},{9,13},{2,6},{6,10},{10,14},{3,7},{... | collective-permute-start | bytes 48392 | tf_op jit(solution)/shard_map/ppermute | solution.py:15
  84.3 17.7 %collective-permute-start.7 = (bf16[192,14,3]{0,2,1:T(4,128)(2,1)S(1)}, bf16[192,14,3]{0,2,1:T(4,128)(2,1)S(1)}, u32[]{:S(2)}, u32[]{:S(2)}) collective-permute-start(bf16[192,14,3]{0,2,1:T(4,128)(2,1)S(1)} %get-tuple-element.42), channel_id=1, source_target_pairs={{4,0},{8,4},{12,8},{5,1},{9,5},{13,9},{6,2},{10,6},{14,10},{7,3},{... | collective-permute-start | bytes 48392 | tf_op jit(solution)/shard_map/ppermute | solution.py:16
  (4 other events, 3.8 us)
Sparse Core Ops, SparseCore 0:
  100.9 74.0 all-reduce.4
where the time goes:
time: 184 us
  blocking collectives  60.4 us (33%)
  matrix products  24.9 us (14%)
  starting transfers between devices  22.7 us (12%)
  waiting for transfers between devices  20 us (11%)
  other arithmetic  20 us (11%)
  between operations  15.2 us (8%)
  local copies, waits for them, and re-layouts  10.4 us (6%)
  Pallas kernels  10 us (5%)
    psum x1, blocking collectives, shards(): lax.psum((grad_kernel, grad_conv_bias, gain_portion, bias_portion), ('row...  40.3 us
    psum x1, waiting for transfers between devices, shards(): lax.psum((grad_w_in, grad_b_in, grad_w_out, grad_b_out, grad_layer_scale)...  19.8 us
    ppermute x4, starting transfers between devices, extended(): before = lax.ppermute(last, axis, up)  17.3 us
    conv_general_dilated x2, matrix products, depthwise(): lax.conv_general_dilated(padded[None], kernel[:, :, None, :], (1, 1), 'VA...  12.6 us
    pallas_call x1, Pallas kernels, kernel_grad(): pl.pallas_call(kernel_grad_body, out_shape=jax.ShapeDtypeStruct((side * s...  10 us
    dot_general x4, matrix products, contract(): lax.dot_general(left, right, (((dim_left,), (dim_right,)), ((), ())), pre...  9.6 us
    unnamed x1, blocking collectives  6.75 us
    all_gather x1, blocking collectives, shards(): w_out_all = lax.all_gather(w_out, 'chan', axis=0, tiled=True)  6.75 us
  transfers between devices with their start and end apart: 9, of which 2 were waited for; matrix products, arithmetic and copies ran while one was open for 15% of the time, Pallas kernels for 5%

commit v1 on v0

--- a/solution.py
+++ b/solution.py
@@ -101,6 +101,46 @@
         out_shape=jax.ShapeDtypeStruct((side * side, 8, channel_count), jnp.float32),
     )(d_t, p_t)
     return jnp.sum(partial, axis=1).reshape(side, side, channel_count)
+
+
+def butterfly_sum(values, axes):
+    shapes = [v.shape for v in values]
+    flat = jnp.concatenate([v.reshape(-1) for v in values])
+    for axis in axes:
+        devices = lax.axis_size(axis)
+        if devices & (devices - 1):
+            flat = lax.psum(flat, axis)
+            continue
+        step = 1
+        while step < devices:
+            flat = flat + lax.ppermute(flat, axis, [(i, i ^ step) for i in range(devices)])
+            step *= 2
+    out = []
+    offset = 0
+    for shape in shapes:
+        size = 1
+        for s in shape:
+            size *= s
+        out.append(flat[offset : offset + size].reshape(shape))
+        offset += size
+    return out
+
+
+def gathered_weights(w_in, b_in, w_out):
+    channel_count = w_in.shape[0]
+    pieces = []
+    rest = b_in
+    for _ in range(3):
+        piece = rest.astype(jnp.bfloat16)
+        rest = rest - piece.astype(jnp.float32)
+        pieces.append(piece[:, None])
+    packed = jnp.concatenate([w_in.T, w_out] + pieces, axis=1)
+    full = lax.all_gather(packed, "chan", axis=0, tiled=True)
+    w_in_all = full[:, :channel_count].T
+    w_out_all = full[:, channel_count : 2 * channel_count]
+    parts = full[:, 2 * channel_count :].astype(jnp.float32)
+    b_in_all = (parts[:, 0] + parts[:, 1]) + parts[:, 2]
+    return w_in_all, b_in_all, w_out_all
 
 
 def shards(
@@ -121,9 +161,7 @@
     blocks = lax.axis_size("chan")
     share = w_in.shape[1]
     own = lax.axis_index("chan")
-    w_in_all = lax.all_gather(w_in, "chan", axis=1, tiled=True)
-    b_in_all = lax.all_gather(b_in, "chan", axis=0, tiled=True)
-    w_out_all = lax.all_gather(w_out, "chan", axis=0, tiled=True)
+    w_in_all, b_in_all, w_out_all = gathered_weights(w_in, b_in, w_out)
     padded_bf = extended(feature, (("row", 1), ("col", 2)), 3)
     padded = padded_bf.astype(jnp.float32)
     total_pixels = pixel_count * lax.axis_size("row") * lax.axis_size("col")
@@ -164,7 +202,7 @@
     grad_w_out = contract(hidden_own, g_out, 1, 1)
     grad_b_in = jnp.sum(d_pre_own, axis=1)
     grad_w_in = contract(normalized_output, g_pre_own, 1, 1)
-    (grad_w_in, grad_b_in, grad_w_out, grad_b_out, grad_layer_scale) = lax.psum(
+    (grad_w_in, grad_b_in, grad_w_out, grad_b_out, grad_layer_scale) = butterfly_sum(
         (grad_w_in, grad_b_in, grad_w_out, grad_b_out, grad_layer_scale), ("row", "col")
     )
     w_in_blocks = jnp.transpose(w_in_all.reshape(channel_count, blocks, share), (1, 0, 2))
@@ -182,7 +220,7 @@
     grad_conv_bias = jnp.sum(convolved_gradient, axis=1)
     d_grid = convolved_gradient.reshape(channel_count, tile_rows, tile_cols)
     grad_kernel = kernel_grad(d_grid, padded)
-    (grad_kernel, grad_conv_bias, gain_portion, bias_portion) = lax.psum(
+    (grad_kernel, grad_conv_bias, gain_portion, bias_portion) = butterfly_sum(
         (grad_kernel, grad_conv_bias, gain_portion, bias_portion), ("row", "col")
     )
     d_padded = extended(shortened(d_grid), (("row", 1), ("col", 2)), 3).astype(d_grid.dtype)

time: 184 us -> 139 us (0.76)
  blocking collectives: 60.4 us -> 8.6 us
  between operations: 15.2 us -> 1.21 us
  waiting for transfers between devices: 20 us -> 29.8 us
  local copies, waits for them, and re-layouts: 10.4 us -> 18 us
  starting transfers between devices: 22.7 us -> 28.6 us
  matrix products: 24.9 us -> 22.5 us
    psum x1 -> x0, blocking collectives: 40.3 us -> none  [shards(): lax.psum((grad_kernel, grad_conv_bias, gain_portion, bias_portion), ('row...]
    ppermute x0 -> x6, waiting for transfers between devices: none -> 21.1 us  [butterfly_sum(): lax.ppermute(flat, axis, [(i, i ^ step) for i in range(devices)])]
    psum x1 -> x0, waiting for transfers between devices: 19.8 us -> none  [shards(): lax.psum((grad_w_in, grad_b_in, grad_w_out, grad_b_out, grad_layer_scale)...]
    ppermute x4, waiting for transfers between devices: 0.21 us -> 7.21 us  [extended(): after = lax.ppermute(leading, axis, down)]
    unnamed x1 -> x0, blocking collectives: 6.75 us -> none
    ppermute x0 -> x6, starting transfers between devices: none -> 6.1 us  [butterfly_sum(): lax.ppermute(flat, axis, [(i, i ^ step) for i in range(devices)])]
    all_gather x2 -> x1, blocking collectives: 13.3 us -> 8.6 us  [gathered_weights(): full = lax.all_gather(packed, 'chan', axis=0, tiled=True)]
    reshape x1 -> x2, local copies, waits for them, and re-layouts: 0.01 us -> 2.49 us  [butterfly_sum(): flat = jnp.concatenate([v.reshape(-1) for v in values])]
  transfers between devices with their start and end apart: 9 -> 14, of which waited for: 2 -> 7; matrix products, arithmetic and copies ran while one was open for 15% -> 12% of each run, Pallas kernels for 5% -> 7%
where the time goes in v1:
time: 139 us
  waiting for transfers between devices  29.8 us (21%)
  starting transfers between devices  28.6 us (21%)
  matrix products  22.5 us (16%)
  other arithmetic  20 us (14%)
  local copies, waits for them, and re-layouts  18 us (13%)
  Pallas kernels  10 us (7%)
  blocking collectives  8.6 us (6%)
    ppermute x6, waiting for transfers between devices, butterfly_sum(): lax.ppermute(flat, axis, [(i, i ^ step) for i in range(devices)])  21.1 us
    ppermute x4, starting transfers between devices, extended(): before = lax.ppermute(last, axis, up)  17.1 us
    conv_general_dilated x2, matrix products, depthwise(): lax.conv_general_dilated(padded[None], kernel[:, :, None, :], (1, 1), 'VA...  12.6 us
    pallas_call x1, Pallas kernels, kernel_grad(): pl.pallas_call(kernel_grad_body, out_shape=jax.ShapeDtypeStruct((side * s...  10 us
    all_gather x1, blocking collectives, gathered_weights(): full = lax.all_gather(packed, 'chan', axis=0, tiled=True)  8.6 us
    dot_general x4, matrix products, contract(): lax.dot_general(left, right, (((dim_left,), (dim_right,)), ((), ())), pre...  8 us
    ppermute x4, waiting for transfers between devices, extended(): after = lax.ppermute(leading, axis, down)  7.21 us
    ppermute x6, starting transfers between devices, butterfly_sum(): lax.ppermute(flat, axis, [(i, i ^ step) for i in range(devices)])  6.1 us
  transfers between devices with their start and end apart: 14, of which 7 were waited for; matrix products, arithmetic and copies ran while one was open for 12% of the time, Pallas kernels for 7%

profile of v1, /device:TPU:0, one launch (start us, length us, event | category | flops | bytes accessed | tf_op | source)
XLA Modules:
  0.0 138.7 jit_solution(4100896561320058636)
XLA Ops:
  2.0 4.9 %collective-permute-start = (bf16[192,3,128]{0,2,1:T(8,128)(2,1)S(1)}, bf16[192,3,128]{0,2,1:T(8,128)(2,1)S(1)}, u32[]{:S(2)}, u32[]{:S(2)}) collective-permute-start(bf16[192,3,128]{0,2,1:T(8,128)(2,1)S(1)} %get-tuple-element.41), channel_id=1, source_target_pairs={{0,16},{1,17},{2,18},{3,19},{4,20},{5,21},{6,22},{7,23},{8,24},{9,... | collective-permute-start | bytes 442376 | tf_op jit(solution)/shard_map/ppermute | solution.py:15
  10.4 8.6 %all_gather.3 = bf16[768,387]{1,0:T(8,128)(2,1)S(1)} all-gather(bf16[192,387]{1,0:T(8,128)(2,1)S(1)} %concatenate.21), channel_id=1, replica_groups=mesh['row'=2,'col'=4,'chan'=4] {'chan'}, dimensions={0}, use_global_device_ids=true | all-gather | bytes 743040 | tf_op jit(solution)/shard_map/all_gather | solution.py:138
  20.0 3.5 %collective-permute-start.2 = (bf16[192,14,3]{0,2,1:T(4,128)(2,1)S(1)}, bf16[192,14,3]{0,2,1:T(4,128)(2,1)S(1)}, u32[]{:S(2)}, u32[]{:S(2)}) collective-permute-start(bf16[192,14,3]{0,2,1:T(4,128)(2,1)S(1)} %get-tuple-element.34), channel_id=1, source_target_pairs={{0,4},{4,8},{8,12},{1,5},{5,9},{9,13},{2,6},{6,10},{10,14},{3,7},{... | collective-permute-start | bytes 48392 | tf_op jit(solution)/shard_map/ppermute | solution.py:15
  26.4 2.9 %collective-permute-done.3 = bf16[192,14,3]{0,2,1:T(4,128)(2,1)S(1)} collective-permute-done((bf16[192,14,3]{0,2,1:T(4,128)(2,1)S(1)}, bf16[192,14,3]{0,2,1:T(4,128)(2,1)S(1)}, u32[]{:S(2)}, u32[]{:S(2)}) %collective-permute-start.3) | collective-permute-done | bytes 16160 | tf_op jit(solution)/shard_map/ppermute | solution.py:16
  29.3 1.6 %convert_bitcast_fusion = (f32[14,134,192]{2,1,0:T(8,128)}, bf16[1,192,14,134]{1,3,2,0:T(8,128)(2,1)S(1)}) fusion(bf16[192,14,3]{0,2,1:T(4,128)(2,1)S(1)} %collective-permute-done.3, bf16[192,3,128]{0,2,1:T(8,128)(2,1)S(1)} %collective-permute-done.1, bf16[192,8,128]{0,2,1:T(8,128)(2,1)S(1)} %copy.89, bf16[192,3,128]{0,2,1:T(8,128)(2,1)S(1)} %collective-permute-done, ...), kind=kLoop, calls=%fused_computation.13 | loop fusion | flops 3962112 | bytes 2881536 | tf_op jit(solution)/shard_map/transpose | solution.py:96
  30.9 8.4 %fusion.6 = f32[1,192,8,128]{1,0,3,2:T(1,128)S(1)} fusion(bf16[1,192,14,134]{1,3,2,0:T(8,128)(2,1)S(1)} %get-tuple-element.31, f32[7,7,1,192]{3,1,0,2:T(8,128)S(1)} %bitcast.124), kind=kOutput, calls=%fused_computation.14 | convolution fusion | flops 115605504 | bytes 1544448 | tf_op jit(solution)/shard_map/conv_general_dilated | solution.py:27
  41.2 2.2 %multiply_convert_fusion = (bf16[768,1024]{1,0:T(8,128)(2,1)}, f32[768,1024]{1,0:T(8,128)S(1)}) fusion(f32[768]{0:T(1024)S(1)} %fusion.32, f32[24,8,8,128]{3,2,1,0:T(8,128)S(1)} %bitcast.110, f32[192]{0:T(256)S(1)} %copy-done.20, f32[192]{0:T(256)S(1)} %copy-done.14, f32[1024]{0:T(1024)S(1)} %get-tuple-element.53, f32[1024]{0:T(1024)S(1)} %get-tuple-element.54, ...), kind=kOutput, calls=%fused_computation.9 | convolution fusion | flops 307888128 | bytes 5913600 | tf_op jit(solution)/shard_map/dot_general | solution.py:45
  43.4 3.3 %fusion.61 = (bf16[768,1024]{1,0:T(8,128)(2,1)S(1)}, f32[768,1024]{1,0:T(8,128)}) fusion(f32[768,1024]{1,0:T(8,128)S(1)} %get-tuple-element.60, f32[768]{0:T(1024)S(1)} %fusion.32, f32[24,8,8,128]{3,2,1,0:T(8,128)S(1)} %convert.2, f32[192]{0:T(256)S(1)} %copy-done.15, bf16[768,387]{1,0:T(8,128)(2,1)S(1)} %all_gather.3), kind=kOutput, calls=%fused_computation.107 | convolution fusion | flops 311033856 | bytes 9049088 | tf_op jit(solution)/shard_map/dot_general | solution.py:45
  49.4 2.1 %fusion.36 = f32[192,192]{1,0:T(8,128)} fusion(bf16[768,1024]{1,0:T(8,128)(2,1)} %copy-done.21, s32[]{:T(128)S(6)} %select_n.2, f32[24,8,8,128]{3,2,1,0:T(8,128)S(1)} %bitcast.111, f32[192]{0:T(256)S(1)} %copy-done.20, f32[192]{0:T(256)S(1)} %copy-done.14, f32[1024]{0:T(1024)S(1)} %get-tuple-element.53, f32[1024]{0:T(1024)S(1)} %get-tuple-element.54, ...), kind=kOutput, calls=%fused_computation.64 | convolution fusion | flops 76677120 | bytes 1337604 | tf_op jit(solution)/shard_map/dot_general | solution.py:45
  54.5 4.7 %collective-permute-start.4 = (bf16[192,3,128]{0,2,1:T(8,128)(2,1)S(1)}, bf16[192,3,128]{0,2,1:T(8,128)(2,1)S(1)}, u32[]{:S(2)}, u32[]{:S(2)}) collective-permute-start(bf16[192,3,128]{0,2,1:T(8,128)(2,1)S(1)} %get-tuple-element.39), channel_id=1, source_target_pairs={{0,16},{1,17},{2,18},{3,19},{4,20},{5,21},{6,22},{7,23},{8,24},{9,... | collective-permute-start | bytes 442376 | tf_op jit(solution)/shard_map/ppermute | solution.py:15
  62.5 4.3 %collective-permute-done.5 = bf16[192,3,128]{0,2,1:T(8,128)(2,1)S(1)} collective-permute-done((bf16[192,3,128]{0,2,1:T(8,128)(2,1)S(1)}, bf16[192,3,128]{0,2,1:T(8,128)(2,1)S(1)}, u32[]{:S(2)}, u32[]{:S(2)}) %collective-permute-start.5) | collective-permute-done | bytes 147488 | tf_op jit(solution)/shard_map/ppermute | solution.py:16
  67.5 4.1 %collective-permute-start.6 = (bf16[192,14,3]{0,2,1:T(4,128)(2,1)}, bf16[192,14,3]{0,2,1:T(4,128)(2,1)}, u32[]{:S(2)}, u32[]{:S(2)}) collective-permute-start(bf16[192,14,3]{0,2,1:T(4,128)(2,1)} %get-tuple-element.32), channel_id=1, source_target_pairs={{0,4},{4,8},{8,12},{1,5},{5,9},{9,13},{2,6},{6,10},{10,14},{3,7},{... | collective-permute-start | bytes 48392 | tf_op jit(solution)/shard_map/ppermute | solution.py:15
  73.6 1.7 %reshape.278 = f32[36864]{0:T(1024)} reshape(f32[192,192]{1,0:T(8,128)} %fusion.36) | data formatting | bytes 294912 | tf_op jit(solution)/shard_map/reshape | solution.py:108
  80.5 4.2 %fusion.15 = f32[8,8,17,192]{3,1,2,0:T(8,128)S(1)} fusion(bf16[192,14,1,7,6]{0,3,4,1,2:T(8,128)(2,1)S(1)} %slice.120, bf16[192,14,1,8,17]{0,3,4,1,2:T(8,128)(2,1)S(1)} %copy.104, pred[8,17]{0,1:T(8,128)(4,1)S(1)} %copy-done.22, f32[7,7,1,192]{3,1,0,2:T(8,128)S(1)} %bitcast.125), kind=kOutput, calls=%fused_computation.24 | convolution fusion | flops 126007296 | bytes 1830280 | tf_op jit(solution)/shard_map/conv_general_dilated | solution.py:27
  85.7 5.2 %multiply_reduce_fusion = (f32[192]{0:T(256)S(1)}, f32[192]{0:T(256)S(1)}, bf16[192,8,128]{2,1,0:T(8,128)(2,1)}, bf16[192,8,128]{2,1,0:T(8,128)(2,1)}) fusion(f32[24,8,8,128]{3,2,1,0:T(8,128)} %copy.118, bf16[192,8,128]{2,1,0:T(8,128)(2,1)} %param.21, f32[192]{0:T(256)S(1)} %copy-done.18, f32[192]{0:T(256)S(1)} %copy-done.17, ...), kind=kLoop, calls=%fused_computation.47 | loop fusion | flops 2358912 | bytes 3148800 | tf_op jit(solution)/shard_map/reduce_sum | solution.py:194
  90.9 1.8 %concatenate.27 = f32[74304]{0:T(1024)S(1)} concatenate(f32[36864]{0:T(1024)S(1)} %copy-done.8, f32[192]{0:T(256)S(1)} %dynamic-slice_reduce_fusion, f32[36864]{0:T(1024)S(1)} %copy-done.9, f32[192]{0:T(256)S(1)} %get-tuple-element.27, f32[192]{0:T(256)S(1)} %get-tuple-element.26), dimensions={0} | concatenate | bytes 594432 | tf_op jit(solution)/shard_map/concatenate | solution.py:108
  92.7 10.0 %shard_map.194 = f32[49,8,192]{2,1,0:T(8,128)} custom-call(f32[8,128,192]{2,1,0:T(8,128)} %get-tuple-element.28.d_ref, f32[14,134,192]{2,1,0:T(8,128)} %get-tuple-element.30.p_ref), custom_call_target="tpu_custom_call" | custom-call | tf_op jit(solution)/shard_map/pallas_call | solution.py:99
  104.0 2.7 %collective-permute-start.12 = (f32[74304]{0:T(1024)S(1)}, f32[74304]{0:T(1024)S(1)}, u32[]{:S(2)}, u32[]{:S(2)}) collective-permute-start(f32[74304]{0:T(1024)S(1)} %add.136), channel_id=1, source_target_pairs={{0,4},{4,0},{8,12},{12,8},{1,5},{5,1},{9,13},{13,9},{2,6},{6,2},{1... | collective-permute-start | bytes 891656 | tf_op jit(solution)/shard_map/ppermute | solution.py:116
  106.7 3.7 %fusion.23 = (f32[192]{0:T(256)S(1)}, f32[192]{0:T(256)S(1)}) fusion(f32[1,192,8,128]{3,2,1,0:T(8,128)S(1)} %copy.94, f32[8,128]{1,0:T(8,128)S(1)} %get-tuple-element.52, f32[8,128]{1,0:T(8,128)S(1)} %get-tuple-element.55, f32[192]{0:T(256)S(1)} %copy-done.13, f32[8,128]{1,0:T(8,128)S(1)} %broadcast_multiply_fusion, f32[8,128]{1,0:T(8,128)S(1)} %multiply_bitcast_fusion, ...), kind=kLoop, calls=%fused_computation.36 | loop fusion | flops 2162304 | bytes 1592320 | tf_op jit(solution)/shard_map/reduce_sum | solution.py:71
  110.5 2.0 %collective-permute-start.8 = (f32[9984]{0:T(1024)S(1)}, f32[9984]{0:T(1024)S(1)}, u32[]{:S(2)}, u32[]{:S(2)}) collective-permute-start(f32[9984]{0:T(1024)S(1)} %concatenate.26), channel_id=1, source_target_pairs={{0,16},{16,0},{1,17},{17,1},{2,18},{18,2},{3,19},{19,3},{4,20},{20... | collective-permute-start | bytes 119816 | tf_op jit(solution)/shard_map/ppermute | solution.py:116
  112.5 2.0 %collective-permute-done.8 = f32[9984]{0:T(1024)S(1)} collective-permute-done((f32[9984]{0:T(1024)S(1)}, f32[9984]{0:T(1024)S(1)}, u32[]{:S(2)}, u32[]{:S(2)}) %collective-permute-start.8) | collective-permute-done | bytes 39968 | tf_op jit(solution)/shard_map/ppermute | solution.py:116
  114.5 4.0 %collective-permute-done.9 = f32[9984]{0:T(1024)S(1)} collective-permute-done((f32[9984]{0:T(1024)S(1)}, f32[9984]{0:T(1024)S(1)}, u32[]{:S(2)}, u32[]{:S(2)}) %collective-permute-start.9) | collective-permute-done | bytes 39968 | tf_op jit(solution)/shard_map/ppermute | solution.py:116
  119.8 5.6 %collective-permute-done.10 = f32[9984]{0:T(1024)S(1)} collective-permute-done((f32[9984]{0:T(1024)S(1)}, f32[9984]{0:T(1024)S(1)}, u32[]{:S(2)}, u32[]{:S(2)}) %collective-permute-start.10) | collective-permute-done | bytes 39968 | tf_op jit(solution)/shard_map/ppermute | solution.py:116
  126.8 9.5 %collective-permute-done.13 = f32[74304]{0:T(1024)S(1)} collective-permute-done((f32[74304]{0:T(1024)S(1)}, f32[74304]{0:T(1024)S(1)}, u32[]{:S(2)}, u32[]{:S(2)}) %collective-permute-start.13) | collective-permute-done | bytes 297248 | tf_op jit(solution)/shard_map/ppermute | solution.py:116
  (121 shorter events, 34.6 us)
Async XLA Ops:
  0.6 9.6 %copy-start.11 = (bf16[192,192]{1,0:T(8,128)(2,1)S(1)}, bf16[192,192]{1,0:T(8,128)(2,1)}, u32[]{:S(2)}) copy-start(bf16[192,192]{1,0:T(8,128)(2,1)} %param.18) | copy-start | bytes 221188
  2.0 18.0 %collective-permute-start = (bf16[192,3,128]{0,2,1:T(8,128)(2,1)S(1)}, bf16[192,3,128]{0,2,1:T(8,128)(2,1)S(1)}, u32[]{:S(2)}, u32[]{:S(2)}) collective-permute-start(bf16[192,3,128]{0,2,1:T(8,128)(2,1)S(1)} %get-tuple-element.41), channel_id=1, source_target_pairs={{0,16},{1,17},{2,18},{3,19},{4,20},{5,21},{6,22},{7,23},{8,24},{9,... | collective-permute-start | bytes 442376 | tf_op jit(solution)/shard_map/ppermute | solution.py:15
  6.9 13.1 %collective-permute-start.1 = (bf16[192,3,128]{0,2,1:T(8,128)(2,1)S(1)}, bf16[192,3,128]{0,2,1:T(8,128)(2,1)S(1)}, u32[]{:S(2)}, u32[]{:S(2)}) collective-permute-start(bf16[192,3,128]{0,2,1:T(8,128)(2,1)S(1)} %get-tuple-element.42), channel_id=1, source_target_pairs={{16,0},{17,1},{18,2},{19,3},{20,4},{21,5},{22,6},{23,7},{24,8},{25... | collective-permute-start | bytes 442376 | tf_op jit(solution)/shard_map/ppermute | solution.py:16
  19.0 6.2 %copy-start.6 = (bf16[192,8,128]{2,1,0:T(8,128)(2,1)S(1)}, bf16[192,8,128]{2,1,0:T(8,128)(2,1)}, u32[]{:S(2)}) copy-start(bf16[192,8,128]{2,1,0:T(8,128)(2,1)} %param.21) | copy-start | bytes 1179652
  19.9 6.4 %copy-start.12 = (f32[7,7,192]{2,1,0:T(8,128)S(1)}, f32[7,7,192]{2,1,0:T(8,128)}, u32[]{:S(2)}) copy-start(f32[7,7,192]{2,1,0:T(8,128)} %param.12) | copy-start | bytes 112900
  20.0 6.4 %collective-permute-start.2 = (bf16[192,14,3]{0,2,1:T(4,128)(2,1)S(1)}, bf16[192,14,3]{0,2,1:T(4,128)(2,1)S(1)}, u32[]{:S(2)}, u32[]{:S(2)}) collective-permute-start(bf16[192,14,3]{0,2,1:T(4,128)(2,1)S(1)} %get-tuple-element.34), channel_id=1, source_target_pairs={{0,4},{4,8},{8,12},{1,5},{5,9},{9,13},{2,6},{6,10},{10,14},{3,7},{... | collective-permute-start | bytes 48392 | tf_op jit(solution)/shard_map/ppermute | solution.py:15
  23.5 5.8 %collective-permute-start.3 = (bf16[192,14,3]{0,2,1:T(4,128)(2,1)S(1)}, bf16[192,14,3]{0,2,1:T(4,128)(2,1)S(1)}, u32[]{:S(2)}, u32[]{:S(2)}) collective-permute-start(bf16[192,14,3]{0,2,1:T(4,128)(2,1)S(1)} %get-tuple-element.35), channel_id=1, source_target_pairs={{4,0},{8,4},{12,8},{5,1},{9,5},{13,9},{6,2},{10,6},{14,10},{7,3},{... | collective-permute-start | bytes 48392 | tf_op jit(solution)/shard_map/ppermute | solution.py:16
  25.3 18.1 %copy-start.3 = (f32[24,8,8,128]{3,2,1,0:T(8,128)}, f32[24,8,8,128]{3,2,1,0:T(8,128)S(1)}, u32[]{:S(2)}) copy-start(f32[24,8,8,128]{3,2,1,0:T(8,128)S(1)} %convert.2) | copy-start | bytes 2359300
  30.9 9.7 %copy-start.13 = (f32[192]{0:T(256)S(1)}, f32[192]{0:T(256)}, u32[]{:S(2)}) copy-start(f32[192]{0:T(256)} %param.13) | copy-start | bytes 2308
  53.0 7.5 %copy-start.4 = (f32[24,8,8,128]{3,2,1,0:T(8,128)S(1)}, f32[24,8,8,128]{3,2,1,0:T(8,128)}, u32[]{:S(2)}) copy-start(f32[24,8,8,128]{3,2,1,0:T(8,128)} %copy-done.3) | copy-start | bytes 2359300
  53.0 7.5 %copy-start.5 = (bf16[768,1024]{1,0:T(8,128)(2,1)S(1)}, bf16[768,1024]{1,0:T(8,128)(2,1)}, u32[]{:S(2)}) copy-start(bf16[768,1024]{1,0:T(8,128)(2,1)} %get-tuple-element.59) | copy-start | bytes 4718596
  53.0 7.5 %copy-start.16 = (f32[192]{0:T(256)S(1)}, f32[192]{0:T(256)}, u32[]{:S(2)}) copy-start(f32[192]{0:T(256)} %param.20) | copy-start | bytes 2308
  54.5 18.5 %copy-start.7 = (bf16[768,192]{1,0:T(8,128)(2,1)S(1)}, bf16[768,192]{1,0:T(8,128)(2,1)}, u32[]{:S(2)}) copy-start(bf16[768,192]{1,0:T(8,128)(2,1)} %get-tuple-element.38) | copy-start | bytes 884740
  54.5 7.9 %collective-permute-start.4 = (bf16[192,3,128]{0,2,1:T(8,128)(2,1)S(1)}, bf16[192,3,128]{0,2,1:T(8,128)(2,1)S(1)}, u32[]{:S(2)}, u32[]{:S(2)}) collective-permute-start(bf16[192,3,128]{0,2,1:T(8,128)(2,1)S(1)} %get-tuple-element.39), channel_id=1, source_target_pairs={{0,16},{1,17},{2,18},{3,19},{4,20},{5,21},{6,22},{7,23},{8,24},{9,... | collective-permute-start | bytes 442376 | tf_op jit(solution)/shard_map/ppermute | solution.py:15
  59.2 7.6 %collective-permute-start.5 = (bf16[192,3,128]{0,2,1:T(8,128)(2,1)S(1)}, bf16[192,3,128]{0,2,1:T(8,128)(2,1)S(1)}, u32[]{:S(2)}, u32[]{:S(2)}) collective-permute-start(bf16[192,3,128]{0,2,1:T(8,128)(2,1)S(1)} %get-tuple-element.40), channel_id=1, source_target_pairs={{16,0},{17,1},{18,2},{19,3},{20,4},{21,5},{22,6},{23,7},{24,8},{25... | collective-permute-start | bytes 442376 | tf_op jit(solution)/shard_map/ppermute | solution.py:16
  67.5 11.0 %collective-permute-start.6 = (bf16[192,14,3]{0,2,1:T(4,128)(2,1)}, bf16[192,14,3]{0,2,1:T(4,128)(2,1)}, u32[]{:S(2)}, u32[]{:S(2)}) collective-permute-start(bf16[192,14,3]{0,2,1:T(4,128)(2,1)} %get-tuple-element.32), channel_id=1, source_target_pairs={{0,4},{4,8},{8,12},{1,5},{5,9},{9,13},{2,6},{6,10},{10,14},{3,7},{... | collective-permute-start | bytes 48392 | tf_op jit(solution)/shard_map/ppermute | solution.py:15
  71.5 6.9 %collective-permute-start.7 = (bf16[192,14,3]{0,2,1:T(4,128)(2,1)}, bf16[192,14,3]{0,2,1:T(4,128)(2,1)}, u32[]{:S(2)}, u32[]{:S(2)}) collective-permute-start(bf16[192,14,3]{0,2,1:T(4,128)(2,1)} %get-tuple-element.33), channel_id=1, source_target_pairs={{4,0},{8,4},{12,8},{5,1},{9,5},{13,9},{6,2},{10,6},{14,10},{7,3},{... | collective-permute-start | bytes 48392 | tf_op jit(solution)/shard_map/ppermute | solution.py:16
  92.7 11.2 %collective-permute-start.11 = (f32[74304]{0:T(1024)S(1)}, f32[74304]{0:T(1024)S(1)}, u32[]{:S(2)}, u32[]{:S(2)}) collective-permute-start(f32[74304]{0:T(1024)S(1)} %concatenate.27), channel_id=1, source_target_pairs={{0,16},{16,0},{1,17},{17,1},{2,18},{18,2},{3,19},{19,3},{4,20},{20... | collective-permute-start | bytes 891656 | tf_op jit(solution)/shard_map/ppermute | solution.py:116
  102.7 7.7 %copy-start.19 = (f32[192]{0:T(256)S(1)}, f32[192]{0:T(256)}, u32[]{:S(2)}) copy-start(f32[192]{0:T(256)} %get-tuple-element.24) | copy-start | bytes 2308
  104.0 21.4 %collective-permute-start.12 = (f32[74304]{0:T(1024)S(1)}, f32[74304]{0:T(1024)S(1)}, u32[]{:S(2)}, u32[]{:S(2)}) collective-permute-start(f32[74304]{0:T(1024)S(1)} %add.136), channel_id=1, source_target_pairs={{0,4},{4,0},{8,12},{12,8},{1,5},{5,1},{9,13},{13,9},{2,6},{6,2},{1... | collective-permute-start | bytes 891656 | tf_op jit(solution)/shard_map/ppermute | solution.py:116
  110.5 4.0 %collective-permute-start.8 = (f32[9984]{0:T(1024)S(1)}, f32[9984]{0:T(1024)S(1)}, u32[]{:S(2)}, u32[]{:S(2)}) collective-permute-start(f32[9984]{0:T(1024)S(1)} %concatenate.26), channel_id=1, source_target_pairs={{0,16},{16,0},{1,17},{17,1},{2,18},{18,2},{3,19},{19,3},{4,20},{20... | collective-permute-start | bytes 119816 | tf_op jit(solution)/shard_map/ppermute | solution.py:116
  114.5 4.0 %collective-permute-start.9 = (f32[9984]{0:T(1024)S(1)}, f32[9984]{0:T(1024)S(1)}, u32[]{:S(2)}, u32[]{:S(2)}) collective-permute-start(f32[9984]{0:T(1024)S(1)} %add.132), channel_id=1, source_target_pairs={{0,4},{4,0},{8,12},{12,8},{1,5},{5,1},{9,13},{13,9},{2,6},{6,2},{1... | collective-permute-start | bytes 119816 | tf_op jit(solution)/shard_map/ppermute | solution.py:116
  118.5 6.9 %collective-permute-start.10 = (f32[9984]{0:T(1024)S(1)}, f32[9984]{0:T(1024)S(1)}, u32[]{:S(2)}, u32[]{:S(2)}) collective-permute-start(f32[9984]{0:T(1024)S(1)} %add.133), channel_id=1, source_target_pairs={{0,8},{4,12},{8,0},{12,4},{1,9},{5,13},{9,1},{13,5},{2,10},{6,14},... | collective-permute-start | bytes 119816 | tf_op jit(solution)/shard_map/ppermute | solution.py:116
  125.4 10.9 %collective-permute-start.13 = (f32[74304]{0:T(1024)S(1)}, f32[74304]{0:T(1024)S(1)}, u32[]{:S(2)}, u32[]{:S(2)}) collective-permute-start(f32[74304]{0:T(1024)S(1)} %add.137), channel_id=1, source_target_pairs={{0,8},{4,12},{8,0},{12,4},{1,9},{5,13},{9,1},{13,5},{2,10},{6,14},... | collective-permute-start | bytes 891656 | tf_op jit(solution)/shard_map/ppermute | solution.py:116
  (13 other events, 29.8 us)

commit v2 on v1

--- a/solution.py
+++ b/solution.py
@@ -103,27 +103,45 @@
     return jnp.sum(partial, axis=1).reshape(side, side, channel_count)
 
 
-def butterfly_sum(values, axes):
-    shapes = [v.shape for v in values]
-    flat = jnp.concatenate([v.reshape(-1) for v in values])
+def flat_pack(values):
+    return jnp.concatenate([v.reshape(-1) for v in values])
+
+
+def flat_unpack(flat, values):
+    out = []
+    offset = 0
+    for v in values:
+        out.append(flat[offset : offset + v.size].reshape(v.shape))
+        offset += v.size
+    return out
+
+
+def butterfly_steps(axes):
+    steps = []
     for axis in axes:
         devices = lax.axis_size(axis)
         if devices & (devices - 1):
-            flat = lax.psum(flat, axis)
+            steps.append((axis, 0))
             continue
         step = 1
         while step < devices:
-            flat = flat + lax.ppermute(flat, axis, [(i, i ^ step) for i in range(devices)])
+            steps.append((axis, step))
             step *= 2
-    out = []
-    offset = 0
-    for shape in shapes:
-        size = 1
-        for s in shape:
-            size *= s
-        out.append(flat[offset : offset + size].reshape(shape))
-        offset += size
-    return out
+    return steps
+
+
+def butterfly_step(flat, axis, step):
+    if step == 0:
+        return lax.psum(flat, axis)
+    devices = lax.axis_size(axis)
+    return flat + lax.ppermute(flat, axis, [(i, i ^ step) for i in range(devices)])
+
+
+def butterfly_sum(values, axes):
+    flat = flat_pack(values)
+    for axis, step in butterfly_steps(axes):
+        flat = butterfly_step(flat, axis, step)
+    return flat_unpack(flat, values)
 
 
 def gathered_weights(w_in, b_in, w_out):
@@ -202,9 +220,9 @@
     grad_w_out = contract(hidden_own, g_out, 1, 1)
     grad_b_in = jnp.sum(d_pre_own, axis=1)
     grad_w_in = contract(normalized_output, g_pre_own, 1, 1)
-    (grad_w_in, grad_b_in, grad_w_out, grad_b_out, grad_layer_scale) = butterfly_sum(
-        (grad_w_in, grad_b_in, grad_w_out, grad_b_out, grad_layer_scale), ("row", "col")
-    )
+    early = (grad_w_in, grad_b_in, grad_w_out, grad_b_out, grad_layer_scale)
+    early_flat = flat_pack(early)
+    pending = butterfly_steps(("row", "col"))
     w_in_blocks = jnp.transpose(w_in_all.reshape(channel_count, blocks, share), (1, 0, 2))
     g_pre_blocks = g_pre.reshape(blocks, share, pixel_count)
     dn_partials = lax.dot_general(
@@ -214,16 +232,28 @@
         preferred_element_type=jnp.float32,
     )
     normalized_gradient = jnp.sum(dn_partials.astype(jnp.bfloat16).astype(jnp.float32), axis=0)
+    if pending:
+        early_flat = butterfly_step(early_flat, *pending.pop(0))
+        early_flat, normalized_gradient = lax.optimization_barrier((early_flat, normalized_gradient))
     convolved_gradient, gain_portion, bias_portion = layer_norm_backward(
         normalized_gradient, standardized_input, inverse_deviation, norm_gain
     )
     grad_conv_bias = jnp.sum(convolved_gradient, axis=1)
     d_grid = convolved_gradient.reshape(channel_count, tile_rows, tile_cols)
+    if pending:
+        early_flat = butterfly_step(early_flat, *pending.pop(0))
+        early_flat, d_grid = lax.optimization_barrier((early_flat, d_grid))
     grad_kernel = kernel_grad(d_grid, padded)
     (grad_kernel, grad_conv_bias, gain_portion, bias_portion) = butterfly_sum(
         (grad_kernel, grad_conv_bias, gain_portion, bias_portion), ("row", "col")
     )
     d_padded = extended(shortened(d_grid), (("row", 1), ("col", 2)), 3).astype(d_grid.dtype)
+    if pending:
+        early_flat = butterfly_step(early_flat, *pending.pop(0))
+        early_flat, d_padded = lax.optimization_barrier((early_flat, d_padded))
+    for axis, step in pending:
+        early_flat = butterfly_step(early_flat, axis, step)
+    (grad_w_in, grad_b_in, grad_w_out, grad_b_out, grad_layer_scale) = flat_unpack(early_flat, early)
     grad_feature = (cotangent.astype(jnp.float32) + depthwise(d_padded, kernel[::-1, ::-1])).astype(
         jnp.bfloat16
     )

time: 139 us -> 155 us (1.12)
  matrix products: 22.5 us -> 33 us
  other arithmetic: 20 us -> 29.2 us
  waiting for transfers between devices: 29.8 us -> 21.7 us
  starting transfers between devices: 28.6 us -> 31.7 us
    reduce_sum x1, other arithmetic: 0.27 us -> 14.9 us  [layer_norm_forward(): variance = jnp.mean(centered_values * centered_values, axis=0)]
    conv_general_dilated x2, matrix products: 12.6 us -> 21.5 us  [depthwise(): lax.conv_general_dilated(padded[None], kernel[:, :, None, :], (1, 1), 'VA...]
    ppermute x6, waiting for transfers between devices: 21.1 us -> 12.6 us  [butterfly_step(): lax.ppermute(flat, axis, [(i, i ^ step) for i in range(devices)])]
    conv_general_dilated x5 -> x6, local copies, waits for them, and re-layouts: 2.08 us -> 7.13 us  [depthwise(): lax.conv_general_dilated(padded[None], kernel[:, :, None, :], (1, 1), 'VA...]
    ppermute x6, starting transfers between devices: 6.1 us -> 10.3 us  [butterfly_step(): lax.ppermute(flat, axis, [(i, i ^ step) for i in range(devices)])]
    reduce_sum x1, other arithmetic: 3.67 us -> 0.56 us  [layer_norm_backward(): jnp.sum(normalized_gradient * standardized_input, axis=1)]
    reshape x2, local copies, waits for them, and re-layouts: 2.49 us -> 0.24 us  [flat_pack(): return jnp.concatenate([v.reshape(-1) for v in values])]
    unnamed x52 -> x42, local copies, waits for them, and re-layouts: 5.3 us -> 4.2 us
  transfers between devices with their start and end apart: 14 -> 14, of which waited for: 7 -> 8; matrix products, arithmetic and copies ran while one was open for 12% -> 7% of each run, Pallas kernels for 7% -> 0%
where the time goes in v2:
time: 155 us; the launch traced here: 154 us
  matrix products  33 us (21%)
  starting transfers between devices  31.7 us (20%)
  other arithmetic  29.2 us (19%)
  waiting for transfers between devices  21.7 us (14%)
  local copies, waits for them, and re-layouts  18.8 us (12%)
  Pallas kernels  10.1 us (7%)
  blocking collectives  8.6 us (6%)
    conv_general_dilated x2, matrix products, depthwise(): lax.conv_general_dilated(padded[None], kernel[:, :, None, :], (1, 1), 'VA...  21.5 us
    ppermute x4, starting transfers between devices, extended(): before = lax.ppermute(last, axis, up)  16.3 us
    reduce_sum x1, other arithmetic, layer_norm_forward(): variance = jnp.mean(centered_values * centered_values, axis=0)  14.9 us
    ppermute x6, waiting for transfers between devices, butterfly_step(): lax.ppermute(flat, axis, [(i, i ^ step) for i in range(devices)])  12.6 us
    ppermute x6, starting transfers between devices, butterfly_step(): lax.ppermute(flat, axis, [(i, i ^ step) for i in range(devices)])  10.3 us
    pallas_call x1, Pallas kernels, kernel_grad(): pl.pallas_call(kernel_grad_body, out_shape=jax.ShapeDtypeStruct((side * s...  10.1 us
    all_gather x1, blocking collectives, gathered_weights(): full = lax.all_gather(packed, 'chan', axis=0, tiled=True)  8.6 us
    ppermute x4, waiting for transfers between devices, extended(): after = lax.ppermute(leading, axis, down)  7.47 us
  transfers between devices with their start and end apart: 14, of which 8 were waited for; matrix products, arithmetic and copies ran while one was open for 7% of the time, Pallas kernels for 0%

profile of v2, /device:TPU:0, one launch (start us, length us, event | category | flops | bytes accessed | tf_op | source)
XLA Modules:
  0.0 154.3 jit_solution(7145607886275164408)
XLA Ops:
  2.0 4.9 %collective-permute-start = (bf16[192,3,128]{0,2,1:T(8,128)(2,1)S(1)}, bf16[192,3,128]{0,2,1:T(8,128)(2,1)S(1)}, u32[]{:S(2)}, u32[]{:S(2)}) collective-permute-start(bf16[192,3,128]{0,2,1:T(8,128)(2,1)S(1)} %get-tuple-element.53), channel_id=1, source_target_pairs={{0,16},{1,17},{2,18},{3,19},{4,20},{5,21},{6,22},{7,23},{8,24},{9,... | collective-permute-start | bytes 442376 | tf_op jit(solution)/shard_map/ppermute | solution.py:15
  10.4 8.6 %all_gather.3 = bf16[768,387]{1,0:T(8,128)(2,1)S(1)} all-gather(bf16[192,387]{1,0:T(8,128)(2,1)S(1)} %concatenate.21), channel_id=1, replica_groups=mesh['row'=2,'col'=4,'chan'=4] {'chan'}, dimensions={0}, use_global_device_ids=true | all-gather | bytes 743040 | tf_op jit(solution)/shard_map/all_gather | solution.py:156
  20.0 3.5 %collective-permute-start.2 = (bf16[192,14,3]{0,2,1:T(4,128)(2,1)S(1)}, bf16[192,14,3]{0,2,1:T(4,128)(2,1)S(1)}, u32[]{:S(2)}, u32[]{:S(2)}) collective-permute-start(bf16[192,14,3]{0,2,1:T(4,128)(2,1)S(1)} %get-tuple-element.46), channel_id=1, source_target_pairs={{0,4},{4,8},{8,12},{1,5},{5,9},{9,13},{2,6},{6,10},{10,14},{3,7},{... | collective-permute-start | bytes 48392 | tf_op jit(solution)/shard_map/ppermute | solution.py:15
  26.2 3.1 %collective-permute-done.3 = bf16[192,14,3]{0,2,1:T(4,128)(2,1)S(1)} collective-permute-done((bf16[192,14,3]{0,2,1:T(4,128)(2,1)S(1)}, bf16[192,14,3]{0,2,1:T(4,128)(2,1)S(1)}, u32[]{:S(2)}, u32[]{:S(2)}) %collective-permute-start.3) | collective-permute-done | bytes 16160 | tf_op jit(solution)/shard_map/ppermute | solution.py:16
  30.9 17.3 %add_reduce_fusion = (f32[8,128]{1,0:T(8,128)S(1)}, f32[1,192,8,128]{1,0,3,2:T(1,128)S(1)}) fusion(f32[192]{0:T(256)S(1)} %copy-done.8, f32[7,7,1,192]{3,1,0,2:T(8,128)S(1)} %bitcast.97, bf16[1,192,14,134]{1,3,2,0:T(8,128)(2,1)S(1)} %get-tuple-element.43), kind=kOutput, calls=%fused_computation.44 | convolution fusion | flops 115997696 | bytes 1549312 | tf_op jit(solution)/shard_map/conv_general_dilated | solution.py:27
  49.4 14.9 %multiply_reduce_fusion = f32[8,128]{1,0:T(8,128)S(1)} fusion(f32[1,192,8,128]{1,0,3,2:T(1,128)S(1)} %get-tuple-element.69, f32[8,128]{1,0:T(8,128)S(1)} %get-tuple-element.64, f32[192]{0:T(256)S(1)} %copy-done.8), kind=kLoop, calls=%fused_computation.24 | loop fusion | flops 785408 | bytes 795392 | tf_op jit(solution)/shard_map/reduce_sum | solution.py:53
  64.4 2.2 %multiply_convert_fusion = (bf16[768,1024]{1,0:T(8,128)(2,1)}, f32[768,1024]{1,0:T(8,128)S(1)}) fusion(f32[768]{0:T(1024)S(1)} %fusion.21, f32[192]{0:T(256)S(1)} %copy-done.17, f32[192]{0:T(256)S(1)} %copy-done.10, f32[1024]{0:T(1024)S(1)} %rsqrt_bitcast_fusion, f32[1024]{0:T(1024)S(1)} %get-tuple-element.63, f32[192]{0:T(256)S(1)} %copy-done.8, ...), kind=kOutput, calls=%fused_computation.8 | convolution fusion | flops 307888128 | bytes 5913600 | tf_op jit(solution)/shard_map/dot_general | solution.py:45
  66.6 3.3 %fusion.48 = (bf16[768,1024]{1,0:T(8,128)(2,1)S(1)}, f32[768,1024]{1,0:T(8,128)}) fusion(f32[768,1024]{1,0:T(8,128)S(1)} %get-tuple-element.71, f32[768]{0:T(1024)S(1)} %fusion.21, f32[24,8,8,128]{3,2,1,0:T(8,128)S(1)} %copy-done.2, f32[192]{0:T(256)S(1)} %copy-done.13, bf16[768,387]{1,0:T(8,128)(2,1)S(1)} %all_gather.3), kind=kOutput, calls=%fused_computation.92 | convolution fusion | flops 311033856 | bytes 9049088 | tf_op jit(solution)/shard_map/dot_general | solution.py:45
  71.5 1.8 %dynamic-slice_reduce_fusion = f32[192]{0:T(256)} fusion(f32[768,1024]{1,0:T(8,128)} %get-tuple-element.73, s32[]{:T(128)S(6)} %select_n.2), kind=kLoop, calls=%fused_computation.40 | loop fusion | flops 196416 | bytes 787204 | tf_op jit(solution)/shard_map/reduce_sum | solution.py:221
  74.8 2.1 %convert_reduce_fusion.1 = f32[192,1024]{1,0:T(8,128)S(1)} fusion(bf16[4,192,192]{2,1,0:T(8,128)(2,1)S(1)} %bitcast.95, bf16[4,192,1024]{2,1,0:T(8,128)(2,1)} %bitcast.92), kind=kOutput, calls=%fused_computation.7 | convolution fusion | flops 304152576 | bytes 2654208 | tf_op jit(solution)/shard_map/dot_general | solution.py:196
  77.3 3.7 %multiply_reduce_fusion.3 = (f32[192]{0:T(256)S(1)}, f32[192]{0:T(256)S(1)}, bf16[192,8,128]{2,1,0:T(8,128)(2,1)}) fusion(f32[24,8,8,128]{3,2,1,0:T(8,128)S(1)} %copy.81, bf16[192,8,128]{2,1,0:T(8,128)(2,1)S(1)} %copy-done.1, f32[192]{0:T(256)S(1)} %copy-done.16, f32[192]{0:T(256)S(1)} %copy-done.15, bf16[192,8,128]{2,1,0:T(8,128)(2,1)S(1)} %copy-done.4), kind=kLoop, calls=%fused_computation.38 | loop fusion | flops 1965696 | bytes 1969152 | tf_op jit(solution)/shard_map/reduce_sum | solution.py:212
  82.7 2.7 %collective-permute-start.4 = (f32[74304]{0:T(1024)S(1)}, f32[74304]{0:T(1024)S(1)}, u32[]{:S(2)}, u32[]{:S(2)}) collective-permute-start(f32[74304]{0:T(1024)S(1)} %concatenate.24), channel_id=1, source_target_pairs={{0,16},{16,0},{1,17},{17,1},{2,18},{18,2},{3,19},{19,3},{4,20},{20... | collective-permute-start | bytes 891656 | tf_op jit(solution)/shard_map/ppermute | solution.py:137
  85.6 2.0 %convert_reduce_fusion = f32[192,1024]{1,0:T(8,128)S(1)} fusion(bf16[4,192,1024]{2,1,0:T(8,128)(2,1)} %bitcast.94, bf16[192,4,192]{2,0,1:T(8,128)(2,1)S(1)} %copy.67), kind=kOutput, calls=%fused_computation.6 | convolution fusion | flops 304152576 | bytes 2654208 | tf_op jit(solution)/shard_map/dot_general | solution.py:228
  87.7 3.9 %collective-permute-done.4 = f32[74304]{0:T(1024)S(1)} collective-permute-done((f32[74304]{0:T(1024)S(1)}, f32[74304]{0:T(1024)S(1)}, u32[]{:S(2)}, u32[]{:S(2)}) %collective-permute-start.4) | collective-permute-done | bytes 297248 | tf_op jit(solution)/shard_map/ppermute | solution.py:137
  95.7 3.9 %collective-permute-done.5 = f32[74304]{0:T(1024)S(1)} collective-permute-done((f32[74304]{0:T(1024)S(1)}, f32[74304]{0:T(1024)S(1)}, u32[]{:S(2)}, u32[]{:S(2)}) %collective-permute-start.5) | collective-permute-done | bytes 297248 | tf_op jit(solution)/shard_map/ppermute | solution.py:137
  99.6 10.1 %shard_map.194 = f32[49,8,192]{2,1,0:T(8,128)} custom-call(f32[8,128,192]{2,1,0:T(8,128)} %bitcast.82, f32[14,134,192]{2,1,0:T(8,128)} %get-tuple-element.42.p_ref), custom_call_target="tpu_custom_call" | custom-call | tf_op jit(solution)/shard_map/pallas_call | solution.py:99
  112.4 2.5 %collective-permute-done.11 = f32[9984]{0:T(1024)S(1)} collective-permute-done((f32[9984]{0:T(1024)S(1)}, f32[9984]{0:T(1024)S(1)}, u32[]{:S(2)}, u32[]{:S(2)}) %collective-permute-start.11) | collective-permute-done | bytes 39968 | tf_op jit(solution)/shard_map/ppermute | solution.py:137
  116.7 2.3 %collective-permute-done.12 = f32[9984]{0:T(1024)S(1)} collective-permute-done((f32[9984]{0:T(1024)S(1)}, f32[9984]{0:T(1024)S(1)}, u32[]{:S(2)}, u32[]{:S(2)}) %collective-permute-start.12) | collective-permute-done | bytes 39968 | tf_op jit(solution)/shard_map/ppermute | solution.py:137
  119.0 2.6 %collective-permute-start.13 = (f32[9984]{0:T(1024)S(1)}, f32[9984]{0:T(1024)S(1)}, u32[]{:S(2)}, u32[]{:S(2)}) collective-permute-start(f32[9984]{0:T(1024)S(1)} %add.126), channel_id=1, source_target_pairs={{0,8},{4,12},{8,0},{12,4},{1,9},{5,13},{9,1},{13,5},{2,10},{6,14},... | collective-permute-start | bytes 119816 | tf_op jit(solution)/shard_map/ppermute | solution.py:137
  121.6 3.4 %collective-permute-start.7 = (bf16[192,3,128]{0,2,1:T(8,128)(2,1)S(1)}, bf16[192,3,128]{0,2,1:T(8,128)(2,1)S(1)}, u32[]{:S(2)}, u32[]{:S(2)}) collective-permute-start(bf16[192,3,128]{0,2,1:T(8,128)(2,1)S(1)} %get-tuple-element.51), channel_id=1, source_target_pairs={{0,16},{1,17},{2,18},{3,19},{4,20},{5,21},{6,22},{7,23},{8,24},{9,... | collective-permute-start | bytes 442376 | tf_op jit(solution)/shard_map/ppermute | solution.py:15
  128.1 4.4 %collective-permute-done.8 = bf16[192,3,128]{0,2,1:T(8,128)(2,1)S(1)} collective-permute-done((bf16[192,3,128]{0,2,1:T(8,128)(2,1)S(1)}, bf16[192,3,128]{0,2,1:T(8,128)(2,1)S(1)}, u32[]{:S(2)}, u32[]{:S(2)}) %collective-permute-start.8) | collective-permute-done | bytes 147488 | tf_op jit(solution)/shard_map/ppermute | solution.py:16
  133.9 4.5 %collective-permute-start.9 = (bf16[192,14,3]{0,2,1:T(4,128)(2,1)S(1)}, bf16[192,14,3]{0,2,1:T(4,128)(2,1)S(1)}, u32[]{:S(2)}, u32[]{:S(2)}) collective-permute-start(bf16[192,14,3]{0,2,1:T(4,128)(2,1)S(1)} %get-tuple-element.44), channel_id=1, source_target_pairs={{0,4},{4,8},{8,12},{1,5},{5,9},{9,13},{2,6},{6,10},{10,14},{3,7},{... | collective-permute-start | bytes 48392 | tf_op jit(solution)/shard_map/ppermute | solution.py:15
  141.2 3.7 %reshape.152 = f32[192,14,1,8,17]{0,2,4,3,1:T(1,128)} reshape(f32[192,14,1,136]{0,3,1,2:T(8,128)S(1)} %pad) | data formatting | bytes 2924544 | tf_op jit(solution)/shard_map/conv_general_dilated | solution.py:27
  146.7 4.3 %fusion.14 = f32[8,8,17,192]{3,1,2,0:T(8,128)S(1)} fusion(f32[192,14,1,7,6]{0,3,4,1,2:T(8,128)S(1)} %slice.120, f32[192,14,1,8,17]{0,3,4,1,2:T(8,128)S(1)} %copy.70, pred[8,17]{0,1:T(8,128)(4,1)S(1)} %copy-done.18, f32[7,7,1,192]{3,1,0,2:T(8,128)S(1)} %bitcast.98), kind=kOutput, calls=%fused_computation.23 | convolution fusion | flops 124523520 | bytes 2787208 | tf_op jit(solution)/shard_map/conv_general_dilated | solution.py:27
  (110 shorter events, 37.5 us)
Async XLA Ops:
  0.6 9.6 %copy-start.6 = (bf16[192,192]{1,0:T(8,128)(2,1)S(1)}, bf16[192,192]{1,0:T(8,128)(2,1)}, u32[]{:S(2)}) copy-start(bf16[192,192]{1,0:T(8,128)(2,1)} %param.18) | copy-start | bytes 221188
  2.0 18.0 %collective-permute-start = (bf16[192,3,128]{0,2,1:T(8,128)(2,1)S(1)}, bf16[192,3,128]{0,2,1:T(8,128)(2,1)S(1)}, u32[]{:S(2)}, u32[]{:S(2)}) collective-permute-start(bf16[192,3,128]{0,2,1:T(8,128)(2,1)S(1)} %get-tuple-element.53), channel_id=1, source_target_pairs={{0,16},{1,17},{2,18},{3,19},{4,20},{5,21},{6,22},{7,23},{8,24},{9,... | collective-permute-start | bytes 442376 | tf_op jit(solution)/shard_map/ppermute | solution.py:15
  6.9 13.1 %collective-permute-start.1 = (bf16[192,3,128]{0,2,1:T(8,128)(2,1)S(1)}, bf16[192,3,128]{0,2,1:T(8,128)(2,1)S(1)}, u32[]{:S(2)}, u32[]{:S(2)}) collective-permute-start(bf16[192,3,128]{0,2,1:T(8,128)(2,1)S(1)} %get-tuple-element.54), channel_id=1, source_target_pairs={{16,0},{17,1},{18,2},{19,3},{20,4},{21,5},{22,6},{23,7},{24,8},{25... | collective-permute-start | bytes 442376 | tf_op jit(solution)/shard_map/ppermute | solution.py:16
  19.0 6.2 %copy-start.1 = (bf16[192,8,128]{2,1,0:T(8,128)(2,1)S(1)}, bf16[192,8,128]{2,1,0:T(8,128)(2,1)}, u32[]{:S(2)}) copy-start(bf16[192,8,128]{2,1,0:T(8,128)(2,1)} %param.21) | copy-start | bytes 1179652
  20.0 6.2 %collective-permute-start.2 = (bf16[192,14,3]{0,2,1:T(4,128)(2,1)S(1)}, bf16[192,14,3]{0,2,1:T(4,128)(2,1)S(1)}, u32[]{:S(2)}, u32[]{:S(2)}) collective-permute-start(bf16[192,14,3]{0,2,1:T(4,128)(2,1)S(1)} %get-tuple-element.46), channel_id=1, source_target_pairs={{0,4},{4,8},{8,12},{1,5},{5,9},{9,13},{2,6},{6,10},{10,14},{3,7},{... | collective-permute-start | bytes 48392 | tf_op jit(solution)/shard_map/ppermute | solution.py:15
  23.5 5.8 %collective-permute-start.3 = (bf16[192,14,3]{0,2,1:T(4,128)(2,1)S(1)}, bf16[192,14,3]{0,2,1:T(4,128)(2,1)S(1)}, u32[]{:S(2)}, u32[]{:S(2)}) collective-permute-start(bf16[192,14,3]{0,2,1:T(4,128)(2,1)S(1)} %get-tuple-element.47), channel_id=1, source_target_pairs={{4,0},{8,4},{12,8},{5,1},{9,5},{13,9},{6,2},{10,6},{14,10},{7,3},{... | collective-permute-start | bytes 48392 | tf_op jit(solution)/shard_map/ppermute | solution.py:16
  26.2 4.7 %copy-start.7 = (f32[7,7,192]{2,1,0:T(8,128)S(1)}, f32[7,7,192]{2,1,0:T(8,128)}, u32[]{:S(2)}) copy-start(f32[7,7,192]{2,1,0:T(8,128)} %param.12) | copy-start | bytes 112900
  26.2 4.7 %copy-start.8 = (f32[192]{0:T(256)S(1)}, f32[192]{0:T(256)}, u32[]{:S(2)}) copy-start(f32[192]{0:T(256)} %param.13) | copy-start | bytes 2308
  48.2 16.2 %copy-start.10 = (f32[192]{0:T(256)S(1)}, f32[192]{0:T(256)}, u32[]{:S(2)}) copy-start(f32[192]{0:T(256)} %param.14) | copy-start | bytes 2308
  48.2 16.2 %copy-start.17 = (f32[192]{0:T(256)S(1)}, f32[192]{0:T(256)}, u32[]{:S(2)}) copy-start(f32[192]{0:T(256)} %param.15) | copy-start | bytes 2308
  77.0 4.1 %copy-start.12 = (f32[192]{0:T(256)S(1)}, f32[192]{0:T(256)}, u32[]{:S(2)}) copy-start(f32[192]{0:T(256)} %dynamic-slice_reduce_fusion) | copy-start | bytes 2308
  82.7 8.8 %collective-permute-start.4 = (f32[74304]{0:T(1024)S(1)}, f32[74304]{0:T(1024)S(1)}, u32[]{:S(2)}, u32[]{:S(2)}) collective-permute-start(f32[74304]{0:T(1024)S(1)} %concatenate.24), channel_id=1, source_target_pairs={{0,16},{16,0},{1,17},{17,1},{2,18},{18,2},{3,19},{19,3},{4,20},{20... | collective-permute-start | bytes 891656 | tf_op jit(solution)/shard_map/ppermute | solution.py:137
  85.6 6.0 %copy-start.9 = (f32[192]{0:T(256)S(1)}, f32[192]{0:T(256)}, u32[]{:S(2)}) copy-start(f32[192]{0:T(256)} %param.13) | copy-start | bytes 2308
  85.6 6.0 %copy-start.11 = (f32[192]{0:T(256)S(1)}, f32[192]{0:T(256)}, u32[]{:S(2)}) copy-start(f32[192]{0:T(256)} %param.14) | copy-start | bytes 2308
  92.2 7.3 %collective-permute-start.5 = (f32[74304]{0:T(1024)S(1)}, f32[74304]{0:T(1024)S(1)}, u32[]{:S(2)}, u32[]{:S(2)}) collective-permute-start(f32[74304]{0:T(1024)S(1)} %add.121), channel_id=1, source_target_pairs={{0,4},{4,0},{8,12},{12,8},{1,5},{5,1},{9,13},{13,9},{2,6},{6,2},{1... | collective-permute-start | bytes 891656 | tf_op jit(solution)/shard_map/ppermute | solution.py:137
  99.6 17.0 %copy-start = (f32[192,1024]{0,1:T(8,128)S(1)}, f32[192,1024]{0,1:T(8,128)}, u32[]{:S(2)}) copy-start(f32[192,1024]{0,1:T(8,128)} %copy.68) | copy-start | bytes 2359300
  111.0 4.0 %collective-permute-start.11 = (f32[9984]{0:T(1024)S(1)}, f32[9984]{0:T(1024)S(1)}, u32[]{:S(2)}, u32[]{:S(2)}) collective-permute-start(f32[9984]{0:T(1024)S(1)} %concatenate.27), channel_id=1, source_target_pairs={{0,16},{16,0},{1,17},{17,1},{2,18},{18,2},{3,19},{19,3},{4,20},{20... | collective-permute-start | bytes 119816 | tf_op jit(solution)/shard_map/ppermute | solution.py:137
  115.0 4.0 %collective-permute-start.12 = (f32[9984]{0:T(1024)S(1)}, f32[9984]{0:T(1024)S(1)}, u32[]{:S(2)}, u32[]{:S(2)}) collective-permute-start(f32[9984]{0:T(1024)S(1)} %add.125), channel_id=1, source_target_pairs={{0,4},{4,0},{8,12},{12,8},{1,5},{5,1},{9,13},{13,9},{2,6},{6,2},{1... | collective-permute-start | bytes 119816 | tf_op jit(solution)/shard_map/ppermute | solution.py:137
  119.0 7.7 %collective-permute-start.13 = (f32[9984]{0:T(1024)S(1)}, f32[9984]{0:T(1024)S(1)}, u32[]{:S(2)}, u32[]{:S(2)}) collective-permute-start(f32[9984]{0:T(1024)S(1)} %add.126), channel_id=1, source_target_pairs={{0,8},{4,12},{8,0},{12,4},{1,9},{5,13},{9,1},{13,5},{2,10},{6,14},... | collective-permute-start | bytes 119816 | tf_op jit(solution)/shard_map/ppermute | solution.py:137
  121.6 6.5 %collective-permute-start.7 = (bf16[192,3,128]{0,2,1:T(8,128)(2,1)S(1)}, bf16[192,3,128]{0,2,1:T(8,128)(2,1)S(1)}, u32[]{:S(2)}, u32[]{:S(2)}) collective-permute-start(bf16[192,3,128]{0,2,1:T(8,128)(2,1)S(1)} %get-tuple-element.51), channel_id=1, source_target_pairs={{0,16},{1,17},{2,18},{3,19},{4,20},{5,21},{6,22},{7,23},{8,24},{9,... | collective-permute-start | bytes 442376 | tf_op jit(solution)/shard_map/ppermute | solution.py:15
  125.0 7.6 %collective-permute-start.8 = (bf16[192,3,128]{0,2,1:T(8,128)(2,1)S(1)}, bf16[192,3,128]{0,2,1:T(8,128)(2,1)S(1)}, u32[]{:S(2)}, u32[]{:S(2)}) collective-permute-start(bf16[192,3,128]{0,2,1:T(8,128)(2,1)S(1)} %get-tuple-element.52), channel_id=1, source_target_pairs={{16,0},{17,1},{18,2},{19,3},{20,4},{21,5},{22,6},{23,7},{24,8},{25... | collective-permute-start | bytes 442376 | tf_op jit(solution)/shard_map/ppermute | solution.py:16
  126.3 14.0 %collective-permute-start.6 = (f32[74304]{0:T(1024)S(1)}, f32[74304]{0:T(1024)S(1)}, u32[]{:S(2)}, u32[]{:S(2)}) collective-permute-start(f32[74304]{0:T(1024)S(1)} %add.122), channel_id=1, source_target_pairs={{0,8},{4,12},{8,0},{12,4},{1,9},{5,13},{9,1},{13,5},{2,10},{6,14},... | collective-permute-start | bytes 891656 | tf_op jit(solution)/shard_map/ppermute | solution.py:137
  132.6 7.2 %collective-permute-start.10 = (bf16[192,14,3]{0,2,1:T(4,128)(2,1)S(1)}, bf16[192,14,3]{0,2,1:T(4,128)(2,1)S(1)}, u32[]{:S(2)}, u32[]{:S(2)}) collective-permute-start(bf16[192,14,3]{0,2,1:T(4,128)(2,1)S(1)} %get-tuple-element.45), channel_id=1, source_target_pairs={{4,0},{8,4},{12,8},{5,1},{9,5},{13,9},{6,2},{10,6},{14,10},{7,3},{... | collective-permute-start | bytes 48392 | tf_op jit(solution)/shard_map/ppermute | solution.py:16
  133.9 6.1 %collective-permute-start.9 = (bf16[192,14,3]{0,2,1:T(4,128)(2,1)S(1)}, bf16[192,14,3]{0,2,1:T(4,128)(2,1)S(1)}, u32[]{:S(2)}, u32[]{:S(2)}) collective-permute-start(bf16[192,14,3]{0,2,1:T(4,128)(2,1)S(1)} %get-tuple-element.44), channel_id=1, source_target_pairs={{0,4},{4,8},{8,12},{1,5},{5,9},{9,13},{2,6},{6,10},{10,14},{3,7},{... | collective-permute-start | bytes 48392 | tf_op jit(solution)/shard_map/ppermute | solution.py:15
  (9 other events, 22.1 us)

commit v3 on v1

--- a/solution.py
+++ b/solution.py
@@ -202,9 +202,6 @@
     grad_w_out = contract(hidden_own, g_out, 1, 1)
     grad_b_in = jnp.sum(d_pre_own, axis=1)
     grad_w_in = contract(normalized_output, g_pre_own, 1, 1)
-    (grad_w_in, grad_b_in, grad_w_out, grad_b_out, grad_layer_scale) = butterfly_sum(
-        (grad_w_in, grad_b_in, grad_w_out, grad_b_out, grad_layer_scale), ("row", "col")
-    )
     w_in_blocks = jnp.transpose(w_in_all.reshape(channel_count, blocks, share), (1, 0, 2))
     g_pre_blocks = g_pre.reshape(blocks, share, pixel_count)
     dn_partials = lax.dot_general(
@@ -220,8 +217,29 @@
     grad_conv_bias = jnp.sum(convolved_gradient, axis=1)
     d_grid = convolved_gradient.reshape(channel_count, tile_rows, tile_cols)
     grad_kernel = kernel_grad(d_grid, padded)
-    (grad_kernel, grad_conv_bias, gain_portion, bias_portion) = butterfly_sum(
-        (grad_kernel, grad_conv_bias, gain_portion, bias_portion), ("row", "col")
+    (
+        grad_kernel,
+        grad_conv_bias,
+        gain_portion,
+        bias_portion,
+        grad_w_in,
+        grad_b_in,
+        grad_w_out,
+        grad_b_out,
+        grad_layer_scale,
+    ) = butterfly_sum(
+        (
+            grad_kernel,
+            grad_conv_bias,
+            gain_portion,
+            bias_portion,
+            grad_w_in,
+            grad_b_in,
+            grad_w_out,
+            grad_b_out,
+            grad_layer_scale,
+        ),
+        ("row", "col"),
     )
     d_padded = extended(shortened(d_grid), (("row", 1), ("col", 2)), 3).astype(d_grid.dtype)
     grad_feature = (cotangent.astype(jnp.float32) + depthwise(d_padded, kernel[::-1, ::-1])).astype(

time: 139 us -> 139 us (level)
  waiting for transfers between devices: 29.8 us -> 31.8 us
    ppermute x6 -> x3, waiting for transfers between devices: 21.1 us -> 24.2 us  [butterfly_sum(): lax.ppermute(flat, axis, [(i, i ^ step) for i in range(devices)])]
    ppermute x6 -> x3, starting transfers between devices: 6.1 us -> 5.31 us  [butterfly_sum(): lax.ppermute(flat, axis, [(i, i ^ step) for i in range(devices)])]
  transfers between devices with their start and end apart: 14 -> 11, of which waited for: 7 -> 6; matrix products, arithmetic and copies ran while one was open for 12% -> 11% of each run, Pallas kernels for 7% -> 7%
where the time goes in v3:
time: 139 us
  waiting for transfers between devices  31.8 us (23%)
  starting transfers between devices  27.6 us (20%)
  matrix products  22.4 us (16%)
  other arithmetic  19.2 us (14%)
  local copies, waits for them, and re-layouts  17.6 us (13%)
  Pallas kernels  10.2 us (7%)
  blocking collectives  8.6 us (6%)
    ppermute x3, waiting for transfers between devices, butterfly_sum(): lax.ppermute(flat, axis, [(i, i ^ step) for i in range(devices)])  24.2 us
    ppermute x4, starting transfers between devices, extended(): before = lax.ppermute(last, axis, up)  17.1 us
    conv_general_dilated x2, matrix products, depthwise(): lax.conv_general_dilated(padded[None], kernel[:, :, None, :], (1, 1), 'VA...  12.6 us
    pallas_call x1, Pallas kernels, kernel_grad(): pl.pallas_call(kernel_grad_body, out_shape=jax.ShapeDtypeStruct((side * s...  10.2 us
    all_gather x1, blocking collectives, gathered_weights(): full = lax.all_gather(packed, 'chan', axis=0, tiled=True)  8.6 us
    dot_general x4, matrix products, contract(): lax.dot_general(left, right, (((dim_left,), (dim_right,)), ((), ())), pre...  7.96 us
    ppermute x4, waiting for transfers between devices, extended(): after = lax.ppermute(leading, axis, down)  6.69 us
    ppermute x3, starting transfers between devices, butterfly_sum(): lax.ppermute(flat, axis, [(i, i ^ step) for i in range(devices)])  5.31 us
  transfers between devices with their start and end apart: 11, of which 6 were waited for; matrix products, arithmetic and copies ran while one was open for 11% of the time, Pallas kernels for 7%

profile of v3, /device:TPU:0, one launch (start us, length us, event | category | flops | bytes accessed | tf_op | source)
XLA Modules:
  0.0 138.5 jit_solution(13943525248105196833)
XLA Ops:
  2.0 4.9 %collective-permute-start = (bf16[192,3,128]{0,2,1:T(8,128)(2,1)S(1)}, bf16[192,3,128]{0,2,1:T(8,128)(2,1)S(1)}, u32[]{:S(2)}, u32[]{:S(2)}) collective-permute-start(bf16[192,3,128]{0,2,1:T(8,128)(2,1)S(1)} %get-tuple-element.41), channel_id=1, source_target_pairs={{0,16},{1,17},{2,18},{3,19},{4,20},{5,21},{6,22},{7,23},{8,24},{9,... | collective-permute-start | bytes 442376 | tf_op jit(solution)/shard_map/ppermute | solution.py:15
  10.4 8.6 %all_gather.3 = bf16[768,387]{1,0:T(8,128)(2,1)S(1)} all-gather(bf16[192,387]{1,0:T(8,128)(2,1)S(1)} %concatenate.18), channel_id=1, replica_groups=mesh['row'=2,'col'=4,'chan'=4] {'chan'}, dimensions={0}, use_global_device_ids=true | all-gather | bytes 743040 | tf_op jit(solution)/shard_map/all_gather | solution.py:138
  20.0 3.5 %collective-permute-start.2 = (bf16[192,14,3]{0,2,1:T(4,128)(2,1)S(1)}, bf16[192,14,3]{0,2,1:T(4,128)(2,1)S(1)}, u32[]{:S(2)}, u32[]{:S(2)}) collective-permute-start(bf16[192,14,3]{0,2,1:T(4,128)(2,1)S(1)} %get-tuple-element.34), channel_id=1, source_target_pairs={{0,4},{4,8},{8,12},{1,5},{5,9},{9,13},{2,6},{6,10},{10,14},{3,7},{... | collective-permute-start | bytes 48392 | tf_op jit(solution)/shard_map/ppermute | solution.py:15
  26.9 2.3 %collective-permute-done.3 = bf16[192,14,3]{0,2,1:T(4,128)(2,1)S(1)} collective-permute-done((bf16[192,14,3]{0,2,1:T(4,128)(2,1)S(1)}, bf16[192,14,3]{0,2,1:T(4,128)(2,1)S(1)}, u32[]{:S(2)}, u32[]{:S(2)}) %collective-permute-start.3) | collective-permute-done | bytes 16160 | tf_op jit(solution)/shard_map/ppermute | solution.py:16
  29.3 1.6 %convert_bitcast_fusion = (f32[14,134,192]{2,1,0:T(8,128)}, bf16[1,192,14,134]{1,3,2,0:T(8,128)(2,1)S(1)}) fusion(bf16[192,14,3]{0,2,1:T(4,128)(2,1)S(1)} %collective-permute-done.3, bf16[192,3,128]{0,2,1:T(8,128)(2,1)S(1)} %collective-permute-done.1, bf16[192,8,128]{0,2,1:T(8,128)(2,1)S(1)} %copy.89, bf16[192,3,128]{0,2,1:T(8,128)(2,1)S(1)} %collective-permute-done, ...), kind=kLoop, calls=%fused_computation.13 | loop fusion | flops 3962112 | bytes 2881536 | tf_op jit(solution)/shard_map/transpose | solution.py:96
  30.9 8.4 %fusion.6 = f32[1,192,8,128]{1,0,3,2:T(1,128)S(1)} fusion(bf16[1,192,14,134]{1,3,2,0:T(8,128)(2,1)S(1)} %get-tuple-element.31, f32[7,7,1,192]{3,1,0,2:T(8,128)S(1)} %bitcast.124), kind=kOutput, calls=%fused_computation.14 | convolution fusion | flops 115605504 | bytes 1544448 | tf_op jit(solution)/shard_map/conv_general_dilated | solution.py:27
  41.2 2.2 %multiply_convert_fusion = (bf16[768,1024]{1,0:T(8,128)(2,1)}, f32[768,1024]{1,0:T(8,128)S(1)}) fusion(f32[768]{0:T(1024)S(1)} %fusion.32, f32[24,8,8,128]{3,2,1,0:T(8,128)S(1)} %bitcast.110, f32[192]{0:T(256)S(1)} %copy-done.20, f32[192]{0:T(256)S(1)} %copy-done.14, f32[1024]{0:T(1024)S(1)} %get-tuple-element.53, f32[1024]{0:T(1024)S(1)} %get-tuple-element.54, ...), kind=kOutput, calls=%fused_computation.9 | convolution fusion | flops 307888128 | bytes 5913600 | tf_op jit(solution)/shard_map/dot_general | solution.py:45
  43.4 3.3 %fusion.61 = (bf16[768,1024]{1,0:T(8,128)(2,1)S(1)}, f32[768,1024]{1,0:T(8,128)}) fusion(f32[768,1024]{1,0:T(8,128)S(1)} %get-tuple-element.60, f32[768]{0:T(1024)S(1)} %fusion.32, f32[24,8,8,128]{3,2,1,0:T(8,128)S(1)} %convert.2, f32[192]{0:T(256)S(1)} %copy-done.15, bf16[768,387]{1,0:T(8,128)(2,1)S(1)} %all_gather.3), kind=kOutput, calls=%fused_computation.107 | convolution fusion | flops 311033856 | bytes 9049088 | tf_op jit(solution)/shard_map/dot_general | solution.py:45
  48.1 1.4 %copy.99 = f32[192,1024]{0,1:T(8,128)} copy(f32[192,1024]{1,0:T(8,128)S(1)} %get-tuple-element.25) | data formatting | bytes 1572864 | tf_op jit(solution)/shard_map/reduce_sum | solution.py:213
  49.5 2.1 %fusion.36 = f32[192,192]{1,0:T(8,128)} fusion(bf16[768,1024]{1,0:T(8,128)(2,1)} %copy-done.21, s32[]{:T(128)S(6)} %select_n.2, f32[24,8,8,128]{3,2,1,0:T(8,128)S(1)} %bitcast.111, f32[192]{0:T(256)S(1)} %copy-done.20, f32[192]{0:T(256)S(1)} %copy-done.14, f32[1024]{0:T(1024)S(1)} %get-tuple-element.53, f32[1024]{0:T(1024)S(1)} %get-tuple-element.54, ...), kind=kOutput, calls=%fused_computation.64 | convolution fusion | flops 76677120 | bytes 1337604 | tf_op jit(solution)/shard_map/dot_general | solution.py:45
  52.8 1.5 %fusion.48 = (f32[8,128,192]{2,1,0:T(8,128)}, bf16[192,8,128]{0,2,1:T(8,128)(2,1)S(1)}) fusion(f32[8,128]{1,0:T(8,128)S(1)} %broadcast_multiply_fusion, f32[8,128]{1,0:T(8,128)S(1)} %get-tuple-element.55, f32[192]{0:T(256)S(1)} %copy-done.13, f32[1,192,8,128]{1,0,3,2:T(1,128)S(1)} %fusion.6, f32[8,128]{1,0:T(8,128)S(1)} %multiply_bitcast_fusion, ...), kind=kLoop, calls=%fused_computation.98 | loop fusion | flops 1769472 | bytes 2770432 | tf_op jit(solution)/shard_map/transpose | solution.py:95
  54.3 4.7 %collective-permute-start.4 = (bf16[192,3,128]{0,2,1:T(8,128)(2,1)S(1)}, bf16[192,3,128]{0,2,1:T(8,128)(2,1)S(1)}, u32[]{:S(2)}, u32[]{:S(2)}) collective-permute-start(bf16[192,3,128]{0,2,1:T(8,128)(2,1)S(1)} %get-tuple-element.39), channel_id=1, source_target_pairs={{0,16},{1,17},{2,18},{3,19},{4,20},{5,21},{6,22},{7,23},{8,24},{9,... | collective-permute-start | bytes 442376 | tf_op jit(solution)/shard_map/ppermute | solution.py:15
  62.2 4.3 %collective-permute-done.5 = bf16[192,3,128]{0,2,1:T(8,128)(2,1)S(1)} collective-permute-done((bf16[192,3,128]{0,2,1:T(8,128)(2,1)S(1)}, bf16[192,3,128]{0,2,1:T(8,128)(2,1)S(1)}, u32[]{:S(2)}, u32[]{:S(2)}) %collective-permute-start.5) | collective-permute-done | bytes 147488 | tf_op jit(solution)/shard_map/ppermute | solution.py:16
  67.2 4.1 %collective-permute-start.6 = (bf16[192,14,3]{0,2,1:T(4,128)(2,1)}, bf16[192,14,3]{0,2,1:T(4,128)(2,1)}, u32[]{:S(2)}, u32[]{:S(2)}) collective-permute-start(bf16[192,14,3]{0,2,1:T(4,128)(2,1)} %get-tuple-element.32), channel_id=1, source_target_pairs={{0,4},{4,8},{8,12},{1,5},{5,9},{9,13},{2,6},{6,10},{10,14},{3,7},{... | collective-permute-start | bytes 48392 | tf_op jit(solution)/shard_map/ppermute | solution.py:15
  72.6 3.7 %fusion.23 = (f32[192]{0:T(256)S(1)}, f32[192]{0:T(256)S(1)}) fusion(f32[1,192,8,128]{3,2,1,0:T(8,128)S(1)} %copy.94, f32[8,128]{1,0:T(8,128)S(1)} %get-tuple-element.52, f32[8,128]{1,0:T(8,128)S(1)} %get-tuple-element.55, f32[192]{0:T(256)S(1)} %copy-done.13, f32[8,128]{1,0:T(8,128)S(1)} %broadcast_multiply_fusion, f32[8,128]{1,0:T(8,128)S(1)} %multiply_bitcast_fusion, ...), kind=kLoop, calls=%fused_computation.36 | loop fusion | flops 2162304 | bytes 1592320 | tf_op jit(solution)/shard_map/reduce_sum | solution.py:71
  77.2 10.2 %shard_map.194 = f32[49,8,192]{2,1,0:T(8,128)} custom-call(f32[8,128,192]{2,1,0:T(8,128)} %get-tuple-element.28.d_ref, f32[14,134,192]{2,1,0:T(8,128)} %get-tuple-element.30.p_ref), custom_call_target="tpu_custom_call" | custom-call | tf_op jit(solution)/shard_map/pallas_call | solution.py:99
  93.4 4.2 %fusion.15 = f32[8,8,17,192]{3,1,2,0:T(8,128)S(1)} fusion(bf16[192,14,1,7,6]{0,3,4,1,2:T(8,128)(2,1)S(1)} %slice.120, bf16[192,14,1,8,17]{0,3,4,1,2:T(8,128)(2,1)S(1)} %copy.104, pred[8,17]{0,1:T(8,128)(4,1)S(1)} %copy-done.22, f32[7,7,1,192]{3,1,0,2:T(8,128)S(1)} %bitcast.125), kind=kOutput, calls=%fused_computation.24 | convolution fusion | flops 126007296 | bytes 1830280 | tf_op jit(solution)/shard_map/conv_general_dilated | solution.py:27
  99.0 4.9 %multiply_reduce_fusion = (f32[192]{0:T(256)S(1)}, f32[192]{0:T(256)S(1)}, bf16[192,8,128]{2,1,0:T(8,128)(2,1)}, bf16[192,8,128]{2,1,0:T(8,128)(2,1)}) fusion(f32[24,8,8,128]{3,2,1,0:T(8,128)S(1)} %copy.118, bf16[192,8,128]{2,1,0:T(8,128)(2,1)} %param.21, f32[192]{0:T(256)S(1)} %copy-done.18, f32[192]{0:T(256)S(1)} %copy-done.17, ...), kind=kLoop, calls=%fused_computation.47 | loop fusion | flops 2358912 | bytes 3148800 | tf_op jit(solution)/shard_map/reduce_sum | solution.py:194
  103.9 1.9 %concatenate.23 = f32[84288]{0:T(1024)S(1)} concatenate(f32[9408]{0:T(1024)S(1)} %copy-done.9, f32[192]{0:T(256)S(1)} %get-tuple-element.23, f32[192]{0:T(256)S(1)} %get-tuple-element.22, f32[192]{0:T(256)S(1)} %copy-done.19, f32[36864]{0:T(1024)S(1)} %copy-done.5, f32[192]{0:T(256)S(1)} %dynamic-slice_reduce_fusion, f32[36864]{0:T(1024)S(1)} %copy-done.6, ...), dimensions={0} | concatenate | bytes 674304 | tf_op jit(solution)/shard_map/concatenate | solution.py:108
  105.8 7.2 %collective-permute-done.8 = f32[84288]{0:T(1024)S(1)} collective-permute-done((f32[84288]{0:T(1024)S(1)}, f32[84288]{0:T(1024)S(1)}, u32[]{:S(2)}, u32[]{:S(2)}) %collective-permute-start.8) | collective-permute-done | bytes 337184 | tf_op jit(solution)/shard_map/ppermute | solution.py:116
  113.0 2.7 %collective-permute-start.9 = (f32[84288]{0:T(1024)S(1)}, f32[84288]{0:T(1024)S(1)}, u32[]{:S(2)}, u32[]{:S(2)}) collective-permute-start(f32[84288]{0:T(1024)S(1)} %add.124), channel_id=1, source_target_pairs={{0,4},{4,0},{8,12},{12,8},{1,5},{5,1},{9,13},{13,9},{2,6},{6,2},{1... | collective-permute-start | bytes 1011464 | tf_op jit(solution)/shard_map/ppermute | solution.py:116
  115.7 6.4 %collective-permute-done.9 = f32[84288]{0:T(1024)S(1)} collective-permute-done((f32[84288]{0:T(1024)S(1)}, f32[84288]{0:T(1024)S(1)}, u32[]{:S(2)}, u32[]{:S(2)}) %collective-permute-start.9) | collective-permute-done | bytes 337184 | tf_op jit(solution)/shard_map/ppermute | solution.py:116
  122.2 2.6 %collective-permute-start.10 = (f32[84288]{0:T(1024)S(1)}, f32[84288]{0:T(1024)S(1)}, u32[]{:S(2)}, u32[]{:S(2)}) collective-permute-start(f32[84288]{0:T(1024)S(1)} %add.125), channel_id=1, source_target_pairs={{0,8},{4,12},{8,0},{12,4},{1,9},{5,13},{9,1},{13,5},{2,10},{6,14},... | collective-permute-start | bytes 1011464 | tf_op jit(solution)/shard_map/ppermute | solution.py:116
  124.8 10.6 %collective-permute-done.10 = f32[84288]{0:T(1024)S(1)} collective-permute-done((f32[84288]{0:T(1024)S(1)}, f32[84288]{0:T(1024)S(1)}, u32[]{:S(2)}, u32[]{:S(2)}) %collective-permute-start.10) | collective-permute-done | bytes 337184 | tf_op jit(solution)/shard_map/ppermute | solution.py:116
  (110 shorter events, 30.1 us)
Async XLA Ops:
  0.6 9.6 %copy-start.10 = (bf16[192,192]{1,0:T(8,128)(2,1)S(1)}, bf16[192,192]{1,0:T(8,128)(2,1)}, u32[]{:S(2)}) copy-start(bf16[192,192]{1,0:T(8,128)(2,1)} %param.18) | copy-start | bytes 221188
  2.0 18.0 %collective-permute-start = (bf16[192,3,128]{0,2,1:T(8,128)(2,1)S(1)}, bf16[192,3,128]{0,2,1:T(8,128)(2,1)S(1)}, u32[]{:S(2)}, u32[]{:S(2)}) collective-permute-start(bf16[192,3,128]{0,2,1:T(8,128)(2,1)S(1)} %get-tuple-element.41), channel_id=1, source_target_pairs={{0,16},{1,17},{2,18},{3,19},{4,20},{5,21},{6,22},{7,23},{8,24},{9,... | collective-permute-start | bytes 442376 | tf_op jit(solution)/shard_map/ppermute | solution.py:15
  6.9 13.1 %collective-permute-start.1 = (bf16[192,3,128]{0,2,1:T(8,128)(2,1)S(1)}, bf16[192,3,128]{0,2,1:T(8,128)(2,1)S(1)}, u32[]{:S(2)}, u32[]{:S(2)}) collective-permute-start(bf16[192,3,128]{0,2,1:T(8,128)(2,1)S(1)} %get-tuple-element.42), channel_id=1, source_target_pairs={{16,0},{17,1},{18,2},{19,3},{20,4},{21,5},{22,6},{23,7},{24,8},{25... | collective-permute-start | bytes 442376 | tf_op jit(solution)/shard_map/ppermute | solution.py:16
  19.0 6.2 %copy-start.3 = (bf16[192,8,128]{2,1,0:T(8,128)(2,1)S(1)}, bf16[192,8,128]{2,1,0:T(8,128)(2,1)}, u32[]{:S(2)}) copy-start(bf16[192,8,128]{2,1,0:T(8,128)(2,1)} %param.21) | copy-start | bytes 1179652
  19.9 6.3 %copy-start.11 = (f32[7,7,192]{2,1,0:T(8,128)S(1)}, f32[7,7,192]{2,1,0:T(8,128)}, u32[]{:S(2)}) copy-start(f32[7,7,192]{2,1,0:T(8,128)} %param.12) | copy-start | bytes 112900
  20.0 6.9 %collective-permute-start.2 = (bf16[192,14,3]{0,2,1:T(4,128)(2,1)S(1)}, bf16[192,14,3]{0,2,1:T(4,128)(2,1)S(1)}, u32[]{:S(2)}, u32[]{:S(2)}) collective-permute-start(bf16[192,14,3]{0,2,1:T(4,128)(2,1)S(1)} %get-tuple-element.34), channel_id=1, source_target_pairs={{0,4},{4,8},{8,12},{1,5},{5,9},{9,13},{2,6},{6,10},{10,14},{3,7},{... | collective-permute-start | bytes 48392 | tf_op jit(solution)/shard_map/ppermute | solution.py:15
  23.5 5.8 %collective-permute-start.3 = (bf16[192,14,3]{0,2,1:T(4,128)(2,1)S(1)}, bf16[192,14,3]{0,2,1:T(4,128)(2,1)S(1)}, u32[]{:S(2)}, u32[]{:S(2)}) collective-permute-start(bf16[192,14,3]{0,2,1:T(4,128)(2,1)S(1)} %get-tuple-element.35), channel_id=1, source_target_pairs={{4,0},{8,4},{12,8},{5,1},{9,5},{13,9},{6,2},{10,6},{14,10},{7,3},{... | collective-permute-start | bytes 48392 | tf_op jit(solution)/shard_map/ppermute | solution.py:16
  30.9 9.7 %copy-start.13 = (f32[192]{0:T(256)S(1)}, f32[192]{0:T(256)}, u32[]{:S(2)}) copy-start(f32[192]{0:T(256)} %param.13) | copy-start | bytes 2308
  43.4 3.3 %copy-start.7 = (bf16[192,4,192]{2,0,1:T(8,128)(2,1)S(1)}, bf16[192,4,192]{2,0,1:T(8,128)(2,1)}, u32[]{:S(2)}) copy-start(bf16[192,4,192]{2,0,1:T(8,128)(2,1)} %copy.98) | copy-start | bytes 884740
  52.8 7.5 %copy-start.1 = (bf16[768,1024]{1,0:T(8,128)(2,1)S(1)}, bf16[768,1024]{1,0:T(8,128)(2,1)}, u32[]{:S(2)}) copy-start(bf16[768,1024]{1,0:T(8,128)(2,1)} %get-tuple-element.59) | copy-start | bytes 4718596
  52.8 7.5 %copy-start.16 = (f32[192]{0:T(256)S(1)}, f32[192]{0:T(256)}, u32[]{:S(2)}) copy-start(f32[192]{0:T(256)} %param.20) | copy-start | bytes 2308
  54.3 6.5 %copy-start.4 = (bf16[768,192]{1,0:T(8,128)(2,1)S(1)}, bf16[768,192]{1,0:T(8,128)(2,1)}, u32[]{:S(2)}) copy-start(bf16[768,192]{1,0:T(8,128)(2,1)} %get-tuple-element.38) | copy-start | bytes 884740
  54.3 7.9 %collective-permute-start.4 = (bf16[192,3,128]{0,2,1:T(8,128)(2,1)S(1)}, bf16[192,3,128]{0,2,1:T(8,128)(2,1)S(1)}, u32[]{:S(2)}, u32[]{:S(2)}) collective-permute-start(bf16[192,3,128]{0,2,1:T(8,128)(2,1)S(1)} %get-tuple-element.39), channel_id=1, source_target_pairs={{0,16},{1,17},{2,18},{3,19},{4,20},{5,21},{6,22},{7,23},{8,24},{9,... | collective-permute-start | bytes 442376 | tf_op jit(solution)/shard_map/ppermute | solution.py:15
  59.0 7.6 %collective-permute-start.5 = (bf16[192,3,128]{0,2,1:T(8,128)(2,1)S(1)}, bf16[192,3,128]{0,2,1:T(8,128)(2,1)S(1)}, u32[]{:S(2)}, u32[]{:S(2)}) collective-permute-start(bf16[192,3,128]{0,2,1:T(8,128)(2,1)S(1)} %get-tuple-element.40), channel_id=1, source_target_pairs={{16,0},{17,1},{18,2},{19,3},{20,4},{21,5},{22,6},{23,7},{24,8},{25... | collective-permute-start | bytes 442376 | tf_op jit(solution)/shard_map/ppermute | solution.py:16
  61.4 14.9 %copy-start.8 = (f32[192,192]{1,0:T(8,128)S(1)}, f32[192,192]{1,0:T(8,128)}, u32[]{:S(2)}) copy-start(f32[192,192]{1,0:T(8,128)} %fusion.36) | copy-start | bytes 442372
  67.2 24.0 %collective-permute-start.6 = (bf16[192,14,3]{0,2,1:T(4,128)(2,1)}, bf16[192,14,3]{0,2,1:T(4,128)(2,1)}, u32[]{:S(2)}, u32[]{:S(2)}) collective-permute-start(bf16[192,14,3]{0,2,1:T(4,128)(2,1)} %get-tuple-element.32), channel_id=1, source_target_pairs={{0,4},{4,8},{8,12},{1,5},{5,9},{9,13},{2,6},{6,10},{10,14},{3,7},{... | collective-permute-start | bytes 48392 | tf_op jit(solution)/shard_map/ppermute | solution.py:15
  71.3 19.9 %collective-permute-start.7 = (bf16[192,14,3]{0,2,1:T(4,128)(2,1)}, bf16[192,14,3]{0,2,1:T(4,128)(2,1)}, u32[]{:S(2)}, u32[]{:S(2)}) collective-permute-start(bf16[192,14,3]{0,2,1:T(4,128)(2,1)} %get-tuple-element.33), channel_id=1, source_target_pairs={{4,0},{8,4},{12,8},{5,1},{9,5},{13,9},{6,2},{10,6},{14,10},{7,3},{... | collective-permute-start | bytes 48392 | tf_op jit(solution)/shard_map/ppermute | solution.py:16
  98.9 4.9 %copy-start.5 = (f32[36864]{0:T(1024)S(1)}, f32[36864]{0:T(1024)}, u32[]{:S(2)}) copy-start(f32[36864]{0:T(1024)} %reshape.278) | copy-start | bytes 442372
  98.9 5.0 %copy-start.6 = (f32[36864]{0:T(1024)S(1)}, f32[36864]{0:T(1024)}, u32[]{:S(2)}) copy-start(f32[36864]{0:T(1024)} %reshape.279) | copy-start | bytes 442372
  98.9 4.9 %copy-start.9 = (f32[9408]{0:T(1024)S(1)}, f32[9408]{0:T(1024)}, u32[]{:S(2)}) copy-start(f32[9408]{0:T(1024)} %reshape_reshape.3) | copy-start | bytes 112900
  98.9 4.9 %copy-start.19 = (f32[192]{0:T(256)S(1)}, f32[192]{0:T(256)}, u32[]{:S(2)}) copy-start(f32[192]{0:T(256)} %get-tuple-element.24) | copy-start | bytes 2308
  105.8 7.2 %collective-permute-start.8 = (f32[84288]{0:T(1024)S(1)}, f32[84288]{0:T(1024)S(1)}, u32[]{:S(2)}, u32[]{:S(2)}) collective-permute-start(f32[84288]{0:T(1024)S(1)} %concatenate.23), channel_id=1, source_target_pairs={{0,16},{16,0},{1,17},{17,1},{2,18},{18,2},{3,19},{19,3},{4,20},{20... | collective-permute-start | bytes 1011464 | tf_op jit(solution)/shard_map/ppermute | solution.py:116
  113.0 9.1 %collective-permute-start.9 = (f32[84288]{0:T(1024)S(1)}, f32[84288]{0:T(1024)S(1)}, u32[]{:S(2)}, u32[]{:S(2)}) collective-permute-start(f32[84288]{0:T(1024)S(1)} %add.124), channel_id=1, source_target_pairs={{0,4},{4,0},{8,12},{12,8},{1,5},{5,1},{9,13},{13,9},{2,6},{6,2},{1... | collective-permute-start | bytes 1011464 | tf_op jit(solution)/shard_map/ppermute | solution.py:116
  122.2 13.2 %collective-permute-start.10 = (f32[84288]{0:T(1024)S(1)}, f32[84288]{0:T(1024)S(1)}, u32[]{:S(2)}, u32[]{:S(2)}) collective-permute-start(f32[84288]{0:T(1024)S(1)} %add.125), channel_id=1, source_target_pairs={{0,8},{4,12},{8,0},{12,4},{1,9},{5,13},{9,1},{13,5},{2,10},{6,14},... | collective-permute-start | bytes 1011464 | tf_op jit(solution)/shard_map/ppermute | solution.py:116
  (10 other events, 13.1 us)

commit v4 on v3

--- a/solution.py
+++ b/solution.py
@@ -12,8 +12,15 @@
         down = [(j, i) for i, j in up]
         last = lax.slice_in_dim(x, length - width, length, axis=dim)
         leading = lax.slice_in_dim(x, 0, width, axis=dim)
-        before = lax.ppermute(last, axis, up)
-        after = lax.ppermute(leading, axis, down)
+        if devices == 2:
+            first = lax.axis_index(axis) == 0
+            got = lax.ppermute(jnp.where(first, last, leading), axis, [(0, 1), (1, 0)])
+            nothing = jnp.zeros_like(got)
+            before = jnp.where(first, nothing, got)
+            after = jnp.where(first, got, nothing)
+        else:
+            before = lax.ppermute(last, axis, up)
+            after = lax.ppermute(leading, axis, down)
         x = jnp.concatenate([before, x, after], axis=dim)
     return x
 

time: 139 us -> 130 us (0.935)
  starting transfers between devices: 27.6 us -> 21.2 us
  waiting for transfers between devices: 31.8 us -> 30 us
    ppermute x4 -> x2, starting transfers between devices: 17.1 us -> 6.96 us  [extended(): before = lax.ppermute(last, axis, up)]
    ppermute x4 -> x2, waiting for transfers between devices: 6.69 us -> 2.35 us  [extended(): after = lax.ppermute(leading, axis, down)]
    ppermute x0 -> x2, waiting for transfers between devices: none -> 4.15 us  [extended(): got = lax.ppermute(jnp.where(first, last, leading), axis, [(0, 1), (1, 0)])]
    ppermute x0 -> x2, starting transfers between devices: none -> 3.61 us  [extended(): got = lax.ppermute(jnp.where(first, last, leading), axis, [(0, 1), (1, 0)])]
    ppermute x3, starting transfers between devices: 5.31 us -> 8.07 us  [butterfly_sum(): lax.ppermute(flat, axis, [(i, i ^ step) for i in range(devices)])]
    ppermute x4 -> x2, starting transfers between devices: 5.16 us -> 2.58 us  [extended(): after = lax.ppermute(leading, axis, down)]
    unnamed x52 -> x46, local copies, waits for them, and re-layouts: 4.5 us -> 4.55 us
  transfers between devices with their start and end apart: 11 -> 9, of which waited for: 6 -> 5; matrix products, arithmetic and copies ran while one was open for 11% -> 12% of each run, Pallas kernels for 7% -> 8%
where the time goes in v4:
time: 130 us; the launch traced here: 129 us
  waiting for transfers between devices  30 us (23%)
  matrix products  22.4 us (17%)
  starting transfers between devices  21.2 us (16%)
  other arithmetic  18.1 us (14%)
  local copies, waits for them, and re-layouts  17.9 us (14%)
  Pallas kernels  10.2 us (8%)
  blocking collectives  8.6 us (7%)
    ppermute x3, waiting for transfers between devices, butterfly_sum(): lax.ppermute(flat, axis, [(i, i ^ step) for i in range(devices)])  23.5 us
    conv_general_dilated x2, matrix products, depthwise(): lax.conv_general_dilated(padded[None], kernel[:, :, None, :], (1, 1), 'VA...  12.6 us
    pallas_call x1, Pallas kernels, kernel_grad(): pl.pallas_call(kernel_grad_body, out_shape=jax.ShapeDtypeStruct((side * s...  10.2 us
    all_gather x1, blocking collectives, gathered_weights(): full = lax.all_gather(packed, 'chan', axis=0, tiled=True)  8.6 us
    ppermute x3, starting transfers between devices, butterfly_sum(): lax.ppermute(flat, axis, [(i, i ^ step) for i in range(devices)])  8.07 us
    dot_general x4, matrix products, contract(): lax.dot_general(left, right, (((dim_left,), (dim_right,)), ((), ())), pre...  7.95 us
    ppermute x2, starting transfers between devices, extended(): before = lax.ppermute(last, axis, up)  6.96 us
    unnamed x46, local copies, waits for them, and re-layouts  4.55 us
  transfers between devices with their start and end apart: 9, of which 5 were waited for; matrix products, arithmetic and copies ran while one was open for 12% of the time, Pallas kernels for 8%

profile of v4, /device:TPU:0, one launch (start us, length us, event | category | flops | bytes accessed | tf_op | source)
XLA Modules:
  0.0 129.5 jit_solution(9994100445970441722)
XLA Ops:
  1.9 3.0 %collective-permute-start = (bf16[192,3,128]{0,2,1:T(8,128)(2,1)S(1)}, bf16[192,3,128]{0,2,1:T(8,128)(2,1)S(1)}, u32[]{:S(2)}, u32[]{:S(2)}) collective-permute-start(bf16[192,3,128]{0,2,1:T(8,128)(2,1)S(1)} %slice_select_fusion.1), channel_id=1, source_target_pairs={{0,16},{16,0},{1,17},{17,1},{2,18},{18,2},{3,19},{19,3},{4,20},{20... | collective-permute-start | bytes 442376 | tf_op jit(solution)/shard_map/ppermute | solution.py:17
  8.1 8.6 %all_gather.3 = bf16[768,387]{1,0:T(8,128)(2,1)S(1)} all-gather(bf16[192,387]{1,0:T(8,128)(2,1)S(1)} %concatenate.18), channel_id=1, replica_groups=mesh['row'=2,'col'=4,'chan'=4] {'chan'}, dimensions={0}, use_global_device_ids=true | all-gather | bytes 743040 | tf_op jit(solution)/shard_map/all_gather | solution.py:145
  17.7 3.5 %collective-permute-start.1 = (bf16[192,14,3]{0,2,1:T(4,128)(2,1)S(1)}, bf16[192,14,3]{0,2,1:T(4,128)(2,1)S(1)}, u32[]{:S(2)}, u32[]{:S(2)}) collective-permute-start(bf16[192,14,3]{0,2,1:T(4,128)(2,1)S(1)} %get-tuple-element.34), channel_id=1, source_target_pairs={{0,4},{4,8},{8,12},{1,5},{5,9},{9,13},{2,6},{6,10},{10,14},{3,7},{... | collective-permute-start | bytes 48392 | tf_op jit(solution)/shard_map/ppermute | solution.py:22
  24.6 2.3 %collective-permute-done.2 = bf16[192,14,3]{0,2,1:T(4,128)(2,1)S(1)} collective-permute-done((bf16[192,14,3]{0,2,1:T(4,128)(2,1)S(1)}, bf16[192,14,3]{0,2,1:T(4,128)(2,1)S(1)}, u32[]{:S(2)}, u32[]{:S(2)}) %collective-permute-start.2) | collective-permute-done | bytes 16160 | tf_op jit(solution)/shard_map/ppermute | solution.py:23
  27.0 1.6 %convert_bitcast_fusion = (f32[14,134,192]{2,1,0:T(8,128)}, bf16[1,192,14,134]{1,3,2,0:T(8,128)(2,1)S(1)}) fusion(bf16[192,14,3]{0,2,1:T(4,128)(2,1)S(1)} %collective-permute-done.2, bf16[192,3,128]{0,2,1:T(8,128)(2,1)S(1)} %get-tuple-element.51, bf16[192,8,128]{0,2,1:T(8,128)(2,1)S(1)} %copy.89, bf16[192,3,128]{0,2,1:T(8,128)(2,1)S(1)} %get-tuple-element.50, ...), kind=kLoop, calls=%fused_computation.13 | loop fusion | flops 3962112 | bytes 2881536 | tf_op jit(solution)/shard_map/transpose | solution.py:103
  28.6 8.4 %fusion.6 = f32[1,192,8,128]{1,0,3,2:T(1,128)S(1)} fusion(bf16[1,192,14,134]{1,3,2,0:T(8,128)(2,1)S(1)} %get-tuple-element.31, f32[7,7,1,192]{3,1,0,2:T(8,128)S(1)} %bitcast.124), kind=kOutput, calls=%fused_computation.14 | convolution fusion | flops 115605504 | bytes 1544448 | tf_op jit(solution)/shard_map/conv_general_dilated | solution.py:34
  38.9 2.2 %multiply_convert_fusion = (bf16[768,1024]{1,0:T(8,128)(2,1)}, f32[768,1024]{1,0:T(8,128)S(1)}) fusion(f32[768]{0:T(1024)S(1)} %fusion.32, f32[24,8,8,128]{3,2,1,0:T(8,128)S(1)} %bitcast.110, f32[192]{0:T(256)S(1)} %copy-done.17, f32[192]{0:T(256)S(1)} %copy-done.13, f32[1024]{0:T(1024)S(1)} %get-tuple-element.53, f32[1024]{0:T(1024)S(1)} %get-tuple-element.54, ...), kind=kOutput, calls=%fused_computation.9 | convolution fusion | flops 307888128 | bytes 5913600 | tf_op jit(solution)/shard_map/dot_general | solution.py:52
  41.1 3.3 %fusion.59 = (bf16[768,1024]{1,0:T(8,128)(2,1)S(1)}, f32[768,1024]{1,0:T(8,128)}) fusion(f32[768,1024]{1,0:T(8,128)S(1)} %get-tuple-element.60, f32[768]{0:T(1024)S(1)} %fusion.32, f32[24,8,8,128]{3,2,1,0:T(8,128)S(1)} %convert.2, f32[192]{0:T(256)S(1)} %copy-done.14, bf16[768,387]{1,0:T(8,128)(2,1)S(1)} %all_gather.3), kind=kOutput, calls=%fused_computation.111 | convolution fusion | flops 311033856 | bytes 9049088 | tf_op jit(solution)/shard_map/dot_general | solution.py:52
  45.8 1.4 %copy.99 = f32[192,1024]{0,1:T(8,128)} copy(f32[192,1024]{1,0:T(8,128)S(1)} %get-tuple-element.25) | data formatting | bytes 1572864 | tf_op jit(solution)/shard_map/reduce_sum | solution.py:220
  47.2 2.1 %fusion.36 = f32[192,192]{1,0:T(8,128)} fusion(bf16[768,1024]{1,0:T(8,128)(2,1)} %copy-done.18, s32[]{:T(128)S(6)} %select_n.40, f32[24,8,8,128]{3,2,1,0:T(8,128)S(1)} %bitcast.111, f32[192]{0:T(256)S(1)} %copy-done.17, f32[192]{0:T(256)S(1)} %copy-done.13, f32[1024]{0:T(1024)S(1)} %get-tuple-element.53, f32[1024]{0:T(1024)S(1)} %get-tuple-element.54, ...), kind=kOutput, calls=%fused_computation.64 | convolution fusion | flops 76677120 | bytes 1337604 | tf_op jit(solution)/shard_map/dot_general | solution.py:52
  50.5 1.5 %fusion.48 = (f32[8,128,192]{2,1,0:T(8,128)}, bf16[192,8,128]{0,2,1:T(8,128)(2,1)S(1)}) fusion(f32[8,128]{1,0:T(8,128)S(1)} %broadcast_multiply_fusion, f32[8,128]{1,0:T(8,128)S(1)} %get-tuple-element.55, f32[192]{0:T(256)S(1)} %copy-done.12, f32[1,192,8,128]{1,0,3,2:T(1,128)S(1)} %fusion.6, f32[8,128]{1,0:T(8,128)S(1)} %multiply_bitcast_fusion, ...), kind=kLoop, calls=%fused_computation.104 | loop fusion | flops 1769472 | bytes 2770432 | tf_op jit(solution)/shard_map/transpose | solution.py:102
  53.6 4.1 %collective-permute-done.3 = bf16[192,3,128]{0,2,1:T(8,128)(2,1)S(1)} collective-permute-done((bf16[192,3,128]{0,2,1:T(8,128)(2,1)S(1)}, bf16[192,3,128]{0,2,1:T(8,128)(2,1)S(1)}, u32[]{:S(2)}, u32[]{:S(2)}) %collective-permute-start.3) | collective-permute-done | bytes 147488 | tf_op jit(solution)/shard_map/ppermute | solution.py:17
  58.5 3.5 %collective-permute-start.4 = (bf16[192,14,3]{0,2,1:T(4,128)(2,1)}, bf16[192,14,3]{0,2,1:T(4,128)(2,1)S(1)}, u32[]{:S(2)}, u32[]{:S(2)}) collective-permute-start(bf16[192,14,3]{0,2,1:T(4,128)(2,1)} %get-tuple-element.32), channel_id=1, source_target_pairs={{0,4},{4,8},{8,12},{1,5},{5,9},{9,13},{2,6},{6,10},{10,14},{3,7},{... | collective-permute-start | bytes 48392 | tf_op jit(solution)/shard_map/ppermute | solution.py:22
  62.0 1.3 collective-permute-start.5
  63.3 3.7 %fusion.23 = (f32[192]{0:T(256)S(1)}, f32[192]{0:T(256)S(1)}) fusion(f32[1,192,8,128]{3,2,1,0:T(8,128)S(1)} %copy.94, f32[8,128]{1,0:T(8,128)S(1)} %get-tuple-element.52, f32[8,128]{1,0:T(8,128)S(1)} %get-tuple-element.55, f32[192]{0:T(256)S(1)} %copy-done.12, f32[8,128]{1,0:T(8,128)S(1)} %broadcast_multiply_fusion, f32[8,128]{1,0:T(8,128)S(1)} %multiply_bitcast_fusion, ...), kind=kLoop, calls=%fused_computation.36 | loop fusion | flops 2162304 | bytes 1592320 | tf_op jit(solution)/shard_map/reduce_sum | solution.py:78
  67.9 10.2 %shard_map.194 = f32[49,8,192]{2,1,0:T(8,128)} custom-call(f32[8,128,192]{2,1,0:T(8,128)} %get-tuple-element.28.d_ref, f32[14,134,192]{2,1,0:T(8,128)} %get-tuple-element.30.p_ref), custom_call_target="tpu_custom_call" | custom-call | tf_op jit(solution)/shard_map/pallas_call | solution.py:106
  83.4 4.2 %fusion.15 = f32[8,8,17,192]{3,1,2,0:T(8,128)S(1)} fusion(bf16[192,14,1,7,6]{0,3,4,1,2:T(8,128)(2,1)S(1)} %slice.120, bf16[192,14,1,8,17]{0,3,4,1,2:T(8,128)(2,1)S(1)} %copy.104, pred[8,17]{0,1:T(8,128)(4,1)S(1)} %copy-done.19, f32[7,7,1,192]{3,1,0,2:T(8,128)S(1)} %bitcast.125), kind=kOutput, calls=%fused_computation.24 | convolution fusion | flops 126007296 | bytes 1830280 | tf_op jit(solution)/shard_map/conv_general_dilated | solution.py:34
  89.1 3.8 %multiply_reduce_fusion = (f32[192]{0:T(256)S(1)}, f32[192]{0:T(256)S(1)}, bf16[192,8,128]{2,1,0:T(8,128)(2,1)}, bf16[192,8,128]{2,1,0:T(8,128)(2,1)}) fusion(f32[24,8,8,128]{3,2,1,0:T(8,128)S(1)} %copy.118, bf16[192,8,128]{2,1,0:T(8,128)(2,1)S(1)} %copy-done.4, f32[192]{0:T(256)S(1)} %copy-done.15, f32[192]{0:T(256)S(1)} %copy-done.14, ...), kind=kLoop, calls=%fused_computation.47 | loop fusion | flops 2358912 | bytes 3148800 | tf_op jit(solution)/shard_map/reduce_sum | solution.py:201
  92.9 1.9 %concatenate.23 = f32[84288]{0:T(1024)S(1)} concatenate(f32[9408]{0:T(1024)S(1)} %reshape_reshape.3, f32[192]{0:T(256)S(1)} %get-tuple-element.23, f32[192]{0:T(256)S(1)} %get-tuple-element.22, f32[192]{0:T(256)S(1)} %copy-done.16, f32[36864]{0:T(1024)S(1)} %copy-done.6, f32[192]{0:T(256)S(1)} %dynamic-slice_reduce_fusion, f32[36864]{0:T(1024)S(1)} %copy-done.7, ...), dimensions={0} | concatenate | bytes 674304 | tf_op jit(solution)/shard_map/concatenate | solution.py:115
  95.3 6.8 %collective-permute-done.6 = f32[84288]{0:T(1024)S(1)} collective-permute-done((f32[84288]{0:T(1024)S(1)}, f32[84288]{0:T(1024)S(1)}, u32[]{:S(2)}, u32[]{:S(2)}) %collective-permute-start.6) | collective-permute-done | bytes 337184 | tf_op jit(solution)/shard_map/ppermute | solution.py:123
  102.1 2.6 %collective-permute-start.7 = (f32[84288]{0:T(1024)S(1)}, f32[84288]{0:T(1024)S(1)}, u32[]{:S(2)}, u32[]{:S(2)}) collective-permute-start(f32[84288]{0:T(1024)S(1)} %add.124), channel_id=1, source_target_pairs={{0,4},{4,0},{8,12},{12,8},{1,5},{5,1},{9,13},{13,9},{2,6},{6,2},{1... | collective-permute-start | bytes 1011464 | tf_op jit(solution)/shard_map/ppermute | solution.py:123
  104.7 5.2 %collective-permute-done.7 = f32[84288]{0:T(1024)S(1)} collective-permute-done((f32[84288]{0:T(1024)S(1)}, f32[84288]{0:T(1024)S(1)}, u32[]{:S(2)}, u32[]{:S(2)}) %collective-permute-start.7) | collective-permute-done | bytes 337184 | tf_op jit(solution)/shard_map/ppermute | solution.py:123
  109.9 5.0 %collective-permute-start.8 = (f32[84288]{0:T(1024)S(1)}, f32[84288]{0:T(1024)S(1)}, u32[]{:S(2)}, u32[]{:S(2)}) collective-permute-start(f32[84288]{0:T(1024)S(1)} %add.125), channel_id=1, source_target_pairs={{0,8},{4,12},{8,0},{12,4},{1,9},{5,13},{9,1},{13,5},{2,10},{6,14},... | collective-permute-start | bytes 1011464 | tf_op jit(solution)/shard_map/ppermute | solution.py:123
  114.9 11.5 %collective-permute-done.8 = f32[84288]{0:T(1024)S(1)} collective-permute-done((f32[84288]{0:T(1024)S(1)}, f32[84288]{0:T(1024)S(1)}, u32[]{:S(2)}, u32[]{:S(2)}) %collective-permute-start.8) | collective-permute-done | bytes 337184 | tf_op jit(solution)/shard_map/ppermute | solution.py:123
  (102 shorter events, 26.8 us)
Async XLA Ops:
  1.9 15.7 %collective-permute-start = (bf16[192,3,128]{0,2,1:T(8,128)(2,1)S(1)}, bf16[192,3,128]{0,2,1:T(8,128)(2,1)S(1)}, u32[]{:S(2)}, u32[]{:S(2)}) collective-permute-start(bf16[192,3,128]{0,2,1:T(8,128)(2,1)S(1)} %slice_select_fusion.1), channel_id=1, source_target_pairs={{0,16},{16,0},{1,17},{17,1},{2,18},{18,2},{3,19},{19,3},{4,20},{20... | collective-permute-start | bytes 442376 | tf_op jit(solution)/shard_map/ppermute | solution.py:17
  17.6 5.3 %copy-start.3 = (bf16[192,8,128]{2,1,0:T(8,128)(2,1)S(1)}, bf16[192,8,128]{2,1,0:T(8,128)(2,1)}, u32[]{:S(2)}) copy-start(bf16[192,8,128]{2,1,0:T(8,128)(2,1)} %param.21) | copy-start | bytes 1179652
  17.7 6.3 %copy-start.10 = (f32[7,7,192]{2,1,0:T(8,128)S(1)}, f32[7,7,192]{2,1,0:T(8,128)}, u32[]{:S(2)}) copy-start(f32[7,7,192]{2,1,0:T(8,128)} %param.12) | copy-start | bytes 112900
  17.7 6.9 %collective-permute-start.1 = (bf16[192,14,3]{0,2,1:T(4,128)(2,1)S(1)}, bf16[192,14,3]{0,2,1:T(4,128)(2,1)S(1)}, u32[]{:S(2)}, u32[]{:S(2)}) collective-permute-start(bf16[192,14,3]{0,2,1:T(4,128)(2,1)S(1)} %get-tuple-element.34), channel_id=1, source_target_pairs={{0,4},{4,8},{8,12},{1,5},{5,9},{9,13},{2,6},{6,10},{10,14},{3,7},{... | collective-permute-start | bytes 48392 | tf_op jit(solution)/shard_map/ppermute | solution.py:22
  21.2 5.8 %collective-permute-start.2 = (bf16[192,14,3]{0,2,1:T(4,128)(2,1)S(1)}, bf16[192,14,3]{0,2,1:T(4,128)(2,1)S(1)}, u32[]{:S(2)}, u32[]{:S(2)}) collective-permute-start(bf16[192,14,3]{0,2,1:T(4,128)(2,1)S(1)} %get-tuple-element.35), channel_id=1, source_target_pairs={{4,0},{8,4},{12,8},{5,1},{9,5},{13,9},{6,2},{10,6},{14,10},{7,3},{... | collective-permute-start | bytes 48392 | tf_op jit(solution)/shard_map/ppermute | solution.py:23
  28.6 9.7 %copy-start.12 = (f32[192]{0:T(256)S(1)}, f32[192]{0:T(256)}, u32[]{:S(2)}) copy-start(f32[192]{0:T(256)} %param.13) | copy-start | bytes 2308
  37.0 1.9 %copy-start.13 = (f32[192]{0:T(256)S(1)}, f32[192]{0:T(256)}, u32[]{:S(2)}) copy-start(f32[192]{0:T(256)} %param.14) | copy-start | bytes 2308
  37.0 1.9 %copy-start.17 = (f32[192]{0:T(256)S(1)}, f32[192]{0:T(256)}, u32[]{:S(2)}) copy-start(f32[192]{0:T(256)} %param.15) | copy-start | bytes 2308
  38.9 2.2 %copy-start.14 = (f32[192]{0:T(256)S(1)}, f32[192]{0:T(256)}, u32[]{:S(2)}) copy-start(f32[192]{0:T(256)} %param.20) | copy-start | bytes 2308
  41.1 3.3 %copy-start.8 = (bf16[192,4,192]{2,0,1:T(8,128)(2,1)S(1)}, bf16[192,4,192]{2,0,1:T(8,128)(2,1)}, u32[]{:S(2)}) copy-start(bf16[192,4,192]{2,0,1:T(8,128)(2,1)} %copy.98) | copy-start | bytes 884740
  44.4 1.3 copy-start.18
  49.3 1.2 copy-start
  50.5 2.1 %copy-start.1 = (bf16[768,1024]{1,0:T(8,128)(2,1)S(1)}, bf16[768,1024]{1,0:T(8,128)(2,1)}, u32[]{:S(2)}) copy-start(bf16[768,1024]{1,0:T(8,128)(2,1)} %get-tuple-element.59) | copy-start | bytes 4718596
  50.5 2.5 %copy-start.5 = (bf16[768,192]{1,0:T(8,128)(2,1)S(1)}, bf16[768,192]{1,0:T(8,128)(2,1)}, u32[]{:S(2)}) copy-start(bf16[768,192]{1,0:T(8,128)(2,1)} %get-tuple-element.38) | copy-start | bytes 884740
  52.0 5.8 %collective-permute-start.3 = (bf16[192,3,128]{0,2,1:T(8,128)(2,1)S(1)}, bf16[192,3,128]{0,2,1:T(8,128)(2,1)S(1)}, u32[]{:S(2)}, u32[]{:S(2)}) collective-permute-start(bf16[192,3,128]{0,2,1:T(8,128)(2,1)S(1)} %slice_select_fusion), channel_id=1, source_target_pairs={{0,16},{16,0},{1,17},{17,1},{2,18},{18,2},{3,19},{19,3},{4,20},{20... | collective-permute-start | bytes 442376 | tf_op jit(solution)/shard_map/ppermute | solution.py:17
  53.6 13.3 %copy-start.9 = (f32[192,192]{1,0:T(8,128)S(1)}, f32[192,192]{1,0:T(8,128)}, u32[]{:S(2)}) copy-start(f32[192,192]{1,0:T(8,128)} %fusion.36) | copy-start | bytes 442372
  58.5 22.8 %collective-permute-start.4 = (bf16[192,14,3]{0,2,1:T(4,128)(2,1)}, bf16[192,14,3]{0,2,1:T(4,128)(2,1)S(1)}, u32[]{:S(2)}, u32[]{:S(2)}) collective-permute-start(bf16[192,14,3]{0,2,1:T(4,128)(2,1)} %get-tuple-element.32), channel_id=1, source_target_pairs={{0,4},{4,8},{8,12},{1,5},{5,9},{9,13},{2,6},{6,10},{10,14},{3,7},{... | collective-permute-start | bytes 48392 | tf_op jit(solution)/shard_map/ppermute | solution.py:22
  62.0 19.3 %collective-permute-start.5 = (bf16[192,14,3]{0,2,1:T(4,128)(2,1)}, bf16[192,14,3]{0,2,1:T(4,128)(2,1)}, u32[]{:S(2)}, u32[]{:S(2)}) collective-permute-start(bf16[192,14,3]{0,2,1:T(4,128)(2,1)} %get-tuple-element.33), channel_id=1, source_target_pairs={{4,0},{8,4},{12,8},{5,1},{9,5},{13,9},{6,2},{10,6},{14,10},{7,3},{... | collective-permute-start | bytes 48392 | tf_op jit(solution)/shard_map/ppermute | solution.py:23
  89.1 3.8 %copy-start.6 = (f32[36864]{0:T(1024)S(1)}, f32[36864]{0:T(1024)}, u32[]{:S(2)}) copy-start(f32[36864]{0:T(1024)} %reshape.278) | copy-start | bytes 442372
  89.1 3.8 %copy-start.7 = (f32[36864]{0:T(1024)S(1)}, f32[36864]{0:T(1024)}, u32[]{:S(2)}) copy-start(f32[36864]{0:T(1024)} %reshape.279) | copy-start | bytes 442372
  89.1 3.8 %copy-start.16 = (f32[192]{0:T(256)S(1)}, f32[192]{0:T(256)}, u32[]{:S(2)}) copy-start(f32[192]{0:T(256)} %get-tuple-element.24) | copy-start | bytes 2308
  94.8 7.3 %collective-permute-start.6 = (f32[84288]{0:T(1024)S(1)}, f32[84288]{0:T(1024)S(1)}, u32[]{:S(2)}, u32[]{:S(2)}) collective-permute-start(f32[84288]{0:T(1024)S(1)} %concatenate.23), channel_id=1, source_target_pairs={{0,16},{16,0},{1,17},{17,1},{2,18},{18,2},{3,19},{19,3},{4,20},{20... | collective-permute-start | bytes 1011464 | tf_op jit(solution)/shard_map/ppermute | solution.py:123
  102.1 7.8 %collective-permute-start.7 = (f32[84288]{0:T(1024)S(1)}, f32[84288]{0:T(1024)S(1)}, u32[]{:S(2)}, u32[]{:S(2)}) collective-permute-start(f32[84288]{0:T(1024)S(1)} %add.124), channel_id=1, source_target_pairs={{0,4},{4,0},{8,12},{12,8},{1,5},{5,1},{9,13},{13,9},{2,6},{6,2},{1... | collective-permute-start | bytes 1011464 | tf_op jit(solution)/shard_map/ppermute | solution.py:123
  109.9 16.5 %collective-permute-start.8 = (f32[84288]{0:T(1024)S(1)}, f32[84288]{0:T(1024)S(1)}, u32[]{:S(2)}, u32[]{:S(2)}) collective-permute-start(f32[84288]{0:T(1024)S(1)} %add.125), channel_id=1, source_target_pairs={{0,8},{4,12},{8,0},{12,4},{1,9},{5,13},{9,1},{13,5},{2,10},{6,14},... | collective-permute-start | bytes 1011464 | tf_op jit(solution)/shard_map/ppermute | solution.py:123
  (5 other events, 4.8 us)

commit v5 on v4

--- a/solution.py
+++ b/solution.py
@@ -98,11 +98,9 @@
     lax.fori_loop(0, rows, row_step, 0)
 
 
-def kernel_grad(d_grid, padded):
-    d_t = jnp.transpose(d_grid, (1, 2, 0))
-    p_t = jnp.transpose(padded, (1, 2, 0))
-    side = padded.shape[1] - d_grid.shape[1] + 1
-    channel_count = d_grid.shape[0]
+def kernel_grad_minor(d_t, p_t):
+    side = p_t.shape[0] - d_t.shape[0] + 1
+    channel_count = d_t.shape[-1]
     partial = pl.pallas_call(
         kernel_grad_body,
         out_shape=jax.ShapeDtypeStruct((side * side, 8, channel_count), jnp.float32),
@@ -150,6 +148,19 @@
     return w_in_all, b_in_all, w_out_all
 
 
+def depthwise_minor(padded_t, kernel):
+    channel_count = padded_t.shape[-1]
+    return lax.conv_general_dilated(
+        padded_t[None],
+        kernel[:, :, None, :],
+        (1, 1),
+        "VALID",
+        dimension_numbers=("NHWC", "HWIO", "NHWC"),
+        feature_group_count=channel_count,
+        precision=lax.Precision.HIGHEST,
+    )[0]
+
+
 def shards(
     feature,
     kernel,
@@ -170,60 +181,62 @@
     own = lax.axis_index("chan")
     w_in_all, b_in_all, w_out_all = gathered_weights(w_in, b_in, w_out)
     padded_bf = extended(feature, (("row", 1), ("col", 2)), 3)
-    padded = padded_bf.astype(jnp.float32)
+    padded_t = jnp.transpose(padded_bf, (1, 2, 0)).astype(jnp.float32)
     total_pixels = pixel_count * lax.axis_size("row") * lax.axis_size("col")
     norm_factor = 1.0 / jnp.sqrt(jnp.float32(total_pixels))
-    convolved_output = depthwise(padded, kernel) + conv_bias[:, None, None]
-    standardized_input, inverse_deviation, normalized_output = layer_norm_forward(
-        convolved_output.reshape(channel_count, pixel_count), norm_gain, norm_bias
-    )
-    pre_act = contract(w_in_all, normalized_output, 0, 0) + b_in_all[:, None]
+    conv_flat = (depthwise_minor(padded_t, kernel) + conv_bias).reshape(pixel_count, channel_count)
+    mean_val = jnp.mean(conv_flat, axis=1, keepdims=True)
+    centered_values = conv_flat - mean_val
+    variance = jnp.mean(centered_values * centered_values, axis=1, keepdims=True)
+    inverse_deviation = lax.rsqrt(variance + 1e-06)
+    standardized_input = centered_values * inverse_deviation
+    normalized_output = (standardized_input * norm_gain + norm_bias).astype(jnp.bfloat16)
+    pre_act = contract(normalized_output, w_in_all, 1, 0) + b_in_all
     gelu_val, gelu_slope = gelu_parts(pre_act)
     hidden = gelu_val.astype(jnp.bfloat16)
-    w_out_blocks = w_out_all.reshape(blocks, share, channel_count)
-    hidden_blocks = hidden.reshape(blocks, share, pixel_count)
     out_partials = lax.dot_general(
-        w_out_blocks,
-        hidden_blocks,
-        (((1,), (1,)), ((0,), (0,))),
+        hidden.reshape(pixel_count, blocks, share),
+        w_out_all.reshape(blocks, share, channel_count),
+        (((2,), (1,)), ((1,), (0,))),
         preferred_element_type=jnp.float32,
     )
     mixed_sum = jnp.sum(out_partials.astype(jnp.bfloat16).astype(jnp.float32), axis=0)
-    branch = mixed_sum + b_out[:, None]
-    feature_flat = feature.reshape(channel_count, pixel_count)
-    result = (
-        (feature_flat.astype(jnp.float32) + layer_scale[:, None] * branch)
-        .astype(jnp.bfloat16)
-        .reshape(channel_count, tile_rows, tile_cols)
-    )
-    grad_out = cotangent.reshape(channel_count, pixel_count).astype(jnp.float32)
-    g_branch = grad_out * layer_scale[:, None]
-    grad_layer_scale = jnp.sum(grad_out * branch, axis=1)
-    grad_b_out = jnp.sum(g_branch, axis=1)
+    branch = mixed_sum + b_out
+    feature_t = jnp.transpose(feature, (1, 2, 0)).reshape(pixel_count, channel_count)
+    result_t = (feature_t.astype(jnp.float32) + layer_scale * branch).astype(jnp.bfloat16)
+    result = jnp.transpose(result_t.reshape(tile_rows, tile_cols, channel_count), (2, 0, 1))
+    cotangent_t = jnp.transpose(cotangent, (1, 2, 0))
+    grad_out = cotangent_t.reshape(pixel_count, channel_count).astype(jnp.float32)
+    g_branch = grad_out * layer_scale
+    grad_layer_scale = jnp.sum(grad_out * branch, axis=0)
+    grad_b_out = jnp.sum(g_branch, axis=0)
     g_out = g_branch.astype(jnp.bfloat16)
-    d_pre = contract(w_out_all, g_out, 1, 0) * gelu_slope
+    d_pre = contract(g_out, w_out_all, 1, 1) * gelu_slope
     g_pre = d_pre.astype(jnp.bfloat16)
-    hidden_own = lax.dynamic_slice_in_dim(hidden, own * share, share, axis=0)
-    g_pre_own = lax.dynamic_slice_in_dim(g_pre, own * share, share, axis=0)
-    d_pre_own = lax.dynamic_slice_in_dim(d_pre, own * share, share, axis=0)
-    grad_w_out = contract(hidden_own, g_out, 1, 1)
-    grad_b_in = jnp.sum(d_pre_own, axis=1)
-    grad_w_in = contract(normalized_output, g_pre_own, 1, 1)
-    w_in_blocks = jnp.transpose(w_in_all.reshape(channel_count, blocks, share), (1, 0, 2))
-    g_pre_blocks = g_pre.reshape(blocks, share, pixel_count)
+    hidden_own = lax.dynamic_slice_in_dim(hidden, own * share, share, axis=1)
+    g_pre_own = lax.dynamic_slice_in_dim(g_pre, own * share, share, axis=1)
+    d_pre_own = lax.dynamic_slice_in_dim(d_pre, own * share, share, axis=1)
+    grad_w_out = contract(hidden_own, g_out, 0, 0)
+    grad_b_in = jnp.sum(d_pre_own, axis=0)
+    grad_w_in = contract(normalized_output, g_pre_own, 0, 0)
     dn_partials = lax.dot_general(
-        w_in_blocks,
-        g_pre_blocks,
-        (((2,), (1,)), ((0,), (0,))),
+        g_pre.reshape(pixel_count, blocks, share),
+        w_in_all.reshape(channel_count, blocks, share),
+        (((2,), (2,)), ((1,), (1,))),
         preferred_element_type=jnp.float32,
     )
     normalized_gradient = jnp.sum(dn_partials.astype(jnp.bfloat16).astype(jnp.float32), axis=0)
-    convolved_gradient, gain_portion, bias_portion = layer_norm_backward(
-        normalized_gradient, standardized_input, inverse_deviation, norm_gain
-    )
-    grad_conv_bias = jnp.sum(convolved_gradient, axis=1)
-    d_grid = convolved_gradient.reshape(channel_count, tile_rows, tile_cols)
-    grad_kernel = kernel_grad(d_grid, padded)
+    standardized_gradient = normalized_gradient * norm_gain
+    initial_mean = jnp.mean(standardized_gradient, axis=1, keepdims=True)
+    product_mean = jnp.mean(standardized_gradient * standardized_input, axis=1, keepdims=True)
+    convolved_gradient = inverse_deviation * (
+        standardized_gradient - initial_mean - standardized_input * product_mean
+    )
+    gain_portion = jnp.sum(normalized_gradient * standardized_input, axis=0)
+    bias_portion = jnp.sum(normalized_gradient, axis=0)
+    grad_conv_bias = jnp.sum(convolved_gradient, axis=0)
+    d_t = convolved_gradient.reshape(tile_rows, tile_cols, channel_count)
+    grad_kernel = kernel_grad_minor(d_t, padded_t)
     (
         grad_kernel,
         grad_conv_bias,
@@ -248,10 +261,11 @@
         ),
         ("row", "col"),
     )
-    d_padded = extended(shortened(d_grid), (("row", 1), ("col", 2)), 3).astype(d_grid.dtype)
-    grad_feature = (cotangent.astype(jnp.float32) + depthwise(d_padded, kernel[::-1, ::-1])).astype(
-        jnp.bfloat16
-    )
+    d_padded = extended(d_t.astype(jnp.bfloat16), (("row", 0), ("col", 1)), 3).astype(jnp.float32)
+    grad_feature_t = (
+        cotangent_t.astype(jnp.float32) + depthwise_minor(d_padded, kernel[::-1, ::-1])
+    ).astype(jnp.bfloat16)
+    grad_feature = jnp.transpose(grad_feature_t, (2, 0, 1))
     return (
         result,
         grad_feature,

time: 130 us -> 128 us (0.985)
  other arithmetic: 18.1 us -> 15.2 us
  starting transfers between devices: 21.2 us -> 19.6 us
  matrix products: 22.4 us -> 23.8 us
    convert_element_type x0 -> x2, other arithmetic: none -> 3.11 us  [the longest x1 1.62 us: shards(): padded_t = jnp.transpose(padded_bf, (1, 2, 0)).astype(jnp.float32)]
    transpose x2 -> x0, other arithmetic: 3.09 us -> none  [the longest x1 1.61 us: kernel_grad(): p_t = jnp.transpose(padded, (1, 2, 0))]
    ppermute x3, starting transfers between devices: 8.07 us -> 6.28 us  [butterfly_sum(): lax.ppermute(flat, axis, [(i, i ^ step) for i in range(devices)])]
    reduce_sum x8, other arithmetic: 11 us -> 9.42 us  [the longest x1 4.66 us: shards(): grad_layer_scale = jnp.sum(grad_out * branch, axis=0)]
    dot_general x4, matrix products: 7.95 us -> 9.34 us  [contract(): lax.dot_general(left, right, (((dim_left,), (dim_right,)), ((), ())), pre...]
    conv_general_dilated x5 -> x6, local copies, waits for them, and re-layouts: 2.08 us -> 3.34 us  [depthwise_minor(): lax.conv_general_dilated(padded_t[None], kernel[:, :, None, :], (1, 1), '...]
    unnamed x46 -> x50, local copies, waits for them, and re-layouts: 4.55 us -> 4.75 us
  transfers between devices with their start and end apart: 9 -> 9, of which waited for: 5 -> 5; matrix products, arithmetic and copies ran while one was open for 12% -> 9% of each run, Pallas kernels for 8% -> 8%
where the time goes in v5:
time: 128 us; the launch traced here: 127 us
  waiting for transfers between devices  30.3 us (24%)
  matrix products  23.8 us (19%)
  starting transfers between devices  19.6 us (15%)
  local copies, waits for them, and re-layouts  18.4 us (14%)
  other arithmetic  15.2 us (12%)
  Pallas kernels  9.99 us (8%)
  blocking collectives  8.6 us (7%)
    ppermute x3, waiting for transfers between devices, butterfly_sum(): lax.ppermute(flat, axis, [(i, i ^ step) for i in range(devices)])  22.9 us
    conv_general_dilated x2, matrix products, depthwise_minor(): lax.conv_general_dilated(padded_t[None], kernel[:, :, None, :], (1, 1), '...  12.5 us
    pallas_call x1, Pallas kernels, kernel_grad_minor(): pl.pallas_call(kernel_grad_body, out_shape=jax.ShapeDtypeStruct((side * s...  9.99 us
    dot_general x4, matrix products, contract(): lax.dot_general(left, right, (((dim_left,), (dim_right,)), ((), ())), pre...  9.34 us
    all_gather x1, blocking collectives, gathered_weights(): full = lax.all_gather(packed, 'chan', axis=0, tiled=True)  8.6 us
    ppermute x2, starting transfers between devices, extended(): before = lax.ppermute(last, axis, up)  6.98 us
    ppermute x3, starting transfers between devices, butterfly_sum(): lax.ppermute(flat, axis, [(i, i ^ step) for i in range(devices)])  6.28 us
    unnamed x50, local copies, waits for them, and re-layouts  4.75 us
  transfers between devices with their start and end apart: 9, of which 5 were waited for; matrix products, arithmetic and copies ran while one was open for 9% of the time, Pallas kernels for 8%

profile of v5, /device:TPU:0, one launch (start us, length us, event | category | flops | bytes accessed | tf_op | source)
XLA Modules:
  0.0 127.2 jit_solution(10518636248623048770)
XLA Ops:
  1.9 3.0 %collective-permute-start = (bf16[192,3,128]{0,2,1:T(8,128)(2,1)S(1)}, bf16[192,3,128]{0,2,1:T(8,128)(2,1)S(1)}, u32[]{:S(2)}, u32[]{:S(2)}) collective-permute-start(bf16[192,3,128]{0,2,1:T(8,128)(2,1)S(1)} %slice_select_fusion.1), channel_id=1, source_target_pairs={{0,16},{16,0},{1,17},{17,1},{2,18},{18,2},{3,19},{19,3},{4,20},{20... | collective-permute-start | bytes 442376 | tf_op jit(solution)/shard_map/ppermute | solution.py:17
  8.1 8.6 %all_gather.3 = bf16[768,387]{1,0:T(8,128)(2,1)S(1)} all-gather(bf16[192,387]{1,0:T(8,128)(2,1)S(1)} %concatenate.20), channel_id=1, replica_groups=mesh['row'=2,'col'=4,'chan'=4] {'chan'}, dimensions={0}, use_global_device_ids=true | all-gather | bytes 743040 | tf_op jit(solution)/shard_map/all_gather | solution.py:143
  17.8 3.5 %collective-permute-start.1 = (bf16[192,14,3]{0,2,1:T(4,128)(2,1)S(1)}, bf16[192,14,3]{0,2,1:T(4,128)(2,1)S(1)}, u32[]{:S(2)}, u32[]{:S(2)}) collective-permute-start(bf16[192,14,3]{0,2,1:T(4,128)(2,1)S(1)} %get-tuple-element.34), channel_id=1, source_target_pairs={{0,4},{4,8},{8,12},{1,5},{5,9},{9,13},{2,6},{6,10},{10,14},{3,7},{... | collective-permute-start | bytes 48392 | tf_op jit(solution)/shard_map/ppermute | solution.py:22
  23.8 3.3 %collective-permute-done.2 = bf16[192,14,3]{0,2,1:T(4,128)(2,1)S(1)} collective-permute-done((bf16[192,14,3]{0,2,1:T(4,128)(2,1)S(1)}, bf16[192,14,3]{0,2,1:T(4,128)(2,1)S(1)}, u32[]{:S(2)}, u32[]{:S(2)}) %collective-permute-start.2) | collective-permute-done | bytes 16160 | tf_op jit(solution)/shard_map/ppermute | solution.py:23
  27.0 1.6 %bitcast_convert_fusion = (f32[14,134,192]{2,1,0:T(8,128)}, bf16[1,14,134,192]{3,2,1,0:T(8,128)(2,1)S(1)}) fusion(bf16[192,14,3]{0,2,1:T(4,128)(2,1)S(1)} %collective-permute-done.2, bf16[192,3,128]{0,2,1:T(8,128)(2,1)S(1)} %get-tuple-element.51, bf16[192,8,128]{0,2,1:T(8,128)(2,1)S(1)} %copy.84, bf16[192,3,128]{0,2,1:T(8,128)(2,1)S(1)} %get-tuple-element.50, ...), kind=kLoop, calls=%fused_computation.32 | loop fusion | flops 3962112 | bytes 2881536 | tf_op jit(solution)/shard_map/convert_element_type | solution.py:184
  28.7 8.4 %fusion.6 = f32[1,8,128,192]{3,0,2,1:T(1,128)S(1)} fusion(bf16[1,14,134,192]{3,2,1,0:T(8,128)(2,1)S(1)} %get-tuple-element.31, f32[7,7,1,192]{3,1,0,2:T(8,128)S(1)} %bitcast.132), kind=kOutput, calls=%fused_computation.13 | convolution fusion | flops 115605504 | bytes 1544448 | tf_op jit(solution)/shard_map/conv_general_dilated | solution.py:153
  37.8 1.9 %copy.89 = f32[1,8,128,192]{2,1,3,0:T(8,128)} copy(f32[1,8,128,192]{3,0,2,1:T(1,128)S(1)} %fusion.6) | data formatting | bytes 1572864 | tf_op jit(solution)/shard_map/conv_general_dilated | solution.py:153
  40.0 3.3 %multiply_convert_fusion = (bf16[1024,768]{0,1:T(8,128)(2,1)}, f32[1024,768]{0,1:T(8,128)S(1)}) fusion(f32[768]{0:T(1024)S(1)} %fusion.35, f32[24,8,8,128]{3,2,1,0:T(8,128)} %bitcast.127, f32[192]{0:T(256)S(1)} %copy-done.19, f32[192]{0:T(256)S(1)} %copy-done.13, f32[1024]{0:T(1024)S(1)} %get-tuple-element.53, f32[1024]{0:T(1024)S(1)} %get-tuple-element.54, ...), kind=kOutput, calls=%fused_computation.9 | convolution fusion | flops 307888128 | bytes 5913600 | tf_op jit(solution)/shard_map/dot_general | solution.py:52
  43.3 3.3 %fusion.61 = (bf16[1024,768]{0,1:T(8,128)(2,1)S(1)}, f32[1024,768]{0,1:T(8,128)}) fusion(f32[1024,768]{0,1:T(8,128)S(1)} %get-tuple-element.60, f32[768]{0:T(1024)S(1)} %fusion.35, f32[24,8,8,128]{3,2,1,0:T(8,128)S(1)} %convert.4, f32[192]{0:T(256)S(1)} %copy-done.17, bf16[768,387]{1,0:T(8,128)(2,1)S(1)} %all_gather.3), kind=kOutput, calls=%fused_computation.112 | convolution fusion | flops 311033856 | bytes 9049088 | tf_op jit(solution)/shard_map/dot_general | solution.py:52
  49.5 2.3 %fusion.38 = f32[192,192]{1,0:T(8,128)} fusion(bf16[1024,768]{0,1:T(8,128)(2,1)} %copy-done.20, s32[]{:T(128)S(6)} %select_n.45, f32[24,8,8,128]{3,2,1,0:T(8,128)} %bitcast.128, f32[192]{0:T(256)S(1)} %copy-done.19, f32[192]{0:T(256)S(1)} %copy-done.13, f32[1024]{0:T(1024)S(1)} %get-tuple-element.53, f32[1024]{0:T(1024)S(1)} %get-tuple-element.54, ...), kind=kOutput, calls=%fused_computation.66 | convolution fusion | flops 76677120 | bytes 1337604 | tf_op jit(solution)/shard_map/dot_general | solution.py:52
  53.0 1.5 %fusion.58 = (bf16[8,128,192]{2,1,0:T(8,128)(2,1)S(1)}, f32[8,128,192]{2,1,0:T(8,128)}) fusion(f32[8,128]{1,0:T(8,128)S(1)} %broadcast_multiply_fusion, f32[8,128]{1,0:T(8,128)S(1)} %get-tuple-element.55, f32[192]{0:T(256)S(1)} %copy-done.12, f32[1,8,128,192]{3,0,2,1:T(1,128)S(1)} %fusion.6, f32[8,128]{1,0:T(8,128)S(1)} %multiply_bitcast_fusion, ...), kind=kLoop, calls=%fused_computation.110 | loop fusion | flops 1769472 | bytes 2770432 | tf_op jit(solution)/shard_map/convert_element_type | solution.py:264
  56.2 4.1 %collective-permute-done.3 = bf16[3,128,192]{2,1,0:T(8,128)(2,1)S(1)} collective-permute-done((bf16[3,128,192]{2,1,0:T(8,128)(2,1)S(1)}, bf16[3,128,192]{2,1,0:T(8,128)(2,1)S(1)}, u32[]{:S(2)}, u32[]{:S(2)}) %collective-permute-start.3) | collective-permute-done | bytes 147488 | tf_op jit(solution)/shard_map/ppermute | solution.py:17
  60.4 3.5 %collective-permute-start.4 = (bf16[14,3,192]{2,1,0:T(4,128)(2,1)S(1)}, bf16[14,3,192]{2,1,0:T(4,128)(2,1)S(1)}, u32[]{:S(2)}, u32[]{:S(2)}) collective-permute-start(bf16[14,3,192]{2,1,0:T(4,128)(2,1)S(1)} %get-tuple-element.32), channel_id=1, source_target_pairs={{0,4},{4,8},{8,12},{1,5},{5,9},{9,13},{2,6},{6,10},{10,14},{3,7},{... | collective-permute-start | bytes 48392 | tf_op jit(solution)/shard_map/ppermute | solution.py:22
  63.9 1.5 %collective-permute-start.5 = (bf16[14,3,192]{2,1,0:T(4,128)(2,1)S(1)}, bf16[14,3,192]{2,1,0:T(4,128)(2,1)S(1)}, u32[]{:S(2)}, u32[]{:S(2)}) collective-permute-start(bf16[14,3,192]{2,1,0:T(4,128)(2,1)S(1)} %get-tuple-element.33), channel_id=1, source_target_pairs={{4,0},{8,4},{12,8},{5,1},{9,5},{13,9},{6,2},{10,6},{14,10},{7,3},{... | collective-permute-start | bytes 48392 | tf_op jit(solution)/shard_map/ppermute | solution.py:23
  66.8 10.0 %shard_map.194 = f32[49,8,192]{2,1,0:T(8,128)} custom-call(f32[8,128,192]{2,1,0:T(8,128)} %get-tuple-element.29.d_ref, f32[14,134,192]{2,1,0:T(8,128)} %get-tuple-element.30.p_ref), custom_call_target="tpu_custom_call" | custom-call | tf_op jit(solution)/shard_map/pallas_call | solution.py:104
  79.4 1.8 %dynamic-slice_reduce_fusion = f32[192]{0:T(256)} fusion(f32[1024,768]{0,1:T(8,128)} %get-tuple-element.62, s32[]{:T(128)S(6)} %select_n.45), kind=kLoop, calls=%fused_computation.50 | loop fusion | flops 196416 | bytes 787204 | tf_op jit(solution)/shard_map/reduce_sum | solution.py:220
  82.6 4.1 %fusion.15 = f32[8,8,17,192]{3,1,2,0:T(8,128)S(1)} fusion(bf16[14,1,7,6,192]{4,2,3,0,1:T(8,128)(2,1)S(1)} %slice.120, bf16[14,1,8,17,192]{4,2,3,0,1:T(8,128)(2,1)S(1)} %copy.105, pred[8,17]{0,1:T(8,128)(4,1)S(1)} %copy-done.21, f32[7,7,1,192]{3,1,0,2:T(8,128)S(1)} %bitcast.133), kind=kOutput, calls=%fused_computation.23 | convolution fusion | flops 126007296 | bytes 1830280 | tf_op jit(solution)/shard_map/conv_general_dilated | solution.py:153
  88.2 4.7 %fusion.31 = (f32[192]{0:T(256)S(1)}, f32[192]{0:T(256)S(1)}, bf16[8,128,192]{1,0,2:T(8,128)(2,1)}, bf16[192,8,128]{2,1,0:T(8,128)(2,1)}) fusion(f32[24,8,8,128]{3,2,1,0:T(8,128)S(1)} %copy.120, bf16[192,8,128]{2,1,0:T(8,128)(2,1)S(1)} %copy-done.4, f32[192]{0:T(256)} %param.19, f32[192]{0:T(256)} %param.20, bf16[192,8,128]{2,1,0:T(8,128)(2,1)S(1)} %copy-done.2, ...), kind=kLoop, calls=%fused_computation.47 | loop fusion | flops 2358912 | bytes 3148800 | tf_op jit(solution)/shard_map/reduce_sum | solution.py:211
  92.9 1.9 %concatenate.23 = f32[84288]{0:T(1024)S(1)} concatenate(f32[9408]{0:T(1024)S(1)} %copy-done.9, f32[192]{0:T(256)S(1)} %copy-done.15, f32[192]{0:T(256)S(1)} %copy-done.14, f32[192]{0:T(256)S(1)} %copy-done.18, f32[36864]{0:T(1024)S(1)} %reshape.310, f32[192]{0:T(256)S(1)} %copy-done.16, f32[36864]{0:T(1024)S(1)} %copy-done.6, f32[192]{0:T(256)S(1)} %get-tuple-element.27, ...), dimensions={0} | concatenate | bytes 674304 | tf_op jit(solution)/shard_map/concatenate | solution.py:113
  95.3 6.8 %collective-permute-done.6 = f32[84288]{0:T(1024)S(1)} collective-permute-done((f32[84288]{0:T(1024)S(1)}, f32[84288]{0:T(1024)S(1)}, u32[]{:S(2)}, u32[]{:S(2)}) %collective-permute-start.6) | collective-permute-done | bytes 337184 | tf_op jit(solution)/shard_map/ppermute | solution.py:121
  102.2 2.6 %collective-permute-start.7 = (f32[84288]{0:T(1024)S(1)}, f32[84288]{0:T(1024)S(1)}, u32[]{:S(2)}, u32[]{:S(2)}) collective-permute-start(f32[84288]{0:T(1024)S(1)} %add.133), channel_id=1, source_target_pairs={{0,4},{4,0},{8,12},{12,8},{1,5},{5,1},{9,13},{13,9},{2,6},{6,2},{1... | collective-permute-start | bytes 1011464 | tf_op jit(solution)/shard_map/ppermute | solution.py:121
  104.8 7.3 %collective-permute-done.7 = f32[84288]{0:T(1024)S(1)} collective-permute-done((f32[84288]{0:T(1024)S(1)}, f32[84288]{0:T(1024)S(1)}, u32[]{:S(2)}, u32[]{:S(2)}) %collective-permute-start.7) | collective-permute-done | bytes 337184 | tf_op jit(solution)/shard_map/ppermute | solution.py:121
  112.1 3.2 %collective-permute-start.8 = (f32[84288]{0:T(1024)S(1)}, f32[84288]{0:T(1024)S(1)}, u32[]{:S(2)}, u32[]{:S(2)}) collective-permute-start(f32[84288]{0:T(1024)S(1)} %add.134), channel_id=1, source_target_pairs={{0,8},{4,12},{8,0},{12,4},{1,9},{5,13},{9,1},{13,5},{2,10},{6,14},... | collective-permute-start | bytes 1011464 | tf_op jit(solution)/shard_map/ppermute | solution.py:121
  115.3 8.8 %collective-permute-done.8 = f32[84288]{0:T(1024)S(1)} collective-permute-done((f32[84288]{0:T(1024)S(1)}, f32[84288]{0:T(1024)S(1)}, u32[]{:S(2)}, u32[]{:S(2)}) %collective-permute-start.8) | collective-permute-done | bytes 337184 | tf_op jit(solution)/shard_map/ppermute | solution.py:121
  (106 shorter events, 25.1 us)
Async XLA Ops:
  1.9 15.8 %collective-permute-start = (bf16[192,3,128]{0,2,1:T(8,128)(2,1)S(1)}, bf16[192,3,128]{0,2,1:T(8,128)(2,1)S(1)}, u32[]{:S(2)}, u32[]{:S(2)}) collective-permute-start(bf16[192,3,128]{0,2,1:T(8,128)(2,1)S(1)} %slice_select_fusion.1), channel_id=1, source_target_pairs={{0,16},{16,0},{1,17},{17,1},{2,18},{18,2},{3,19},{19,3},{4,20},{20... | collective-permute-start | bytes 442376 | tf_op jit(solution)/shard_map/ppermute | solution.py:17
  17.7 5.3 %copy-start.3 = (bf16[192,8,128]{2,1,0:T(8,128)(2,1)S(1)}, bf16[192,8,128]{2,1,0:T(8,128)(2,1)}, u32[]{:S(2)}) copy-start(bf16[192,8,128]{2,1,0:T(8,128)(2,1)} %param.21) | copy-start | bytes 1179652
  17.7 5.4 %copy-start.10 = (f32[7,7,192]{2,1,0:T(8,128)S(1)}, f32[7,7,192]{2,1,0:T(8,128)}, u32[]{:S(2)}) copy-start(f32[7,7,192]{2,1,0:T(8,128)} %param.12) | copy-start | bytes 112900
  17.8 6.0 %collective-permute-start.1 = (bf16[192,14,3]{0,2,1:T(4,128)(2,1)S(1)}, bf16[192,14,3]{0,2,1:T(4,128)(2,1)S(1)}, u32[]{:S(2)}, u32[]{:S(2)}) collective-permute-start(bf16[192,14,3]{0,2,1:T(4,128)(2,1)S(1)} %get-tuple-element.34), channel_id=1, source_target_pairs={{0,4},{4,8},{8,12},{1,5},{5,9},{9,13},{2,6},{6,10},{10,14},{3,7},{... | collective-permute-start | bytes 48392 | tf_op jit(solution)/shard_map/ppermute | solution.py:22
  21.3 5.8 %collective-permute-start.2 = (bf16[192,14,3]{0,2,1:T(4,128)(2,1)S(1)}, bf16[192,14,3]{0,2,1:T(4,128)(2,1)S(1)}, u32[]{:S(2)}, u32[]{:S(2)}) collective-permute-start(bf16[192,14,3]{0,2,1:T(4,128)(2,1)S(1)} %get-tuple-element.35), channel_id=1, source_target_pairs={{4,0},{8,4},{12,8},{5,1},{9,5},{13,9},{6,2},{10,6},{14,10},{7,3},{... | collective-permute-start | bytes 48392 | tf_op jit(solution)/shard_map/ppermute | solution.py:23
  37.1 2.5 %copy-start.12 = (f32[192]{0:T(256)S(1)}, f32[192]{0:T(256)}, u32[]{:S(2)}) copy-start(f32[192]{0:T(256)} %param.13) | copy-start | bytes 2308
  37.7 2.2 %copy-start.13 = (f32[192]{0:T(256)S(1)}, f32[192]{0:T(256)}, u32[]{:S(2)}) copy-start(f32[192]{0:T(256)} %param.14) | copy-start | bytes 2308
  37.7 2.2 %copy-start.19 = (f32[192]{0:T(256)S(1)}, f32[192]{0:T(256)}, u32[]{:S(2)}) copy-start(f32[192]{0:T(256)} %param.15) | copy-start | bytes 2308
  40.0 3.4 %copy-start.17 = (f32[192]{0:T(256)S(1)}, f32[192]{0:T(256)}, u32[]{:S(2)}) copy-start(f32[192]{0:T(256)} %param.20) | copy-start | bytes 2308
  43.3 3.3 %copy-start.7 = (bf16[768,192]{1,0:T(8,128)(2,1)S(1)}, bf16[768,192]{1,0:T(8,128)(2,1)}, u32[]{:S(2)}) copy-start(bf16[768,192]{1,0:T(8,128)(2,1)} %get-tuple-element.37) | copy-start | bytes 884740
  53.0 2.5 %copy-start.5 = (bf16[768,192]{1,0:T(8,128)(2,1)S(1)}, bf16[768,192]{1,0:T(8,128)(2,1)}, u32[]{:S(2)}) copy-start(bf16[768,192]{1,0:T(8,128)(2,1)} %get-tuple-element.38) | copy-start | bytes 884740
  54.5 5.8 %collective-permute-start.3 = (bf16[3,128,192]{2,1,0:T(8,128)(2,1)S(1)}, bf16[3,128,192]{2,1,0:T(8,128)(2,1)S(1)}, u32[]{:S(2)}, u32[]{:S(2)}) collective-permute-start(bf16[3,128,192]{2,1,0:T(8,128)(2,1)S(1)} %slice_select_fusion), channel_id=1, source_target_pairs={{0,16},{16,0},{1,17},{17,1},{2,18},{18,2},{3,19},{19,3},{4,20},{20... | collective-permute-start | bytes 442376 | tf_op jit(solution)/shard_map/ppermute | solution.py:17
  56.2 10.3 %copy-start.8 = (f32[192,192]{1,0:T(8,128)S(1)}, f32[192,192]{1,0:T(8,128)}, u32[]{:S(2)}) copy-start(f32[192,192]{1,0:T(8,128)} %fusion.38) | copy-start | bytes 442372
  60.4 20.8 %collective-permute-start.4 = (bf16[14,3,192]{2,1,0:T(4,128)(2,1)S(1)}, bf16[14,3,192]{2,1,0:T(4,128)(2,1)S(1)}, u32[]{:S(2)}, u32[]{:S(2)}) collective-permute-start(bf16[14,3,192]{2,1,0:T(4,128)(2,1)S(1)} %get-tuple-element.32), channel_id=1, source_target_pairs={{0,4},{4,8},{8,12},{1,5},{5,9},{9,13},{2,6},{6,10},{10,14},{3,7},{... | collective-permute-start | bytes 48392 | tf_op jit(solution)/shard_map/ppermute | solution.py:22
  63.9 17.3 %collective-permute-start.5 = (bf16[14,3,192]{2,1,0:T(4,128)(2,1)S(1)}, bf16[14,3,192]{2,1,0:T(4,128)(2,1)S(1)}, u32[]{:S(2)}, u32[]{:S(2)}) collective-permute-start(bf16[14,3,192]{2,1,0:T(4,128)(2,1)S(1)} %get-tuple-element.33), channel_id=1, source_target_pairs={{4,0},{8,4},{12,8},{5,1},{9,5},{13,9},{6,2},{10,6},{14,10},{7,3},{... | collective-permute-start | bytes 48392 | tf_op jit(solution)/shard_map/ppermute | solution.py:23
  88.2 4.7 %copy-start.6 = (f32[36864]{0:T(1024)S(1)}, f32[36864]{0:T(1024)}, u32[]{:S(2)}) copy-start(f32[36864]{0:T(1024)} %reshape.311) | copy-start | bytes 442372
  88.2 4.7 %copy-start.9 = (f32[9408]{0:T(1024)S(1)}, f32[9408]{0:T(1024)}, u32[]{:S(2)}) copy-start(f32[9408]{0:T(1024)} %reshape_reshape.3) | copy-start | bytes 112900
  88.2 4.7 %copy-start.14 = (f32[192]{0:T(256)S(1)}, f32[192]{0:T(256)}, u32[]{:S(2)}) copy-start(f32[192]{0:T(256)} %get-tuple-element.22) | copy-start | bytes 2308
  88.2 4.7 %copy-start.15 = (f32[192]{0:T(256)S(1)}, f32[192]{0:T(256)}, u32[]{:S(2)}) copy-start(f32[192]{0:T(256)} %get-tuple-element.23) | copy-start | bytes 2308
  88.2 4.7 %copy-start.16 = (f32[192]{0:T(256)S(1)}, f32[192]{0:T(256)}, u32[]{:S(2)}) copy-start(f32[192]{0:T(256)} %dynamic-slice_reduce_fusion) | copy-start | bytes 2308
  88.2 4.7 %copy-start.18 = (f32[192]{0:T(256)S(1)}, f32[192]{0:T(256)}, u32[]{:S(2)}) copy-start(f32[192]{0:T(256)} %get-tuple-element.24) | copy-start | bytes 2308
  94.8 7.3 %collective-permute-start.6 = (f32[84288]{0:T(1024)S(1)}, f32[84288]{0:T(1024)S(1)}, u32[]{:S(2)}, u32[]{:S(2)}) collective-permute-start(f32[84288]{0:T(1024)S(1)} %concatenate.23), channel_id=1, source_target_pairs={{0,16},{16,0},{1,17},{17,1},{2,18},{18,2},{3,19},{19,3},{4,20},{20... | collective-permute-start | bytes 1011464 | tf_op jit(solution)/shard_map/ppermute | solution.py:121
  102.2 9.9 %collective-permute-start.7 = (f32[84288]{0:T(1024)S(1)}, f32[84288]{0:T(1024)S(1)}, u32[]{:S(2)}, u32[]{:S(2)}) collective-permute-start(f32[84288]{0:T(1024)S(1)} %add.133), channel_id=1, source_target_pairs={{0,4},{4,0},{8,12},{12,8},{1,5},{5,1},{9,13},{13,9},{2,6},{6,2},{1... | collective-permute-start | bytes 1011464 | tf_op jit(solution)/shard_map/ppermute | solution.py:121
  112.1 12.0 %collective-permute-start.8 = (f32[84288]{0:T(1024)S(1)}, f32[84288]{0:T(1024)S(1)}, u32[]{:S(2)}, u32[]{:S(2)}) collective-permute-start(f32[84288]{0:T(1024)S(1)} %add.134), channel_id=1, source_target_pairs={{0,8},{4,12},{8,0},{12,4},{1,9},{5,13},{9,1},{13,5},{2,10},{6,14},... | collective-permute-start | bytes 1011464 | tf_op jit(solution)/shard_map/ppermute | solution.py:121
  (7 other events, 8.4 us)

commit v6 on v5

--- a/solution.py
+++ b/solution.py
@@ -108,27 +108,50 @@
     return jnp.sum(partial, axis=1).reshape(side, side, channel_count)
 
 
-def butterfly_sum(values, axes):
-    shapes = [v.shape for v in values]
-    flat = jnp.concatenate([v.reshape(-1) for v in values])
+def flat_pack(values):
+    return jnp.concatenate([v.reshape(-1) for v in values])
+
+
+def flat_unpack(flat, values):
+    out = []
+    offset = 0
+    for v in values:
+        out.append(flat[offset : offset + v.size].reshape(v.shape))
+        offset += v.size
+    return out
+
+
+def butterfly_steps(axes):
+    steps = []
     for axis in axes:
         devices = lax.axis_size(axis)
         if devices & (devices - 1):
-            flat = lax.psum(flat, axis)
+            steps.append((axis, 0))
             continue
         step = 1
         while step < devices:
-            flat = flat + lax.ppermute(flat, axis, [(i, i ^ step) for i in range(devices)])
+            steps.append((axis, step))
             step *= 2
-    out = []
-    offset = 0
-    for shape in shapes:
-        size = 1
-        for s in shape:
-            size *= s
-        out.append(flat[offset : offset + size].reshape(shape))
-        offset += size
-    return out
+    return steps
+
+
+def butterfly_step(flat, axis, step):
+    if step == 0:
+        return lax.psum(flat, axis)
+    devices = lax.axis_size(axis)
+    return flat + lax.ppermute(flat, axis, [(i, i ^ step) for i in range(devices)])
+
+
+def butterfly_sum(values, axes):
+    flat = flat_pack(values)
+    first = butterfly_steps(axes[:1])
+    order_a = first + butterfly_steps(axes[1:])[::-1]
+    order_b = order_a[len(first) :] + order_a[: len(first)]
+    half = flat.shape[0] // 2
+    part_a, part_b = flat[:half], flat[half:]
+    for step_a, step_b in zip(order_a, order_b):
+        part_a, part_b = butterfly_step(part_a, *step_a), butterfly_step(part_b, *step_b)
+    return flat_unpack(jnp.concatenate([part_a, part_b]), values)
 
 
 def gathered_weights(w_in, b_in, w_out):

time: 128 us -> 125 us (0.977)
  waiting for transfers between devices: 30.3 us -> 26.2 us
    ppermute x3 -> x6, waiting for transfers between devices: 22.9 us -> 18.8 us  [butterfly_step(): lax.ppermute(flat, axis, [(i, i ^ step) for i in range(devices)])]
    ppermute x3 -> x6, starting transfers between devices: 6.28 us -> 6.41 us  [butterfly_step(): lax.ppermute(flat, axis, [(i, i ^ step) for i in range(devices)])]
    unnamed x50 -> x48, local copies, waits for them, and re-layouts: 4.75 us -> 4.74 us
  transfers between devices with their start and end apart: 9 -> 12, of which waited for: 5 -> 7; matrix products, arithmetic and copies ran while one was open for 9% -> 22% of each run, Pallas kernels for 8% -> 8%
where the time goes in v6:
time: 125 us; the launch traced here: 124 us
  waiting for transfers between devices  26.2 us (21%)
  matrix products  23.8 us (19%)
  starting transfers between devices  19.6 us (16%)
  local copies, waits for them, and re-layouts  18.4 us (15%)
  other arithmetic  16.2 us (13%)
  Pallas kernels  10.2 us (8%)
  blocking collectives  8.6 us (7%)
    ppermute x6, waiting for transfers between devices, butterfly_step(): lax.ppermute(flat, axis, [(i, i ^ step) for i in range(devices)])  18.8 us
    conv_general_dilated x2, matrix products, depthwise_minor(): lax.conv_general_dilated(padded_t[None], kernel[:, :, None, :], (1, 1), '...  12.5 us
    pallas_call x1, Pallas kernels, kernel_grad_minor(): pl.pallas_call(kernel_grad_body, out_shape=jax.ShapeDtypeStruct((side * s...  10.2 us
    dot_general x4, matrix products, contract(): lax.dot_general(left, right, (((dim_left,), (dim_right,)), ((), ())), pre...  9.34 us
    all_gather x1, blocking collectives, gathered_weights(): full = lax.all_gather(packed, 'chan', axis=0, tiled=True)  8.6 us
    ppermute x2, starting transfers between devices, extended(): before = lax.ppermute(last, axis, up)  6.97 us
    ppermute x6, starting transfers between devices, butterfly_step(): lax.ppermute(flat, axis, [(i, i ^ step) for i in range(devices)])  6.41 us
    unnamed x48, local copies, waits for them, and re-layouts  4.74 us
  transfers between devices with their start and end apart: 12, of which 7 were waited for; matrix products, arithmetic and copies ran while one was open for 22% of the time, Pallas kernels for 8%

profile of v6, /device:TPU:0, one launch (start us, length us, event | category | flops | bytes accessed | tf_op | source)
XLA Modules:
  0.0 124.2 jit_solution(14395236628038479684)
XLA Ops:
  1.9 3.0 %collective-permute-start = (bf16[192,3,128]{0,2,1:T(8,128)(2,1)S(1)}, bf16[192,3,128]{0,2,1:T(8,128)(2,1)S(1)}, u32[]{:S(2)}, u32[]{:S(2)}) collective-permute-start(bf16[192,3,128]{0,2,1:T(8,128)(2,1)S(1)} %slice_select_fusion.1), channel_id=1, source_target_pairs={{0,16},{16,0},{1,17},{17,1},{2,18},{18,2},{3,19},{19,3},{4,20},{20... | collective-permute-start | bytes 442376 | tf_op jit(solution)/shard_map/ppermute | solution.py:17
  8.1 8.6 %all_gather.3 = bf16[768,387]{1,0:T(8,128)(2,1)S(1)} all-gather(bf16[192,387]{1,0:T(8,128)(2,1)S(1)} %concatenate.27), channel_id=1, replica_groups=mesh['row'=2,'col'=4,'chan'=4] {'chan'}, dimensions={0}, use_global_device_ids=true | all-gather | bytes 743040 | tf_op jit(solution)/shard_map/all_gather | solution.py:166
  17.8 3.5 %collective-permute-start.1 = (bf16[192,14,3]{0,2,1:T(4,128)(2,1)S(1)}, bf16[192,14,3]{0,2,1:T(4,128)(2,1)S(1)}, u32[]{:S(2)}, u32[]{:S(2)}) collective-permute-start(bf16[192,14,3]{0,2,1:T(4,128)(2,1)S(1)} %get-tuple-element.34), channel_id=1, source_target_pairs={{0,4},{4,8},{8,12},{1,5},{5,9},{9,13},{2,6},{6,10},{10,14},{3,7},{... | collective-permute-start | bytes 48392 | tf_op jit(solution)/shard_map/ppermute | solution.py:22
  23.8 3.3 %collective-permute-done.2 = bf16[192,14,3]{0,2,1:T(4,128)(2,1)S(1)} collective-permute-done((bf16[192,14,3]{0,2,1:T(4,128)(2,1)S(1)}, bf16[192,14,3]{0,2,1:T(4,128)(2,1)S(1)}, u32[]{:S(2)}, u32[]{:S(2)}) %collective-permute-start.2) | collective-permute-done | bytes 16160 | tf_op jit(solution)/shard_map/ppermute | solution.py:23
  27.0 1.6 %bitcast_convert_fusion = (f32[14,134,192]{2,1,0:T(8,128)}, bf16[1,14,134,192]{3,2,1,0:T(8,128)(2,1)S(1)}) fusion(bf16[192,14,3]{0,2,1:T(4,128)(2,1)S(1)} %collective-permute-done.2, bf16[192,3,128]{0,2,1:T(8,128)(2,1)S(1)} %get-tuple-element.43, bf16[192,8,128]{0,2,1:T(8,128)(2,1)S(1)} %copy.84, bf16[192,3,128]{0,2,1:T(8,128)(2,1)S(1)} %get-tuple-element.42, ...), kind=kLoop, calls=%fused_computation.32 | loop fusion | flops 3962112 | bytes 2881536 | tf_op jit(solution)/shard_map/convert_element_type | solution.py:207
  28.7 8.4 %fusion.6 = f32[1,8,128,192]{3,0,2,1:T(1,128)S(1)} fusion(bf16[1,14,134,192]{3,2,1,0:T(8,128)(2,1)S(1)} %get-tuple-element.31, f32[7,7,1,192]{3,1,0,2:T(8,128)S(1)} %bitcast.132), kind=kOutput, calls=%fused_computation.13 | convolution fusion | flops 115605504 | bytes 1544448 | tf_op jit(solution)/shard_map/conv_general_dilated | solution.py:176
  37.8 1.9 %copy.89 = f32[1,8,128,192]{2,1,3,0:T(8,128)} copy(f32[1,8,128,192]{3,0,2,1:T(1,128)S(1)} %fusion.6) | data formatting | bytes 1572864 | tf_op jit(solution)/shard_map/conv_general_dilated | solution.py:176
  40.0 3.3 %multiply_convert_fusion = (bf16[1024,768]{0,1:T(8,128)(2,1)}, f32[1024,768]{0,1:T(8,128)S(1)}) fusion(f32[768]{0:T(1024)S(1)} %fusion.35, f32[24,8,8,128]{3,2,1,0:T(8,128)} %bitcast.127, f32[192]{0:T(256)S(1)} %copy-done.18, f32[192]{0:T(256)S(1)} %copy-done.14, f32[1024]{0:T(1024)S(1)} %get-tuple-element.53, f32[1024]{0:T(1024)S(1)} %get-tuple-element.54, ...), kind=kOutput, calls=%fused_computation.9 | convolution fusion | flops 307888128 | bytes 5913600 | tf_op jit(solution)/shard_map/dot_general | solution.py:52
  43.3 3.3 %fusion.62 = (bf16[1024,768]{0,1:T(8,128)(2,1)S(1)}, f32[1024,768]{0,1:T(8,128)}) fusion(f32[1024,768]{0,1:T(8,128)S(1)} %get-tuple-element.60, f32[768]{0:T(1024)S(1)} %fusion.35, f32[24,8,8,128]{3,2,1,0:T(8,128)S(1)} %convert.4, f32[192]{0:T(256)S(1)} %copy-done.16, bf16[768,387]{1,0:T(8,128)(2,1)S(1)} %all_gather.3), kind=kOutput, calls=%fused_computation.115 | convolution fusion | flops 311033856 | bytes 9049088 | tf_op jit(solution)/shard_map/dot_general | solution.py:52
  49.5 2.3 %fusion.38 = f32[192,192]{1,0:T(8,128)} fusion(bf16[1024,768]{0,1:T(8,128)(2,1)} %copy-done.19, s32[]{:T(128)S(6)} %select_n.45, f32[24,8,8,128]{3,2,1,0:T(8,128)} %bitcast.128, f32[192]{0:T(256)S(1)} %copy-done.18, f32[192]{0:T(256)S(1)} %copy-done.14, f32[1024]{0:T(1024)S(1)} %get-tuple-element.53, f32[1024]{0:T(1024)S(1)} %get-tuple-element.54, ...), kind=kOutput, calls=%fused_computation.66 | convolution fusion | flops 76677120 | bytes 1337604 | tf_op jit(solution)/shard_map/dot_general | solution.py:52
  53.0 1.5 %fusion.59 = (bf16[8,128,192]{2,1,0:T(8,128)(2,1)S(1)}, f32[8,128,192]{2,1,0:T(8,128)}) fusion(f32[8,128]{1,0:T(8,128)S(1)} %broadcast_multiply_fusion, f32[8,128]{1,0:T(8,128)S(1)} %get-tuple-element.55, f32[192]{0:T(256)S(1)} %copy-done.13, f32[1,8,128,192]{3,0,2,1:T(1,128)S(1)} %fusion.6, f32[8,128]{1,0:T(8,128)S(1)} %multiply_bitcast_fusion, ...), kind=kLoop, calls=%fused_computation.113 | loop fusion | flops 1769472 | bytes 2770432 | tf_op jit(solution)/shard_map/convert_element_type | solution.py:287
  56.2 4.1 %collective-permute-done.3 = bf16[3,128,192]{2,1,0:T(8,128)(2,1)S(1)} collective-permute-done((bf16[3,128,192]{2,1,0:T(8,128)(2,1)S(1)}, bf16[3,128,192]{2,1,0:T(8,128)(2,1)S(1)}, u32[]{:S(2)}, u32[]{:S(2)}) %collective-permute-start.3) | collective-permute-done | bytes 147488 | tf_op jit(solution)/shard_map/ppermute | solution.py:17
  60.4 3.5 %collective-permute-start.4 = (bf16[14,3,192]{2,1,0:T(4,128)(2,1)S(1)}, bf16[14,3,192]{2,1,0:T(4,128)(2,1)S(1)}, u32[]{:S(2)}, u32[]{:S(2)}) collective-permute-start(bf16[14,3,192]{2,1,0:T(4,128)(2,1)S(1)} %get-tuple-element.32), channel_id=1, source_target_pairs={{0,4},{4,8},{8,12},{1,5},{5,9},{9,13},{2,6},{6,10},{10,14},{3,7},{... | collective-permute-start | bytes 48392 | tf_op jit(solution)/shard_map/ppermute | solution.py:22
  66.8 10.2 %shard_map.194 = f32[49,8,192]{2,1,0:T(8,128)} custom-call(f32[8,128,192]{2,1,0:T(8,128)} %get-tuple-element.29.d_ref, f32[14,134,192]{2,1,0:T(8,128)} %get-tuple-element.30.p_ref), custom_call_target="tpu_custom_call" | custom-call | tf_op jit(solution)/shard_map/pallas_call | solution.py:104
  79.5 1.8 %dynamic-slice_reduce_fusion = f32[192]{0:T(256)} fusion(f32[1024,768]{0,1:T(8,128)} %get-tuple-element.62, s32[]{:T(128)S(6)} %select_n.45), kind=kLoop, calls=%fused_computation.50 | loop fusion | flops 196416 | bytes 787204 | tf_op jit(solution)/shard_map/reduce_sum | solution.py:243
  82.8 4.1 %fusion.15 = f32[8,8,17,192]{3,1,2,0:T(8,128)S(1)} fusion(bf16[14,1,7,6,192]{4,2,3,0,1:T(8,128)(2,1)S(1)} %slice.122, bf16[14,1,8,17,192]{4,2,3,0,1:T(8,128)(2,1)S(1)} %copy.105, pred[8,17]{0,1:T(8,128)(4,1)S(1)} %copy-done.20, f32[7,7,1,192]{3,1,0,2:T(8,128)S(1)} %bitcast.133), kind=kOutput, calls=%fused_computation.23 | convolution fusion | flops 126007296 | bytes 1830280 | tf_op jit(solution)/shard_map/conv_general_dilated | solution.py:176
  88.4 4.6 %fusion.31 = (f32[192]{0:T(256)S(1)}, f32[192]{0:T(256)S(1)}, bf16[8,128,192]{1,0,2:T(8,128)(2,1)}, bf16[192,8,128]{2,1,0:T(8,128)(2,1)}) fusion(f32[24,8,8,128]{3,2,1,0:T(8,128)S(1)} %copy.120, bf16[192,8,128]{2,1,0:T(8,128)(2,1)S(1)} %copy-done.4, f32[192]{0:T(256)} %param.19, f32[192]{0:T(256)} %param.20, bf16[192,8,128]{2,1,0:T(8,128)(2,1)S(1)} %copy-done.2, ...), kind=kLoop, calls=%fused_computation.47 | loop fusion | flops 2358912 | bytes 3148800 | tf_op jit(solution)/shard_map/reduce_sum | solution.py:234
  93.0 1.6 %concatenate.31 = f32[74304]{0:T(1024)S(1)} concatenate(f32[36864]{0:T(1024)S(1)} %reshape.302, f32[192]{0:T(256)S(1)} %copy-done.15, f32[36864]{0:T(1024)S(1)} %copy-done.8, f32[192]{0:T(256)S(1)} %get-tuple-element.27, f32[192]{0:T(256)S(1)} %get-tuple-element.26), dimensions={0} | concatenate | bytes 594432 | tf_op jit(solution)/shard_map/concatenate | solution.py:112
  94.7 3.7 %collective-permute-start.9 = (f32[42144]{0:T(1024)S(1)}, f32[42144]{0:T(1024)S(1)}, u32[]{:S(2)}, u32[]{:S(2)}) collective-permute-start(f32[42144]{0:T(1024)S(1)} %slice.129), channel_id=1, source_target_pairs={{0,8},{4,12},{8,0},{12,4},{1,9},{5,13},{9,1},{13,5},{2,10},{6,14},... | collective-permute-start | bytes 505736 | tf_op jit(solution)/shard_map/ppermute | solution.py:142
  99.4 9.7 %collective-permute-done.9 = f32[42144]{0:T(1024)S(1)} collective-permute-done((f32[42144]{0:T(1024)S(1)}, f32[42144]{0:T(1024)S(1)}, u32[]{:S(2)}, u32[]{:S(2)}) %collective-permute-start.9) | collective-permute-done | bytes 168608 | tf_op jit(solution)/shard_map/ppermute | solution.py:142
  109.3 1.7 %collective-permute-done.7 = f32[42144]{0:T(1024)S(1)} collective-permute-done((f32[42144]{0:T(1024)S(1)}, f32[42144]{0:T(1024)S(1)}, u32[]{:S(2)}, u32[]{:S(2)}) %collective-permute-start.7) | collective-permute-done | bytes 168608 | tf_op jit(solution)/shard_map/ppermute | solution.py:142
  111.4 5.0 %collective-permute-done.10 = f32[42144]{0:T(1024)S(1)} collective-permute-done((f32[42144]{0:T(1024)S(1)}, f32[42144]{0:T(1024)S(1)}, u32[]{:S(2)}, u32[]{:S(2)}) %collective-permute-start.10) | collective-permute-done | bytes 168608 | tf_op jit(solution)/shard_map/ppermute | solution.py:142
  116.4 1.6 %collective-permute-start.11 = (f32[42144]{0:T(1024)S(1)}, f32[42144]{0:T(1024)S(1)}, u32[]{:S(2)}, u32[]{:S(2)}) collective-permute-start(f32[42144]{0:T(1024)S(1)} %add.146), channel_id=1, source_target_pairs={{0,16},{16,0},{1,17},{17,1},{2,18},{18,2},{3,19},{19,3},{4,20},{20... | collective-permute-start | bytes 505736 | tf_op jit(solution)/shard_map/ppermute | solution.py:142
  119.6 2.3 %collective-permute-done.11 = f32[42144]{0:T(1024)S(1)} collective-permute-done((f32[42144]{0:T(1024)S(1)}, f32[42144]{0:T(1024)S(1)}, u32[]{:S(2)}, u32[]{:S(2)}) %collective-permute-start.11) | collective-permute-done | bytes 168608 | tf_op jit(solution)/shard_map/ppermute | solution.py:142
  (117 shorter events, 28.6 us)
Async XLA Ops:
  1.9 15.8 %collective-permute-start = (bf16[192,3,128]{0,2,1:T(8,128)(2,1)S(1)}, bf16[192,3,128]{0,2,1:T(8,128)(2,1)S(1)}, u32[]{:S(2)}, u32[]{:S(2)}) collective-permute-start(bf16[192,3,128]{0,2,1:T(8,128)(2,1)S(1)} %slice_select_fusion.1), channel_id=1, source_target_pairs={{0,16},{16,0},{1,17},{17,1},{2,18},{18,2},{3,19},{19,3},{4,20},{20... | collective-permute-start | bytes 442376 | tf_op jit(solution)/shard_map/ppermute | solution.py:17
  17.7 5.3 %copy-start.3 = (bf16[192,8,128]{2,1,0:T(8,128)(2,1)S(1)}, bf16[192,8,128]{2,1,0:T(8,128)(2,1)}, u32[]{:S(2)}) copy-start(bf16[192,8,128]{2,1,0:T(8,128)(2,1)} %param.21) | copy-start | bytes 1179652
  17.7 5.4 %copy-start.11 = (f32[7,7,192]{2,1,0:T(8,128)S(1)}, f32[7,7,192]{2,1,0:T(8,128)}, u32[]{:S(2)}) copy-start(f32[7,7,192]{2,1,0:T(8,128)} %param.12) | copy-start | bytes 112900
  17.8 6.0 %collective-permute-start.1 = (bf16[192,14,3]{0,2,1:T(4,128)(2,1)S(1)}, bf16[192,14,3]{0,2,1:T(4,128)(2,1)S(1)}, u32[]{:S(2)}, u32[]{:S(2)}) collective-permute-start(bf16[192,14,3]{0,2,1:T(4,128)(2,1)S(1)} %get-tuple-element.34), channel_id=1, source_target_pairs={{0,4},{4,8},{8,12},{1,5},{5,9},{9,13},{2,6},{6,10},{10,14},{3,7},{... | collective-permute-start | bytes 48392 | tf_op jit(solution)/shard_map/ppermute | solution.py:22
  21.3 5.8 %collective-permute-start.2 = (bf16[192,14,3]{0,2,1:T(4,128)(2,1)S(1)}, bf16[192,14,3]{0,2,1:T(4,128)(2,1)S(1)}, u32[]{:S(2)}, u32[]{:S(2)}) collective-permute-start(bf16[192,14,3]{0,2,1:T(4,128)(2,1)S(1)} %get-tuple-element.35), channel_id=1, source_target_pairs={{4,0},{8,4},{12,8},{5,1},{9,5},{13,9},{6,2},{10,6},{14,10},{7,3},{... | collective-permute-start | bytes 48392 | tf_op jit(solution)/shard_map/ppermute | solution.py:23
  37.1 2.6 %copy-start.13 = (f32[192]{0:T(256)S(1)}, f32[192]{0:T(256)}, u32[]{:S(2)}) copy-start(f32[192]{0:T(256)} %param.13) | copy-start | bytes 2308
  40.0 3.4 %copy-start.16 = (f32[192]{0:T(256)S(1)}, f32[192]{0:T(256)}, u32[]{:S(2)}) copy-start(f32[192]{0:T(256)} %param.20) | copy-start | bytes 2308
  43.3 3.3 %copy-start.9 = (bf16[768,192]{1,0:T(8,128)(2,1)S(1)}, bf16[768,192]{1,0:T(8,128)(2,1)}, u32[]{:S(2)}) copy-start(bf16[768,192]{1,0:T(8,128)(2,1)} %get-tuple-element.37) | copy-start | bytes 884740
  53.0 2.5 %copy-start.5 = (bf16[768,192]{1,0:T(8,128)(2,1)S(1)}, bf16[768,192]{1,0:T(8,128)(2,1)}, u32[]{:S(2)}) copy-start(bf16[768,192]{1,0:T(8,128)(2,1)} %get-tuple-element.38) | copy-start | bytes 884740
  54.5 5.8 %collective-permute-start.3 = (bf16[3,128,192]{2,1,0:T(8,128)(2,1)S(1)}, bf16[3,128,192]{2,1,0:T(8,128)(2,1)S(1)}, u32[]{:S(2)}, u32[]{:S(2)}) collective-permute-start(bf16[3,128,192]{2,1,0:T(8,128)(2,1)S(1)} %slice_select_fusion), channel_id=1, source_target_pairs={{0,16},{16,0},{1,17},{17,1},{2,18},{18,2},{3,19},{19,3},{4,20},{20... | collective-permute-start | bytes 442376 | tf_op jit(solution)/shard_map/ppermute | solution.py:17
  56.2 9.6 %copy-start.10 = (f32[192,192]{1,0:T(8,128)S(1)}, f32[192,192]{1,0:T(8,128)}, u32[]{:S(2)}) copy-start(f32[192,192]{1,0:T(8,128)} %fusion.38) | copy-start | bytes 442372
  60.4 21.0 %collective-permute-start.4 = (bf16[14,3,192]{2,1,0:T(4,128)(2,1)S(1)}, bf16[14,3,192]{2,1,0:T(4,128)(2,1)S(1)}, u32[]{:S(2)}, u32[]{:S(2)}) collective-permute-start(bf16[14,3,192]{2,1,0:T(4,128)(2,1)S(1)} %get-tuple-element.32), channel_id=1, source_target_pairs={{0,4},{4,8},{8,12},{1,5},{5,9},{9,13},{2,6},{6,10},{10,14},{3,7},{... | collective-permute-start | bytes 48392 | tf_op jit(solution)/shard_map/ppermute | solution.py:22
  63.9 17.5 %collective-permute-start.5 = (bf16[14,3,192]{2,1,0:T(4,128)(2,1)S(1)}, bf16[14,3,192]{2,1,0:T(4,128)(2,1)S(1)}, u32[]{:S(2)}, u32[]{:S(2)}) collective-permute-start(bf16[14,3,192]{2,1,0:T(4,128)(2,1)S(1)} %get-tuple-element.33), channel_id=1, source_target_pairs={{4,0},{8,4},{12,8},{5,1},{9,5},{13,9},{6,2},{10,6},{14,10},{7,3},{... | collective-permute-start | bytes 48392 | tf_op jit(solution)/shard_map/ppermute | solution.py:23
  66.8 11.4 %copy-start.17 = (f32[192]{0:T(256)S(1)}, f32[192]{0:T(256)}, u32[]{:S(2)}) copy-start(f32[192]{0:T(256)} %get-tuple-element.24) | copy-start | bytes 2308
  78.3 3.7 %copy-start.6 = (f32[46848]{0:T(1024)}, f32[46848]{0:T(1024)S(1)}, u32[]{:S(2)}) copy-start(f32[46848]{0:T(1024)S(1)} %concatenate.30) | copy-start | bytes 562180
  79.0 19.4 %collective-permute-start.6 = (f32[42144]{0:T(1024)}, f32[42144]{0:T(1024)}, u32[]{:S(2)}, u32[]{:S(2)}) collective-permute-start(f32[42144]{0:T(1024)} %slice.124), channel_id=1, source_target_pairs={{0,16},{16,0},{1,17},{17,1},{2,18},{18,2},{3,19},{19,3},{4,20},{20... | collective-permute-start | bytes 505736 | tf_op jit(solution)/shard_map/ppermute | solution.py:142
  88.4 4.6 %copy-start.8 = (f32[36864]{0:T(1024)S(1)}, f32[36864]{0:T(1024)}, u32[]{:S(2)}) copy-start(f32[36864]{0:T(1024)} %reshape.303) | copy-start | bytes 442372
  88.4 4.6 %copy-start.15 = (f32[192]{0:T(256)S(1)}, f32[192]{0:T(256)}, u32[]{:S(2)}) copy-start(f32[192]{0:T(256)} %dynamic-slice_reduce_fusion) | copy-start | bytes 2308
  88.4 10.0 %copy-start.7 = (f32[46848]{0:T(1024)S(1)}, f32[46848]{0:T(1024)}, u32[]{:S(2)}) copy-start(f32[46848]{0:T(1024)} %copy-done.6) | copy-start | bytes 562180
  94.7 14.4 %collective-permute-start.9 = (f32[42144]{0:T(1024)S(1)}, f32[42144]{0:T(1024)S(1)}, u32[]{:S(2)}, u32[]{:S(2)}) collective-permute-start(f32[42144]{0:T(1024)S(1)} %slice.129), channel_id=1, source_target_pairs={{0,8},{4,12},{8,0},{12,4},{1,9},{5,13},{9,1},{13,5},{2,10},{6,14},... | collective-permute-start | bytes 505736 | tf_op jit(solution)/shard_map/ppermute | solution.py:142
  99.3 11.6 %collective-permute-start.7 = (f32[42144]{0:T(1024)S(1)}, f32[42144]{0:T(1024)S(1)}, u32[]{:S(2)}, u32[]{:S(2)}) collective-permute-start(f32[42144]{0:T(1024)S(1)} %slice_add_fusion.3), channel_id=1, source_target_pairs={{0,8},{4,12},{8,0},{12,4},{1,9},{5,13},{9,1},{13,5},{2,10},{6,14},... | collective-permute-start | bytes 505736 | tf_op jit(solution)/shard_map/ppermute | solution.py:142
  109.2 7.2 %collective-permute-start.10 = (f32[42144]{0:T(1024)S(1)}, f32[42144]{0:T(1024)S(1)}, u32[]{:S(2)}, u32[]{:S(2)}) collective-permute-start(f32[42144]{0:T(1024)S(1)} %slice_add_fusion.2), channel_id=1, source_target_pairs={{0,4},{4,0},{8,12},{12,8},{1,5},{5,1},{9,13},{13,9},{2,6},{6,2},{1... | collective-permute-start | bytes 505736 | tf_op jit(solution)/shard_map/ppermute | solution.py:142
  111.0 7.2 %collective-permute-start.8 = (f32[42144]{0:T(1024)S(1)}, f32[42144]{0:T(1024)S(1)}, u32[]{:S(2)}, u32[]{:S(2)}) collective-permute-start(f32[42144]{0:T(1024)S(1)} %add.143), channel_id=1, source_target_pairs={{0,4},{4,0},{8,12},{12,8},{1,5},{5,1},{9,13},{13,9},{2,6},{6,2},{1... | collective-permute-start | bytes 505736 | tf_op jit(solution)/shard_map/ppermute | solution.py:142
  116.4 5.5 %collective-permute-start.11 = (f32[42144]{0:T(1024)S(1)}, f32[42144]{0:T(1024)S(1)}, u32[]{:S(2)}, u32[]{:S(2)}) collective-permute-start(f32[42144]{0:T(1024)S(1)} %add.146), channel_id=1, source_target_pairs={{0,16},{16,0},{1,17},{17,1},{2,18},{18,2},{3,19},{19,3},{4,20},{20... | collective-permute-start | bytes 505736 | tf_op jit(solution)/shard_map/ppermute | solution.py:142
  (9 other events, 12.9 us)

commit v7 on v6

--- a/solution.py
+++ b/solution.py
@@ -163,7 +163,14 @@
         rest = rest - piece.astype(jnp.float32)
         pieces.append(piece[:, None])
     packed = jnp.concatenate([w_in.T, w_out] + pieces, axis=1)
-    full = lax.all_gather(packed, "chan", axis=0, tiled=True)
+    devices = lax.axis_size("chan")
+    own = lax.axis_index("chan")
+    received = [packed] + [
+        lax.ppermute(packed, "chan", [(i, (i + shift) % devices) for i in range(devices)])
+        for shift in range(1, devices)
+    ]
+    order = (own - jnp.arange(devices)) % devices
+    full = jnp.stack(received)[order].reshape(devices * packed.shape[0], packed.shape[1])
     w_in_all = full[:, :channel_count].T
     w_out_all = full[:, channel_count : 2 * channel_count]
     parts = full[:, 2 * channel_count :].astype(jnp.float32)

time: 125 us -> 130 us (1.040)
  blocking collectives: 8.6 us -> 0 us
  local copies, waits for them, and re-layouts: 18.4 us -> 23.1 us
  starting transfers between devices: 19.6 us -> 23.8 us
  waiting for transfers between devices: 26.2 us -> 28.8 us
    all_gather x1 -> x0, blocking collectives: 8.6 us -> none  [gathered_weights(): full = lax.all_gather(packed, 'chan', axis=0, tiled=True)]
    ppermute x2, waiting for transfers between devices: 4.15 us -> 8.52 us  [extended(): got = lax.ppermute(jnp.where(first, last, leading), axis, [(0, 1), (1, 0)])]
    ppermute x0 -> x3, starting transfers between devices: none -> 3.5 us  [gathered_weights(): lax.ppermute(packed, 'chan', [(i, (i + shift) % devices) for i in range(d...]
    ppermute x2, waiting for transfers between devices: 3.26 us -> 0.01 us  [extended(): after = lax.ppermute(leading, axis, down)]
    reshape x0 -> x2, local copies, waits for them, and re-layouts: none -> 3.04 us  [the longest x1 2.09 us: shards(): w_in_all.reshape(channel_count, blocks, share)]
    ppermute x6, waiting for transfers between devices: 18.8 us -> 20.3 us  [butterfly_step(): lax.ppermute(flat, axis, [(i, i ^ step) for i in range(devices)])]
    ppermute x2, starting transfers between devices: 6.97 us -> 8.34 us  [extended(): before = lax.ppermute(last, axis, up)]
    unnamed x48 -> x53, local copies, waits for them, and re-layouts: 4.74 us -> 5.91 us
  transfers between devices with their start and end apart: 12 -> 15, of which waited for: 7 -> 7; matrix products, arithmetic and copies ran while one was open for 22% -> 24% of each run, Pallas kernels for 8% -> 8%
where the time goes in v7:
time: 130 us; the launch traced here: 129 us
  waiting for transfers between devices  28.8 us (22%)
  matrix products  24.4 us (19%)
  starting transfers between devices  23.8 us (18%)
  local copies, waits for them, and re-layouts  23.1 us (18%)
  other arithmetic  17.3 us (13%)
  Pallas kernels  10.2 us (8%)
    ppermute x6, waiting for transfers between devices, butterfly_step(): lax.ppermute(flat, axis, [(i, i ^ step) for i in range(devices)])  20.3 us
    conv_general_dilated x2, matrix products, depthwise_minor(): lax.conv_general_dilated(padded_t[None], kernel[:, :, None, :], (1, 1), '...  12.5 us
    pallas_call x1, Pallas kernels, kernel_grad_minor(): pl.pallas_call(kernel_grad_body, out_shape=jax.ShapeDtypeStruct((side * s...  10.2 us
    dot_general x4, matrix products, contract(): lax.dot_general(left, right, (((dim_left,), (dim_right,)), ((), ())), pre...  10 us
    ppermute x2, waiting for transfers between devices, extended(): got = lax.ppermute(jnp.where(first, last, leading), axis, [(0, 1), (1, 0)])  8.52 us
    ppermute x2, starting transfers between devices, extended(): before = lax.ppermute(last, axis, up)  8.34 us
    ppermute x6, starting transfers between devices, butterfly_step(): lax.ppermute(flat, axis, [(i, i ^ step) for i in range(devices)])  6.2 us
    unnamed x53, local copies, waits for them, and re-layouts  5.91 us
  transfers between devices with their start and end apart: 15, of which 7 were waited for; matrix products, arithmetic and copies ran while one was open for 24% of the time, Pallas kernels for 8%

profile of v7, /device:TPU:0, one launch (start us, length us, event | category | flops | bytes accessed | tf_op | source)
XLA Modules:
  0.0 128.9 jit_solution(15057593822261716012)
XLA Ops:
  3.8 2.4 %collective-permute-start.5 = (bf16[192,387]{1,0:T(8,128)(2,1)S(1)}, bf16[192,387]{1,0:T(8,128)(2,1)S(1)}, u32[]{:S(2)}, u32[]{:S(2)}) collective-permute-start(bf16[192,387]{1,0:T(8,128)(2,1)S(1)} %concatenate.27), channel_id=1, source_target_pairs={{0,3},{1,0},{2,1},{3,2},{4,7},{5,4},{6,5},{7,6},{8,11},{9,8},{10,9... | collective-permute-start | bytes 445832 | tf_op jit(solution)/shard_map/ppermute | solution.py:169
  8.6 1.6 %collective-permute-start = (bf16[192,3,128]{0,2,1:T(8,128)(2,1)S(1)}, bf16[192,3,128]{0,2,1:T(8,128)(2,1)S(1)}, u32[]{:S(2)}, u32[]{:S(2)}) collective-permute-start(bf16[192,3,128]{0,2,1:T(8,128)(2,1)S(1)} %slice_select_fusion.1), channel_id=1, source_target_pairs={{0,16},{16,0},{1,17},{17,1},{2,18},{18,2},{3,19},{19,3},{4,20},{20... | collective-permute-start | bytes 442376 | tf_op jit(solution)/shard_map/ppermute | solution.py:17
  10.9 5.3 %collective-permute-done = bf16[192,3,128]{0,2,1:T(8,128)(2,1)S(1)} collective-permute-done((bf16[192,3,128]{0,2,1:T(8,128)(2,1)S(1)}, bf16[192,3,128]{0,2,1:T(8,128)(2,1)S(1)}, u32[]{:S(2)}, u32[]{:S(2)}) %collective-permute-start) | collective-permute-done | bytes 147488 | tf_op jit(solution)/shard_map/ppermute | solution.py:17
  16.9 4.1 %collective-permute-start.1 = (bf16[192,14,3]{0,2,1:T(4,128)(2,1)}, bf16[192,14,3]{0,2,1:T(4,128)(2,1)}, u32[]{:S(2)}, u32[]{:S(2)}) collective-permute-start(bf16[192,14,3]{0,2,1:T(4,128)(2,1)} %get-tuple-element.34), channel_id=1, source_target_pairs={{0,4},{4,8},{8,12},{1,5},{5,9},{9,13},{2,6},{6,10},{10,14},{3,7},{... | collective-permute-start | bytes 48392 | tf_op jit(solution)/shard_map/ppermute | solution.py:22
  24.3 2.1 %reshape.354 = bf16[192,4,192]{2,1,0:T(4,128)(2,1)} reshape(bf16[192,768]{1,0:T(8,128)(2,1)} %bitcast.135) | data formatting | bytes 589824 | tf_op jit(solution)/shard_map/reshape | solution.py:254
  27.3 2.4 %bitcast_convert_fusion = (f32[14,134,192]{2,1,0:T(8,128)}, bf16[1,14,134,192]{3,2,1,0:T(8,128)(2,1)S(1)}) fusion(bf16[192,14,3]{0,2,1:T(4,128)(2,1)} %collective-permute-done.2, bf16[192,3,128]{0,2,1:T(8,128)(2,1)S(1)} %get-tuple-element.43, bf16[192,8,128]{0,2,1:T(8,128)(2,1)S(1)} %copy.86, bf16[192,3,128]{0,2,1:T(8,128)(2,1)S(1)} %get-tuple-element.42, ...), kind=kLoop, calls=%fused_computation.33 | loop fusion | flops 3962112 | bytes 2881536 | tf_op jit(solution)/shard_map/convert_element_type | solution.py:214
  29.7 8.4 %fusion.6 = f32[1,8,128,192]{3,0,2,1:T(1,128)S(1)} fusion(bf16[1,14,134,192]{3,2,1,0:T(8,128)(2,1)S(1)} %get-tuple-element.31, f32[7,7,1,192]{3,1,0,2:T(8,128)S(1)} %bitcast.144), kind=kOutput, calls=%fused_computation.14 | convolution fusion | flops 115605504 | bytes 1544448 | tf_op jit(solution)/shard_map/conv_general_dilated | solution.py:183
  38.8 1.9 %copy.91 = f32[1,8,128,192]{2,1,3,0:T(8,128)} copy(f32[1,8,128,192]{3,0,2,1:T(1,128)S(1)} %fusion.6) | data formatting | bytes 1572864 | tf_op jit(solution)/shard_map/conv_general_dilated | solution.py:183
  41.1 3.3 %multiply_convert_fusion = (bf16[1024,768]{0,1:T(8,128)(2,1)}, f32[1024,768]{0,1:T(8,128)S(1)}) fusion(f32[768]{0:T(1024)S(1)} %fusion.43, f32[24,8,8,128]{3,2,1,0:T(8,128)} %bitcast.136, f32[192]{0:T(256)S(1)} %copy-done.19, f32[192]{0:T(256)S(1)} %copy-done.15, f32[1024]{0:T(1024)S(1)} %get-tuple-element.53, f32[1024]{0:T(1024)S(1)} %get-tuple-element.54, ...), kind=kOutput, calls=%fused_computation.10 | convolution fusion | flops 307888128 | bytes 5913600 | tf_op jit(solution)/shard_map/dot_general | solution.py:52
  44.4 3.3 %fusion.65 = (bf16[1024,768]{0,1:T(8,128)(2,1)S(1)}, f32[1024,768]{0,1:T(8,128)}) fusion(f32[1024,768]{0,1:T(8,128)S(1)} %get-tuple-element.60, f32[768]{0:T(1024)S(1)} %fusion.43, f32[24,8,8,128]{3,2,1,0:T(8,128)S(1)} %convert.5, f32[192]{0:T(256)S(1)} %copy-done.17, bf16[768,387]{1,0:T(8,128)(2,1)S(1)} %bitcast.130), kind=kOutput, calls=%fused_computation.124 | convolution fusion | flops 311033856 | bytes 9049088 | tf_op jit(solution)/shard_map/dot_general | solution.py:52
  50.5 2.3 %fusion.38 = f32[192,192]{1,0:T(8,128)} fusion(bf16[1024,768]{0,1:T(8,128)(2,1)} %copy-done.20, s32[]{:T(128)S(6)} %select_n.71, f32[24,8,8,128]{3,2,1,0:T(8,128)} %bitcast.137, f32[192]{0:T(256)S(1)} %copy-done.19, f32[192]{0:T(256)S(1)} %copy-done.15, f32[1024]{0:T(1024)S(1)} %get-tuple-element.53, f32[1024]{0:T(1024)S(1)} %get-tuple-element.54, ...), kind=kOutput, calls=%fused_computation.66 | convolution fusion | flops 76677120 | bytes 1337604 | tf_op jit(solution)/shard_map/dot_general | solution.py:52
  58.8 3.2 %collective-permute-done.6 = bf16[3,128,192]{2,1,0:T(8,128)(2,1)S(1)} collective-permute-done((bf16[3,128,192]{2,1,0:T(8,128)(2,1)S(1)}, bf16[3,128,192]{2,1,0:T(8,128)(2,1)S(1)}, u32[]{:S(2)}, u32[]{:S(2)}) %collective-permute-start.6) | collective-permute-done | bytes 147488 | tf_op jit(solution)/shard_map/ppermute | solution.py:17
  62.1 4.3 %collective-permute-start.7 = (bf16[14,3,192]{2,1,0:T(4,128)(2,1)S(1)}, bf16[14,3,192]{2,1,0:T(4,128)(2,1)S(1)}, u32[]{:S(2)}, u32[]{:S(2)}) collective-permute-start(bf16[14,3,192]{2,1,0:T(4,128)(2,1)S(1)} %get-tuple-element.32), channel_id=1, source_target_pairs={{0,4},{4,8},{8,12},{1,5},{5,9},{9,13},{2,6},{6,10},{10,14},{3,7},{... | collective-permute-start | bytes 48392 | tf_op jit(solution)/shard_map/ppermute | solution.py:22
  68.5 1.7 %reshape.356 = f32[36864]{0:T(1024)} reshape(f32[192,192]{1,0:T(8,128)} %fusion.36) | data formatting | bytes 294912 | tf_op jit(solution)/shard_map/reshape | solution.py:112
  70.2 10.2 %shard_map.194 = f32[49,8,192]{2,1,0:T(8,128)} custom-call(f32[8,128,192]{2,1,0:T(8,128)} %get-tuple-element.29.d_ref, f32[14,134,192]{2,1,0:T(8,128)} %get-tuple-element.30.p_ref), custom_call_target="tpu_custom_call" | custom-call | tf_op jit(solution)/shard_map/pallas_call | solution.py:104
  84.0 1.8 %dynamic-slice_reduce_fusion = f32[192]{0:T(256)} fusion(f32[1024,768]{0,1:T(8,128)} %get-tuple-element.62, s32[]{:T(128)S(6)} %select_n.71), kind=kLoop, calls=%fused_computation.52 | loop fusion | flops 196416 | bytes 787204 | tf_op jit(solution)/shard_map/reduce_sum | solution.py:250
  87.2 4.1 %fusion.15 = f32[8,8,17,192]{3,1,2,0:T(8,128)S(1)} fusion(bf16[14,1,7,6,192]{4,2,3,0,1:T(8,128)(2,1)S(1)} %slice.124, bf16[14,1,8,17,192]{4,2,3,0,1:T(8,128)(2,1)S(1)} %copy.108, pred[8,17]{0,1:T(8,128)(4,1)S(1)} %copy-done.21, f32[7,7,1,192]{3,1,0,2:T(8,128)S(1)} %bitcast.145), kind=kOutput, calls=%fused_computation.24 | convolution fusion | flops 126007296 | bytes 1830280 | tf_op jit(solution)/shard_map/conv_general_dilated | solution.py:183
  92.8 4.6 %fusion.31 = (f32[192]{0:T(256)S(1)}, f32[192]{0:T(256)S(1)}, bf16[8,128,192]{1,0,2:T(8,128)(2,1)}, bf16[192,8,128]{2,1,0:T(8,128)(2,1)}) fusion(f32[24,8,8,128]{3,2,1,0:T(8,128)S(1)} %copy.124, bf16[192,8,128]{2,1,0:T(8,128)(2,1)S(1)} %copy-done.4, f32[192]{0:T(256)} %param.19, f32[192]{0:T(256)} %param.20, bf16[192,8,128]{2,1,0:T(8,128)(2,1)S(1)} %copy-done.2, ...), kind=kLoop, calls=%fused_computation.49 | loop fusion | flops 2358912 | bytes 3148800 | tf_op jit(solution)/shard_map/reduce_sum | solution.py:241
  99.1 3.3 %collective-permute-start.12 = (f32[42144]{0:T(1024)S(1)}, f32[42144]{0:T(1024)S(1)}, u32[]{:S(2)}, u32[]{:S(2)}) collective-permute-start(f32[42144]{0:T(1024)S(1)} %slice.131), channel_id=1, source_target_pairs={{0,8},{4,12},{8,0},{12,4},{1,9},{5,13},{9,1},{13,5},{2,10},{6,14},... | collective-permute-start | bytes 505736 | tf_op jit(solution)/shard_map/ppermute | solution.py:142
  103.4 10.2 %collective-permute-done.12 = f32[42144]{0:T(1024)S(1)} collective-permute-done((f32[42144]{0:T(1024)S(1)}, f32[42144]{0:T(1024)S(1)}, u32[]{:S(2)}, u32[]{:S(2)}) %collective-permute-start.12) | collective-permute-done | bytes 168608 | tf_op jit(solution)/shard_map/ppermute | solution.py:142
  113.8 2.2 %collective-permute-done.10 = f32[42144]{0:T(1024)S(1)} collective-permute-done((f32[42144]{0:T(1024)S(1)}, f32[42144]{0:T(1024)S(1)}, u32[]{:S(2)}, u32[]{:S(2)}) %collective-permute-start.10) | collective-permute-done | bytes 168608 | tf_op jit(solution)/shard_map/ppermute | solution.py:142
  116.7 4.4 %collective-permute-done.13 = f32[42144]{0:T(1024)S(1)} collective-permute-done((f32[42144]{0:T(1024)S(1)}, f32[42144]{0:T(1024)S(1)}, u32[]{:S(2)}, u32[]{:S(2)}) %collective-permute-start.13) | collective-permute-done | bytes 168608 | tf_op jit(solution)/shard_map/ppermute | solution.py:142
  121.6 1.6 %collective-permute-done.11 = f32[42144]{0:T(1024)S(1)} collective-permute-done((f32[42144]{0:T(1024)S(1)}, f32[42144]{0:T(1024)S(1)}, u32[]{:S(2)}, u32[]{:S(2)}) %collective-permute-start.11) | collective-permute-done | bytes 168608 | tf_op jit(solution)/shard_map/ppermute | solution.py:142
  124.6 2.0 %collective-permute-done.14 = f32[42144]{0:T(1024)S(1)} collective-permute-done((f32[42144]{0:T(1024)S(1)}, f32[42144]{0:T(1024)S(1)}, u32[]{:S(2)}, u32[]{:S(2)}) %collective-permute-start.14) | collective-permute-done | bytes 168608 | tf_op jit(solution)/shard_map/ppermute | solution.py:142
  (133 shorter events, 37.2 us)
Async XLA Ops:
  0.6 9.5 %copy-start.3 = (bf16[192,8,128]{2,1,0:T(8,128)(2,1)S(1)}, bf16[192,8,128]{2,1,0:T(8,128)(2,1)}, u32[]{:S(2)}) copy-start(bf16[192,8,128]{2,1,0:T(8,128)(2,1)} %param.21) | copy-start | bytes 1179652
  0.7 9.6 %copy-start.11 = (f32[7,7,192]{2,1,0:T(8,128)S(1)}, f32[7,7,192]{2,1,0:T(8,128)}, u32[]{:S(2)}) copy-start(f32[7,7,192]{2,1,0:T(8,128)} %param.12) | copy-start | bytes 112900
  3.8 18.5 %collective-permute-start.5 = (bf16[192,387]{1,0:T(8,128)(2,1)S(1)}, bf16[192,387]{1,0:T(8,128)(2,1)S(1)}, u32[]{:S(2)}, u32[]{:S(2)}) collective-permute-start(bf16[192,387]{1,0:T(8,128)(2,1)S(1)} %concatenate.27), channel_id=1, source_target_pairs={{0,3},{1,0},{2,1},{3,2},{4,7},{5,4},{6,5},{7,6},{8,11},{9,8},{10,9... | collective-permute-start | bytes 445832 | tf_op jit(solution)/shard_map/ppermute | solution.py:169
  6.2 16.1 %collective-permute-start.3 = (bf16[192,387]{1,0:T(8,128)(2,1)S(1)}, bf16[192,387]{1,0:T(8,128)(2,1)S(1)}, u32[]{:S(2)}, u32[]{:S(2)}) collective-permute-start(bf16[192,387]{1,0:T(8,128)(2,1)S(1)} %concatenate.27), channel_id=1, source_target_pairs={{0,1},{1,2},{2,3},{3,0},{4,5},{5,6},{6,7},{7,4},{8,9},{9,10},{10,1... | collective-permute-start | bytes 445832 | tf_op jit(solution)/shard_map/ppermute | solution.py:169
  6.2 16.1 %collective-permute-start.4 = (bf16[192,387]{1,0:T(8,128)(2,1)S(1)}, bf16[192,387]{1,0:T(8,128)(2,1)S(1)}, u32[]{:S(2)}, u32[]{:S(2)}) collective-permute-start(bf16[192,387]{1,0:T(8,128)(2,1)S(1)} %concatenate.27), channel_id=1, source_target_pairs={{0,2},{1,3},{2,0},{3,1},{4,6},{5,7},{6,4},{7,5},{8,10},{9,11},{10,... | collective-permute-start | bytes 445832 | tf_op jit(solution)/shard_map/ppermute | solution.py:169
  8.6 7.7 %collective-permute-start = (bf16[192,3,128]{0,2,1:T(8,128)(2,1)S(1)}, bf16[192,3,128]{0,2,1:T(8,128)(2,1)S(1)}, u32[]{:S(2)}, u32[]{:S(2)}) collective-permute-start(bf16[192,3,128]{0,2,1:T(8,128)(2,1)S(1)} %slice_select_fusion.1), channel_id=1, source_target_pairs={{0,16},{16,0},{1,17},{17,1},{2,18},{18,2},{3,19},{19,3},{4,20},{20... | collective-permute-start | bytes 442376 | tf_op jit(solution)/shard_map/ppermute | solution.py:17
  16.9 10.4 %collective-permute-start.1 = (bf16[192,14,3]{0,2,1:T(4,128)(2,1)}, bf16[192,14,3]{0,2,1:T(4,128)(2,1)}, u32[]{:S(2)}, u32[]{:S(2)}) collective-permute-start(bf16[192,14,3]{0,2,1:T(4,128)(2,1)} %get-tuple-element.34), channel_id=1, source_target_pairs={{0,4},{4,8},{8,12},{1,5},{5,9},{9,13},{2,6},{6,10},{10,14},{3,7},{... | collective-permute-start | bytes 48392 | tf_op jit(solution)/shard_map/ppermute | solution.py:22
  21.0 6.4 %collective-permute-start.2 = (bf16[192,14,3]{0,2,1:T(4,128)(2,1)}, bf16[192,14,3]{0,2,1:T(4,128)(2,1)}, u32[]{:S(2)}, u32[]{:S(2)}) collective-permute-start(bf16[192,14,3]{0,2,1:T(4,128)(2,1)} %get-tuple-element.35), channel_id=1, source_target_pairs={{4,0},{8,4},{12,8},{5,1},{9,5},{13,9},{6,2},{10,6},{14,10},{7,3},{... | collective-permute-start | bytes 48392 | tf_op jit(solution)/shard_map/ppermute | solution.py:23
  54.0 4.2 %copy-start.5 = (bf16[4,192,192]{1,2,0:T(8,128)(2,1)S(1)}, bf16[4,192,192]{1,2,0:T(8,128)(2,1)}, u32[]{:S(2)}) copy-start(bf16[4,192,192]{1,2,0:T(8,128)(2,1)} %copy.100) | copy-start | bytes 884740
  55.5 6.5 %collective-permute-start.6 = (bf16[3,128,192]{2,1,0:T(8,128)(2,1)S(1)}, bf16[3,128,192]{2,1,0:T(8,128)(2,1)S(1)}, u32[]{:S(2)}, u32[]{:S(2)}) collective-permute-start(bf16[3,128,192]{2,1,0:T(8,128)(2,1)S(1)} %slice_select_fusion), channel_id=1, source_target_pairs={{0,16},{16,0},{1,17},{17,1},{2,18},{18,2},{3,19},{19,3},{4,20},{20... | collective-permute-start | bytes 442376 | tf_op jit(solution)/shard_map/ppermute | solution.py:17
  58.8 9.4 %copy-start.10 = (f32[192,192]{1,0:T(8,128)S(1)}, f32[192,192]{1,0:T(8,128)}, u32[]{:S(2)}) copy-start(f32[192,192]{1,0:T(8,128)} %fusion.38) | copy-start | bytes 442372
  62.1 23.6 %collective-permute-start.7 = (bf16[14,3,192]{2,1,0:T(4,128)(2,1)S(1)}, bf16[14,3,192]{2,1,0:T(4,128)(2,1)S(1)}, u32[]{:S(2)}, u32[]{:S(2)}) collective-permute-start(bf16[14,3,192]{2,1,0:T(4,128)(2,1)S(1)} %get-tuple-element.32), channel_id=1, source_target_pairs={{0,4},{4,8},{8,12},{1,5},{5,9},{9,13},{2,6},{6,10},{10,14},{3,7},{... | collective-permute-start | bytes 48392 | tf_op jit(solution)/shard_map/ppermute | solution.py:22
  66.4 19.4 %collective-permute-start.8 = (bf16[14,3,192]{2,1,0:T(4,128)(2,1)S(1)}, bf16[14,3,192]{2,1,0:T(4,128)(2,1)S(1)}, u32[]{:S(2)}, u32[]{:S(2)}) collective-permute-start(bf16[14,3,192]{2,1,0:T(4,128)(2,1)S(1)} %get-tuple-element.33), channel_id=1, source_target_pairs={{4,0},{8,4},{12,8},{5,1},{9,5},{13,9},{6,2},{10,6},{14,10},{7,3},{... | collective-permute-start | bytes 48392 | tf_op jit(solution)/shard_map/ppermute | solution.py:23
  70.2 11.4 %copy-start.18 = (f32[192]{0:T(256)S(1)}, f32[192]{0:T(256)}, u32[]{:S(2)}) copy-start(f32[192]{0:T(256)} %get-tuple-element.24) | copy-start | bytes 2308
  81.7 4.6 %copy-start.6 = (f32[46848]{0:T(1024)}, f32[46848]{0:T(1024)S(1)}, u32[]{:S(2)}) copy-start(f32[46848]{0:T(1024)S(1)} %concatenate.30) | copy-start | bytes 562180
  82.4 19.9 %collective-permute-start.9 = (f32[42144]{0:T(1024)}, f32[42144]{0:T(1024)}, u32[]{:S(2)}, u32[]{:S(2)}) collective-permute-start(f32[42144]{0:T(1024)} %slice.126), channel_id=1, source_target_pairs={{0,16},{16,0},{1,17},{17,1},{2,18},{18,2},{3,19},{19,3},{4,20},{20... | collective-permute-start | bytes 505736 | tf_op jit(solution)/shard_map/ppermute | solution.py:142
  92.8 4.6 %copy-start.8 = (f32[36864]{0:T(1024)S(1)}, f32[36864]{0:T(1024)}, u32[]{:S(2)}) copy-start(f32[36864]{0:T(1024)} %reshape.356) | copy-start | bytes 442372
  92.8 4.6 %copy-start.16 = (f32[192]{0:T(256)S(1)}, f32[192]{0:T(256)}, u32[]{:S(2)}) copy-start(f32[192]{0:T(256)} %dynamic-slice_reduce_fusion) | copy-start | bytes 2308
  92.8 9.6 %copy-start.7 = (f32[46848]{0:T(1024)S(1)}, f32[46848]{0:T(1024)}, u32[]{:S(2)}) copy-start(f32[46848]{0:T(1024)} %copy-done.6) | copy-start | bytes 562180
  99.1 14.5 %collective-permute-start.12 = (f32[42144]{0:T(1024)S(1)}, f32[42144]{0:T(1024)S(1)}, u32[]{:S(2)}, u32[]{:S(2)}) collective-permute-start(f32[42144]{0:T(1024)S(1)} %slice.131), channel_id=1, source_target_pairs={{0,8},{4,12},{8,0},{12,4},{1,9},{5,13},{9,1},{13,5},{2,10},{6,14},... | collective-permute-start | bytes 505736 | tf_op jit(solution)/shard_map/ppermute | solution.py:142
  103.3 12.6 %collective-permute-start.10 = (f32[42144]{0:T(1024)S(1)}, f32[42144]{0:T(1024)S(1)}, u32[]{:S(2)}, u32[]{:S(2)}) collective-permute-start(f32[42144]{0:T(1024)S(1)} %slice_add_fusion.3), channel_id=1, source_target_pairs={{0,8},{4,12},{8,0},{12,4},{1,9},{5,13},{9,1},{13,5},{2,10},{6,14},... | collective-permute-start | bytes 505736 | tf_op jit(solution)/shard_map/ppermute | solution.py:142
  113.7 7.4 %collective-permute-start.13 = (f32[42144]{0:T(1024)S(1)}, f32[42144]{0:T(1024)S(1)}, u32[]{:S(2)}, u32[]{:S(2)}) collective-permute-start(f32[42144]{0:T(1024)S(1)} %slice_add_fusion.2), channel_id=1, source_target_pairs={{0,4},{4,0},{8,12},{12,8},{1,5},{5,1},{9,13},{13,9},{2,6},{6,2},{1... | collective-permute-start | bytes 505736 | tf_op jit(solution)/shard_map/ppermute | solution.py:142
  116.0 7.2 %collective-permute-start.11 = (f32[42144]{0:T(1024)S(1)}, f32[42144]{0:T(1024)S(1)}, u32[]{:S(2)}, u32[]{:S(2)}) collective-permute-start(f32[42144]{0:T(1024)S(1)} %add.168), channel_id=1, source_target_pairs={{0,4},{4,0},{8,12},{12,8},{1,5},{5,1},{9,13},{13,9},{2,6},{6,2},{1... | collective-permute-start | bytes 505736 | tf_op jit(solution)/shard_map/ppermute | solution.py:142
  121.1 5.5 %collective-permute-start.14 = (f32[42144]{0:T(1024)S(1)}, f32[42144]{0:T(1024)S(1)}, u32[]{:S(2)}, u32[]{:S(2)}) collective-permute-start(f32[42144]{0:T(1024)S(1)} %add.171), channel_id=1, source_target_pairs={{0,16},{16,0},{1,17},{17,1},{2,18},{18,2},{3,19},{19,3},{4,20},{20... | collective-permute-start | bytes 505736 | tf_op jit(solution)/shard_map/ppermute | solution.py:142
  (13 other events, 25.4 us)

commit v8 on v6

--- a/solution.py
+++ b/solution.py
@@ -2,6 +2,7 @@
 import jax.numpy as jnp
 from jax import lax
 from jax.experimental import pallas as pl
+from jax.experimental.pallas import tpu as pltpu
 from jax.sharding import PartitionSpec as P
 
 
@@ -80,17 +81,19 @@
     )
 
 
-def kernel_grad_body(d_ref, p_ref, o_ref):
+def kernel_grad_body(d_ref, p_ref, o_ref, shifted_ref):
     rows, cols, _ = d_ref.shape
     taps = o_ref.shape[0]
     side = int(round(taps ** 0.5))
     o_ref[...] = jnp.zeros(o_ref.shape, o_ref.dtype)
+    for j in range(side):
+        shifted_ref[j] = p_ref[:, j : j + cols, :]
 
     def row_step(h, carry):
         d_row = d_ref[h]
         for i in range(side):
             for j in range(side):
-                prod = d_row * p_ref[h + i, j : j + cols, :]
+                prod = d_row * shifted_ref[j, h + i]
                 part = jnp.sum(prod.reshape(cols // 8, 8, prod.shape[-1]), axis=0)
                 o_ref[i * side + j] += part
         return carry
@@ -104,6 +107,7 @@
     partial = pl.pallas_call(
         kernel_grad_body,
         out_shape=jax.ShapeDtypeStruct((side * side, 8, channel_count), jnp.float32),
+        scratch_shapes=[pltpu.VMEM((side,) + p_t.shape[:1] + d_t.shape[1:], jnp.float32)],
     )(d_t, p_t)
     return jnp.sum(partial, axis=1).reshape(side, side, channel_count)
 

time: 125 us -> 123 us (0.984)
  Pallas kernels: 10.2 us -> 8.01 us
    pallas_call x1, Pallas kernels: 10.2 us -> 8.01 us  [kernel_grad_minor(): pl.pallas_call(kernel_grad_body, out_shape=jax.ShapeDtypeStruct((side * s...]
  transfers between devices with their start and end apart: 12 -> 12, of which waited for: 7 -> 7; matrix products, arithmetic and copies ran while one was open for 22% -> 22% of each run, Pallas kernels for 8% -> 7%
where the time goes in v8:
time: 123 us; the launch traced here: 122 us
  waiting for transfers between devices  26.2 us (21%)
  matrix products  23.8 us (19%)
  starting transfers between devices  19.6 us (16%)
  local copies, waits for them, and re-layouts  18.4 us (15%)
  other arithmetic  16.2 us (13%)
  blocking collectives  8.6 us (7%)
  Pallas kernels  8.01 us (7%)
    ppermute x6, waiting for transfers between devices, butterfly_step(): lax.ppermute(flat, axis, [(i, i ^ step) for i in range(devices)])  18.8 us
    conv_general_dilated x2, matrix products, depthwise_minor(): lax.conv_general_dilated(padded_t[None], kernel[:, :, None, :], (1, 1), '...  12.5 us
    dot_general x4, matrix products, contract(): lax.dot_general(left, right, (((dim_left,), (dim_right,)), ((), ())), pre...  9.34 us
    all_gather x1, blocking collectives, gathered_weights(): full = lax.all_gather(packed, 'chan', axis=0, tiled=True)  8.6 us
    pallas_call x1, Pallas kernels, kernel_grad_minor(): pl.pallas_call(kernel_grad_body, out_shape=jax.ShapeDtypeStruct((side * s...  8.01 us
    ppermute x2, starting transfers between devices, extended(): before = lax.ppermute(last, axis, up)  6.97 us
    ppermute x6, starting transfers between devices, butterfly_step(): lax.ppermute(flat, axis, [(i, i ^ step) for i in range(devices)])  6.41 us
    unnamed x48, local copies, waits for them, and re-layouts  4.74 us
  transfers between devices with their start and end apart: 12, of which 7 were waited for; matrix products, arithmetic and copies ran while one was open for 22% of the time, Pallas kernels for 7%

profile of v8, /device:TPU:0, one launch (start us, length us, event | category | flops | bytes accessed | tf_op | source)
XLA Modules:
  0.0 122.0 jit_solution(11197077670249019108)
XLA Ops:
  1.9 3.0 %collective-permute-start = (bf16[192,3,128]{0,2,1:T(8,128)(2,1)S(1)}, bf16[192,3,128]{0,2,1:T(8,128)(2,1)S(1)}, u32[]{:S(2)}, u32[]{:S(2)}) collective-permute-start(bf16[192,3,128]{0,2,1:T(8,128)(2,1)S(1)} %slice_select_fusion.1), channel_id=1, source_target_pairs={{0,16},{16,0},{1,17},{17,1},{2,18},{18,2},{3,19},{19,3},{4,20},{20... | collective-permute-start | bytes 442376 | tf_op jit(solution)/shard_map/ppermute | solution.py:18
  8.1 8.6 %all_gather.3 = bf16[768,387]{1,0:T(8,128)(2,1)S(1)} all-gather(bf16[192,387]{1,0:T(8,128)(2,1)S(1)} %concatenate.27), channel_id=1, replica_groups=mesh['row'=2,'col'=4,'chan'=4] {'chan'}, dimensions={0}, use_global_device_ids=true | all-gather | bytes 743040 | tf_op jit(solution)/shard_map/all_gather | solution.py:170
  17.8 3.5 %collective-permute-start.1 = (bf16[192,14,3]{0,2,1:T(4,128)(2,1)S(1)}, bf16[192,14,3]{0,2,1:T(4,128)(2,1)S(1)}, u32[]{:S(2)}, u32[]{:S(2)}) collective-permute-start(bf16[192,14,3]{0,2,1:T(4,128)(2,1)S(1)} %get-tuple-element.34), channel_id=1, source_target_pairs={{0,4},{4,8},{8,12},{1,5},{5,9},{9,13},{2,6},{6,10},{10,14},{3,7},{... | collective-permute-start | bytes 48392 | tf_op jit(solution)/shard_map/ppermute | solution.py:23
  23.8 3.3 %collective-permute-done.2 = bf16[192,14,3]{0,2,1:T(4,128)(2,1)S(1)} collective-permute-done((bf16[192,14,3]{0,2,1:T(4,128)(2,1)S(1)}, bf16[192,14,3]{0,2,1:T(4,128)(2,1)S(1)}, u32[]{:S(2)}, u32[]{:S(2)}) %collective-permute-start.2) | collective-permute-done | bytes 16160 | tf_op jit(solution)/shard_map/ppermute | solution.py:24
  27.0 1.6 %bitcast_convert_fusion = (f32[14,134,192]{2,1,0:T(8,128)}, bf16[1,14,134,192]{3,2,1,0:T(8,128)(2,1)S(1)}) fusion(bf16[192,14,3]{0,2,1:T(4,128)(2,1)S(1)} %collective-permute-done.2, bf16[192,3,128]{0,2,1:T(8,128)(2,1)S(1)} %get-tuple-element.43, bf16[192,8,128]{0,2,1:T(8,128)(2,1)S(1)} %copy.84, bf16[192,3,128]{0,2,1:T(8,128)(2,1)S(1)} %get-tuple-element.42, ...), kind=kLoop, calls=%fused_computation.32 | loop fusion | flops 3962112 | bytes 2881536 | tf_op jit(solution)/shard_map/convert_element_type | solution.py:211
  28.7 8.4 %fusion.6 = f32[1,8,128,192]{3,0,2,1:T(1,128)S(1)} fusion(bf16[1,14,134,192]{3,2,1,0:T(8,128)(2,1)S(1)} %get-tuple-element.31, f32[7,7,1,192]{3,1,0,2:T(8,128)S(1)} %bitcast.132), kind=kOutput, calls=%fused_computation.13 | convolution fusion | flops 115605504 | bytes 1544448 | tf_op jit(solution)/shard_map/conv_general_dilated | solution.py:180
  37.8 1.9 %copy.89 = f32[1,8,128,192]{2,1,3,0:T(8,128)} copy(f32[1,8,128,192]{3,0,2,1:T(1,128)S(1)} %fusion.6) | data formatting | bytes 1572864 | tf_op jit(solution)/shard_map/conv_general_dilated | solution.py:180
  40.0 3.3 %multiply_convert_fusion = (bf16[1024,768]{0,1:T(8,128)(2,1)}, f32[1024,768]{0,1:T(8,128)S(1)}) fusion(f32[768]{0:T(1024)S(1)} %fusion.35, f32[24,8,8,128]{3,2,1,0:T(8,128)} %bitcast.127, f32[192]{0:T(256)S(1)} %copy-done.18, f32[192]{0:T(256)S(1)} %copy-done.14, f32[1024]{0:T(1024)S(1)} %get-tuple-element.53, f32[1024]{0:T(1024)S(1)} %get-tuple-element.54, ...), kind=kOutput, calls=%fused_computation.9 | convolution fusion | flops 307888128 | bytes 5913600 | tf_op jit(solution)/shard_map/dot_general | solution.py:53
  43.3 3.3 %fusion.62 = (bf16[1024,768]{0,1:T(8,128)(2,1)S(1)}, f32[1024,768]{0,1:T(8,128)}) fusion(f32[1024,768]{0,1:T(8,128)S(1)} %get-tuple-element.60, f32[768]{0:T(1024)S(1)} %fusion.35, f32[24,8,8,128]{3,2,1,0:T(8,128)S(1)} %convert.4, f32[192]{0:T(256)S(1)} %copy-done.16, bf16[768,387]{1,0:T(8,128)(2,1)S(1)} %all_gather.3), kind=kOutput, calls=%fused_computation.115 | convolution fusion | flops 311033856 | bytes 9049088 | tf_op jit(solution)/shard_map/dot_general | solution.py:53
  49.5 2.3 %fusion.38 = f32[192,192]{1,0:T(8,128)} fusion(bf16[1024,768]{0,1:T(8,128)(2,1)} %copy-done.19, s32[]{:T(128)S(6)} %select_n.45, f32[24,8,8,128]{3,2,1,0:T(8,128)} %bitcast.128, f32[192]{0:T(256)S(1)} %copy-done.18, f32[192]{0:T(256)S(1)} %copy-done.14, f32[1024]{0:T(1024)S(1)} %get-tuple-element.53, f32[1024]{0:T(1024)S(1)} %get-tuple-element.54, ...), kind=kOutput, calls=%fused_computation.66 | convolution fusion | flops 76677120 | bytes 1337604 | tf_op jit(solution)/shard_map/dot_general | solution.py:53
  53.0 1.5 %fusion.59 = (bf16[8,128,192]{2,1,0:T(8,128)(2,1)S(1)}, f32[8,128,192]{2,1,0:T(8,128)}) fusion(f32[8,128]{1,0:T(8,128)S(1)} %broadcast_multiply_fusion, f32[8,128]{1,0:T(8,128)S(1)} %get-tuple-element.55, f32[192]{0:T(256)S(1)} %copy-done.13, f32[1,8,128,192]{3,0,2,1:T(1,128)S(1)} %fusion.6, f32[8,128]{1,0:T(8,128)S(1)} %multiply_bitcast_fusion, ...), kind=kLoop, calls=%fused_computation.113 | loop fusion | flops 1769472 | bytes 2770432 | tf_op jit(solution)/shard_map/convert_element_type | solution.py:291
  56.2 4.1 %collective-permute-done.3 = bf16[3,128,192]{2,1,0:T(8,128)(2,1)S(1)} collective-permute-done((bf16[3,128,192]{2,1,0:T(8,128)(2,1)S(1)}, bf16[3,128,192]{2,1,0:T(8,128)(2,1)S(1)}, u32[]{:S(2)}, u32[]{:S(2)}) %collective-permute-start.3) | collective-permute-done | bytes 147488 | tf_op jit(solution)/shard_map/ppermute | solution.py:18
  60.4 3.5 %collective-permute-start.4 = (bf16[14,3,192]{2,1,0:T(4,128)(2,1)S(1)}, bf16[14,3,192]{2,1,0:T(4,128)(2,1)S(1)}, u32[]{:S(2)}, u32[]{:S(2)}) collective-permute-start(bf16[14,3,192]{2,1,0:T(4,128)(2,1)S(1)} %get-tuple-element.32), channel_id=1, source_target_pairs={{0,4},{4,8},{8,12},{1,5},{5,9},{9,13},{2,6},{6,10},{10,14},{3,7},{... | collective-permute-start | bytes 48392 | tf_op jit(solution)/shard_map/ppermute | solution.py:23
  66.8 8.0 %shard_map.194 = f32[49,8,192]{2,1,0:T(8,128)} custom-call(f32[8,128,192]{2,1,0:T(8,128)} %get-tuple-element.29.d_ref, f32[14,134,192]{2,1,0:T(8,128)} %get-tuple-element.30.p_ref), custom_call_target="tpu_custom_call" | custom-call | tf_op jit(solution)/shard_map/pallas_call | solution.py:107
  77.3 1.8 %dynamic-slice_reduce_fusion = f32[192]{0:T(256)} fusion(f32[1024,768]{0,1:T(8,128)} %get-tuple-element.62, s32[]{:T(128)S(6)} %select_n.45), kind=kLoop, calls=%fused_computation.50 | loop fusion | flops 196416 | bytes 787204 | tf_op jit(solution)/shard_map/reduce_sum | solution.py:247
  80.6 4.1 %fusion.15 = f32[8,8,17,192]{3,1,2,0:T(8,128)S(1)} fusion(bf16[14,1,7,6,192]{4,2,3,0,1:T(8,128)(2,1)S(1)} %slice.122, bf16[14,1,8,17,192]{4,2,3,0,1:T(8,128)(2,1)S(1)} %copy.105, pred[8,17]{0,1:T(8,128)(4,1)S(1)} %copy-done.20, f32[7,7,1,192]{3,1,0,2:T(8,128)S(1)} %bitcast.133), kind=kOutput, calls=%fused_computation.23 | convolution fusion | flops 126007296 | bytes 1830280 | tf_op jit(solution)/shard_map/conv_general_dilated | solution.py:180
  86.2 4.6 %fusion.31 = (f32[192]{0:T(256)S(1)}, f32[192]{0:T(256)S(1)}, bf16[8,128,192]{1,0,2:T(8,128)(2,1)}, bf16[192,8,128]{2,1,0:T(8,128)(2,1)}) fusion(f32[24,8,8,128]{3,2,1,0:T(8,128)S(1)} %copy.120, bf16[192,8,128]{2,1,0:T(8,128)(2,1)S(1)} %copy-done.4, f32[192]{0:T(256)} %param.19, f32[192]{0:T(256)} %param.20, bf16[192,8,128]{2,1,0:T(8,128)(2,1)S(1)} %copy-done.2, ...), kind=kLoop, calls=%fused_computation.47 | loop fusion | flops 2358912 | bytes 3148800 | tf_op jit(solution)/shard_map/reduce_sum | solution.py:238
  90.8 1.6 %concatenate.31 = f32[74304]{0:T(1024)S(1)} concatenate(f32[36864]{0:T(1024)S(1)} %reshape.302, f32[192]{0:T(256)S(1)} %copy-done.15, f32[36864]{0:T(1024)S(1)} %copy-done.8, f32[192]{0:T(256)S(1)} %get-tuple-element.27, f32[192]{0:T(256)S(1)} %get-tuple-element.26), dimensions={0} | concatenate | bytes 594432 | tf_op jit(solution)/shard_map/concatenate | solution.py:116
  92.5 3.7 %collective-permute-start.9 = (f32[42144]{0:T(1024)S(1)}, f32[42144]{0:T(1024)S(1)}, u32[]{:S(2)}, u32[]{:S(2)}) collective-permute-start(f32[42144]{0:T(1024)S(1)} %slice.129), channel_id=1, source_target_pairs={{0,8},{4,12},{8,0},{12,4},{1,9},{5,13},{9,1},{13,5},{2,10},{6,14},... | collective-permute-start | bytes 505736 | tf_op jit(solution)/shard_map/ppermute | solution.py:146
  97.2 9.7 %collective-permute-done.9 = f32[42144]{0:T(1024)S(1)} collective-permute-done((f32[42144]{0:T(1024)S(1)}, f32[42144]{0:T(1024)S(1)}, u32[]{:S(2)}, u32[]{:S(2)}) %collective-permute-start.9) | collective-permute-done | bytes 168608 | tf_op jit(solution)/shard_map/ppermute | solution.py:146
  107.1 1.7 %collective-permute-done.7 = f32[42144]{0:T(1024)S(1)} collective-permute-done((f32[42144]{0:T(1024)S(1)}, f32[42144]{0:T(1024)S(1)}, u32[]{:S(2)}, u32[]{:S(2)}) %collective-permute-start.7) | collective-permute-done | bytes 168608 | tf_op jit(solution)/shard_map/ppermute | solution.py:146
  109.2 5.0 %collective-permute-done.10 = f32[42144]{0:T(1024)S(1)} collective-permute-done((f32[42144]{0:T(1024)S(1)}, f32[42144]{0:T(1024)S(1)}, u32[]{:S(2)}, u32[]{:S(2)}) %collective-permute-start.10) | collective-permute-done | bytes 168608 | tf_op jit(solution)/shard_map/ppermute | solution.py:146
  114.2 1.6 %collective-permute-start.11 = (f32[42144]{0:T(1024)S(1)}, f32[42144]{0:T(1024)S(1)}, u32[]{:S(2)}, u32[]{:S(2)}) collective-permute-start(f32[42144]{0:T(1024)S(1)} %add.146), channel_id=1, source_target_pairs={{0,16},{16,0},{1,17},{17,1},{2,18},{18,2},{3,19},{19,3},{4,20},{20... | collective-permute-start | bytes 505736 | tf_op jit(solution)/shard_map/ppermute | solution.py:146
  117.4 2.3 %collective-permute-done.11 = f32[42144]{0:T(1024)S(1)} collective-permute-done((f32[42144]{0:T(1024)S(1)}, f32[42144]{0:T(1024)S(1)}, u32[]{:S(2)}, u32[]{:S(2)}) %collective-permute-start.11) | collective-permute-done | bytes 168608 | tf_op jit(solution)/shard_map/ppermute | solution.py:146
  (117 shorter events, 28.5 us)
Async XLA Ops:
  1.9 15.8 %collective-permute-start = (bf16[192,3,128]{0,2,1:T(8,128)(2,1)S(1)}, bf16[192,3,128]{0,2,1:T(8,128)(2,1)S(1)}, u32[]{:S(2)}, u32[]{:S(2)}) collective-permute-start(bf16[192,3,128]{0,2,1:T(8,128)(2,1)S(1)} %slice_select_fusion.1), channel_id=1, source_target_pairs={{0,16},{16,0},{1,17},{17,1},{2,18},{18,2},{3,19},{19,3},{4,20},{20... | collective-permute-start | bytes 442376 | tf_op jit(solution)/shard_map/ppermute | solution.py:18
  17.7 5.3 %copy-start.3 = (bf16[192,8,128]{2,1,0:T(8,128)(2,1)S(1)}, bf16[192,8,128]{2,1,0:T(8,128)(2,1)}, u32[]{:S(2)}) copy-start(bf16[192,8,128]{2,1,0:T(8,128)(2,1)} %param.21) | copy-start | bytes 1179652
  17.7 5.4 %copy-start.11 = (f32[7,7,192]{2,1,0:T(8,128)S(1)}, f32[7,7,192]{2,1,0:T(8,128)}, u32[]{:S(2)}) copy-start(f32[7,7,192]{2,1,0:T(8,128)} %param.12) | copy-start | bytes 112900
  17.8 6.0 %collective-permute-start.1 = (bf16[192,14,3]{0,2,1:T(4,128)(2,1)S(1)}, bf16[192,14,3]{0,2,1:T(4,128)(2,1)S(1)}, u32[]{:S(2)}, u32[]{:S(2)}) collective-permute-start(bf16[192,14,3]{0,2,1:T(4,128)(2,1)S(1)} %get-tuple-element.34), channel_id=1, source_target_pairs={{0,4},{4,8},{8,12},{1,5},{5,9},{9,13},{2,6},{6,10},{10,14},{3,7},{... | collective-permute-start | bytes 48392 | tf_op jit(solution)/shard_map/ppermute | solution.py:23
  21.3 5.8 %collective-permute-start.2 = (bf16[192,14,3]{0,2,1:T(4,128)(2,1)S(1)}, bf16[192,14,3]{0,2,1:T(4,128)(2,1)S(1)}, u32[]{:S(2)}, u32[]{:S(2)}) collective-permute-start(bf16[192,14,3]{0,2,1:T(4,128)(2,1)S(1)} %get-tuple-element.35), channel_id=1, source_target_pairs={{4,0},{8,4},{12,8},{5,1},{9,5},{13,9},{6,2},{10,6},{14,10},{7,3},{... | collective-permute-start | bytes 48392 | tf_op jit(solution)/shard_map/ppermute | solution.py:24
  37.1 2.6 %copy-start.13 = (f32[192]{0:T(256)S(1)}, f32[192]{0:T(256)}, u32[]{:S(2)}) copy-start(f32[192]{0:T(256)} %param.13) | copy-start | bytes 2308
  40.0 3.4 %copy-start.16 = (f32[192]{0:T(256)S(1)}, f32[192]{0:T(256)}, u32[]{:S(2)}) copy-start(f32[192]{0:T(256)} %param.20) | copy-start | bytes 2308
  43.3 3.3 %copy-start.9 = (bf16[768,192]{1,0:T(8,128)(2,1)S(1)}, bf16[768,192]{1,0:T(8,128)(2,1)}, u32[]{:S(2)}) copy-start(bf16[768,192]{1,0:T(8,128)(2,1)} %get-tuple-element.37) | copy-start | bytes 884740
  53.0 2.5 %copy-start.5 = (bf16[768,192]{1,0:T(8,128)(2,1)S(1)}, bf16[768,192]{1,0:T(8,128)(2,1)}, u32[]{:S(2)}) copy-start(bf16[768,192]{1,0:T(8,128)(2,1)} %get-tuple-element.38) | copy-start | bytes 884740
  54.5 5.8 %collective-permute-start.3 = (bf16[3,128,192]{2,1,0:T(8,128)(2,1)S(1)}, bf16[3,128,192]{2,1,0:T(8,128)(2,1)S(1)}, u32[]{:S(2)}, u32[]{:S(2)}) collective-permute-start(bf16[3,128,192]{2,1,0:T(8,128)(2,1)S(1)} %slice_select_fusion), channel_id=1, source_target_pairs={{0,16},{16,0},{1,17},{17,1},{2,18},{18,2},{3,19},{19,3},{4,20},{20... | collective-permute-start | bytes 442376 | tf_op jit(solution)/shard_map/ppermute | solution.py:18
  56.2 9.6 %copy-start.10 = (f32[192,192]{1,0:T(8,128)S(1)}, f32[192,192]{1,0:T(8,128)}, u32[]{:S(2)}) copy-start(f32[192,192]{1,0:T(8,128)} %fusion.38) | copy-start | bytes 442372
  60.4 18.8 %collective-permute-start.4 = (bf16[14,3,192]{2,1,0:T(4,128)(2,1)S(1)}, bf16[14,3,192]{2,1,0:T(4,128)(2,1)S(1)}, u32[]{:S(2)}, u32[]{:S(2)}) collective-permute-start(bf16[14,3,192]{2,1,0:T(4,128)(2,1)S(1)} %get-tuple-element.32), channel_id=1, source_target_pairs={{0,4},{4,8},{8,12},{1,5},{5,9},{9,13},{2,6},{6,10},{10,14},{3,7},{... | collective-permute-start | bytes 48392 | tf_op jit(solution)/shard_map/ppermute | solution.py:23
  63.9 15.3 %collective-permute-start.5 = (bf16[14,3,192]{2,1,0:T(4,128)(2,1)S(1)}, bf16[14,3,192]{2,1,0:T(4,128)(2,1)S(1)}, u32[]{:S(2)}, u32[]{:S(2)}) collective-permute-start(bf16[14,3,192]{2,1,0:T(4,128)(2,1)S(1)} %get-tuple-element.33), channel_id=1, source_target_pairs={{4,0},{8,4},{12,8},{5,1},{9,5},{13,9},{6,2},{10,6},{14,10},{7,3},{... | collective-permute-start | bytes 48392 | tf_op jit(solution)/shard_map/ppermute | solution.py:24
  66.8 9.2 %copy-start.17 = (f32[192]{0:T(256)S(1)}, f32[192]{0:T(256)}, u32[]{:S(2)}) copy-start(f32[192]{0:T(256)} %get-tuple-element.24) | copy-start | bytes 2308
  76.1 3.6 %copy-start.6 = (f32[46848]{0:T(1024)}, f32[46848]{0:T(1024)S(1)}, u32[]{:S(2)}) copy-start(f32[46848]{0:T(1024)S(1)} %concatenate.30) | copy-start | bytes 562180
  76.8 19.4 %collective-permute-start.6 = (f32[42144]{0:T(1024)}, f32[42144]{0:T(1024)}, u32[]{:S(2)}, u32[]{:S(2)}) collective-permute-start(f32[42144]{0:T(1024)} %slice.124), channel_id=1, source_target_pairs={{0,16},{16,0},{1,17},{17,1},{2,18},{18,2},{3,19},{19,3},{4,20},{20... | collective-permute-start | bytes 505736 | tf_op jit(solution)/shard_map/ppermute | solution.py:146
  86.2 4.6 %copy-start.8 = (f32[36864]{0:T(1024)S(1)}, f32[36864]{0:T(1024)}, u32[]{:S(2)}) copy-start(f32[36864]{0:T(1024)} %reshape.303) | copy-start | bytes 442372
  86.2 4.6 %copy-start.15 = (f32[192]{0:T(256)S(1)}, f32[192]{0:T(256)}, u32[]{:S(2)}) copy-start(f32[192]{0:T(256)} %dynamic-slice_reduce_fusion) | copy-start | bytes 2308
  86.2 10.0 %copy-start.7 = (f32[46848]{0:T(1024)S(1)}, f32[46848]{0:T(1024)}, u32[]{:S(2)}) copy-start(f32[46848]{0:T(1024)} %copy-done.6) | copy-start | bytes 562180
  92.5 14.4 %collective-permute-start.9 = (f32[42144]{0:T(1024)S(1)}, f32[42144]{0:T(1024)S(1)}, u32[]{:S(2)}, u32[]{:S(2)}) collective-permute-start(f32[42144]{0:T(1024)S(1)} %slice.129), channel_id=1, source_target_pairs={{0,8},{4,12},{8,0},{12,4},{1,9},{5,13},{9,1},{13,5},{2,10},{6,14},... | collective-permute-start | bytes 505736 | tf_op jit(solution)/shard_map/ppermute | solution.py:146
  97.1 11.6 %collective-permute-start.7 = (f32[42144]{0:T(1024)S(1)}, f32[42144]{0:T(1024)S(1)}, u32[]{:S(2)}, u32[]{:S(2)}) collective-permute-start(f32[42144]{0:T(1024)S(1)} %slice_add_fusion.3), channel_id=1, source_target_pairs={{0,8},{4,12},{8,0},{12,4},{1,9},{5,13},{9,1},{13,5},{2,10},{6,14},... | collective-permute-start | bytes 505736 | tf_op jit(solution)/shard_map/ppermute | solution.py:146
  107.0 7.2 %collective-permute-start.10 = (f32[42144]{0:T(1024)S(1)}, f32[42144]{0:T(1024)S(1)}, u32[]{:S(2)}, u32[]{:S(2)}) collective-permute-start(f32[42144]{0:T(1024)S(1)} %slice_add_fusion.2), channel_id=1, source_target_pairs={{0,4},{4,0},{8,12},{12,8},{1,5},{5,1},{9,13},{13,9},{2,6},{6,2},{1... | collective-permute-start | bytes 505736 | tf_op jit(solution)/shard_map/ppermute | solution.py:146
  108.8 7.2 %collective-permute-start.8 = (f32[42144]{0:T(1024)S(1)}, f32[42144]{0:T(1024)S(1)}, u32[]{:S(2)}, u32[]{:S(2)}) collective-permute-start(f32[42144]{0:T(1024)S(1)} %add.143), channel_id=1, source_target_pairs={{0,4},{4,0},{8,12},{12,8},{1,5},{5,1},{9,13},{13,9},{2,6},{6,2},{1... | collective-permute-start | bytes 505736 | tf_op jit(solution)/shard_map/ppermute | solution.py:146
  114.2 5.5 %collective-permute-start.11 = (f32[42144]{0:T(1024)S(1)}, f32[42144]{0:T(1024)S(1)}, u32[]{:S(2)}, u32[]{:S(2)}) collective-permute-start(f32[42144]{0:T(1024)S(1)} %add.146), channel_id=1, source_target_pairs={{0,16},{16,0},{1,17},{17,1},{2,18},{18,2},{3,19},{19,3},{4,20},{20... | collective-permute-start | bytes 505736 | tf_op jit(solution)/shard_map/ppermute | solution.py:146
  (9 other events, 12.9 us)

commit v9 on v8

--- a/solution.py
+++ b/solution.py
@@ -148,14 +148,14 @@
 
 def butterfly_sum(values, axes):
     flat = flat_pack(values)
-    first = butterfly_steps(axes[:1])
-    order_a = first + butterfly_steps(axes[1:])[::-1]
-    order_b = order_a[len(first) :] + order_a[: len(first)]
-    half = flat.shape[0] // 2
-    part_a, part_b = flat[:half], flat[half:]
-    for step_a, step_b in zip(order_a, order_b):
-        part_a, part_b = butterfly_step(part_a, *step_a), butterfly_step(part_b, *step_b)
-    return flat_unpack(jnp.concatenate([part_a, part_b]), values)
+    steps = butterfly_steps(axes[:1]) + butterfly_steps(axes[1:])[::-1]
+    count = min(3, len(steps))
+    size = -(-flat.shape[0] // count)
+    parts = [flat[p * size : (p + 1) * size] for p in range(count)]
+    orders = [steps[p * len(steps) // count :] + steps[: p * len(steps) // count] for p in range(count)]
+    for stage in range(len(steps)):
+        parts = [butterfly_step(part, *order[stage]) for part, order in zip(parts, orders)]
+    return flat_unpack(jnp.concatenate(parts), values)
 
 
 def gathered_weights(w_in, b_in, w_out):

time: 123 us -> 124 us (level)
  waiting for transfers between devices: 26.2 us -> 12.1 us
  starting transfers between devices: 19.6 us -> 25.4 us
  other arithmetic: 16.2 us -> 21.4 us
  local copies, waits for them, and re-layouts: 18.4 us -> 21.5 us
    ppermute x6 -> x9, waiting for transfers between devices: 18.8 us -> 8.33 us  [butterfly_step(): lax.ppermute(flat, axis, [(i, i ^ step) for i in range(devices)])]
    ppermute x6 -> x9, starting transfers between devices: 6.41 us -> 11.6 us  [butterfly_step(): lax.ppermute(flat, axis, [(i, i ^ step) for i in range(devices)])]
    ppermute x2, waiting for transfers between devices: 4.15 us -> 0.01 us  [extended(): got = lax.ppermute(jnp.where(first, last, leading), axis, [(0, 1), (1, 0)])]
    add x6 -> x9, other arithmetic: 1.14 us -> 4.45 us  [butterfly_step(): flat + lax.ppermute(flat, axis, [(i, i ^ step) for i in range(devices)])]
    unnamed x48 -> x72, local copies, waits for them, and re-layouts: 4.74 us -> 6.9 us
  transfers between devices with their start and end apart: 12 -> 15, of which waited for: 7 -> 5; matrix products, arithmetic and copies ran while one was open for 22% -> 24% of each run, Pallas kernels for 7% -> 6%
where the time goes in v9:
time: 124 us; the launch traced here: 123 us
  starting transfers between devices  25.4 us (20%)
  matrix products  24.8 us (20%)
  local copies, waits for them, and re-layouts  21.5 us (17%)
  other arithmetic  21.4 us (17%)
  waiting for transfers between devices  12.1 us (10%)
  blocking collectives  8.6 us (7%)
  Pallas kernels  7.84 us (6%)
  between operations  1.34 us (1%)
    conv_general_dilated x2, matrix products, depthwise_minor(): lax.conv_general_dilated(padded_t[None], kernel[:, :, None, :], (1, 1), '...  12.6 us
    ppermute x9, starting transfers between devices, butterfly_step(): lax.ppermute(flat, axis, [(i, i ^ step) for i in range(devices)])  11.6 us
    dot_general x4, matrix products, contract(): lax.dot_general(left, right, (((dim_left,), (dim_right,)), ((), ())), pre...  10.3 us
    all_gather x1, blocking collectives, gathered_weights(): full = lax.all_gather(packed, 'chan', axis=0, tiled=True)  8.6 us
    ppermute x9, waiting for transfers between devices, butterfly_step(): lax.ppermute(flat, axis, [(i, i ^ step) for i in range(devices)])  8.33 us
    pallas_call x1, Pallas kernels, kernel_grad_minor(): pl.pallas_call(kernel_grad_body, out_shape=jax.ShapeDtypeStruct((side * s...  7.84 us
    ppermute x2, starting transfers between devices, extended(): before = lax.ppermute(last, axis, up)  7.41 us
    unnamed x72, local copies, waits for them, and re-layouts  6.9 us
  transfers between devices with their start and end apart: 15, of which 5 were waited for; matrix products, arithmetic and copies ran while one was open for 24% of the time, Pallas kernels for 6%

profile of v9, /device:TPU:0, one launch (start us, length us, event | category | flops | bytes accessed | tf_op | source)
XLA Modules:
  0.0 123.0 jit_solution(1234315389883818110)
XLA Ops:
  1.9 3.0 %collective-permute-start = (bf16[192,3,128]{0,2,1:T(8,128)(2,1)S(1)}, bf16[192,3,128]{0,2,1:T(8,128)(2,1)S(1)}, u32[]{:S(2)}, u32[]{:S(2)}) collective-permute-start(bf16[192,3,128]{0,2,1:T(8,128)(2,1)S(1)} %slice_select_fusion.1), channel_id=1, source_target_pairs={{0,16},{16,0},{1,17},{17,1},{2,18},{18,2},{3,19},{19,3},{4,20},{20... | collective-permute-start | bytes 442376 | tf_op jit(solution)/shard_map/ppermute | solution.py:18
  8.1 8.6 %all_gather.3 = bf16[768,387]{1,0:T(8,128)(2,1)S(1)} all-gather(bf16[192,387]{1,0:T(8,128)(2,1)S(1)} %concatenate.34), channel_id=1, replica_groups=mesh['row'=2,'col'=4,'chan'=4] {'chan'}, dimensions={0}, use_global_device_ids=true | all-gather | bytes 743040 | tf_op jit(solution)/shard_map/all_gather | solution.py:170
  17.8 3.5 %collective-permute-start.1 = (bf16[192,14,3]{0,2,1:T(4,128)(2,1)S(1)}, bf16[192,14,3]{0,2,1:T(4,128)(2,1)S(1)}, u32[]{:S(2)}, u32[]{:S(2)}) collective-permute-start(bf16[192,14,3]{0,2,1:T(4,128)(2,1)S(1)} %get-tuple-element.34), channel_id=1, source_target_pairs={{0,4},{4,8},{8,12},{1,5},{5,9},{9,13},{2,6},{6,10},{10,14},{3,7},{... | collective-permute-start | bytes 48392 | tf_op jit(solution)/shard_map/ppermute | solution.py:23
  24.4 2.7 %collective-permute-done.2 = bf16[192,14,3]{0,2,1:T(4,128)(2,1)S(1)} collective-permute-done((bf16[192,14,3]{0,2,1:T(4,128)(2,1)S(1)}, bf16[192,14,3]{0,2,1:T(4,128)(2,1)S(1)}, u32[]{:S(2)}, u32[]{:S(2)}) %collective-permute-start.2) | collective-permute-done | bytes 16160 | tf_op jit(solution)/shard_map/ppermute | solution.py:24
  27.0 1.6 %bitcast_convert_fusion = (f32[14,134,192]{2,1,0:T(8,128)}, bf16[1,14,134,192]{3,2,1,0:T(8,128)(2,1)S(1)}) fusion(bf16[192,14,3]{0,2,1:T(4,128)(2,1)S(1)} %collective-permute-done.2, bf16[192,3,128]{0,2,1:T(8,128)(2,1)S(1)} %get-tuple-element.43, bf16[192,8,128]{0,2,1:T(8,128)(2,1)S(1)} %copy.84, bf16[192,3,128]{0,2,1:T(8,128)(2,1)S(1)} %get-tuple-element.42, ...), kind=kLoop, calls=%fused_computation.32 | loop fusion | flops 3962112 | bytes 2881536 | tf_op jit(solution)/shard_map/convert_element_type | solution.py:211
  28.6 8.4 %fusion.6 = f32[1,8,128,192]{3,0,2,1:T(1,128)S(1)} fusion(bf16[1,14,134,192]{3,2,1,0:T(8,128)(2,1)S(1)} %get-tuple-element.31, f32[7,7,1,192]{3,1,0,2:T(8,128)S(1)} %bitcast.132), kind=kOutput, calls=%fused_computation.13 | convolution fusion | flops 115605504 | bytes 1544448 | tf_op jit(solution)/shard_map/conv_general_dilated | solution.py:180
  37.8 1.9 %copy.89 = f32[1,8,128,192]{2,1,3,0:T(8,128)} copy(f32[1,8,128,192]{3,0,2,1:T(1,128)S(1)} %fusion.6) | data formatting | bytes 1572864 | tf_op jit(solution)/shard_map/conv_general_dilated | solution.py:180
  41.2 3.3 %multiply_convert_fusion = (bf16[1024,768]{0,1:T(8,128)(2,1)}, f32[1024,768]{0,1:T(8,128)S(1)}) fusion(f32[768]{0:T(1024)S(1)} %copy-done.27, f32[24,8,8,128]{3,2,1,0:T(8,128)} %bitcast.127, f32[192]{0:T(256)S(1)} %copy-done.30, f32[192]{0:T(256)S(1)} %copy-done.23, f32[1024]{0:T(1024)S(1)} %get-tuple-element.52, f32[1024]{0:T(1024)S(1)} %get-tuple-element.53, ...), kind=kOutput, calls=%fused_computation.9 | convolution fusion | flops 307888128 | bytes 5913600 | tf_op jit(solution)/shard_map/dot_general | solution.py:53
  44.5 3.3 %fusion.63 = (bf16[1024,768]{0,1:T(8,128)(2,1)S(1)}, f32[1024,768]{0,1:T(8,128)}) fusion(f32[1024,768]{0,1:T(8,128)S(1)} %get-tuple-element.59, f32[768]{0:T(1024)S(1)} %copy-done.27, f32[24,8,8,128]{3,2,1,0:T(8,128)S(1)} %convert.4, f32[192]{0:T(256)S(1)} %copy-done.28, bf16[768,387]{1,0:T(8,128)(2,1)S(1)} %all_gather.3), kind=kOutput, calls=%fused_computation.117 | convolution fusion | flops 311033856 | bytes 9049088 | tf_op jit(solution)/shard_map/dot_general | solution.py:53
  51.2 2.3 %fusion.38 = f32[192,192]{1,0:T(8,128)} fusion(bf16[1024,768]{0,1:T(8,128)(2,1)} %copy-done.31, s32[]{:T(128)S(6)} %select_n.45, f32[24,8,8,128]{3,2,1,0:T(8,128)} %bitcast.128, f32[192]{0:T(256)S(1)} %copy-done.30, f32[192]{0:T(256)S(1)} %copy-done.23, f32[1024]{0:T(1024)S(1)} %get-tuple-element.52, f32[1024]{0:T(1024)S(1)} %get-tuple-element.53, ...), kind=kOutput, calls=%fused_computation.66 | convolution fusion | flops 76677120 | bytes 1337604 | tf_op jit(solution)/shard_map/dot_general | solution.py:53
  53.5 1.7 %reshape.294 = f32[36864]{0:T(1024)} reshape(f32[192,192]{1,0:T(8,128)} %fusion.38) | data formatting | bytes 294912 | tf_op jit(solution)/shard_map/reshape | solution.py:116
  58.2 1.5 %concatenate.38 = f32[73920]{0:T(1024)S(1)} concatenate(f32[36864]{0:T(1024)S(1)} %copy-done.8, f32[192]{0:T(256)S(1)} %dynamic-slice_reduce_fusion, f32[36864]{0:T(1024)S(1)} %reshape.295), dimensions={0} | concatenate | bytes 591360 | tf_op jit(solution)/shard_map/concatenate | solution.py:116
  60.4 2.6 %collective-permute-start.9 = (f32[28096]{0:T(1024)}, f32[28096]{0:T(1024)}, u32[]{:S(2)}, u32[]{:S(2)}) collective-permute-start(f32[28096]{0:T(1024)} %slice.128), channel_id=1, source_target_pairs={{0,8},{4,12},{8,0},{12,4},{1,9},{5,13},{9,1},{13,5},{2,10},{6,14},... | collective-permute-start | bytes 337160 | tf_op jit(solution)/shard_map/ppermute | solution.py:146
  64.8 1.5 %fusion.60 = (bf16[8,128,192]{2,1,0:T(8,128)(2,1)S(1)}, f32[8,128,192]{2,1,0:T(8,128)}) fusion(f32[8,128]{1,0:T(8,128)S(1)} %broadcast_multiply_fusion, f32[8,128]{1,0:T(8,128)S(1)} %copy-done.14, f32[192]{0:T(256)S(1)} %copy-done.22, f32[1,8,128,192]{3,0,2,1:T(1,128)S(1)} %fusion.6, f32[8,128]{1,0:T(8,128)S(1)} %multiply_bitcast_fusion, ...), kind=kLoop, calls=%fused_computation.115 | loop fusion | flops 1769472 | bytes 2770432 | tf_op jit(solution)/shard_map/convert_element_type | solution.py:291
  68.6 7.8 %shard_map.194 = f32[49,8,192]{2,1,0:T(8,128)} custom-call(f32[8,128,192]{2,1,0:T(8,128)} %get-tuple-element.29.d_ref, f32[14,134,192]{2,1,0:T(8,128)} %get-tuple-element.30.p_ref), custom_call_target="tpu_custom_call" | custom-call | tf_op jit(solution)/shard_map/pallas_call | solution.py:107
  78.3 1.6 %collective-permute-start.6 = (f32[28096]{0:T(1024)S(1)}, f32[28096]{0:T(1024)S(1)}, u32[]{:S(2)}, u32[]{:S(2)}) collective-permute-start(f32[28096]{0:T(1024)S(1)} %slice.123), channel_id=1, source_target_pairs={{0,16},{16,0},{1,17},{17,1},{2,18},{18,2},{3,19},{19,3},{4,20},{20... | collective-permute-start | bytes 337160 | tf_op jit(solution)/shard_map/ppermute | solution.py:146
  79.9 1.7 %slice_add_fusion.3 = f32[28096]{0:T(1024)} fusion(f32[28096]{0:T(1024)} %collective-permute-done.9, f32[73920]{0:T(1024)} %copy-done.10), kind=kLoop, calls=%fused_computation.109 | loop fusion | flops 28096 | bytes 337152 | tf_op jit(solution)/shard_map/add | solution.py:146
  81.7 3.9 %collective-permute-start.4 = (bf16[14,3,192]{2,1,0:T(4,128)(2,1)S(1)}, bf16[14,3,192]{2,1,0:T(4,128)(2,1)S(1)}, u32[]{:S(2)}, u32[]{:S(2)}) collective-permute-start(bf16[14,3,192]{2,1,0:T(4,128)(2,1)S(1)} %get-tuple-element.32), channel_id=1, source_target_pairs={{0,4},{4,8},{8,12},{1,5},{5,9},{9,13},{2,6},{6,10},{10,14},{3,7},{... | collective-permute-start | bytes 48392 | tf_op jit(solution)/shard_map/ppermute | solution.py:23
  85.6 1.5 %collective-permute-start.5 = (bf16[14,3,192]{2,1,0:T(4,128)(2,1)S(1)}, bf16[14,3,192]{2,1,0:T(4,128)(2,1)S(1)}, u32[]{:S(2)}, u32[]{:S(2)}) collective-permute-start(bf16[14,3,192]{2,1,0:T(4,128)(2,1)S(1)} %get-tuple-element.33), channel_id=1, source_target_pairs={{4,0},{8,4},{12,8},{5,1},{9,5},{13,9},{6,2},{10,6},{14,10},{7,3},{... | collective-permute-start | bytes 48392 | tf_op jit(solution)/shard_map/ppermute | solution.py:24
  87.7 2.5 %collective-permute-start.7 = (f32[28096]{0:T(1024)}, f32[28096]{0:T(1024)}, u32[]{:S(2)}, u32[]{:S(2)}) collective-permute-start(f32[28096]{0:T(1024)} %slice_add_fusion.4), channel_id=1, source_target_pairs={{0,8},{4,12},{8,0},{12,4},{1,9},{5,13},{9,1},{13,5},{2,10},{6,14},... | collective-permute-start | bytes 337160 | tf_op jit(solution)/shard_map/ppermute | solution.py:146
  92.8 4.2 %fusion.15 = f32[8,8,17,192]{3,1,2,0:T(8,128)S(1)} fusion(bf16[14,1,7,6,192]{4,2,3,0,1:T(8,128)(2,1)S(1)} %slice.121, bf16[14,1,8,17,192]{4,2,3,0,1:T(8,128)(2,1)S(1)} %copy.105, pred[8,17]{0,1:T(8,128)(4,1)S(1)} %copy-done.32, f32[7,7,1,192]{3,1,0,2:T(8,128)S(1)} %bitcast.133), kind=kOutput, calls=%fused_computation.23 | convolution fusion | flops 126007296 | bytes 1830280 | tf_op jit(solution)/shard_map/conv_general_dilated | solution.py:180
  98.7 4.5 %fusion.31 = (f32[192]{0:T(256)S(1)}, f32[192]{0:T(256)S(1)}, bf16[8,128,192]{1,0,2:T(8,128)(2,1)}, bf16[192,8,128]{2,1,0:T(8,128)(2,1)}) fusion(f32[24,8,8,128]{3,2,1,0:T(8,128)S(1)} %copy-done.2, bf16[192,8,128]{2,1,0:T(8,128)(2,1)S(1)} %copy-done.6, f32[192]{0:T(256)} %param.19, f32[192]{0:T(256)} %param.20, bf16[192,8,128]{2,1,0:T(8,128)(2,1)S(1)} %copy-done.4, ...), kind=kLoop, calls=%fused_computation.47 | loop fusion | flops 2358912 | bytes 3148800 | tf_op jit(solution)/shard_map/reduce_sum | solution.py:238
  109.8 2.7 %collective-permute-done.8 = f32[28096]{0:T(1024)S(1)} collective-permute-done((f32[28096]{0:T(1024)S(1)}, f32[28096]{0:T(1024)S(1)}, u32[]{:S(2)}, u32[]{:S(2)}) %collective-permute-start.8) | collective-permute-done | bytes 112416 | tf_op jit(solution)/shard_map/ppermute | solution.py:146
  115.2 5.5 %collective-permute-done.14 = f32[28096]{0:T(1024)S(1)} collective-permute-done((f32[28096]{0:T(1024)S(1)}, f32[28096]{0:T(1024)S(1)}, u32[]{:S(2)}, u32[]{:S(2)}) %collective-permute-start.14) | collective-permute-done | bytes 112416 | tf_op jit(solution)/shard_map/ppermute | solution.py:146
  (153 shorter events, 39.9 us)
Async XLA Ops:
  1.9 15.8 %collective-permute-start = (bf16[192,3,128]{0,2,1:T(8,128)(2,1)S(1)}, bf16[192,3,128]{0,2,1:T(8,128)(2,1)S(1)}, u32[]{:S(2)}, u32[]{:S(2)}) collective-permute-start(bf16[192,3,128]{0,2,1:T(8,128)(2,1)S(1)} %slice_select_fusion.1), channel_id=1, source_target_pairs={{0,16},{16,0},{1,17},{17,1},{2,18},{18,2},{3,19},{19,3},{4,20},{20... | collective-permute-start | bytes 442376 | tf_op jit(solution)/shard_map/ppermute | solution.py:18
  17.8 6.6 %collective-permute-start.1 = (bf16[192,14,3]{0,2,1:T(4,128)(2,1)S(1)}, bf16[192,14,3]{0,2,1:T(4,128)(2,1)S(1)}, u32[]{:S(2)}, u32[]{:S(2)}) collective-permute-start(bf16[192,14,3]{0,2,1:T(4,128)(2,1)S(1)} %get-tuple-element.34), channel_id=1, source_target_pairs={{0,4},{4,8},{8,12},{1,5},{5,9},{9,13},{2,6},{6,10},{10,14},{3,7},{... | collective-permute-start | bytes 48392 | tf_op jit(solution)/shard_map/ppermute | solution.py:23
  21.3 5.8 %collective-permute-start.2 = (bf16[192,14,3]{0,2,1:T(4,128)(2,1)S(1)}, bf16[192,14,3]{0,2,1:T(4,128)(2,1)S(1)}, u32[]{:S(2)}, u32[]{:S(2)}) collective-permute-start(bf16[192,14,3]{0,2,1:T(4,128)(2,1)S(1)} %get-tuple-element.35), channel_id=1, source_target_pairs={{4,0},{8,4},{12,8},{5,1},{9,5},{13,9},{6,2},{10,6},{14,10},{7,3},{... | collective-permute-start | bytes 48392 | tf_op jit(solution)/shard_map/ppermute | solution.py:24
  56.5 7.8 %copy-start.13 = (f32[8,128]{1,0:T(8,128)S(1)}, f32[8,128]{1,0:T(8,128)}, u32[]{:S(2)}) copy-start(f32[8,128]{1,0:T(8,128)} %copy-done.12) | copy-start | bytes 12292
  56.5 7.8 %copy-start.15 = (f32[8,128]{1,0:T(8,128)S(1)}, f32[8,128]{1,0:T(8,128)}, u32[]{:S(2)}) copy-start(f32[8,128]{1,0:T(8,128)} %get-tuple-element.51) | copy-start | bytes 12292
  56.5 7.8 %copy-start.21 = (f32[192]{0:T(256)S(1)}, f32[192]{0:T(256)}, u32[]{:S(2)}) copy-start(f32[192]{0:T(256)} %param.13) | copy-start | bytes 2308
  56.5 7.8 %copy-start.24 = (f32[192]{0:T(256)S(1)}, f32[192]{0:T(256)}, u32[]{:S(2)}) copy-start(f32[192]{0:T(256)} %param.14) | copy-start | bytes 2308
  58.1 6.6 %copy-start.14 = (f32[8,128]{1,0:T(8,128)S(1)}, f32[8,128]{1,0:T(8,128)}, u32[]{:S(2)}) copy-start(f32[8,128]{1,0:T(8,128)} %copy-done.12) | copy-start | bytes 12292
  58.1 6.6 %copy-start.16 = (f32[8,128]{1,0:T(8,128)S(1)}, f32[8,128]{1,0:T(8,128)}, u32[]{:S(2)}) copy-start(f32[8,128]{1,0:T(8,128)} %get-tuple-element.51) | copy-start | bytes 12292
  58.2 6.6 %copy-start.22 = (f32[192]{0:T(256)S(1)}, f32[192]{0:T(256)}, u32[]{:S(2)}) copy-start(f32[192]{0:T(256)} %param.13) | copy-start | bytes 2308
  60.4 19.4 %collective-permute-start.9 = (f32[28096]{0:T(1024)}, f32[28096]{0:T(1024)}, u32[]{:S(2)}, u32[]{:S(2)}) collective-permute-start(f32[28096]{0:T(1024)} %slice.128), channel_id=1, source_target_pairs={{0,8},{4,12},{8,0},{12,4},{1,9},{5,13},{9,1},{13,5},{2,10},{6,14},... | collective-permute-start | bytes 337160 | tf_op jit(solution)/shard_map/ppermute | solution.py:146
  66.4 15.2 %collective-permute-start.3 = (bf16[3,128,192]{2,1,0:T(8,128)(2,1)S(1)}, bf16[3,128,192]{2,1,0:T(8,128)(2,1)S(1)}, u32[]{:S(2)}, u32[]{:S(2)}) collective-permute-start(bf16[3,128,192]{2,1,0:T(8,128)(2,1)S(1)} %slice_select_fusion), channel_id=1, source_target_pairs={{0,16},{16,0},{1,17},{17,1},{2,18},{18,2},{3,19},{19,3},{4,20},{20... | collective-permute-start | bytes 442376 | tf_op jit(solution)/shard_map/ppermute | solution.py:18
  68.6 9.6 %copy-start.9 = (f32[36864]{0:T(1024)S(1)}, f32[36864]{0:T(1024)}, u32[]{:S(2)}) copy-start(f32[36864]{0:T(1024)} %reshape.294) | copy-start | bytes 442372
  68.6 9.6 %copy-start.29 = (f32[192]{0:T(256)S(1)}, f32[192]{0:T(256)}, u32[]{:S(2)}) copy-start(f32[192]{0:T(256)} %get-tuple-element.24) | copy-start | bytes 2308
  78.3 8.8 %collective-permute-start.6 = (f32[28096]{0:T(1024)S(1)}, f32[28096]{0:T(1024)S(1)}, u32[]{:S(2)}, u32[]{:S(2)}) collective-permute-start(f32[28096]{0:T(1024)S(1)} %slice.123), channel_id=1, source_target_pairs={{0,16},{16,0},{1,17},{17,1},{2,18},{18,2},{3,19},{19,3},{4,20},{20... | collective-permute-start | bytes 337160 | tf_op jit(solution)/shard_map/ppermute | solution.py:146
  81.6 22.6 %collective-permute-start.10 = (f32[28096]{0:T(1024)}, f32[28096]{0:T(1024)}, u32[]{:S(2)}, u32[]{:S(2)}) collective-permute-start(f32[28096]{0:T(1024)} %slice_add_fusion.3), channel_id=1, source_target_pairs={{0,4},{4,0},{8,12},{12,8},{1,5},{5,1},{9,13},{13,9},{2,6},{6,2},{1... | collective-permute-start | bytes 337160 | tf_op jit(solution)/shard_map/ppermute | solution.py:146
  81.7 8.6 %collective-permute-start.4 = (bf16[14,3,192]{2,1,0:T(4,128)(2,1)S(1)}, bf16[14,3,192]{2,1,0:T(4,128)(2,1)S(1)}, u32[]{:S(2)}, u32[]{:S(2)}) collective-permute-start(bf16[14,3,192]{2,1,0:T(4,128)(2,1)S(1)} %get-tuple-element.32), channel_id=1, source_target_pairs={{0,4},{4,8},{8,12},{1,5},{5,9},{9,13},{2,6},{6,10},{10,14},{3,7},{... | collective-permute-start | bytes 48392 | tf_op jit(solution)/shard_map/ppermute | solution.py:23
  85.6 5.8 %collective-permute-start.5 = (bf16[14,3,192]{2,1,0:T(4,128)(2,1)S(1)}, bf16[14,3,192]{2,1,0:T(4,128)(2,1)S(1)}, u32[]{:S(2)}, u32[]{:S(2)}) collective-permute-start(bf16[14,3,192]{2,1,0:T(4,128)(2,1)S(1)} %get-tuple-element.33), channel_id=1, source_target_pairs={{4,0},{8,4},{12,8},{5,1},{9,5},{13,9},{6,2},{10,6},{14,10},{7,3},{... | collective-permute-start | bytes 48392 | tf_op jit(solution)/shard_map/ppermute | solution.py:24
  87.7 18.0 %collective-permute-start.7 = (f32[28096]{0:T(1024)}, f32[28096]{0:T(1024)}, u32[]{:S(2)}, u32[]{:S(2)}) collective-permute-start(f32[28096]{0:T(1024)} %slice_add_fusion.4), channel_id=1, source_target_pairs={{0,8},{4,12},{8,0},{12,4},{1,9},{5,13},{9,1},{13,5},{2,10},{6,14},... | collective-permute-start | bytes 337160 | tf_op jit(solution)/shard_map/ppermute | solution.py:146
  103.4 4.9 %collective-permute-start.12 = (f32[28096]{0:T(1024)S(1)}, f32[28096]{0:T(1024)S(1)}, u32[]{:S(2)}, u32[]{:S(2)}) collective-permute-start(f32[28096]{0:T(1024)S(1)} %slice.130), channel_id=1, source_target_pairs={{0,4},{4,0},{8,12},{12,8},{1,5},{5,1},{9,13},{13,9},{2,6},{6,2},{1... | collective-permute-start | bytes 337160 | tf_op jit(solution)/shard_map/ppermute | solution.py:146
  105.1 8.0 %collective-permute-start.11 = (f32[28096]{0:T(1024)S(1)}, f32[28096]{0:T(1024)S(1)}, u32[]{:S(2)}, u32[]{:S(2)}) collective-permute-start(f32[28096]{0:T(1024)S(1)} %add.155), channel_id=1, source_target_pairs={{0,16},{16,0},{1,17},{17,1},{2,18},{18,2},{3,19},{19,3},{4,20},{20... | collective-permute-start | bytes 337160 | tf_op jit(solution)/shard_map/ppermute | solution.py:146
  106.7 5.7 %collective-permute-start.8 = (f32[28096]{0:T(1024)S(1)}, f32[28096]{0:T(1024)S(1)}, u32[]{:S(2)}, u32[]{:S(2)}) collective-permute-start(f32[28096]{0:T(1024)S(1)} %add.152), channel_id=1, source_target_pairs={{0,4},{4,0},{8,12},{12,8},{1,5},{5,1},{9,13},{13,9},{2,6},{6,2},{1... | collective-permute-start | bytes 337160 | tf_op jit(solution)/shard_map/ppermute | solution.py:146
  108.4 5.5 %collective-permute-start.13 = (f32[28096]{0:T(1024)S(1)}, f32[28096]{0:T(1024)S(1)}, u32[]{:S(2)}, u32[]{:S(2)}) collective-permute-start(f32[28096]{0:T(1024)S(1)} %slice_add_fusion.2), channel_id=1, source_target_pairs={{0,16},{16,0},{1,17},{17,1},{2,18},{18,2},{3,19},{19,3},{4,20},{20... | collective-permute-start | bytes 337160 | tf_op jit(solution)/shard_map/ppermute | solution.py:146
  113.8 6.9 %collective-permute-start.14 = (f32[28096]{0:T(1024)S(1)}, f32[28096]{0:T(1024)S(1)}, u32[]{:S(2)}, u32[]{:S(2)}) collective-permute-start(f32[28096]{0:T(1024)S(1)} %add.158), channel_id=1, source_target_pairs={{0,8},{4,12},{8,0},{12,4},{1,9},{5,13},{9,1},{13,5},{2,10},{6,14},... | collective-permute-start | bytes 337160 | tf_op jit(solution)/shard_map/ppermute | solution.py:146
  (24 other events, 77.8 us)

commit v10 on v8

--- a/solution.py
+++ b/solution.py
@@ -264,6 +264,9 @@
     grad_conv_bias = jnp.sum(convolved_gradient, axis=0)
     d_t = convolved_gradient.reshape(tile_rows, tile_cols, channel_count)
     grad_kernel = kernel_grad_minor(d_t, padded_t)
+    d_rows = extended(d_t.astype(jnp.bfloat16), (("row", 0),), 3)
+    grad_kernel, d_rows = lax.optimization_barrier((grad_kernel, d_rows))
+    d_padded = extended(d_rows, (("col", 1),), 3).astype(jnp.float32)
     (
         grad_kernel,
         grad_conv_bias,
@@ -288,7 +291,6 @@
         ),
         ("row", "col"),
     )
-    d_padded = extended(d_t.astype(jnp.bfloat16), (("row", 0), ("col", 1)), 3).astype(jnp.float32)
     grad_feature_t = (
         cotangent_t.astype(jnp.float32) + depthwise_minor(d_padded, kernel[::-1, ::-1])
     ).astype(jnp.bfloat16)

time: 123 us -> 127 us (1.033)
  matrix products: 23.8 us -> 27.7 us
  waiting for transfers between devices: 26.2 us -> 23.7 us
  local copies, waits for them, and re-layouts: 18.4 us -> 20.3 us
    ppermute x2, waiting for transfers between devices: 4.15 us -> 0.01 us  [extended(): got = lax.ppermute(jnp.where(first, last, leading), axis, [(0, 1), (1, 0)])]
    dot_general x1, matrix products: 0.62 us -> 2.98 us  [shards(): lax.dot_general(hidden.reshape(pixel_count, blocks, share), w_out_all.res...]
    ppermute x6, waiting for transfers between devices: 18.8 us -> 20.6 us  [butterfly_step(): lax.ppermute(flat, axis, [(i, i ^ step) for i in range(devices)])]
    dot_general x4, matrix products: 9.34 us -> 10.8 us  [contract(): lax.dot_general(left, right, (((dim_left,), (dim_right,)), ((), ())), pre...]
    unnamed x48 -> x62, local copies, waits for them, and re-layouts: 4.74 us -> 5.89 us
  transfers between devices with their start and end apart: 12 -> 12, of which waited for: 7 -> 6; matrix products, arithmetic and copies ran while one was open for 22% -> 26% of each run, Pallas kernels for 7% -> 6%
where the time goes in v10:
time: 127 us; the launch traced here: 126 us
  matrix products  27.7 us (22%)
  waiting for transfers between devices  23.7 us (19%)
  local copies, waits for them, and re-layouts  20.3 us (16%)
  starting transfers between devices  19.6 us (15%)
  other arithmetic  17 us (13%)
  blocking collectives  8.6 us (7%)
  Pallas kernels  7.9 us (6%)
    ppermute x6, waiting for transfers between devices, butterfly_step(): lax.ppermute(flat, axis, [(i, i ^ step) for i in range(devices)])  20.6 us
    conv_general_dilated x2, matrix products, depthwise_minor(): lax.conv_general_dilated(padded_t[None], kernel[:, :, None, :], (1, 1), '...  12.5 us
    dot_general x4, matrix products, contract(): lax.dot_general(left, right, (((dim_left,), (dim_right,)), ((), ())), pre...  10.8 us
    all_gather x1, blocking collectives, gathered_weights(): full = lax.all_gather(packed, 'chan', axis=0, tiled=True)  8.6 us
    pallas_call x1, Pallas kernels, kernel_grad_minor(): pl.pallas_call(kernel_grad_body, out_shape=jax.ShapeDtypeStruct((side * s...  7.9 us
    ppermute x2, starting transfers between devices, extended(): before = lax.ppermute(last, axis, up)  7.11 us
    ppermute x6, starting transfers between devices, butterfly_step(): lax.ppermute(flat, axis, [(i, i ^ step) for i in range(devices)])  6.06 us
    unnamed x62, local copies, waits for them, and re-layouts  5.89 us
  transfers between devices with their start and end apart: 12, of which 6 were waited for; matrix products, arithmetic and copies ran while one was open for 26% of the time, Pallas kernels for 6%

profile of v10, /device:TPU:0, one launch (start us, length us, event | category | flops | bytes accessed | tf_op | source)
XLA Modules:
  0.0 126.0 jit_solution(18123352862009419760)
XLA Ops:
  1.9 3.0 %collective-permute-start = (bf16[192,3,128]{0,2,1:T(8,128)(2,1)S(1)}, bf16[192,3,128]{0,2,1:T(8,128)(2,1)S(1)}, u32[]{:S(2)}, u32[]{:S(2)}) collective-permute-start(bf16[192,3,128]{0,2,1:T(8,128)(2,1)S(1)} %slice_select_fusion.1), channel_id=1, source_target_pairs={{0,16},{16,0},{1,17},{17,1},{2,18},{18,2},{3,19},{19,3},{4,20},{20... | collective-permute-start | bytes 442376 | tf_op jit(solution)/shard_map/ppermute | solution.py:18
  8.1 8.6 %all_gather.3 = bf16[768,387]{1,0:T(8,128)(2,1)S(1)} all-gather(bf16[192,387]{1,0:T(8,128)(2,1)S(1)} %concatenate.27), channel_id=1, replica_groups=mesh['row'=2,'col'=4,'chan'=4] {'chan'}, dimensions={0}, use_global_device_ids=true | all-gather | bytes 743040 | tf_op jit(solution)/shard_map/all_gather | solution.py:170
  17.8 3.5 %collective-permute-start.1 = (bf16[192,14,3]{0,2,1:T(4,128)(2,1)S(1)}, bf16[192,14,3]{0,2,1:T(4,128)(2,1)S(1)}, u32[]{:S(2)}, u32[]{:S(2)}) collective-permute-start(bf16[192,14,3]{0,2,1:T(4,128)(2,1)S(1)} %get-tuple-element.38), channel_id=1, source_target_pairs={{0,4},{4,8},{8,12},{1,5},{5,9},{9,13},{2,6},{6,10},{10,14},{3,7},{... | collective-permute-start | bytes 48392 | tf_op jit(solution)/shard_map/ppermute | solution.py:23
  23.9 3.1 %collective-permute-done.2 = bf16[192,14,3]{0,2,1:T(4,128)(2,1)S(1)} collective-permute-done((bf16[192,14,3]{0,2,1:T(4,128)(2,1)S(1)}, bf16[192,14,3]{0,2,1:T(4,128)(2,1)S(1)}, u32[]{:S(2)}, u32[]{:S(2)}) %collective-permute-start.2) | collective-permute-done | bytes 16160 | tf_op jit(solution)/shard_map/ppermute | solution.py:24
  27.0 1.6 %bitcast_convert_fusion = (f32[14,134,192]{2,1,0:T(8,128)}, bf16[1,14,134,192]{3,2,1,0:T(8,128)(2,1)S(1)}) fusion(bf16[192,14,3]{0,2,1:T(4,128)(2,1)S(1)} %collective-permute-done.2, bf16[192,3,128]{0,2,1:T(8,128)(2,1)S(1)} %get-tuple-element.47, bf16[192,8,128]{0,2,1:T(8,128)(2,1)S(1)} %copy.84, bf16[192,3,128]{0,2,1:T(8,128)(2,1)S(1)} %get-tuple-element.46, ...), kind=kLoop, calls=%fused_computation.32 | loop fusion | flops 3962112 | bytes 2881536 | tf_op jit(solution)/shard_map/convert_element_type | solution.py:211
  28.6 8.4 %fusion.6 = f32[1,8,128,192]{3,0,2,1:T(1,128)S(1)} fusion(bf16[1,14,134,192]{3,2,1,0:T(8,128)(2,1)S(1)} %get-tuple-element.35, f32[7,7,1,192]{3,1,0,2:T(8,128)S(1)} %bitcast.132), kind=kOutput, calls=%fused_computation.13 | convolution fusion | flops 115605504 | bytes 1544448 | tf_op jit(solution)/shard_map/conv_general_dilated | solution.py:180
  37.7 1.9 %copy.89 = f32[1,8,128,192]{2,1,3,0:T(8,128)} copy(f32[1,8,128,192]{3,0,2,1:T(1,128)S(1)} %fusion.6) | data formatting | bytes 1572864 | tf_op jit(solution)/shard_map/conv_general_dilated | solution.py:180
  40.0 3.4 %multiply_convert_fusion = (bf16[1024,768]{0,1:T(8,128)(2,1)}, f32[1024,768]{0,1:T(8,128)S(1)}) fusion(f32[768]{0:T(1024)S(1)} %fusion.35, f32[24,8,8,128]{3,2,1,0:T(8,128)} %bitcast.127, f32[192]{0:T(256)S(1)} %copy-done.25, f32[192]{0:T(256)S(1)} %copy-done.19, f32[1024]{0:T(1024)S(1)} %get-tuple-element.57, f32[1024]{0:T(1024)S(1)} %get-tuple-element.58, ...), kind=kOutput, calls=%fused_computation.9 | convolution fusion | flops 307888128 | bytes 5913600 | tf_op jit(solution)/shard_map/dot_general | solution.py:53
  43.3 3.3 %fusion.63 = (bf16[1024,768]{0,1:T(8,128)(2,1)S(1)}, f32[1024,768]{0,1:T(8,128)}) fusion(f32[1024,768]{0,1:T(8,128)S(1)} %get-tuple-element.66, f32[768]{0:T(1024)S(1)} %fusion.35, f32[24,8,8,128]{3,2,1,0:T(8,128)S(1)} %convert.4, f32[192]{0:T(256)S(1)} %copy-done.22, bf16[768,387]{1,0:T(8,128)(2,1)S(1)} %all_gather.3), kind=kOutput, calls=%fused_computation.114 | convolution fusion | flops 311033856 | bytes 9049088 | tf_op jit(solution)/shard_map/dot_general | solution.py:53
  49.5 2.1 %fusion.38 = f32[192,192]{1,0:T(8,128)} fusion(bf16[1024,768]{0,1:T(8,128)(2,1)} %copy-done.26, s32[]{:T(128)S(6)} %select_n.45, f32[24,8,8,128]{3,2,1,0:T(8,128)S(1)} %bitcast.128, f32[192]{0:T(256)S(1)} %copy-done.25, f32[192]{0:T(256)S(1)} %copy-done.19, f32[1024]{0:T(1024)S(1)} %get-tuple-element.57, f32[1024]{0:T(1024)S(1)} %get-tuple-element.58, ...), kind=kOutput, calls=%fused_computation.67 | convolution fusion | flops 76677120 | bytes 1337604 | tf_op jit(solution)/shard_map/dot_general | solution.py:53
  55.5 7.9 %shard_map.194 = f32[49,8,192]{2,1,0:T(8,128)} custom-call(f32[8,128,192]{2,1,0:T(8,128)} %get-tuple-element.33.d_ref, f32[14,134,192]{2,1,0:T(8,128)} %get-tuple-element.34.p_ref), custom_call_target="tpu_custom_call" | custom-call | tf_op jit(solution)/shard_map/pallas_call | solution.py:107
  65.1 2.1 %fusion.36 = f32[192,192]{1,0:T(8,128)} fusion(bf16[1024,768]{0,1:T(8,128)(2,1)} %get-tuple-element.65, s32[]{:T(128)S(6)} %select_n.45, f32[24,8,8,128]{3,2,1,0:T(8,128)S(1)} %copy-done.2, f32[192]{0:T(256)S(1)} %copy-done.23), kind=kOutput, calls=%fused_computation.65 | convolution fusion | flops 75890688 | bytes 1327876 | tf_op jit(solution)/shard_map/dot_general | solution.py:53
  67.2 3.0 %convert_reduce_fusion.2 = f32[1024,192]{0,1:T(8,128)} fusion(bf16[4,192,192]{2,1,0:T(8,128)(2,1)S(1)} %bitcast.126, bf16[1024,4,192]{0,2,1:T(8,128)(2,1)} %bitcast.124), kind=kOutput, calls=%fused_computation.8 | convolution fusion | flops 304152576 | bytes 2654208 | tf_op jit(solution)/shard_map/dot_general | solution.py:224
  70.5 3.6 %collective-permute-start.4 = (bf16[14,3,192]{2,1,0:T(4,128)(2,1)S(1)}, bf16[14,3,192]{2,1,0:T(4,128)(2,1)S(1)}, u32[]{:S(2)}, u32[]{:S(2)}) collective-permute-start(bf16[14,3,192]{2,1,0:T(4,128)(2,1)S(1)} %get-tuple-element.36), channel_id=1, source_target_pairs={{0,4},{4,8},{8,12},{1,5},{5,9},{9,13},{2,6},{6,10},{10,14},{3,7},{... | collective-permute-start | bytes 48392 | tf_op jit(solution)/shard_map/ppermute | solution.py:23
  74.1 1.6 %collective-permute-start.5 = (bf16[14,3,192]{2,1,0:T(4,128)(2,1)S(1)}, bf16[14,3,192]{2,1,0:T(4,128)(2,1)S(1)}, u32[]{:S(2)}, u32[]{:S(2)}) collective-permute-start(bf16[14,3,192]{2,1,0:T(4,128)(2,1)S(1)} %get-tuple-element.37), channel_id=1, source_target_pairs={{4,0},{8,4},{12,8},{5,1},{9,5},{13,9},{6,2},{10,6},{14,10},{7,3},{... | collective-permute-start | bytes 48392 | tf_op jit(solution)/shard_map/ppermute | solution.py:24
  78.5 1.8 %dynamic-slice_reduce_fusion = f32[192]{0:T(256)} fusion(f32[1024,768]{0,1:T(8,128)} %get-tuple-element.64, s32[]{:T(128)S(6)} %select_n.45), kind=kLoop, calls=%fused_computation.51 | loop fusion | flops 196416 | bytes 787204 | tf_op jit(solution)/shard_map/reduce_sum | solution.py:247
  84.2 4.1 %fusion.15 = f32[8,8,17,192]{3,1,2,0:T(8,128)S(1)} fusion(bf16[14,1,7,6,192]{4,2,3,0,1:T(8,128)(2,1)S(1)} %slice.122, bf16[14,1,8,17,192]{4,2,3,0,1:T(8,128)(2,1)S(1)} %copy.105, pred[8,17]{0,1:T(8,128)(4,1)S(1)} %copy-done.27, f32[7,7,1,192]{3,1,0,2:T(8,128)S(1)} %bitcast.133), kind=kOutput, calls=%fused_computation.23 | convolution fusion | flops 126007296 | bytes 1830280 | tf_op jit(solution)/shard_map/conv_general_dilated | solution.py:180
  89.8 4.6 %fusion.31 = (f32[192]{0:T(256)S(1)}, f32[192]{0:T(256)S(1)}, bf16[8,128,192]{1,0,2:T(8,128)(2,1)}, bf16[192,8,128]{2,1,0:T(8,128)(2,1)}) fusion(f32[24,8,8,128]{3,2,1,0:T(8,128)S(1)} %copy.120, bf16[192,8,128]{2,1,0:T(8,128)(2,1)S(1)} %copy-done.5, f32[192]{0:T(256)} %param.19, f32[192]{0:T(256)} %param.20, bf16[192,8,128]{2,1,0:T(8,128)(2,1)S(1)} %copy-done.3, ...), kind=kLoop, calls=%fused_computation.48 | loop fusion | flops 2358912 | bytes 3148800 | tf_op jit(solution)/shard_map/reduce_sum | solution.py:238
  96.1 3.7 %collective-permute-start.9 = (f32[42144]{0:T(1024)S(1)}, f32[42144]{0:T(1024)S(1)}, u32[]{:S(2)}, u32[]{:S(2)}) collective-permute-start(f32[42144]{0:T(1024)S(1)} %slice.129), channel_id=1, source_target_pairs={{0,8},{4,12},{8,0},{12,4},{1,9},{5,13},{9,1},{13,5},{2,10},{6,14},... | collective-permute-start | bytes 505736 | tf_op jit(solution)/shard_map/ppermute | solution.py:146
  100.8 9.9 %collective-permute-done.9 = f32[42144]{0:T(1024)S(1)} collective-permute-done((f32[42144]{0:T(1024)S(1)}, f32[42144]{0:T(1024)S(1)}, u32[]{:S(2)}, u32[]{:S(2)}) %collective-permute-start.9) | collective-permute-done | bytes 168608 | tf_op jit(solution)/shard_map/ppermute | solution.py:146
  110.9 2.4 %collective-permute-done.7 = f32[42144]{0:T(1024)S(1)} collective-permute-done((f32[42144]{0:T(1024)S(1)}, f32[42144]{0:T(1024)S(1)}, u32[]{:S(2)}, u32[]{:S(2)}) %collective-permute-start.7) | collective-permute-done | bytes 168608 | tf_op jit(solution)/shard_map/ppermute | solution.py:146
  113.4 4.8 %collective-permute-done.10 = f32[42144]{0:T(1024)S(1)} collective-permute-done((f32[42144]{0:T(1024)S(1)}, f32[42144]{0:T(1024)S(1)}, u32[]{:S(2)}, u32[]{:S(2)}) %collective-permute-start.10) | collective-permute-done | bytes 168608 | tf_op jit(solution)/shard_map/ppermute | solution.py:146
  118.8 1.7 %collective-permute-done.8 = f32[42144]{0:T(1024)S(1)} collective-permute-done((f32[42144]{0:T(1024)S(1)}, f32[42144]{0:T(1024)S(1)}, u32[]{:S(2)}, u32[]{:S(2)}) %collective-permute-start.8) | collective-permute-done | bytes 168608 | tf_op jit(solution)/shard_map/ppermute | solution.py:146
  121.9 1.8 %collective-permute-done.11 = f32[42144]{0:T(1024)S(1)} collective-permute-done((f32[42144]{0:T(1024)S(1)}, f32[42144]{0:T(1024)S(1)}, u32[]{:S(2)}, u32[]{:S(2)}) %collective-permute-start.11) | collective-permute-done | bytes 168608 | tf_op jit(solution)/shard_map/ppermute | solution.py:146
  (133 shorter events, 32.9 us)
Async XLA Ops:
  1.9 15.8 %collective-permute-start = (bf16[192,3,128]{0,2,1:T(8,128)(2,1)S(1)}, bf16[192,3,128]{0,2,1:T(8,128)(2,1)S(1)}, u32[]{:S(2)}, u32[]{:S(2)}) collective-permute-start(bf16[192,3,128]{0,2,1:T(8,128)(2,1)S(1)} %slice_select_fusion.1), channel_id=1, source_target_pairs={{0,16},{16,0},{1,17},{17,1},{2,18},{18,2},{3,19},{19,3},{4,20},{20... | collective-permute-start | bytes 442376 | tf_op jit(solution)/shard_map/ppermute | solution.py:18
  17.7 5.3 %copy-start.4 = (bf16[192,8,128]{2,1,0:T(8,128)(2,1)S(1)}, bf16[192,8,128]{2,1,0:T(8,128)(2,1)}, u32[]{:S(2)}) copy-start(bf16[192,8,128]{2,1,0:T(8,128)(2,1)} %param.21) | copy-start | bytes 1179652
  17.7 5.4 %copy-start.15 = (f32[7,7,192]{2,1,0:T(8,128)S(1)}, f32[7,7,192]{2,1,0:T(8,128)}, u32[]{:S(2)}) copy-start(f32[7,7,192]{2,1,0:T(8,128)} %param.12) | copy-start | bytes 112900
  17.8 6.1 %collective-permute-start.1 = (bf16[192,14,3]{0,2,1:T(4,128)(2,1)S(1)}, bf16[192,14,3]{0,2,1:T(4,128)(2,1)S(1)}, u32[]{:S(2)}, u32[]{:S(2)}) collective-permute-start(bf16[192,14,3]{0,2,1:T(4,128)(2,1)S(1)} %get-tuple-element.38), channel_id=1, source_target_pairs={{0,4},{4,8},{8,12},{1,5},{5,9},{9,13},{2,6},{6,10},{10,14},{3,7},{... | collective-permute-start | bytes 48392 | tf_op jit(solution)/shard_map/ppermute | solution.py:23
  21.3 5.8 %collective-permute-start.2 = (bf16[192,14,3]{0,2,1:T(4,128)(2,1)S(1)}, bf16[192,14,3]{0,2,1:T(4,128)(2,1)S(1)}, u32[]{:S(2)}, u32[]{:S(2)}) collective-permute-start(bf16[192,14,3]{0,2,1:T(4,128)(2,1)S(1)} %get-tuple-element.39), channel_id=1, source_target_pairs={{4,0},{8,4},{12,8},{5,1},{9,5},{13,9},{6,2},{10,6},{14,10},{7,3},{... | collective-permute-start | bytes 48392 | tf_op jit(solution)/shard_map/ppermute | solution.py:24
  23.1 20.3 %copy-start.1 = (f32[24,8,8,128]{3,2,1,0:T(8,128)}, f32[24,8,8,128]{3,2,1,0:T(8,128)S(1)}, u32[]{:S(2)}) copy-start(f32[24,8,8,128]{3,2,1,0:T(8,128)S(1)} %convert.4) | copy-start | bytes 2359300
  55.0 15.2 %collective-permute-start.3 = (bf16[3,128,192]{2,1,0:T(8,128)(2,1)}, bf16[3,128,192]{2,1,0:T(8,128)(2,1)S(1)}, u32[]{:S(2)}, u32[]{:S(2)}) collective-permute-start(bf16[3,128,192]{2,1,0:T(8,128)(2,1)} %slice_select_fusion), channel_id=1, source_target_pairs={{0,16},{16,0},{1,17},{17,1},{2,18},{18,2},{3,19},{19,3},{4,20},{20... | collective-permute-start | bytes 442376 | tf_op jit(solution)/shard_map/ppermute | solution.py:18
  55.5 9.7 %copy-start.2 = (f32[24,8,8,128]{3,2,1,0:T(8,128)S(1)}, f32[24,8,8,128]{3,2,1,0:T(8,128)}, u32[]{:S(2)}) copy-start(f32[24,8,8,128]{3,2,1,0:T(8,128)} %copy-done.1) | copy-start | bytes 2359300
  55.5 9.7 %copy-start.23 = (f32[192]{0:T(256)S(1)}, f32[192]{0:T(256)}, u32[]{:S(2)}) copy-start(f32[192]{0:T(256)} %param.20) | copy-start | bytes 2308
  55.5 11.8 %copy-start.6 = (bf16[768,192]{1,0:T(8,128)(2,1)S(1)}, bf16[768,192]{1,0:T(8,128)(2,1)}, u32[]{:S(2)}) copy-start(bf16[768,192]{1,0:T(8,128)(2,1)} %get-tuple-element.42) | copy-start | bytes 884740
  70.2 5.5 %copy-start.18 = (f32[192]{0:T(256)S(1)}, f32[192]{0:T(256)}, u32[]{:S(2)}) copy-start(f32[192]{0:T(256)} %param.13) | copy-start | bytes 2308
  70.2 5.6 %copy-start.20 = (f32[192]{0:T(256)S(1)}, f32[192]{0:T(256)}, u32[]{:S(2)}) copy-start(f32[192]{0:T(256)} %param.14) | copy-start | bytes 2308
  70.2 6.1 %copy-start.14 = (f32[192,192]{1,0:T(8,128)S(1)}, f32[192,192]{1,0:T(8,128)}, u32[]{:S(2)}) copy-start(f32[192,192]{1,0:T(8,128)} %fusion.38) | copy-start | bytes 442372
  70.5 7.3 %copy-start.10 = (f32[192,192]{1,0:T(8,128)S(1)}, f32[192,192]{1,0:T(8,128)}, u32[]{:S(2)}) copy-start(f32[192,192]{1,0:T(8,128)} %fusion.36) | copy-start | bytes 442372
  70.5 12.3 %collective-permute-start.4 = (bf16[14,3,192]{2,1,0:T(4,128)(2,1)S(1)}, bf16[14,3,192]{2,1,0:T(4,128)(2,1)S(1)}, u32[]{:S(2)}, u32[]{:S(2)}) collective-permute-start(bf16[14,3,192]{2,1,0:T(4,128)(2,1)S(1)} %get-tuple-element.36), channel_id=1, source_target_pairs={{0,4},{4,8},{8,12},{1,5},{5,9},{9,13},{2,6},{6,10},{10,14},{3,7},{... | collective-permute-start | bytes 48392 | tf_op jit(solution)/shard_map/ppermute | solution.py:23
  74.1 6.2 %copy-start.13 = (f32[7,7,192]{2,1,0:T(8,128)S(1)}, f32[7,7,192]{2,1,0:T(8,128)}, u32[]{:S(2)}) copy-start(f32[7,7,192]{2,1,0:T(8,128)} %reshape.308) | copy-start | bytes 112900
  74.1 8.6 %collective-permute-start.5 = (bf16[14,3,192]{2,1,0:T(4,128)(2,1)S(1)}, bf16[14,3,192]{2,1,0:T(4,128)(2,1)S(1)}, u32[]{:S(2)}, u32[]{:S(2)}) collective-permute-start(bf16[14,3,192]{2,1,0:T(4,128)(2,1)S(1)} %get-tuple-element.37), channel_id=1, source_target_pairs={{4,0},{8,4},{12,8},{5,1},{9,5},{13,9},{6,2},{10,6},{14,10},{7,3},{... | collective-permute-start | bytes 48392 | tf_op jit(solution)/shard_map/ppermute | solution.py:24
  81.2 18.6 %collective-permute-start.6 = (f32[42144]{0:T(1024)}, f32[42144]{0:T(1024)}, u32[]{:S(2)}, u32[]{:S(2)}) collective-permute-start(f32[42144]{0:T(1024)} %slice.124), channel_id=1, source_target_pairs={{0,16},{16,0},{1,17},{17,1},{2,18},{18,2},{3,19},{19,3},{4,20},{20... | collective-permute-start | bytes 505736 | tf_op jit(solution)/shard_map/ppermute | solution.py:146
  89.8 10.0 %copy-start.8 = (f32[46848]{0:T(1024)S(1)}, f32[46848]{0:T(1024)}, u32[]{:S(2)}) copy-start(f32[46848]{0:T(1024)} %copy-done.7) | copy-start | bytes 562180
  96.1 14.6 %collective-permute-start.9 = (f32[42144]{0:T(1024)S(1)}, f32[42144]{0:T(1024)S(1)}, u32[]{:S(2)}, u32[]{:S(2)}) collective-permute-start(f32[42144]{0:T(1024)S(1)} %slice.129), channel_id=1, source_target_pairs={{0,8},{4,12},{8,0},{12,4},{1,9},{5,13},{9,1},{13,5},{2,10},{6,14},... | collective-permute-start | bytes 505736 | tf_op jit(solution)/shard_map/ppermute | solution.py:146
  100.7 12.6 %collective-permute-start.7 = (f32[42144]{0:T(1024)S(1)}, f32[42144]{0:T(1024)S(1)}, u32[]{:S(2)}, u32[]{:S(2)}) collective-permute-start(f32[42144]{0:T(1024)S(1)} %slice_add_fusion.3), channel_id=1, source_target_pairs={{0,8},{4,12},{8,0},{12,4},{1,9},{5,13},{9,1},{13,5},{2,10},{6,14},... | collective-permute-start | bytes 505736 | tf_op jit(solution)/shard_map/ppermute | solution.py:146
  110.8 7.4 %collective-permute-start.10 = (f32[42144]{0:T(1024)S(1)}, f32[42144]{0:T(1024)S(1)}, u32[]{:S(2)}, u32[]{:S(2)}) collective-permute-start(f32[42144]{0:T(1024)S(1)} %slice_add_fusion.2), channel_id=1, source_target_pairs={{0,4},{4,0},{8,12},{12,8},{1,5},{5,1},{9,13},{13,9},{2,6},{6,2},{1... | collective-permute-start | bytes 505736 | tf_op jit(solution)/shard_map/ppermute | solution.py:146
  113.3 7.2 %collective-permute-start.8 = (f32[42144]{0:T(1024)S(1)}, f32[42144]{0:T(1024)S(1)}, u32[]{:S(2)}, u32[]{:S(2)}) collective-permute-start(f32[42144]{0:T(1024)S(1)} %add.143), channel_id=1, source_target_pairs={{0,4},{4,0},{8,12},{12,8},{1,5},{5,1},{9,13},{13,9},{2,6},{6,2},{1... | collective-permute-start | bytes 505736 | tf_op jit(solution)/shard_map/ppermute | solution.py:146
  118.2 5.5 %collective-permute-start.11 = (f32[42144]{0:T(1024)S(1)}, f32[42144]{0:T(1024)S(1)}, u32[]{:S(2)}, u32[]{:S(2)}) collective-permute-start(f32[42144]{0:T(1024)S(1)} %add.146), channel_id=1, source_target_pairs={{0,16},{16,0},{1,17},{17,1},{2,18},{18,2},{3,19},{19,3},{4,20},{20... | collective-permute-start | bytes 505736 | tf_op jit(solution)/shard_map/ppermute | solution.py:146
  (16 other events, 37.6 us)

commit v11 on v8

--- a/solution.py
+++ b/solution.py
@@ -238,6 +238,7 @@
     grad_layer_scale = jnp.sum(grad_out * branch, axis=0)
     grad_b_out = jnp.sum(g_branch, axis=0)
     g_out = g_branch.astype(jnp.bfloat16)
+    grad_layer_scale, grad_b_out, g_out = lax.optimization_barrier((grad_layer_scale, grad_b_out, g_out))
     d_pre = contract(g_out, w_out_all, 1, 1) * gelu_slope
     g_pre = d_pre.astype(jnp.bfloat16)
     hidden_own = lax.dynamic_slice_in_dim(hidden, own * share, share, axis=1)

time: 123 us -> 112 us (0.911)
  waiting for transfers between devices: 26.2 us -> 16.7 us
  starting transfers between devices: 19.6 us -> 21.3 us
  local copies, waits for them, and re-layouts: 18.4 us -> 16.8 us
    ppermute x6, waiting for transfers between devices: 18.8 us -> 8.82 us  [butterfly_step(): lax.ppermute(flat, axis, [(i, i ^ step) for i in range(devices)])]
    ppermute x6, starting transfers between devices: 6.41 us -> 8 us  [butterfly_step(): lax.ppermute(flat, axis, [(i, i ^ step) for i in range(devices)])]
    unnamed x48 -> x36, local copies, waits for them, and re-layouts: 4.74 us -> 5.12 us
  transfers between devices with their start and end apart: 12 -> 12, of which waited for: 7 -> 5; matrix products, arithmetic and copies ran while one was open for 22% -> 17% of each run, Pallas kernels for 7% -> 7%
where the time goes in v11:
time: 112 us; the launch traced here: 111 us
  matrix products  22.9 us (20%)
  starting transfers between devices  21.3 us (19%)
  local copies, waits for them, and re-layouts  16.8 us (15%)
  waiting for transfers between devices  16.7 us (15%)
  other arithmetic  15.6 us (14%)
  blocking collectives  8.6 us (8%)
  Pallas kernels  7.81 us (7%)
  between operations  1.19 us (1%)
    conv_general_dilated x2, matrix products, depthwise_minor(): lax.conv_general_dilated(padded_t[None], kernel[:, :, None, :], (1, 1), '...  12.6 us
    dot_general x4, matrix products, contract(): lax.dot_general(left, right, (((dim_left,), (dim_right,)), ((), ())), pre...  9.01 us
    ppermute x6, waiting for transfers between devices, butterfly_step(): lax.ppermute(flat, axis, [(i, i ^ step) for i in range(devices)])  8.82 us
    all_gather x1, blocking collectives, gathered_weights(): full = lax.all_gather(packed, 'chan', axis=0, tiled=True)  8.6 us
    ppermute x6, starting transfers between devices, butterfly_step(): lax.ppermute(flat, axis, [(i, i ^ step) for i in range(devices)])  8 us
    pallas_call x1, Pallas kernels, kernel_grad_minor(): pl.pallas_call(kernel_grad_body, out_shape=jax.ShapeDtypeStruct((side * s...  7.81 us
    ppermute x2, starting transfers between devices, extended(): before = lax.ppermute(last, axis, up)  6.94 us
    unnamed x36, local copies, waits for them, and re-layouts  5.12 us
  transfers between devices with their start and end apart: 12, of which 5 were waited for; matrix products, arithmetic and copies ran while one was open for 17% of the time, Pallas kernels for 7%

profile of v11, /device:TPU:0, one launch (start us, length us, event | category | flops | bytes accessed | tf_op | source)
XLA Modules:
  0.0 111.0 jit_solution(2005225093676618455)
XLA Ops:
  2.0 3.0 %collective-permute-start = (bf16[192,3,128]{0,2,1:T(8,128)(2,1)S(1)}, bf16[192,3,128]{0,2,1:T(8,128)(2,1)S(1)}, u32[]{:S(2)}, u32[]{:S(2)}) collective-permute-start(bf16[192,3,128]{0,2,1:T(8,128)(2,1)S(1)} %slice_select_fusion.1), channel_id=1, source_target_pairs={{0,16},{16,0},{1,17},{17,1},{2,18},{18,2},{3,19},{19,3},{4,20},{20... | collective-permute-start | bytes 442376 | tf_op jit(solution)/shard_map/ppermute | solution.py:18
  8.1 8.6 %all_gather.3 = bf16[768,387]{1,0:T(8,128)(2,1)S(1)} all-gather(bf16[192,387]{1,0:T(8,128)(2,1)S(1)} %concatenate.27), channel_id=1, replica_groups=mesh['row'=2,'col'=4,'chan'=4] {'chan'}, dimensions={0}, use_global_device_ids=true | all-gather | bytes 743040 | tf_op jit(solution)/shard_map/all_gather | solution.py:170
  18.2 3.5 %collective-permute-start.1 = (bf16[192,14,3]{0,2,1:T(4,128)(2,1)S(1)}, bf16[192,14,3]{0,2,1:T(4,128)(2,1)S(1)}, u32[]{:S(2)}, u32[]{:S(2)}) collective-permute-start(bf16[192,14,3]{0,2,1:T(4,128)(2,1)S(1)} %get-tuple-element.40), channel_id=1, source_target_pairs={{0,4},{4,8},{8,12},{1,5},{5,9},{9,13},{2,6},{6,10},{10,14},{3,7},{... | collective-permute-start | bytes 48392 | tf_op jit(solution)/shard_map/ppermute | solution.py:23
  23.5 3.9 %collective-permute-done.2 = bf16[192,14,3]{0,2,1:T(4,128)(2,1)S(1)} collective-permute-done((bf16[192,14,3]{0,2,1:T(4,128)(2,1)S(1)}, bf16[192,14,3]{0,2,1:T(4,128)(2,1)S(1)}, u32[]{:S(2)}, u32[]{:S(2)}) %collective-permute-start.2) | collective-permute-done | bytes 16160 | tf_op jit(solution)/shard_map/ppermute | solution.py:24
  27.4 1.6 %bitcast_convert_fusion = (f32[14,134,192]{2,1,0:T(8,128)}, bf16[1,14,134,192]{3,2,1,0:T(8,128)(2,1)S(1)}) fusion(bf16[192,14,3]{0,2,1:T(4,128)(2,1)S(1)} %collective-permute-done.2, bf16[192,3,128]{0,2,1:T(8,128)(2,1)S(1)} %get-tuple-element.48, bf16[192,8,128]{0,2,1:T(8,128)(2,1)S(1)} %copy.84, bf16[192,3,128]{0,2,1:T(8,128)(2,1)S(1)} %get-tuple-element.47, ...), kind=kLoop, calls=%fused_computation.32 | loop fusion | flops 3962112 | bytes 2881536 | tf_op jit(solution)/shard_map/convert_element_type | solution.py:211
  29.0 8.4 %fusion.6 = f32[1,8,128,192]{3,0,2,1:T(1,128)S(1)} fusion(bf16[1,14,134,192]{3,2,1,0:T(8,128)(2,1)S(1)} %get-tuple-element.37, f32[7,7,1,192]{3,1,0,2:T(8,128)S(1)} %bitcast.130), kind=kOutput, calls=%fused_computation.13 | convolution fusion | flops 115605504 | bytes 1544448 | tf_op jit(solution)/shard_map/conv_general_dilated | solution.py:180
  38.1 1.9 %copy.89 = f32[1,8,128,192]{2,1,3,0:T(8,128)} copy(f32[1,8,128,192]{3,0,2,1:T(1,128)S(1)} %fusion.6) | data formatting | bytes 1572864 | tf_op jit(solution)/shard_map/conv_general_dilated | solution.py:180
  40.4 2.2 %multiply_convert_fusion = (bf16[1024,768]{0,1:T(8,128)(2,1)S(1)}, f32[1024,768]{0,1:T(8,128)S(1)}) fusion(f32[768]{0:T(1024)S(1)} %fusion.35, f32[24,8,8,128]{3,2,1,0:T(8,128)} %bitcast.125, f32[192]{0:T(256)S(1)} %copy-done.12, f32[192]{0:T(256)S(1)} %copy-done.9, f32[1024]{0:T(1024)S(1)} %get-tuple-element.58, f32[1024]{0:T(1024)S(1)} %get-tuple-element.59, ...), kind=kOutput, calls=%fused_computation.9 | convolution fusion | flops 307888128 | bytes 5913600 | tf_op jit(solution)/shard_map/dot_general | solution.py:53
  43.9 3.8 %fusion.31 = (f32[192]{0:T(256)S(1)}, f32[192]{0:T(256)S(1)}, bf16[8,128,192]{1,0,2:T(8,128)(2,1)}) fusion(bf16[192,8,128]{2,1,0:T(8,128)(2,1)S(1)} %copy-done.1, f32[192]{0:T(256)S(1)} %copy-done.10, f32[192]{0:T(256)S(1)} %copy-done.11, f32[24,8,8,128]{3,2,1,0:T(8,128)S(1)} %copy.118, bf16[192,8,128]{2,1,0:T(8,128)(2,1)S(1)} %copy-done.3), kind=kLoop, calls=%fused_computation.47 | loop fusion | flops 1965696 | bytes 1969152 | tf_op jit(solution)/shard_map/reduce_sum | solution.py:239
  47.7 3.3 %fusion.60 = (bf16[1024,768]{0,1:T(8,128)(2,1)S(1)}, f32[1024,768]{0,1:T(8,128)}) fusion(f32[1024,768]{0,1:T(8,128)S(1)} %get-tuple-element.65, f32[768]{0:T(1024)S(1)} %fusion.35, bf16[1024,192]{0,1:T(8,128)(2,1)S(1)} %fusion.23, bf16[768,387]{1,0:T(8,128)(2,1)S(1)} %all_gather.3), kind=kOutput, calls=%fused_computation.115 | convolution fusion | flops 310640640 | bytes 8654848 | tf_op jit(solution)/shard_map/dot_general | solution.py:53
  52.2 1.4 %copy.99 = f32[1024,192]{1,0:T(8,128)} copy(f32[1024,192]{0,1:T(8,128)S(1)} %get-tuple-element.31) | data formatting | bytes 1572864 | tf_op jit(solution)/shard_map/reduce_sum | solution.py:256
  53.6 2.3 %fusion.38 = f32[192,192]{1,0:T(8,128)} fusion(bf16[1024,768]{0,1:T(8,128)(2,1)} %copy-done.13, s32[]{:T(128)S(6)} %select_n.45, f32[24,8,8,128]{3,2,1,0:T(8,128)} %bitcast.126, f32[192]{0:T(256)S(1)} %copy-done.12, f32[192]{0:T(256)S(1)} %copy-done.9, f32[1024]{0:T(1024)S(1)} %get-tuple-element.58, f32[1024]{0:T(1024)S(1)} %get-tuple-element.59, ...), kind=kOutput, calls=%fused_computation.66 | convolution fusion | flops 76677120 | bytes 1337604 | tf_op jit(solution)/shard_map/dot_general | solution.py:53
  57.1 1.5 %fusion.57 = (bf16[8,128,192]{2,1,0:T(8,128)(2,1)S(1)}, f32[8,128,192]{2,1,0:T(8,128)}) fusion(f32[8,128]{1,0:T(8,128)S(1)} %broadcast_multiply_fusion, f32[8,128]{1,0:T(8,128)S(1)} %get-tuple-element.60, f32[192]{0:T(256)S(1)} %copy-done.8, f32[1,8,128,192]{3,0,2,1:T(1,128)S(1)} %fusion.6, f32[8,128]{1,0:T(8,128)S(1)} %multiply_bitcast_fusion, ...), kind=kLoop, calls=%fused_computation.113 | loop fusion | flops 1769472 | bytes 2770432 | tf_op jit(solution)/shard_map/convert_element_type | solution.py:292
  60.5 3.9 %collective-permute-done.3 = bf16[3,128,192]{2,1,0:T(8,128)(2,1)S(1)} collective-permute-done((bf16[3,128,192]{2,1,0:T(8,128)(2,1)S(1)}, bf16[3,128,192]{2,1,0:T(8,128)(2,1)S(1)}, u32[]{:S(2)}, u32[]{:S(2)}) %collective-permute-start.3) | collective-permute-done | bytes 147488 | tf_op jit(solution)/shard_map/ppermute | solution.py:18
  65.1 3.5 %collective-permute-start.4 = (bf16[14,3,192]{2,1,0:T(4,128)(2,1)}, bf16[14,3,192]{2,1,0:T(4,128)(2,1)S(1)}, u32[]{:S(2)}, u32[]{:S(2)}) collective-permute-start(bf16[14,3,192]{2,1,0:T(4,128)(2,1)} %get-tuple-element.38), channel_id=1, source_target_pairs={{0,4},{4,8},{8,12},{1,5},{5,9},{9,13},{2,6},{6,10},{10,14},{3,7},{... | collective-permute-start | bytes 48392 | tf_op jit(solution)/shard_map/ppermute | solution.py:23
  68.6 1.5 %collective-permute-start.5 = (bf16[14,3,192]{2,1,0:T(4,128)(2,1)S(1)}, bf16[14,3,192]{2,1,0:T(4,128)(2,1)S(1)}, u32[]{:S(2)}, u32[]{:S(2)}) collective-permute-start(bf16[14,3,192]{2,1,0:T(4,128)(2,1)S(1)} %get-tuple-element.39), channel_id=1, source_target_pairs={{4,0},{8,4},{12,8},{5,1},{9,5},{13,9},{6,2},{10,6},{14,10},{7,3},{... | collective-permute-start | bytes 48392 | tf_op jit(solution)/shard_map/ppermute | solution.py:24
  72.1 1.6 %concatenate.31 = f32[74304]{0:T(1024)S(1)} concatenate(f32[36864]{0:T(1024)S(1)} %reshape.302, f32[192]{0:T(256)S(1)} %dynamic-slice_reduce_fusion, f32[36864]{0:T(1024)S(1)} %reshape.303, f32[192]{0:T(256)S(1)} %get-tuple-element.15, f32[192]{0:T(256)S(1)} %get-tuple-element.16), dimensions={0} | concatenate | bytes 594432 | tf_op jit(solution)/shard_map/concatenate | solution.py:116
  73.8 3.7 %collective-permute-start.9 = (f32[42144]{0:T(1024)S(1)}, f32[42144]{0:T(1024)S(1)}, u32[]{:S(2)}, u32[]{:S(2)}) collective-permute-start(f32[42144]{0:T(1024)S(1)} %slice.129), channel_id=1, source_target_pairs={{0,8},{4,12},{8,0},{12,4},{1,9},{5,13},{9,1},{13,5},{2,10},{6,14},... | collective-permute-start | bytes 505736 | tf_op jit(solution)/shard_map/ppermute | solution.py:146
  77.5 7.8 %shard_map.194 = f32[49,8,192]{2,1,0:T(8,128)} custom-call(f32[8,128,192]{2,1,0:T(8,128)} %get-tuple-element.35.d_ref, f32[14,134,192]{2,1,0:T(8,128)} %get-tuple-element.36.p_ref), custom_call_target="tpu_custom_call" | custom-call | tf_op jit(solution)/shard_map/pallas_call | solution.py:107
  88.5 4.2 %fusion.15 = f32[8,8,17,192]{3,1,2,0:T(8,128)S(1)} fusion(bf16[14,1,7,6,192]{4,2,3,0,1:T(8,128)(2,1)S(1)} %slice.122, bf16[14,1,8,17,192]{4,2,3,0,1:T(8,128)(2,1)S(1)} %copy.105, pred[8,17]{0,1:T(8,128)(4,1)S(1)} %copy-done.14, f32[7,7,1,192]{3,1,0,2:T(8,128)S(1)} %bitcast.131), kind=kOutput, calls=%fused_computation.23 | convolution fusion | flops 126007296 | bytes 1830280 | tf_op jit(solution)/shard_map/conv_general_dilated | solution.py:180
  93.9 2.0 %collective-permute-start.10 = (f32[42144]{0:T(1024)S(1)}, f32[42144]{0:T(1024)S(1)}, u32[]{:S(2)}, u32[]{:S(2)}) collective-permute-start(f32[42144]{0:T(1024)S(1)} %slice_add_fusion.2), channel_id=1, source_target_pairs={{0,4},{4,0},{8,12},{12,8},{1,5},{5,1},{9,13},{13,9},{2,6},{6,2},{1... | collective-permute-start | bytes 505736 | tf_op jit(solution)/shard_map/ppermute | solution.py:146
  95.9 5.6 %collective-permute-done.7 = f32[42144]{0:T(1024)S(1)} collective-permute-done((f32[42144]{0:T(1024)S(1)}, f32[42144]{0:T(1024)S(1)}, u32[]{:S(2)}, u32[]{:S(2)}) %collective-permute-start.7) | collective-permute-done | bytes 168608 | tf_op jit(solution)/shard_map/ppermute | solution.py:146
  102.5 1.6 %collective-permute-start.11 = (f32[42144]{0:T(1024)S(1)}, f32[42144]{0:T(1024)S(1)}, u32[]{:S(2)}, u32[]{:S(2)}) collective-permute-start(f32[42144]{0:T(1024)S(1)} %add.146), channel_id=1, source_target_pairs={{0,16},{16,0},{1,17},{17,1},{2,18},{18,2},{3,19},{19,3},{4,20},{20... | collective-permute-start | bytes 505736 | tf_op jit(solution)/shard_map/ppermute | solution.py:146
  104.1 2.9 %collective-permute-done.8 = f32[42144]{0:T(1024)S(1)} collective-permute-done((f32[42144]{0:T(1024)S(1)}, f32[42144]{0:T(1024)S(1)}, u32[]{:S(2)}, u32[]{:S(2)}) %collective-permute-start.8) | collective-permute-done | bytes 168608 | tf_op jit(solution)/shard_map/ppermute | solution.py:146
  (107 shorter events, 26.3 us)
Async XLA Ops:
  0.6 16.1 %copy-start.1 = (bf16[192,8,128]{2,1,0:T(8,128)(2,1)S(1)}, bf16[192,8,128]{2,1,0:T(8,128)(2,1)}, u32[]{:S(2)}) copy-start(bf16[192,8,128]{2,1,0:T(8,128)(2,1)} %param.21) | copy-start | bytes 1179652
  2.0 16.1 %collective-permute-start = (bf16[192,3,128]{0,2,1:T(8,128)(2,1)S(1)}, bf16[192,3,128]{0,2,1:T(8,128)(2,1)S(1)}, u32[]{:S(2)}, u32[]{:S(2)}) collective-permute-start(bf16[192,3,128]{0,2,1:T(8,128)(2,1)S(1)} %slice_select_fusion.1), channel_id=1, source_target_pairs={{0,16},{16,0},{1,17},{17,1},{2,18},{18,2},{3,19},{19,3},{4,20},{20... | collective-permute-start | bytes 442376 | tf_op jit(solution)/shard_map/ppermute | solution.py:18
  8.1 9.7 %copy-start.10 = (f32[192]{0:T(256)S(1)}, f32[192]{0:T(256)}, u32[]{:S(2)}) copy-start(f32[192]{0:T(256)} %param.20) | copy-start | bytes 2308
  18.0 5.4 %copy-start.7 = (f32[7,7,192]{2,1,0:T(8,128)S(1)}, f32[7,7,192]{2,1,0:T(8,128)}, u32[]{:S(2)}) copy-start(f32[7,7,192]{2,1,0:T(8,128)} %param.12) | copy-start | bytes 112900
  18.2 5.3 %collective-permute-start.1 = (bf16[192,14,3]{0,2,1:T(4,128)(2,1)S(1)}, bf16[192,14,3]{0,2,1:T(4,128)(2,1)S(1)}, u32[]{:S(2)}, u32[]{:S(2)}) collective-permute-start(bf16[192,14,3]{0,2,1:T(4,128)(2,1)S(1)} %get-tuple-element.40), channel_id=1, source_target_pairs={{0,4},{4,8},{8,12},{1,5},{5,9},{9,13},{2,6},{6,10},{10,14},{3,7},{... | collective-permute-start | bytes 48392 | tf_op jit(solution)/shard_map/ppermute | solution.py:23
  21.6 5.8 %collective-permute-start.2 = (bf16[192,14,3]{0,2,1:T(4,128)(2,1)S(1)}, bf16[192,14,3]{0,2,1:T(4,128)(2,1)S(1)}, u32[]{:S(2)}, u32[]{:S(2)}) collective-permute-start(bf16[192,14,3]{0,2,1:T(4,128)(2,1)S(1)} %get-tuple-element.41), channel_id=1, source_target_pairs={{4,0},{8,4},{12,8},{5,1},{9,5},{13,9},{6,2},{10,6},{14,10},{7,3},{... | collective-permute-start | bytes 48392 | tf_op jit(solution)/shard_map/ppermute | solution.py:24
  37.4 2.6 %copy-start.8 = (f32[192]{0:T(256)S(1)}, f32[192]{0:T(256)}, u32[]{:S(2)}) copy-start(f32[192]{0:T(256)} %param.13) | copy-start | bytes 2308
  38.1 2.2 %copy-start.9 = (f32[192]{0:T(256)S(1)}, f32[192]{0:T(256)}, u32[]{:S(2)}) copy-start(f32[192]{0:T(256)} %param.14) | copy-start | bytes 2308
  38.1 2.2 %copy-start.12 = (f32[192]{0:T(256)S(1)}, f32[192]{0:T(256)}, u32[]{:S(2)}) copy-start(f32[192]{0:T(256)} %param.15) | copy-start | bytes 2308
  40.4 2.2 %copy-start.4 = (bf16[768,192]{1,0:T(8,128)(2,1)S(1)}, bf16[768,192]{1,0:T(8,128)(2,1)}, u32[]{:S(2)}) copy-start(bf16[768,192]{1,0:T(8,128)(2,1)} %get-tuple-element.44) | copy-start | bytes 884740
  42.6 1.3 %copy-start.3 = (bf16[192,8,128]{2,1,0:T(8,128)(2,1)S(1)}, bf16[192,8,128]{2,1,0:T(8,128)(2,1)}, u32[]{:S(2)}) copy-start(bf16[192,8,128]{2,1,0:T(8,128)(2,1)} %param.11) | copy-start | bytes 1179652
  42.6 1.3 %copy-start.11 = (f32[192]{0:T(256)S(1)}, f32[192]{0:T(256)}, u32[]{:S(2)}) copy-start(f32[192]{0:T(256)} %param.19) | copy-start | bytes 2308
  47.7 3.3 %copy-start.5 = (bf16[768,192]{1,0:T(8,128)(2,1)S(1)}, bf16[768,192]{1,0:T(8,128)(2,1)}, u32[]{:S(2)}) copy-start(bf16[768,192]{1,0:T(8,128)(2,1)} %get-tuple-element.43) | copy-start | bytes 884740
  55.9 1.2 %copy-start = (f32[1024,192]{1,0:T(8,128)S(1)}, f32[1024,192]{1,0:T(8,128)}, u32[]{:S(2)}) copy-start(f32[1024,192]{1,0:T(8,128)} %copy.99) | copy-start | bytes 2359300
  58.6 5.8 %collective-permute-start.3 = (bf16[3,128,192]{2,1,0:T(8,128)(2,1)S(1)}, bf16[3,128,192]{2,1,0:T(8,128)(2,1)S(1)}, u32[]{:S(2)}, u32[]{:S(2)}) collective-permute-start(bf16[3,128,192]{2,1,0:T(8,128)(2,1)S(1)} %slice_select_fusion), channel_id=1, source_target_pairs={{0,16},{16,0},{1,17},{17,1},{2,18},{18,2},{3,19},{19,3},{4,20},{20... | collective-permute-start | bytes 442376 | tf_op jit(solution)/shard_map/ppermute | solution.py:18
  60.5 10.2 %copy-start.6 = (f32[192,192]{1,0:T(8,128)S(1)}, f32[192,192]{1,0:T(8,128)}, u32[]{:S(2)}) copy-start(f32[192,192]{1,0:T(8,128)} %fusion.38) | copy-start | bytes 442372
  65.1 22.1 %collective-permute-start.4 = (bf16[14,3,192]{2,1,0:T(4,128)(2,1)}, bf16[14,3,192]{2,1,0:T(4,128)(2,1)S(1)}, u32[]{:S(2)}, u32[]{:S(2)}) collective-permute-start(bf16[14,3,192]{2,1,0:T(4,128)(2,1)} %get-tuple-element.38), channel_id=1, source_target_pairs={{0,4},{4,8},{8,12},{1,5},{5,9},{9,13},{2,6},{6,10},{10,14},{3,7},{... | collective-permute-start | bytes 48392 | tf_op jit(solution)/shard_map/ppermute | solution.py:23
  68.6 18.7 %collective-permute-start.5 = (bf16[14,3,192]{2,1,0:T(4,128)(2,1)S(1)}, bf16[14,3,192]{2,1,0:T(4,128)(2,1)S(1)}, u32[]{:S(2)}, u32[]{:S(2)}) collective-permute-start(bf16[14,3,192]{2,1,0:T(4,128)(2,1)S(1)} %get-tuple-element.39), channel_id=1, source_target_pairs={{4,0},{8,4},{12,8},{5,1},{9,5},{13,9},{6,2},{10,6},{14,10},{7,3},{... | collective-permute-start | bytes 48392 | tf_op jit(solution)/shard_map/ppermute | solution.py:24
  73.8 20.0 %collective-permute-start.9 = (f32[42144]{0:T(1024)S(1)}, f32[42144]{0:T(1024)S(1)}, u32[]{:S(2)}, u32[]{:S(2)}) collective-permute-start(f32[42144]{0:T(1024)S(1)} %slice.129), channel_id=1, source_target_pairs={{0,8},{4,12},{8,0},{12,4},{1,9},{5,13},{9,1},{13,5},{2,10},{6,14},... | collective-permute-start | bytes 505736 | tf_op jit(solution)/shard_map/ppermute | solution.py:146
  86.6 7.1 %collective-permute-start.6 = (f32[42144]{0:T(1024)S(1)}, f32[42144]{0:T(1024)S(1)}, u32[]{:S(2)}, u32[]{:S(2)}) collective-permute-start(f32[42144]{0:T(1024)S(1)} %slice.124), channel_id=1, source_target_pairs={{0,16},{16,0},{1,17},{17,1},{2,18},{18,2},{3,19},{19,3},{4,20},{20... | collective-permute-start | bytes 505736 | tf_op jit(solution)/shard_map/ppermute | solution.py:146
  93.7 7.8 %collective-permute-start.7 = (f32[42144]{0:T(1024)S(1)}, f32[42144]{0:T(1024)S(1)}, u32[]{:S(2)}, u32[]{:S(2)}) collective-permute-start(f32[42144]{0:T(1024)S(1)} %slice_add_fusion.3), channel_id=1, source_target_pairs={{0,8},{4,12},{8,0},{12,4},{1,9},{5,13},{9,1},{13,5},{2,10},{6,14},... | collective-permute-start | bytes 505736 | tf_op jit(solution)/shard_map/ppermute | solution.py:146
  93.9 8.5 %collective-permute-start.10 = (f32[42144]{0:T(1024)S(1)}, f32[42144]{0:T(1024)S(1)}, u32[]{:S(2)}, u32[]{:S(2)}) collective-permute-start(f32[42144]{0:T(1024)S(1)} %slice_add_fusion.2), channel_id=1, source_target_pairs={{0,4},{4,0},{8,12},{12,8},{1,5},{5,1},{9,13},{13,9},{2,6},{6,2},{1... | collective-permute-start | bytes 505736 | tf_op jit(solution)/shard_map/ppermute | solution.py:146
  101.5 5.5 %collective-permute-start.8 = (f32[42144]{0:T(1024)S(1)}, f32[42144]{0:T(1024)S(1)}, u32[]{:S(2)}, u32[]{:S(2)}) collective-permute-start(f32[42144]{0:T(1024)S(1)} %add.143), channel_id=1, source_target_pairs={{0,4},{4,0},{8,12},{12,8},{1,5},{5,1},{9,13},{13,9},{2,6},{6,2},{1... | collective-permute-start | bytes 505736 | tf_op jit(solution)/shard_map/ppermute | solution.py:146
  102.5 5.5 %collective-permute-start.11 = (f32[42144]{0:T(1024)S(1)}, f32[42144]{0:T(1024)S(1)}, u32[]{:S(2)}, u32[]{:S(2)}) collective-permute-start(f32[42144]{0:T(1024)S(1)} %add.146), channel_id=1, source_target_pairs={{0,16},{16,0},{1,17},{17,1},{2,18},{18,2},{3,19},{19,3},{4,20},{20... | collective-permute-start | bytes 505736 | tf_op jit(solution)/shard_map/ppermute | solution.py:146
  (3 other events, 3.0 us)

commit v12 on v11

--- a/solution.py
+++ b/solution.py
@@ -266,26 +266,26 @@
     d_t = convolved_gradient.reshape(tile_rows, tile_cols, channel_count)
     grad_kernel = kernel_grad_minor(d_t, padded_t)
     (
+        grad_w_in,
+        grad_w_out,
+        grad_b_in,
+        grad_b_out,
+        grad_layer_scale,
         grad_kernel,
         grad_conv_bias,
         gain_portion,
         bias_portion,
-        grad_w_in,
-        grad_b_in,
-        grad_w_out,
-        grad_b_out,
-        grad_layer_scale,
     ) = butterfly_sum(
         (
+            grad_w_in,
+            grad_w_out,
+            grad_b_in,
+            grad_b_out,
+            grad_layer_scale,
             grad_kernel,
             grad_conv_bias,
             gain_portion,
             bias_portion,
-            grad_w_in,
-            grad_b_in,
-            grad_w_out,
-            grad_b_out,
-            grad_layer_scale,
         ),
         ("row", "col"),
     )

time: 112 us -> 114 us (1.018)
  waiting for transfers between devices: 16.7 us -> 20.3 us
  starting transfers between devices: 21.3 us -> 18.7 us
  other arithmetic: 15.6 us -> 18.1 us
  matrix products: 22.9 us -> 21.3 us
    ppermute x2, waiting for transfers between devices: 3.92 us -> 7.21 us  [extended(): after = lax.ppermute(leading, axis, down)]
    ppermute x6, waiting for transfers between devices: 8.82 us -> 11.3 us  [butterfly_step(): lax.ppermute(flat, axis, [(i, i ^ step) for i in range(devices)])]
    ppermute x6, starting transfers between devices: 8 us -> 5.59 us  [butterfly_step(): lax.ppermute(flat, axis, [(i, i ^ step) for i in range(devices)])]
    dot_general x4, matrix products: 9.01 us -> 6.78 us  [contract(): lax.dot_general(left, right, (((dim_left,), (dim_right,)), ((), ())), pre...]
    ppermute x2, waiting for transfers between devices: 3.94 us -> 1.78 us  [extended(): got = lax.ppermute(jnp.where(first, last, leading), axis, [(0, 1), (1, 0)])]
    concatenate x2 -> x1, local copies, waits for them, and re-layouts: 1.66 us -> 0.1 us  [flat_pack(): return jnp.concatenate([v.reshape(-1) for v in values])]
    reshape x2, local copies, waits for them, and re-layouts: 0.24 us -> 1.56 us  [flat_pack(): return jnp.concatenate([v.reshape(-1) for v in values])]
    unnamed x36 -> x60, local copies, waits for them, and re-layouts: 5.12 us -> 4.78 us
  transfers between devices with their start and end apart: 12 -> 12, of which waited for: 5 -> 5; matrix products, arithmetic and copies ran while one was open for 17% -> 14% of each run, Pallas kernels for 7% -> 0%
where the time goes in v12:
time: 114 us; the launch traced here: 113 us
  matrix products  21.3 us (19%)
  waiting for transfers between devices  20.3 us (18%)
  starting transfers between devices  18.7 us (16%)
  other arithmetic  18.1 us (16%)
  local copies, waits for them, and re-layouts  16.8 us (15%)
  blocking collectives  8.6 us (8%)
  Pallas kernels  8.01 us (7%)
  between operations  1.29 us (1%)
    conv_general_dilated x2, matrix products, depthwise_minor(): lax.conv_general_dilated(padded_t[None], kernel[:, :, None, :], (1, 1), '...  12.6 us
    ppermute x6, waiting for transfers between devices, butterfly_step(): lax.ppermute(flat, axis, [(i, i ^ step) for i in range(devices)])  11.3 us
    all_gather x1, blocking collectives, gathered_weights(): full = lax.all_gather(packed, 'chan', axis=0, tiled=True)  8.6 us
    pallas_call x1, Pallas kernels, kernel_grad_minor(): pl.pallas_call(kernel_grad_body, out_shape=jax.ShapeDtypeStruct((side * s...  8.01 us
    ppermute x2, waiting for transfers between devices, extended(): after = lax.ppermute(leading, axis, down)  7.21 us
    ppermute x2, starting transfers between devices, extended(): before = lax.ppermute(last, axis, up)  6.97 us
    dot_general x4, matrix products, contract(): lax.dot_general(left, right, (((dim_left,), (dim_right,)), ((), ())), pre...  6.78 us
    ppermute x6, starting transfers between devices, butterfly_step(): lax.ppermute(flat, axis, [(i, i ^ step) for i in range(devices)])  5.59 us
  transfers between devices with their start and end apart: 12, of which 5 were waited for; matrix products, arithmetic and copies ran while one was open for 14% of the time, Pallas kernels for 0%

profile of v12, /device:TPU:0, one launch (start us, length us, event | category | flops | bytes accessed | tf_op | source)
XLA Modules:
  0.0 113.1 jit_solution(15977209307727988411)
XLA Ops:
  0.7 1.3 %copy.84 = bf16[192,8,128]{0,2,1:T(8,128)(2,1)S(1)} copy(bf16[192,8,128]{2,1,0:T(8,128)(2,1)} %param.11) | data formatting | bytes 786432 | tf_op args[0]
  2.0 3.0 %collective-permute-start = (bf16[192,3,128]{0,2,1:T(8,128)(2,1)S(1)}, bf16[192,3,128]{0,2,1:T(8,128)(2,1)S(1)}, u32[]{:S(2)}, u32[]{:S(2)}) collective-permute-start(bf16[192,3,128]{0,2,1:T(8,128)(2,1)S(1)} %slice_select_fusion.1), channel_id=1, source_target_pairs={{0,16},{16,0},{1,17},{17,1},{2,18},{18,2},{3,19},{19,3},{4,20},{20... | collective-permute-start | bytes 442376 | tf_op jit(solution)/shard_map/ppermute | solution.py:18
  8.1 8.6 %all_gather.3 = bf16[768,387]{1,0:T(8,128)(2,1)S(1)} all-gather(bf16[192,387]{1,0:T(8,128)(2,1)S(1)} %concatenate.27), channel_id=1, replica_groups=mesh['row'=2,'col'=4,'chan'=4] {'chan'}, dimensions={0}, use_global_device_ids=true | all-gather | bytes 743040 | tf_op jit(solution)/shard_map/all_gather | solution.py:170
  18.9 3.5 %collective-permute-start.1 = (bf16[192,14,3]{0,2,1:T(4,128)(2,1)S(1)}, bf16[192,14,3]{0,2,1:T(4,128)(2,1)S(1)}, u32[]{:S(2)}, u32[]{:S(2)}) collective-permute-start(bf16[192,14,3]{0,2,1:T(4,128)(2,1)S(1)} %get-tuple-element.40), channel_id=1, source_target_pairs={{0,4},{4,8},{8,12},{1,5},{5,9},{9,13},{2,6},{6,10},{10,14},{3,7},{... | collective-permute-start | bytes 48392 | tf_op jit(solution)/shard_map/ppermute | solution.py:23
  24.8 3.4 %collective-permute-done.2 = bf16[192,14,3]{0,2,1:T(4,128)(2,1)S(1)} collective-permute-done((bf16[192,14,3]{0,2,1:T(4,128)(2,1)S(1)}, bf16[192,14,3]{0,2,1:T(4,128)(2,1)S(1)}, u32[]{:S(2)}, u32[]{:S(2)}) %collective-permute-start.2) | collective-permute-done | bytes 16160 | tf_op jit(solution)/shard_map/ppermute | solution.py:24
  28.1 1.6 %bitcast_convert_fusion = (f32[14,134,192]{2,1,0:T(8,128)}, bf16[1,14,134,192]{3,2,1,0:T(8,128)(2,1)S(1)}) fusion(bf16[192,14,3]{0,2,1:T(4,128)(2,1)S(1)} %collective-permute-done.2, bf16[192,3,128]{0,2,1:T(8,128)(2,1)S(1)} %get-tuple-element.48, bf16[192,8,128]{0,2,1:T(8,128)(2,1)S(1)} %copy.84, bf16[192,3,128]{0,2,1:T(8,128)(2,1)S(1)} %get-tuple-element.47, ...), kind=kLoop, calls=%fused_computation.32 | loop fusion | flops 3962112 | bytes 2881536 | tf_op jit(solution)/shard_map/convert_element_type | solution.py:211
  29.7 8.4 %fusion.6 = f32[1,8,128,192]{3,0,2,1:T(1,128)S(1)} fusion(bf16[1,14,134,192]{3,2,1,0:T(8,128)(2,1)S(1)} %get-tuple-element.37, f32[7,7,1,192]{3,1,0,2:T(8,128)S(1)} %bitcast.130), kind=kOutput, calls=%fused_computation.13 | convolution fusion | flops 115605504 | bytes 1544448 | tf_op jit(solution)/shard_map/conv_general_dilated | solution.py:180
  38.8 1.9 %copy.89 = f32[1,8,128,192]{2,1,3,0:T(8,128)} copy(f32[1,8,128,192]{3,0,2,1:T(1,128)S(1)} %fusion.6) | data formatting | bytes 1572864 | tf_op jit(solution)/shard_map/conv_general_dilated | solution.py:180
  41.1 2.2 %multiply_convert_fusion = (bf16[1024,768]{0,1:T(8,128)(2,1)S(1)}, f32[1024,768]{0,1:T(8,128)S(1)}) fusion(f32[768]{0:T(1024)S(1)} %fusion.35, f32[24,8,8,128]{3,2,1,0:T(8,128)} %bitcast.125, f32[192]{0:T(256)S(1)} %copy-done.25, f32[192]{0:T(256)S(1)} %copy-done.16, f32[1024]{0:T(1024)S(1)} %get-tuple-element.58, f32[1024]{0:T(1024)S(1)} %get-tuple-element.59, ...), kind=kOutput, calls=%fused_computation.9 | convolution fusion | flops 307888128 | bytes 5913600 | tf_op jit(solution)/shard_map/dot_general | solution.py:53
  44.3 4.3 %fusion.31 = (f32[192]{0:T(256)}, f32[192]{0:T(256)}, bf16[8,128,192]{1,0,2:T(8,128)(2,1)}) fusion(bf16[192,8,128]{2,1,0:T(8,128)(2,1)S(1)} %copy-done.2, f32[192]{0:T(256)S(1)} %copy-done.22, f32[192]{0:T(256)S(1)} %copy-done.23, f32[24,8,8,128]{3,2,1,0:T(8,128)S(1)} %copy.118, bf16[192,8,128]{2,1,0:T(8,128)(2,1)S(1)} %copy-done.4), kind=kLoop, calls=%fused_computation.47 | loop fusion | flops 1965696 | bytes 1969152 | tf_op jit(solution)/shard_map/reduce_sum | solution.py:239
  49.6 3.2 %fusion.60 = (bf16[1024,768]{0,1:T(8,128)(2,1)S(1)}, f32[1024,768]{0,1:T(8,128)}) fusion(f32[1024,768]{0,1:T(8,128)S(1)} %get-tuple-element.65, f32[768]{0:T(1024)S(1)} %fusion.35, bf16[1024,192]{0,1:T(8,128)(2,1)S(1)} %copy-done.3, bf16[768,387]{1,0:T(8,128)(2,1)S(1)} %all_gather.3), kind=kOutput, calls=%fused_computation.115 | convolution fusion | flops 310640640 | bytes 8654848 | tf_op jit(solution)/shard_map/dot_general | solution.py:53
  53.2 1.3 %convert_reduce_fusion = (f32[192]{0:T(256)}, f32[1024,192]{0,1:T(8,128)S(1)}) fusion(bf16[192,4,192]{0,2,1:T(8,128)(2,1)S(1)} %bitcast.127, bf16[1024,4,192]{0,2,1:T(8,128)(2,1)S(1)} %bitcast.132), kind=kOutput, calls=%fused_computation.1 | convolution fusion | flops 304938816 | bytes 2654976 | tf_op jit(solution)/shard_map/dot_general | solution.py:250
  54.7 1.3 %copy.99 = f32[1024,192]{1,0:T(8,128)} copy(f32[1024,192]{0,1:T(8,128)S(1)} %get-tuple-element.31) | data formatting | bytes 1572864 | tf_op jit(solution)/shard_map/reduce_sum | solution.py:256
  57.6 1.9 %dynamic-slice_reduce_fusion = f32[192]{0:T(256)} fusion(f32[1024,768]{0,1:T(8,128)} %get-tuple-element.67, s32[]{:T(128)S(6)} %select_n.45), kind=kLoop, calls=%fused_computation.52 | loop fusion | flops 196416 | bytes 787204 | tf_op jit(solution)/shard_map/reduce_sum | solution.py:248
  61.8 1.5 %fusion.57 = (bf16[8,128,192]{2,1,0:T(8,128)(2,1)S(1)}, f32[8,128,192]{2,1,0:T(8,128)}) fusion(f32[8,128]{1,0:T(8,128)S(1)} %broadcast_multiply_fusion, f32[8,128]{1,0:T(8,128)S(1)} %get-tuple-element.60, f32[192]{0:T(256)S(1)} %copy-done.14, f32[1,8,128,192]{3,0,2,1:T(1,128)S(1)} %fusion.6, f32[8,128]{1,0:T(8,128)S(1)} %multiply_bitcast_fusion, ...), kind=kLoop, calls=%fused_computation.113 | loop fusion | flops 1769472 | bytes 2770432 | tf_op jit(solution)/shard_map/convert_element_type | solution.py:292
  63.4 8.0 %shard_map.194 = f32[49,8,192]{2,1,0:T(8,128)} custom-call(f32[8,128,192]{2,1,0:T(8,128)} %get-tuple-element.35.d_ref, f32[14,134,192]{2,1,0:T(8,128)} %get-tuple-element.36.p_ref), custom_call_target="tpu_custom_call" | custom-call | tf_op jit(solution)/shard_map/pallas_call | solution.py:107
  74.1 2.7 %collective-permute-start.6 = (f32[42144]{0:T(1024)S(1)}, f32[42144]{0:T(1024)S(1)}, u32[]{:S(2)}, u32[]{:S(2)}) collective-permute-start(f32[42144]{0:T(1024)S(1)} %slice.124), channel_id=1, source_target_pairs={{0,8},{4,12},{8,0},{12,4},{1,9},{5,13},{9,1},{13,5},{2,10},{6,14},... | collective-permute-start | bytes 505736 | tf_op jit(solution)/shard_map/ppermute | solution.py:146
  76.8 1.8 %collective-permute-done.3 = bf16[3,128,192]{2,1,0:T(8,128)(2,1)S(1)} collective-permute-done((bf16[3,128,192]{2,1,0:T(8,128)(2,1)S(1)}, bf16[3,128,192]{2,1,0:T(8,128)(2,1)S(1)}, u32[]{:S(2)}, u32[]{:S(2)}) %collective-permute-start.3) | collective-permute-done | bytes 147488 | tf_op jit(solution)/shard_map/ppermute | solution.py:18
  78.6 3.5 %collective-permute-start.4 = (bf16[14,3,192]{2,1,0:T(4,128)(2,1)S(1)}, bf16[14,3,192]{2,1,0:T(4,128)(2,1)S(1)}, u32[]{:S(2)}, u32[]{:S(2)}) collective-permute-start(bf16[14,3,192]{2,1,0:T(4,128)(2,1)S(1)} %get-tuple-element.38), channel_id=1, source_target_pairs={{0,4},{4,8},{8,12},{1,5},{5,9},{9,13},{2,6},{6,10},{10,14},{3,7},{... | collective-permute-start | bytes 48392 | tf_op jit(solution)/shard_map/ppermute | solution.py:23
  84.0 3.9 %collective-permute-done.5 = bf16[14,3,192]{2,1,0:T(4,128)(2,1)S(1)} collective-permute-done((bf16[14,3,192]{2,1,0:T(4,128)(2,1)S(1)}, bf16[14,3,192]{2,1,0:T(4,128)(2,1)S(1)}, u32[]{:S(2)}, u32[]{:S(2)}) %collective-permute-start.5) | collective-permute-done | bytes 16160 | tf_op jit(solution)/shard_map/ppermute | solution.py:24
  89.3 1.6 %collective-permute-start.7 = (f32[42144]{0:T(1024)S(1)}, f32[42144]{0:T(1024)S(1)}, u32[]{:S(2)}, u32[]{:S(2)}) collective-permute-start(f32[42144]{0:T(1024)S(1)} %slice_add_fusion.2), channel_id=1, source_target_pairs={{0,4},{4,0},{8,12},{12,8},{1,5},{5,1},{9,13},{13,9},{2,6},{6,2},{1... | collective-permute-start | bytes 505736 | tf_op jit(solution)/shard_map/ppermute | solution.py:146
  90.9 4.2 %fusion.15 = f32[8,8,17,192]{3,1,2,0:T(8,128)S(1)} fusion(bf16[14,1,7,6,192]{4,2,3,0,1:T(8,128)(2,1)S(1)} %slice.122, bf16[14,1,8,17,192]{4,2,3,0,1:T(8,128)(2,1)S(1)} %copy.105, pred[8,17]{0,1:T(8,128)(4,1)S(1)} %copy-done.26, f32[7,7,1,192]{3,1,0,2:T(8,128)S(1)} %bitcast.131), kind=kOutput, calls=%fused_computation.23 | convolution fusion | flops 126007296 | bytes 1830280 | tf_op jit(solution)/shard_map/conv_general_dilated | solution.py:180
  98.5 6.7 %collective-permute-done.10 = f32[42144]{0:T(1024)S(1)} collective-permute-done((f32[42144]{0:T(1024)S(1)}, f32[42144]{0:T(1024)S(1)}, u32[]{:S(2)}, u32[]{:S(2)}) %collective-permute-start.10) | collective-permute-done | bytes 168608 | tf_op jit(solution)/shard_map/ppermute | solution.py:146
  106.1 4.6 %collective-permute-done.11 = f32[42144]{0:T(1024)S(1)} collective-permute-done((f32[42144]{0:T(1024)S(1)}, f32[42144]{0:T(1024)S(1)}, u32[]{:S(2)}, u32[]{:S(2)}) %collective-permute-start.11) | collective-permute-done | bytes 168608 | tf_op jit(solution)/shard_map/ppermute | solution.py:146
  (129 shorter events, 27.4 us)
Async XLA Ops:
  0.6 16.1 %copy-start.2 = (bf16[192,8,128]{2,1,0:T(8,128)(2,1)S(1)}, bf16[192,8,128]{2,1,0:T(8,128)(2,1)}, u32[]{:S(2)}) copy-start(bf16[192,8,128]{2,1,0:T(8,128)(2,1)} %param.21) | copy-start | bytes 1179652
  2.0 16.8 %collective-permute-start = (bf16[192,3,128]{0,2,1:T(8,128)(2,1)S(1)}, bf16[192,3,128]{0,2,1:T(8,128)(2,1)S(1)}, u32[]{:S(2)}, u32[]{:S(2)}) collective-permute-start(bf16[192,3,128]{0,2,1:T(8,128)(2,1)S(1)} %slice_select_fusion.1), channel_id=1, source_target_pairs={{0,16},{16,0},{1,17},{17,1},{2,18},{18,2},{3,19},{19,3},{4,20},{20... | collective-permute-start | bytes 442376 | tf_op jit(solution)/shard_map/ppermute | solution.py:18
  8.1 9.7 %copy-start.22 = (f32[192]{0:T(256)S(1)}, f32[192]{0:T(256)}, u32[]{:S(2)}) copy-start(f32[192]{0:T(256)} %param.20) | copy-start | bytes 2308
  18.8 5.3 %copy-start.11 = (f32[7,7,192]{2,1,0:T(8,128)S(1)}, f32[7,7,192]{2,1,0:T(8,128)}, u32[]{:S(2)}) copy-start(f32[7,7,192]{2,1,0:T(8,128)} %param.12) | copy-start | bytes 112900
  18.9 5.9 %collective-permute-start.1 = (bf16[192,14,3]{0,2,1:T(4,128)(2,1)S(1)}, bf16[192,14,3]{0,2,1:T(4,128)(2,1)S(1)}, u32[]{:S(2)}, u32[]{:S(2)}) collective-permute-start(bf16[192,14,3]{0,2,1:T(4,128)(2,1)S(1)} %get-tuple-element.40), channel_id=1, source_target_pairs={{0,4},{4,8},{8,12},{1,5},{5,9},{9,13},{2,6},{6,10},{10,14},{3,7},{... | collective-permute-start | bytes 48392 | tf_op jit(solution)/shard_map/ppermute | solution.py:23
  22.4 5.8 %collective-permute-start.2 = (bf16[192,14,3]{0,2,1:T(4,128)(2,1)S(1)}, bf16[192,14,3]{0,2,1:T(4,128)(2,1)S(1)}, u32[]{:S(2)}, u32[]{:S(2)}) collective-permute-start(bf16[192,14,3]{0,2,1:T(4,128)(2,1)S(1)} %get-tuple-element.41), channel_id=1, source_target_pairs={{4,0},{8,4},{12,8},{5,1},{9,5},{13,9},{6,2},{10,6},{14,10},{7,3},{... | collective-permute-start | bytes 48392 | tf_op jit(solution)/shard_map/ppermute | solution.py:24
  43.9 4.7 %copy-start.3 = (bf16[1024,192]{0,1:T(8,128)(2,1)S(1)}, bf16[1024,192]{0,1:T(8,128)(2,1)}, u32[]{:S(2)}) copy-start(bf16[1024,192]{0,1:T(8,128)(2,1)} %fusion.23) | copy-start | bytes 1179652
  49.6 3.6 %copy-start.10 = (bf16[768,192]{1,0:T(8,128)(2,1)S(1)}, bf16[768,192]{1,0:T(8,128)(2,1)}, u32[]{:S(2)}) copy-start(bf16[768,192]{1,0:T(8,128)(2,1)} %get-tuple-element.43) | copy-start | bytes 884740
  54.6 5.0 %copy-start = (f32[1024,192]{0,1:T(8,128)}, f32[1024,192]{0,1:T(8,128)S(1)}, u32[]{:S(2)}) copy-start(f32[1024,192]{0,1:T(8,128)S(1)} %get-tuple-element.31) | copy-start | bytes 2359300
  57.6 4.2 %copy-start.1 = (f32[1024,192]{1,0:T(8,128)S(1)}, f32[1024,192]{1,0:T(8,128)}, u32[]{:S(2)}) copy-start(f32[1024,192]{1,0:T(8,128)} %copy.99) | copy-start | bytes 2359300
  57.6 4.2 %copy-start.14 = (f32[192]{0:T(256)S(1)}, f32[192]{0:T(256)}, u32[]{:S(2)}) copy-start(f32[192]{0:T(256)} %param.13) | copy-start | bytes 2308
  57.6 4.2 %copy-start.17 = (f32[192]{0:T(256)S(1)}, f32[192]{0:T(256)}, u32[]{:S(2)}) copy-start(f32[192]{0:T(256)} %param.14) | copy-start | bytes 2308
  63.4 10.0 %copy-start.15 = (f32[192]{0:T(256)S(1)}, f32[192]{0:T(256)}, u32[]{:S(2)}) copy-start(f32[192]{0:T(256)} %param.13) | copy-start | bytes 2308
  63.4 10.0 %copy-start.18 = (f32[192]{0:T(256)S(1)}, f32[192]{0:T(256)}, u32[]{:S(2)}) copy-start(f32[192]{0:T(256)} %param.14) | copy-start | bytes 2308
  72.8 10.7 %copy-start.9 = (f32[36864]{0:T(1024)S(1)}, f32[36864]{0:T(1024)}, u32[]{:S(2)}) copy-start(f32[36864]{0:T(1024)} %reshape.303) | copy-start | bytes 442372
  72.8 5.8 %collective-permute-start.3 = (bf16[3,128,192]{2,1,0:T(8,128)(2,1)S(1)}, bf16[3,128,192]{2,1,0:T(8,128)(2,1)S(1)}, u32[]{:S(2)}, u32[]{:S(2)}) collective-permute-start(bf16[3,128,192]{2,1,0:T(8,128)(2,1)S(1)} %slice_select_fusion), channel_id=1, source_target_pairs={{0,16},{16,0},{1,17},{17,1},{2,18},{18,2},{3,19},{19,3},{4,20},{20... | collective-permute-start | bytes 442376 | tf_op jit(solution)/shard_map/ppermute | solution.py:18
  74.1 15.0 %collective-permute-start.6 = (f32[42144]{0:T(1024)S(1)}, f32[42144]{0:T(1024)S(1)}, u32[]{:S(2)}, u32[]{:S(2)}) collective-permute-start(f32[42144]{0:T(1024)S(1)} %slice.124), channel_id=1, source_target_pairs={{0,8},{4,12},{8,0},{12,4},{1,9},{5,13},{9,1},{13,5},{2,10},{6,14},... | collective-permute-start | bytes 505736 | tf_op jit(solution)/shard_map/ppermute | solution.py:146
  78.6 5.4 %collective-permute-start.4 = (bf16[14,3,192]{2,1,0:T(4,128)(2,1)S(1)}, bf16[14,3,192]{2,1,0:T(4,128)(2,1)S(1)}, u32[]{:S(2)}, u32[]{:S(2)}) collective-permute-start(bf16[14,3,192]{2,1,0:T(4,128)(2,1)S(1)} %get-tuple-element.38), channel_id=1, source_target_pairs={{0,4},{4,8},{8,12},{1,5},{5,9},{9,13},{2,6},{6,10},{10,14},{3,7},{... | collective-permute-start | bytes 48392 | tf_op jit(solution)/shard_map/ppermute | solution.py:23
  82.1 5.8 %collective-permute-start.5 = (bf16[14,3,192]{2,1,0:T(4,128)(2,1)S(1)}, bf16[14,3,192]{2,1,0:T(4,128)(2,1)S(1)}, u32[]{:S(2)}, u32[]{:S(2)}) collective-permute-start(bf16[14,3,192]{2,1,0:T(4,128)(2,1)S(1)} %get-tuple-element.39), channel_id=1, source_target_pairs={{4,0},{8,4},{12,8},{5,1},{9,5},{13,9},{6,2},{10,6},{14,10},{7,3},{... | collective-permute-start | bytes 48392 | tf_op jit(solution)/shard_map/ppermute | solution.py:24
  83.5 12.6 %collective-permute-start.9 = (f32[42144]{0:T(1024)S(1)}, f32[42144]{0:T(1024)}, u32[]{:S(2)}, u32[]{:S(2)}) collective-permute-start(f32[42144]{0:T(1024)S(1)} %pad_maximum_fusion.1), channel_id=1, source_target_pairs={{0,16},{16,0},{1,17},{17,1},{2,18},{18,2},{3,19},{19,3},{4,20},{20... | collective-permute-start | bytes 505736 | tf_op jit(solution)/shard_map/ppermute | solution.py:146
  89.3 7.9 %collective-permute-start.7 = (f32[42144]{0:T(1024)S(1)}, f32[42144]{0:T(1024)S(1)}, u32[]{:S(2)}, u32[]{:S(2)}) collective-permute-start(f32[42144]{0:T(1024)S(1)} %slice_add_fusion.2), channel_id=1, source_target_pairs={{0,4},{4,0},{8,12},{12,8},{1,5},{5,1},{9,13},{13,9},{2,6},{6,2},{1... | collective-permute-start | bytes 505736 | tf_op jit(solution)/shard_map/ppermute | solution.py:146
  97.0 8.2 %collective-permute-start.10 = (f32[42144]{0:T(1024)S(1)}, f32[42144]{0:T(1024)S(1)}, u32[]{:S(2)}, u32[]{:S(2)}) collective-permute-start(f32[42144]{0:T(1024)S(1)} %add.145), channel_id=1, source_target_pairs={{0,8},{4,12},{8,0},{12,4},{1,9},{5,13},{9,1},{13,5},{2,10},{6,14},... | collective-permute-start | bytes 505736 | tf_op jit(solution)/shard_map/ppermute | solution.py:146
  97.1 8.2 %collective-permute-start.8 = (f32[42144]{0:T(1024)S(1)}, f32[42144]{0:T(1024)S(1)}, u32[]{:S(2)}, u32[]{:S(2)}) collective-permute-start(f32[42144]{0:T(1024)S(1)} %add.143), channel_id=1, source_target_pairs={{0,16},{16,0},{1,17},{17,1},{2,18},{18,2},{3,19},{19,3},{4,20},{20... | collective-permute-start | bytes 505736 | tf_op jit(solution)/shard_map/ppermute | solution.py:146
  105.3 5.5 %collective-permute-start.11 = (f32[42144]{0:T(1024)S(1)}, f32[42144]{0:T(1024)S(1)}, u32[]{:S(2)}, u32[]{:S(2)}) collective-permute-start(f32[42144]{0:T(1024)S(1)} %add.146), channel_id=1, source_target_pairs={{0,4},{4,0},{8,12},{12,8},{1,5},{5,1},{9,13},{13,9},{2,6},{6,2},{1... | collective-permute-start | bytes 505736 | tf_op jit(solution)/shard_map/ppermute | solution.py:146
  (15 other events, 32.8 us)

commit v13 on v11

--- a/solution.py
+++ b/solution.py
@@ -81,11 +81,11 @@
     )
 
 
-def kernel_grad_body(d_ref, p_ref, o_ref, shifted_ref):
+def kernel_grad_body(d_ref, p_ref, o_ref, shifted_ref, acc_ref):
     rows, cols, _ = d_ref.shape
     taps = o_ref.shape[0]
     side = int(round(taps ** 0.5))
-    o_ref[...] = jnp.zeros(o_ref.shape, o_ref.dtype)
+    acc_ref[...] = jnp.zeros(acc_ref.shape, acc_ref.dtype)
     for j in range(side):
         shifted_ref[j] = p_ref[:, j : j + cols, :]
 
@@ -95,21 +95,25 @@
             for j in range(side):
                 prod = d_row * shifted_ref[j, h + i]
                 part = jnp.sum(prod.reshape(cols // 8, 8, prod.shape[-1]), axis=0)
-                o_ref[i * side + j] += part
+                acc_ref[i * side + j] += part
         return carry
 
     lax.fori_loop(0, rows, row_step, 0)
+    o_ref[...] = jnp.sum(acc_ref[...], axis=1)
 
 
 def kernel_grad_minor(d_t, p_t):
     side = p_t.shape[0] - d_t.shape[0] + 1
     channel_count = d_t.shape[-1]
-    partial = pl.pallas_call(
+    summed = pl.pallas_call(
         kernel_grad_body,
-        out_shape=jax.ShapeDtypeStruct((side * side, 8, channel_count), jnp.float32),
-        scratch_shapes=[pltpu.VMEM((side,) + p_t.shape[:1] + d_t.shape[1:], jnp.float32)],
+        out_shape=jax.ShapeDtypeStruct((side * side, channel_count), jnp.float32),
+        scratch_shapes=[
+            pltpu.VMEM((side,) + p_t.shape[:1] + d_t.shape[1:], jnp.float32),
+            pltpu.VMEM((side * side, 8, channel_count), jnp.float32),
+        ],
     )(d_t, p_t)
-    return jnp.sum(partial, axis=1).reshape(side, side, channel_count)
+    return summed.reshape(side, side, channel_count)
 
 
 def flat_pack(values):

time: 112 us -> 112 us (level)
  no operation moved by 1% of the time
where the time goes in v13:
time: 112 us; the launch traced here: 111 us
  matrix products  23 us (21%)
  starting transfers between devices  21.3 us (19%)
  local copies, waits for them, and re-layouts  17.7 us (16%)
  waiting for transfers between devices  16.6 us (15%)
  other arithmetic  14.5 us (13%)
  blocking collectives  8.6 us (8%)
  Pallas kernels  8.25 us (7%)
  between operations  1.19 us (1%)
    conv_general_dilated x2, matrix products, depthwise_minor(): lax.conv_general_dilated(padded_t[None], kernel[:, :, None, :], (1, 1), '...  12.6 us
    dot_general x4, matrix products, contract(): lax.dot_general(left, right, (((dim_left,), (dim_right,)), ((), ())), pre...  9.02 us
    ppermute x6, waiting for transfers between devices, butterfly_step(): lax.ppermute(flat, axis, [(i, i ^ step) for i in range(devices)])  8.82 us
    all_gather x1, blocking collectives, gathered_weights(): full = lax.all_gather(packed, 'chan', axis=0, tiled=True)  8.6 us
    pallas_call x1, Pallas kernels, kernel_grad_minor(): pl.pallas_call(kernel_grad_body, out_shape=jax.ShapeDtypeStruct((side * s...  8.25 us
    ppermute x6, starting transfers between devices, butterfly_step(): lax.ppermute(flat, axis, [(i, i ^ step) for i in range(devices)])  7.98 us
    ppermute x2, starting transfers between devices, extended(): before = lax.ppermute(last, axis, up)  6.96 us
    unnamed x36, local copies, waits for them, and re-layouts  5.12 us
  transfers between devices with their start and end apart: 12, of which 5 were waited for; matrix products, arithmetic and copies ran while one was open for 17% of the time, Pallas kernels for 7%

profile of v13, /device:TPU:0, one launch (start us, length us, event | category | flops | bytes accessed | tf_op | source)
XLA Modules:
  0.0 111.2 jit_solution(4019356109578236165)
XLA Ops:
  2.0 3.0 %collective-permute-start = (bf16[192,3,128]{0,2,1:T(8,128)(2,1)S(1)}, bf16[192,3,128]{0,2,1:T(8,128)(2,1)S(1)}, u32[]{:S(2)}, u32[]{:S(2)}) collective-permute-start(bf16[192,3,128]{0,2,1:T(8,128)(2,1)S(1)} %slice_select_fusion.1), channel_id=1, source_target_pairs={{0,16},{16,0},{1,17},{17,1},{2,18},{18,2},{3,19},{19,3},{4,20},{20... | collective-permute-start | bytes 442376 | tf_op jit(solution)/shard_map/ppermute | solution.py:18
  8.1 8.6 %all_gather.3 = bf16[768,387]{1,0:T(8,128)(2,1)S(1)} all-gather(bf16[192,387]{1,0:T(8,128)(2,1)S(1)} %concatenate.27), channel_id=1, replica_groups=mesh['row'=2,'col'=4,'chan'=4] {'chan'}, dimensions={0}, use_global_device_ids=true | all-gather | bytes 743040 | tf_op jit(solution)/shard_map/all_gather | solution.py:174
  18.2 3.5 %collective-permute-start.1 = (bf16[192,14,3]{0,2,1:T(4,128)(2,1)S(1)}, bf16[192,14,3]{0,2,1:T(4,128)(2,1)S(1)}, u32[]{:S(2)}, u32[]{:S(2)}) collective-permute-start(bf16[192,14,3]{0,2,1:T(4,128)(2,1)S(1)} %get-tuple-element.40), channel_id=1, source_target_pairs={{0,4},{4,8},{8,12},{1,5},{5,9},{9,13},{2,6},{6,10},{10,14},{3,7},{... | collective-permute-start | bytes 48392 | tf_op jit(solution)/shard_map/ppermute | solution.py:23
  23.5 3.9 %collective-permute-done.2 = bf16[192,14,3]{0,2,1:T(4,128)(2,1)S(1)} collective-permute-done((bf16[192,14,3]{0,2,1:T(4,128)(2,1)S(1)}, bf16[192,14,3]{0,2,1:T(4,128)(2,1)S(1)}, u32[]{:S(2)}, u32[]{:S(2)}) %collective-permute-start.2) | collective-permute-done | bytes 16160 | tf_op jit(solution)/shard_map/ppermute | solution.py:24
  27.4 1.6 %bitcast_convert_fusion = (f32[14,134,192]{2,1,0:T(8,128)}, bf16[1,14,134,192]{3,2,1,0:T(8,128)(2,1)S(1)}) fusion(bf16[192,14,3]{0,2,1:T(4,128)(2,1)S(1)} %collective-permute-done.2, bf16[192,3,128]{0,2,1:T(8,128)(2,1)S(1)} %get-tuple-element.48, bf16[192,8,128]{0,2,1:T(8,128)(2,1)S(1)} %copy.84, bf16[192,3,128]{0,2,1:T(8,128)(2,1)S(1)} %get-tuple-element.47, ...), kind=kLoop, calls=%fused_computation.32 | loop fusion | flops 3962112 | bytes 2881536 | tf_op jit(solution)/shard_map/convert_element_type | solution.py:215
  29.0 8.4 %fusion.6 = f32[1,8,128,192]{3,0,2,1:T(1,128)S(1)} fusion(bf16[1,14,134,192]{3,2,1,0:T(8,128)(2,1)S(1)} %get-tuple-element.37, f32[7,7,1,192]{3,1,0,2:T(8,128)S(1)} %bitcast.130), kind=kOutput, calls=%fused_computation.13 | convolution fusion | flops 115605504 | bytes 1544448 | tf_op jit(solution)/shard_map/conv_general_dilated | solution.py:184
  38.1 1.9 %copy.89 = f32[1,8,128,192]{2,1,3,0:T(8,128)} copy(f32[1,8,128,192]{3,0,2,1:T(1,128)S(1)} %fusion.6) | data formatting | bytes 1572864 | tf_op jit(solution)/shard_map/conv_general_dilated | solution.py:184
  40.4 2.2 %multiply_convert_fusion = (bf16[1024,768]{0,1:T(8,128)(2,1)S(1)}, f32[1024,768]{0,1:T(8,128)S(1)}) fusion(f32[768]{0:T(1024)S(1)} %fusion.35, f32[24,8,8,128]{3,2,1,0:T(8,128)} %bitcast.125, f32[192]{0:T(256)S(1)} %copy-done.12, f32[192]{0:T(256)S(1)} %copy-done.9, f32[1024]{0:T(1024)S(1)} %get-tuple-element.58, f32[1024]{0:T(1024)S(1)} %get-tuple-element.59, ...), kind=kOutput, calls=%fused_computation.9 | convolution fusion | flops 307888128 | bytes 5913600 | tf_op jit(solution)/shard_map/dot_general | solution.py:53
  43.9 3.8 %fusion.31 = (f32[192]{0:T(256)S(1)}, f32[192]{0:T(256)S(1)}, bf16[8,128,192]{1,0,2:T(8,128)(2,1)}) fusion(bf16[192,8,128]{2,1,0:T(8,128)(2,1)S(1)} %copy-done.1, f32[192]{0:T(256)S(1)} %copy-done.10, f32[192]{0:T(256)S(1)} %copy-done.11, f32[24,8,8,128]{3,2,1,0:T(8,128)S(1)} %copy.118, bf16[192,8,128]{2,1,0:T(8,128)(2,1)S(1)} %copy-done.3), kind=kLoop, calls=%fused_computation.47 | loop fusion | flops 1965696 | bytes 1969152 | tf_op jit(solution)/shard_map/reduce_sum | solution.py:243
  47.7 3.3 %fusion.60 = (bf16[1024,768]{0,1:T(8,128)(2,1)S(1)}, f32[1024,768]{0,1:T(8,128)}) fusion(f32[1024,768]{0,1:T(8,128)S(1)} %get-tuple-element.65, f32[768]{0:T(1024)S(1)} %fusion.35, bf16[1024,192]{0,1:T(8,128)(2,1)S(1)} %fusion.23, bf16[768,387]{1,0:T(8,128)(2,1)S(1)} %all_gather.3), kind=kOutput, calls=%fused_computation.115 | convolution fusion | flops 310640640 | bytes 8654848 | tf_op jit(solution)/shard_map/dot_general | solution.py:53
  52.2 1.4 %copy.99 = f32[1024,192]{1,0:T(8,128)} copy(f32[1024,192]{0,1:T(8,128)S(1)} %get-tuple-element.31) | data formatting | bytes 1572864 | tf_op jit(solution)/shard_map/reduce_sum | solution.py:260
  53.6 2.3 %fusion.38 = f32[192,192]{1,0:T(8,128)} fusion(bf16[1024,768]{0,1:T(8,128)(2,1)} %copy-done.13, s32[]{:T(128)S(6)} %select_n.45, f32[24,8,8,128]{3,2,1,0:T(8,128)} %bitcast.126, f32[192]{0:T(256)S(1)} %copy-done.12, f32[192]{0:T(256)S(1)} %copy-done.9, f32[1024]{0:T(1024)S(1)} %get-tuple-element.58, f32[1024]{0:T(1024)S(1)} %get-tuple-element.59, ...), kind=kOutput, calls=%fused_computation.66 | convolution fusion | flops 76677120 | bytes 1337604 | tf_op jit(solution)/shard_map/dot_general | solution.py:53
  57.1 1.5 %fusion.57 = (bf16[8,128,192]{2,1,0:T(8,128)(2,1)S(1)}, f32[8,128,192]{2,1,0:T(8,128)}) fusion(f32[8,128]{1,0:T(8,128)S(1)} %broadcast_multiply_fusion, f32[8,128]{1,0:T(8,128)S(1)} %get-tuple-element.60, f32[192]{0:T(256)S(1)} %copy-done.8, f32[1,8,128,192]{3,0,2,1:T(1,128)S(1)} %fusion.6, f32[8,128]{1,0:T(8,128)S(1)} %multiply_bitcast_fusion, ...), kind=kLoop, calls=%fused_computation.113 | loop fusion | flops 1769472 | bytes 2770432 | tf_op jit(solution)/shard_map/convert_element_type | solution.py:296
  60.6 3.9 %collective-permute-done.3 = bf16[3,128,192]{2,1,0:T(8,128)(2,1)S(1)} collective-permute-done((bf16[3,128,192]{2,1,0:T(8,128)(2,1)S(1)}, bf16[3,128,192]{2,1,0:T(8,128)(2,1)S(1)}, u32[]{:S(2)}, u32[]{:S(2)}) %collective-permute-start.3) | collective-permute-done | bytes 147488 | tf_op jit(solution)/shard_map/ppermute | solution.py:18
  65.1 3.5 %collective-permute-start.4 = (bf16[14,3,192]{2,1,0:T(4,128)(2,1)}, bf16[14,3,192]{2,1,0:T(4,128)(2,1)S(1)}, u32[]{:S(2)}, u32[]{:S(2)}) collective-permute-start(bf16[14,3,192]{2,1,0:T(4,128)(2,1)} %get-tuple-element.38), channel_id=1, source_target_pairs={{0,4},{4,8},{8,12},{1,5},{5,9},{9,13},{2,6},{6,10},{10,14},{3,7},{... | collective-permute-start | bytes 48392 | tf_op jit(solution)/shard_map/ppermute | solution.py:23
  68.6 1.5 %collective-permute-start.5 = (bf16[14,3,192]{2,1,0:T(4,128)(2,1)S(1)}, bf16[14,3,192]{2,1,0:T(4,128)(2,1)S(1)}, u32[]{:S(2)}, u32[]{:S(2)}) collective-permute-start(bf16[14,3,192]{2,1,0:T(4,128)(2,1)S(1)} %get-tuple-element.39), channel_id=1, source_target_pairs={{4,0},{8,4},{12,8},{5,1},{9,5},{13,9},{6,2},{10,6},{14,10},{7,3},{... | collective-permute-start | bytes 48392 | tf_op jit(solution)/shard_map/ppermute | solution.py:24
  72.1 1.6 %concatenate.31 = f32[74304]{0:T(1024)S(1)} concatenate(f32[36864]{0:T(1024)S(1)} %reshape.302, f32[192]{0:T(256)S(1)} %dynamic-slice_reduce_fusion, f32[36864]{0:T(1024)S(1)} %reshape.303, f32[192]{0:T(256)S(1)} %get-tuple-element.15, f32[192]{0:T(256)S(1)} %get-tuple-element.16), dimensions={0} | concatenate | bytes 594432 | tf_op jit(solution)/shard_map/concatenate | solution.py:120
  73.8 3.7 %collective-permute-start.9 = (f32[42144]{0:T(1024)S(1)}, f32[42144]{0:T(1024)S(1)}, u32[]{:S(2)}, u32[]{:S(2)}) collective-permute-start(f32[42144]{0:T(1024)S(1)} %slice.129), channel_id=1, source_target_pairs={{0,8},{4,12},{8,0},{12,4},{1,9},{5,13},{9,1},{13,5},{2,10},{6,14},... | collective-permute-start | bytes 505736 | tf_op jit(solution)/shard_map/ppermute | solution.py:150
  77.6 8.2 %shard_map.194 = f32[49,192]{1,0:T(8,128)} custom-call(f32[8,128,192]{2,1,0:T(8,128)} %get-tuple-element.35.d_ref, f32[14,134,192]{2,1,0:T(8,128)} %get-tuple-element.36.p_ref), custom_call_target="tpu_custom_call" | custom-call | tf_op jit(solution)/shard_map/pallas_call | solution.py:108
  88.7 4.2 %fusion.15 = f32[8,8,17,192]{3,1,2,0:T(8,128)S(1)} fusion(bf16[14,1,7,6,192]{4,2,3,0,1:T(8,128)(2,1)S(1)} %slice.122, bf16[14,1,8,17,192]{4,2,3,0,1:T(8,128)(2,1)S(1)} %copy.105, pred[8,17]{0,1:T(8,128)(4,1)S(1)} %copy-done.14, f32[7,7,1,192]{3,1,0,2:T(8,128)S(1)} %bitcast.131), kind=kOutput, calls=%fused_computation.23 | convolution fusion | flops 126007296 | bytes 1830280 | tf_op jit(solution)/shard_map/conv_general_dilated | solution.py:184
  94.1 2.0 %collective-permute-start.10 = (f32[42144]{0:T(1024)S(1)}, f32[42144]{0:T(1024)S(1)}, u32[]{:S(2)}, u32[]{:S(2)}) collective-permute-start(f32[42144]{0:T(1024)S(1)} %slice_add_fusion.2), channel_id=1, source_target_pairs={{0,4},{4,0},{8,12},{12,8},{1,5},{5,1},{9,13},{13,9},{2,6},{6,2},{1... | collective-permute-start | bytes 505736 | tf_op jit(solution)/shard_map/ppermute | solution.py:150
  96.1 5.6 %collective-permute-done.7 = f32[42144]{0:T(1024)S(1)} collective-permute-done((f32[42144]{0:T(1024)S(1)}, f32[42144]{0:T(1024)S(1)}, u32[]{:S(2)}, u32[]{:S(2)}) %collective-permute-start.7) | collective-permute-done | bytes 168608 | tf_op jit(solution)/shard_map/ppermute | solution.py:150
  102.6 1.6 %collective-permute-start.11 = (f32[42144]{0:T(1024)S(1)}, f32[42144]{0:T(1024)S(1)}, u32[]{:S(2)}, u32[]{:S(2)}) collective-permute-start(f32[42144]{0:T(1024)S(1)} %add.146), channel_id=1, source_target_pairs={{0,16},{16,0},{1,17},{17,1},{2,18},{18,2},{3,19},{19,3},{4,20},{20... | collective-permute-start | bytes 505736 | tf_op jit(solution)/shard_map/ppermute | solution.py:150
  104.2 2.9 %collective-permute-done.8 = f32[42144]{0:T(1024)S(1)} collective-permute-done((f32[42144]{0:T(1024)S(1)}, f32[42144]{0:T(1024)S(1)}, u32[]{:S(2)}, u32[]{:S(2)}) %collective-permute-start.8) | collective-permute-done | bytes 168608 | tf_op jit(solution)/shard_map/ppermute | solution.py:150
  (106 shorter events, 26.0 us)
Async XLA Ops:
  0.6 16.1 %copy-start.1 = (bf16[192,8,128]{2,1,0:T(8,128)(2,1)S(1)}, bf16[192,8,128]{2,1,0:T(8,128)(2,1)}, u32[]{:S(2)}) copy-start(bf16[192,8,128]{2,1,0:T(8,128)(2,1)} %param.21) | copy-start | bytes 1179652
  2.0 16.1 %collective-permute-start = (bf16[192,3,128]{0,2,1:T(8,128)(2,1)S(1)}, bf16[192,3,128]{0,2,1:T(8,128)(2,1)S(1)}, u32[]{:S(2)}, u32[]{:S(2)}) collective-permute-start(bf16[192,3,128]{0,2,1:T(8,128)(2,1)S(1)} %slice_select_fusion.1), channel_id=1, source_target_pairs={{0,16},{16,0},{1,17},{17,1},{2,18},{18,2},{3,19},{19,3},{4,20},{20... | collective-permute-start | bytes 442376 | tf_op jit(solution)/shard_map/ppermute | solution.py:18
  8.1 9.7 %copy-start.10 = (f32[192]{0:T(256)S(1)}, f32[192]{0:T(256)}, u32[]{:S(2)}) copy-start(f32[192]{0:T(256)} %param.20) | copy-start | bytes 2308
  18.0 5.4 %copy-start.7 = (f32[7,7,192]{2,1,0:T(8,128)S(1)}, f32[7,7,192]{2,1,0:T(8,128)}, u32[]{:S(2)}) copy-start(f32[7,7,192]{2,1,0:T(8,128)} %param.12) | copy-start | bytes 112900
  18.2 5.3 %collective-permute-start.1 = (bf16[192,14,3]{0,2,1:T(4,128)(2,1)S(1)}, bf16[192,14,3]{0,2,1:T(4,128)(2,1)S(1)}, u32[]{:S(2)}, u32[]{:S(2)}) collective-permute-start(bf16[192,14,3]{0,2,1:T(4,128)(2,1)S(1)} %get-tuple-element.40), channel_id=1, source_target_pairs={{0,4},{4,8},{8,12},{1,5},{5,9},{9,13},{2,6},{6,10},{10,14},{3,7},{... | collective-permute-start | bytes 48392 | tf_op jit(solution)/shard_map/ppermute | solution.py:23
  21.6 5.8 %collective-permute-start.2 = (bf16[192,14,3]{0,2,1:T(4,128)(2,1)S(1)}, bf16[192,14,3]{0,2,1:T(4,128)(2,1)S(1)}, u32[]{:S(2)}, u32[]{:S(2)}) collective-permute-start(bf16[192,14,3]{0,2,1:T(4,128)(2,1)S(1)} %get-tuple-element.41), channel_id=1, source_target_pairs={{4,0},{8,4},{12,8},{5,1},{9,5},{13,9},{6,2},{10,6},{14,10},{7,3},{... | collective-permute-start | bytes 48392 | tf_op jit(solution)/shard_map/ppermute | solution.py:24
  37.4 2.5 %copy-start.8 = (f32[192]{0:T(256)S(1)}, f32[192]{0:T(256)}, u32[]{:S(2)}) copy-start(f32[192]{0:T(256)} %param.13) | copy-start | bytes 2308
  38.1 2.2 %copy-start.9 = (f32[192]{0:T(256)S(1)}, f32[192]{0:T(256)}, u32[]{:S(2)}) copy-start(f32[192]{0:T(256)} %param.14) | copy-start | bytes 2308
  38.1 2.2 %copy-start.12 = (f32[192]{0:T(256)S(1)}, f32[192]{0:T(256)}, u32[]{:S(2)}) copy-start(f32[192]{0:T(256)} %param.15) | copy-start | bytes 2308
  40.3 2.2 %copy-start.4 = (bf16[768,192]{1,0:T(8,128)(2,1)S(1)}, bf16[768,192]{1,0:T(8,128)(2,1)}, u32[]{:S(2)}) copy-start(bf16[768,192]{1,0:T(8,128)(2,1)} %get-tuple-element.44) | copy-start | bytes 884740
  42.6 1.3 %copy-start.3 = (bf16[192,8,128]{2,1,0:T(8,128)(2,1)S(1)}, bf16[192,8,128]{2,1,0:T(8,128)(2,1)}, u32[]{:S(2)}) copy-start(bf16[192,8,128]{2,1,0:T(8,128)(2,1)} %param.11) | copy-start | bytes 1179652
  42.6 1.3 %copy-start.11 = (f32[192]{0:T(256)S(1)}, f32[192]{0:T(256)}, u32[]{:S(2)}) copy-start(f32[192]{0:T(256)} %param.19) | copy-start | bytes 2308
  47.7 3.3 %copy-start.5 = (bf16[768,192]{1,0:T(8,128)(2,1)S(1)}, bf16[768,192]{1,0:T(8,128)(2,1)}, u32[]{:S(2)}) copy-start(bf16[768,192]{1,0:T(8,128)(2,1)} %get-tuple-element.43) | copy-start | bytes 884740
  55.9 1.2 %copy-start = (f32[1024,192]{1,0:T(8,128)S(1)}, f32[1024,192]{1,0:T(8,128)}, u32[]{:S(2)}) copy-start(f32[1024,192]{1,0:T(8,128)} %copy.99) | copy-start | bytes 2359300
  58.7 5.8 %collective-permute-start.3 = (bf16[3,128,192]{2,1,0:T(8,128)(2,1)S(1)}, bf16[3,128,192]{2,1,0:T(8,128)(2,1)S(1)}, u32[]{:S(2)}, u32[]{:S(2)}) collective-permute-start(bf16[3,128,192]{2,1,0:T(8,128)(2,1)S(1)} %slice_select_fusion), channel_id=1, source_target_pairs={{0,16},{16,0},{1,17},{17,1},{2,18},{18,2},{3,19},{19,3},{4,20},{20... | collective-permute-start | bytes 442376 | tf_op jit(solution)/shard_map/ppermute | solution.py:18
  60.5 10.2 %copy-start.6 = (f32[192,192]{1,0:T(8,128)S(1)}, f32[192,192]{1,0:T(8,128)}, u32[]{:S(2)}) copy-start(f32[192,192]{1,0:T(8,128)} %fusion.38) | copy-start | bytes 442372
  65.1 22.3 %collective-permute-start.4 = (bf16[14,3,192]{2,1,0:T(4,128)(2,1)}, bf16[14,3,192]{2,1,0:T(4,128)(2,1)S(1)}, u32[]{:S(2)}, u32[]{:S(2)}) collective-permute-start(bf16[14,3,192]{2,1,0:T(4,128)(2,1)} %get-tuple-element.38), channel_id=1, source_target_pairs={{0,4},{4,8},{8,12},{1,5},{5,9},{9,13},{2,6},{6,10},{10,14},{3,7},{... | collective-permute-start | bytes 48392 | tf_op jit(solution)/shard_map/ppermute | solution.py:23
  68.6 18.8 %collective-permute-start.5 = (bf16[14,3,192]{2,1,0:T(4,128)(2,1)S(1)}, bf16[14,3,192]{2,1,0:T(4,128)(2,1)S(1)}, u32[]{:S(2)}, u32[]{:S(2)}) collective-permute-start(bf16[14,3,192]{2,1,0:T(4,128)(2,1)S(1)} %get-tuple-element.39), channel_id=1, source_target_pairs={{4,0},{8,4},{12,8},{5,1},{9,5},{13,9},{6,2},{10,6},{14,10},{7,3},{... | collective-permute-start | bytes 48392 | tf_op jit(solution)/shard_map/ppermute | solution.py:24
  73.8 20.1 %collective-permute-start.9 = (f32[42144]{0:T(1024)S(1)}, f32[42144]{0:T(1024)S(1)}, u32[]{:S(2)}, u32[]{:S(2)}) collective-permute-start(f32[42144]{0:T(1024)S(1)} %slice.129), channel_id=1, source_target_pairs={{0,8},{4,12},{8,0},{12,4},{1,9},{5,13},{9,1},{13,5},{2,10},{6,14},... | collective-permute-start | bytes 505736 | tf_op jit(solution)/shard_map/ppermute | solution.py:150
  86.8 7.1 %collective-permute-start.6 = (f32[42144]{0:T(1024)S(1)}, f32[42144]{0:T(1024)S(1)}, u32[]{:S(2)}, u32[]{:S(2)}) collective-permute-start(f32[42144]{0:T(1024)S(1)} %slice.124), channel_id=1, source_target_pairs={{0,16},{16,0},{1,17},{17,1},{2,18},{18,2},{3,19},{19,3},{4,20},{20... | collective-permute-start | bytes 505736 | tf_op jit(solution)/shard_map/ppermute | solution.py:150
  93.9 7.8 %collective-permute-start.7 = (f32[42144]{0:T(1024)S(1)}, f32[42144]{0:T(1024)S(1)}, u32[]{:S(2)}, u32[]{:S(2)}) collective-permute-start(f32[42144]{0:T(1024)S(1)} %slice_add_fusion.3), channel_id=1, source_target_pairs={{0,8},{4,12},{8,0},{12,4},{1,9},{5,13},{9,1},{13,5},{2,10},{6,14},... | collective-permute-start | bytes 505736 | tf_op jit(solution)/shard_map/ppermute | solution.py:150
  94.1 8.5 %collective-permute-start.10 = (f32[42144]{0:T(1024)S(1)}, f32[42144]{0:T(1024)S(1)}, u32[]{:S(2)}, u32[]{:S(2)}) collective-permute-start(f32[42144]{0:T(1024)S(1)} %slice_add_fusion.2), channel_id=1, source_target_pairs={{0,4},{4,0},{8,12},{12,8},{1,5},{5,1},{9,13},{13,9},{2,6},{6,2},{1... | collective-permute-start | bytes 505736 | tf_op jit(solution)/shard_map/ppermute | solution.py:150
  101.7 5.5 %collective-permute-start.8 = (f32[42144]{0:T(1024)S(1)}, f32[42144]{0:T(1024)S(1)}, u32[]{:S(2)}, u32[]{:S(2)}) collective-permute-start(f32[42144]{0:T(1024)S(1)} %add.143), channel_id=1, source_target_pairs={{0,4},{4,0},{8,12},{12,8},{1,5},{5,1},{9,13},{13,9},{2,6},{6,2},{1... | collective-permute-start | bytes 505736 | tf_op jit(solution)/shard_map/ppermute | solution.py:150
  102.6 5.5 %collective-permute-start.11 = (f32[42144]{0:T(1024)S(1)}, f32[42144]{0:T(1024)S(1)}, u32[]{:S(2)}, u32[]{:S(2)}) collective-permute-start(f32[42144]{0:T(1024)S(1)} %add.146), channel_id=1, source_target_pairs={{0,16},{16,0},{1,17},{17,1},{2,18},{18,2},{3,19},{19,3},{4,20},{20... | collective-permute-start | bytes 505736 | tf_op jit(solution)/shard_map/ppermute | solution.py:150
  (3 other events, 3.0 us)

commit v14 on v11

--- a/solution.py
+++ b/solution.py
@@ -149,7 +149,7 @@
 def butterfly_sum(values, axes):
     flat = flat_pack(values)
     first = butterfly_steps(axes[:1])
-    order_a = first + butterfly_steps(axes[1:])[::-1]
+    order_a = first + butterfly_steps(axes[1:])
     order_b = order_a[len(first) :] + order_a[: len(first)]
     half = flat.shape[0] // 2
     part_a, part_b = flat[:half], flat[half:]

time: 112 us -> 115 us (1.027)
  waiting for transfers between devices: 16.7 us -> 19.3 us
    ppermute x6, waiting for transfers between devices: 8.82 us -> 11.5 us  [butterfly_step(): lax.ppermute(flat, axis, [(i, i ^ step) for i in range(devices)])]
  transfers between devices with their start and end apart: 12 -> 12, of which waited for: 5 -> 6; matrix products, arithmetic and copies ran while one was open for 17% -> 17% of each run, Pallas kernels for 7% -> 7%
where the time goes in v14:
time: 115 us; the launch traced here: 114 us
  matrix products  22.9 us (20%)
  starting transfers between devices  21.9 us (19%)
  waiting for transfers between devices  19.3 us (17%)
  local copies, waits for them, and re-layouts  16.8 us (15%)
  other arithmetic  15.6 us (14%)
  blocking collectives  8.6 us (7%)
  Pallas kernels  7.81 us (7%)
  between operations  1.19 us (1%)
    conv_general_dilated x2, matrix products, depthwise_minor(): lax.conv_general_dilated(padded_t[None], kernel[:, :, None, :], (1, 1), '...  12.6 us
    ppermute x6, waiting for transfers between devices, butterfly_step(): lax.ppermute(flat, axis, [(i, i ^ step) for i in range(devices)])  11.5 us
    dot_general x4, matrix products, contract(): lax.dot_general(left, right, (((dim_left,), (dim_right,)), ((), ())), pre...  9.01 us
    all_gather x1, blocking collectives, gathered_weights(): full = lax.all_gather(packed, 'chan', axis=0, tiled=True)  8.6 us
    ppermute x6, starting transfers between devices, butterfly_step(): lax.ppermute(flat, axis, [(i, i ^ step) for i in range(devices)])  8.57 us
    pallas_call x1, Pallas kernels, kernel_grad_minor(): pl.pallas_call(kernel_grad_body, out_shape=jax.ShapeDtypeStruct((side * s...  7.81 us
    ppermute x2, starting transfers between devices, extended(): before = lax.ppermute(last, axis, up)  6.94 us
    unnamed x36, local copies, waits for them, and re-layouts  5.12 us
  transfers between devices with their start and end apart: 12, of which 6 were waited for; matrix products, arithmetic and copies ran while one was open for 17% of the time, Pallas kernels for 7%

profile of v14, /device:TPU:0, one launch (start us, length us, event | category | flops | bytes accessed | tf_op | source)
XLA Modules:
  0.0 114.2 jit_solution(18086591915847795667)
XLA Ops:
  2.0 3.0 %collective-permute-start = (bf16[192,3,128]{0,2,1:T(8,128)(2,1)S(1)}, bf16[192,3,128]{0,2,1:T(8,128)(2,1)S(1)}, u32[]{:S(2)}, u32[]{:S(2)}) collective-permute-start(bf16[192,3,128]{0,2,1:T(8,128)(2,1)S(1)} %slice_select_fusion.1), channel_id=1, source_target_pairs={{0,16},{16,0},{1,17},{17,1},{2,18},{18,2},{3,19},{19,3},{4,20},{20... | collective-permute-start | bytes 442376 | tf_op jit(solution)/shard_map/ppermute | solution.py:18
  8.1 8.6 %all_gather.3 = bf16[768,387]{1,0:T(8,128)(2,1)S(1)} all-gather(bf16[192,387]{1,0:T(8,128)(2,1)S(1)} %concatenate.27), channel_id=1, replica_groups=mesh['row'=2,'col'=4,'chan'=4] {'chan'}, dimensions={0}, use_global_device_ids=true | all-gather | bytes 743040 | tf_op jit(solution)/shard_map/all_gather | solution.py:170
  18.2 3.5 %collective-permute-start.1 = (bf16[192,14,3]{0,2,1:T(4,128)(2,1)S(1)}, bf16[192,14,3]{0,2,1:T(4,128)(2,1)S(1)}, u32[]{:S(2)}, u32[]{:S(2)}) collective-permute-start(bf16[192,14,3]{0,2,1:T(4,128)(2,1)S(1)} %get-tuple-element.40), channel_id=1, source_target_pairs={{0,4},{4,8},{8,12},{1,5},{5,9},{9,13},{2,6},{6,10},{10,14},{3,7},{... | collective-permute-start | bytes 48392 | tf_op jit(solution)/shard_map/ppermute | solution.py:23
  23.5 3.9 %collective-permute-done.2 = bf16[192,14,3]{0,2,1:T(4,128)(2,1)S(1)} collective-permute-done((bf16[192,14,3]{0,2,1:T(4,128)(2,1)S(1)}, bf16[192,14,3]{0,2,1:T(4,128)(2,1)S(1)}, u32[]{:S(2)}, u32[]{:S(2)}) %collective-permute-start.2) | collective-permute-done | bytes 16160 | tf_op jit(solution)/shard_map/ppermute | solution.py:24
  27.4 1.6 %bitcast_convert_fusion = (f32[14,134,192]{2,1,0:T(8,128)}, bf16[1,14,134,192]{3,2,1,0:T(8,128)(2,1)S(1)}) fusion(bf16[192,14,3]{0,2,1:T(4,128)(2,1)S(1)} %collective-permute-done.2, bf16[192,3,128]{0,2,1:T(8,128)(2,1)S(1)} %get-tuple-element.48, bf16[192,8,128]{0,2,1:T(8,128)(2,1)S(1)} %copy.84, bf16[192,3,128]{0,2,1:T(8,128)(2,1)S(1)} %get-tuple-element.47, ...), kind=kLoop, calls=%fused_computation.32 | loop fusion | flops 3962112 | bytes 2881536 | tf_op jit(solution)/shard_map/convert_element_type | solution.py:211
  29.0 8.4 %fusion.6 = f32[1,8,128,192]{3,0,2,1:T(1,128)S(1)} fusion(bf16[1,14,134,192]{3,2,1,0:T(8,128)(2,1)S(1)} %get-tuple-element.37, f32[7,7,1,192]{3,1,0,2:T(8,128)S(1)} %bitcast.130), kind=kOutput, calls=%fused_computation.13 | convolution fusion | flops 115605504 | bytes 1544448 | tf_op jit(solution)/shard_map/conv_general_dilated | solution.py:180
  38.1 1.9 %copy.89 = f32[1,8,128,192]{2,1,3,0:T(8,128)} copy(f32[1,8,128,192]{3,0,2,1:T(1,128)S(1)} %fusion.6) | data formatting | bytes 1572864 | tf_op jit(solution)/shard_map/conv_general_dilated | solution.py:180
  40.4 2.2 %multiply_convert_fusion = (bf16[1024,768]{0,1:T(8,128)(2,1)S(1)}, f32[1024,768]{0,1:T(8,128)S(1)}) fusion(f32[768]{0:T(1024)S(1)} %fusion.35, f32[24,8,8,128]{3,2,1,0:T(8,128)} %bitcast.125, f32[192]{0:T(256)S(1)} %copy-done.12, f32[192]{0:T(256)S(1)} %copy-done.9, f32[1024]{0:T(1024)S(1)} %get-tuple-element.58, f32[1024]{0:T(1024)S(1)} %get-tuple-element.59, ...), kind=kOutput, calls=%fused_computation.9 | convolution fusion | flops 307888128 | bytes 5913600 | tf_op jit(solution)/shard_map/dot_general | solution.py:53
  43.9 3.8 %fusion.31 = (f32[192]{0:T(256)S(1)}, f32[192]{0:T(256)S(1)}, bf16[8,128,192]{1,0,2:T(8,128)(2,1)}) fusion(bf16[192,8,128]{2,1,0:T(8,128)(2,1)S(1)} %copy-done.1, f32[192]{0:T(256)S(1)} %copy-done.10, f32[192]{0:T(256)S(1)} %copy-done.11, f32[24,8,8,128]{3,2,1,0:T(8,128)S(1)} %copy.118, bf16[192,8,128]{2,1,0:T(8,128)(2,1)S(1)} %copy-done.3), kind=kLoop, calls=%fused_computation.47 | loop fusion | flops 1965696 | bytes 1969152 | tf_op jit(solution)/shard_map/reduce_sum | solution.py:239
  47.7 3.3 %fusion.60 = (bf16[1024,768]{0,1:T(8,128)(2,1)S(1)}, f32[1024,768]{0,1:T(8,128)}) fusion(f32[1024,768]{0,1:T(8,128)S(1)} %get-tuple-element.65, f32[768]{0:T(1024)S(1)} %fusion.35, bf16[1024,192]{0,1:T(8,128)(2,1)S(1)} %fusion.23, bf16[768,387]{1,0:T(8,128)(2,1)S(1)} %all_gather.3), kind=kOutput, calls=%fused_computation.115 | convolution fusion | flops 310640640 | bytes 8654848 | tf_op jit(solution)/shard_map/dot_general | solution.py:53
  53.6 2.3 %fusion.38 = f32[192,192]{1,0:T(8,128)} fusion(bf16[1024,768]{0,1:T(8,128)(2,1)} %copy-done.13, s32[]{:T(128)S(6)} %select_n.45, f32[24,8,8,128]{3,2,1,0:T(8,128)} %bitcast.126, f32[192]{0:T(256)S(1)} %copy-done.12, f32[192]{0:T(256)S(1)} %copy-done.9, f32[1024]{0:T(1024)S(1)} %get-tuple-element.58, f32[1024]{0:T(1024)S(1)} %get-tuple-element.59, ...), kind=kOutput, calls=%fused_computation.66 | convolution fusion | flops 76677120 | bytes 1337604 | tf_op jit(solution)/shard_map/dot_general | solution.py:53
  57.1 1.5 %fusion.57 = (bf16[8,128,192]{2,1,0:T(8,128)(2,1)S(1)}, f32[8,128,192]{2,1,0:T(8,128)}) fusion(f32[8,128]{1,0:T(8,128)S(1)} %broadcast_multiply_fusion, f32[8,128]{1,0:T(8,128)S(1)} %get-tuple-element.60, f32[192]{0:T(256)S(1)} %copy-done.8, f32[1,8,128,192]{3,0,2,1:T(1,128)S(1)} %fusion.6, f32[8,128]{1,0:T(8,128)S(1)} %multiply_bitcast_fusion, ...), kind=kLoop, calls=%fused_computation.113 | loop fusion | flops 1769472 | bytes 2770432 | tf_op jit(solution)/shard_map/convert_element_type | solution.py:292
  60.5 3.9 %collective-permute-done.3 = bf16[3,128,192]{2,1,0:T(8,128)(2,1)S(1)} collective-permute-done((bf16[3,128,192]{2,1,0:T(8,128)(2,1)S(1)}, bf16[3,128,192]{2,1,0:T(8,128)(2,1)S(1)}, u32[]{:S(2)}, u32[]{:S(2)}) %collective-permute-start.3) | collective-permute-done | bytes 147488 | tf_op jit(solution)/shard_map/ppermute | solution.py:18
  65.1 3.5 %collective-permute-start.4 = (bf16[14,3,192]{2,1,0:T(4,128)(2,1)}, bf16[14,3,192]{2,1,0:T(4,128)(2,1)S(1)}, u32[]{:S(2)}, u32[]{:S(2)}) collective-permute-start(bf16[14,3,192]{2,1,0:T(4,128)(2,1)} %get-tuple-element.38), channel_id=1, source_target_pairs={{0,4},{4,8},{8,12},{1,5},{5,9},{9,13},{2,6},{6,10},{10,14},{3,7},{... | collective-permute-start | bytes 48392 | tf_op jit(solution)/shard_map/ppermute | solution.py:23
  68.6 1.5 %collective-permute-start.5 = (bf16[14,3,192]{2,1,0:T(4,128)(2,1)S(1)}, bf16[14,3,192]{2,1,0:T(4,128)(2,1)S(1)}, u32[]{:S(2)}, u32[]{:S(2)}) collective-permute-start(bf16[14,3,192]{2,1,0:T(4,128)(2,1)S(1)} %get-tuple-element.39), channel_id=1, source_target_pairs={{4,0},{8,4},{12,8},{5,1},{9,5},{13,9},{6,2},{10,6},{14,10},{7,3},{... | collective-permute-start | bytes 48392 | tf_op jit(solution)/shard_map/ppermute | solution.py:24
  72.1 1.6 %concatenate.31 = f32[74304]{0:T(1024)S(1)} concatenate(f32[36864]{0:T(1024)S(1)} %reshape.302, f32[192]{0:T(256)S(1)} %dynamic-slice_reduce_fusion, f32[36864]{0:T(1024)S(1)} %reshape.303, f32[192]{0:T(256)S(1)} %get-tuple-element.15, f32[192]{0:T(256)S(1)} %get-tuple-element.16), dimensions={0} | concatenate | bytes 594432 | tf_op jit(solution)/shard_map/concatenate | solution.py:116
  73.8 2.7 %collective-permute-start.9 = (f32[42144]{0:T(1024)S(1)}, f32[42144]{0:T(1024)S(1)}, u32[]{:S(2)}, u32[]{:S(2)}) collective-permute-start(f32[42144]{0:T(1024)S(1)} %slice.129), channel_id=1, source_target_pairs={{0,4},{4,0},{8,12},{12,8},{1,5},{5,1},{9,13},{13,9},{2,6},{6,2},{1... | collective-permute-start | bytes 505736 | tf_op jit(solution)/shard_map/ppermute | solution.py:146
  76.5 7.8 %shard_map.194 = f32[49,8,192]{2,1,0:T(8,128)} custom-call(f32[8,128,192]{2,1,0:T(8,128)} %get-tuple-element.35.d_ref, f32[14,134,192]{2,1,0:T(8,128)} %get-tuple-element.36.p_ref), custom_call_target="tpu_custom_call" | custom-call | tf_op jit(solution)/shard_map/pallas_call | solution.py:107
  87.5 4.2 %fusion.15 = f32[8,8,17,192]{3,1,2,0:T(8,128)S(1)} fusion(bf16[14,1,7,6,192]{4,2,3,0,1:T(8,128)(2,1)S(1)} %slice.122, bf16[14,1,8,17,192]{4,2,3,0,1:T(8,128)(2,1)S(1)} %copy.105, pred[8,17]{0,1:T(8,128)(4,1)S(1)} %copy-done.14, f32[7,7,1,192]{3,1,0,2:T(8,128)S(1)} %bitcast.131), kind=kOutput, calls=%fused_computation.23 | convolution fusion | flops 126007296 | bytes 1830280 | tf_op jit(solution)/shard_map/conv_general_dilated | solution.py:180
  92.9 3.1 %collective-permute-start.10 = (f32[42144]{0:T(1024)S(1)}, f32[42144]{0:T(1024)S(1)}, u32[]{:S(2)}, u32[]{:S(2)}) collective-permute-start(f32[42144]{0:T(1024)S(1)} %slice_add_fusion.2), channel_id=1, source_target_pairs={{0,8},{4,12},{8,0},{12,4},{1,9},{5,13},{9,1},{13,5},{2,10},{6,14},... | collective-permute-start | bytes 505736 | tf_op jit(solution)/shard_map/ppermute | solution.py:146
  96.0 3.5 %collective-permute-done.7 = f32[42144]{0:T(1024)S(1)} collective-permute-done((f32[42144]{0:T(1024)S(1)}, f32[42144]{0:T(1024)S(1)}, u32[]{:S(2)}, u32[]{:S(2)}) %collective-permute-start.7) | collective-permute-done | bytes 168608 | tf_op jit(solution)/shard_map/ppermute | solution.py:146
  100.9 4.8 %collective-permute-done.10 = f32[42144]{0:T(1024)S(1)} collective-permute-done((f32[42144]{0:T(1024)S(1)}, f32[42144]{0:T(1024)S(1)}, u32[]{:S(2)}, u32[]{:S(2)}) %collective-permute-start.10) | collective-permute-done | bytes 168608 | tf_op jit(solution)/shard_map/ppermute | solution.py:146
  105.7 1.6 %collective-permute-start.11 = (f32[42144]{0:T(1024)S(1)}, f32[42144]{0:T(1024)S(1)}, u32[]{:S(2)}, u32[]{:S(2)}) collective-permute-start(f32[42144]{0:T(1024)S(1)} %add.146), channel_id=1, source_target_pairs={{0,16},{16,0},{1,17},{17,1},{2,18},{18,2},{3,19},{19,3},{4,20},{20... | collective-permute-start | bytes 505736 | tf_op jit(solution)/shard_map/ppermute | solution.py:146
  109.3 1.9 %collective-permute-done.11 = f32[42144]{0:T(1024)S(1)} collective-permute-done((f32[42144]{0:T(1024)S(1)}, f32[42144]{0:T(1024)S(1)}, u32[]{:S(2)}, u32[]{:S(2)}) %collective-permute-start.11) | collective-permute-done | bytes 168608 | tf_op jit(solution)/shard_map/ppermute | solution.py:146
  (107 shorter events, 29.2 us)
Async XLA Ops:
  0.6 16.1 %copy-start.1 = (bf16[192,8,128]{2,1,0:T(8,128)(2,1)S(1)}, bf16[192,8,128]{2,1,0:T(8,128)(2,1)}, u32[]{:S(2)}) copy-start(bf16[192,8,128]{2,1,0:T(8,128)(2,1)} %param.21) | copy-start | bytes 1179652
  2.0 16.1 %collective-permute-start = (bf16[192,3,128]{0,2,1:T(8,128)(2,1)S(1)}, bf16[192,3,128]{0,2,1:T(8,128)(2,1)S(1)}, u32[]{:S(2)}, u32[]{:S(2)}) collective-permute-start(bf16[192,3,128]{0,2,1:T(8,128)(2,1)S(1)} %slice_select_fusion.1), channel_id=1, source_target_pairs={{0,16},{16,0},{1,17},{17,1},{2,18},{18,2},{3,19},{19,3},{4,20},{20... | collective-permute-start | bytes 442376 | tf_op jit(solution)/shard_map/ppermute | solution.py:18
  8.1 9.7 %copy-start.10 = (f32[192]{0:T(256)S(1)}, f32[192]{0:T(256)}, u32[]{:S(2)}) copy-start(f32[192]{0:T(256)} %param.20) | copy-start | bytes 2308
  18.0 5.4 %copy-start.7 = (f32[7,7,192]{2,1,0:T(8,128)S(1)}, f32[7,7,192]{2,1,0:T(8,128)}, u32[]{:S(2)}) copy-start(f32[7,7,192]{2,1,0:T(8,128)} %param.12) | copy-start | bytes 112900
  18.2 5.3 %collective-permute-start.1 = (bf16[192,14,3]{0,2,1:T(4,128)(2,1)S(1)}, bf16[192,14,3]{0,2,1:T(4,128)(2,1)S(1)}, u32[]{:S(2)}, u32[]{:S(2)}) collective-permute-start(bf16[192,14,3]{0,2,1:T(4,128)(2,1)S(1)} %get-tuple-element.40), channel_id=1, source_target_pairs={{0,4},{4,8},{8,12},{1,5},{5,9},{9,13},{2,6},{6,10},{10,14},{3,7},{... | collective-permute-start | bytes 48392 | tf_op jit(solution)/shard_map/ppermute | solution.py:23
  21.6 5.8 %collective-permute-start.2 = (bf16[192,14,3]{0,2,1:T(4,128)(2,1)S(1)}, bf16[192,14,3]{0,2,1:T(4,128)(2,1)S(1)}, u32[]{:S(2)}, u32[]{:S(2)}) collective-permute-start(bf16[192,14,3]{0,2,1:T(4,128)(2,1)S(1)} %get-tuple-element.41), channel_id=1, source_target_pairs={{4,0},{8,4},{12,8},{5,1},{9,5},{13,9},{6,2},{10,6},{14,10},{7,3},{... | collective-permute-start | bytes 48392 | tf_op jit(solution)/shard_map/ppermute | solution.py:24
  37.4 2.6 %copy-start.8 = (f32[192]{0:T(256)S(1)}, f32[192]{0:T(256)}, u32[]{:S(2)}) copy-start(f32[192]{0:T(256)} %param.13) | copy-start | bytes 2308
  38.1 2.2 %copy-start.9 = (f32[192]{0:T(256)S(1)}, f32[192]{0:T(256)}, u32[]{:S(2)}) copy-start(f32[192]{0:T(256)} %param.14) | copy-start | bytes 2308
  38.1 2.2 %copy-start.12 = (f32[192]{0:T(256)S(1)}, f32[192]{0:T(256)}, u32[]{:S(2)}) copy-start(f32[192]{0:T(256)} %param.15) | copy-start | bytes 2308
  40.4 2.2 %copy-start.4 = (bf16[768,192]{1,0:T(8,128)(2,1)S(1)}, bf16[768,192]{1,0:T(8,128)(2,1)}, u32[]{:S(2)}) copy-start(bf16[768,192]{1,0:T(8,128)(2,1)} %get-tuple-element.44) | copy-start | bytes 884740
  42.6 1.3 %copy-start.3 = (bf16[192,8,128]{2,1,0:T(8,128)(2,1)S(1)}, bf16[192,8,128]{2,1,0:T(8,128)(2,1)}, u32[]{:S(2)}) copy-start(bf16[192,8,128]{2,1,0:T(8,128)(2,1)} %param.11) | copy-start | bytes 1179652
  42.6 1.3 %copy-start.11 = (f32[192]{0:T(256)S(1)}, f32[192]{0:T(256)}, u32[]{:S(2)}) copy-start(f32[192]{0:T(256)} %param.19) | copy-start | bytes 2308
  47.7 3.3 %copy-start.5 = (bf16[768,192]{1,0:T(8,128)(2,1)S(1)}, bf16[768,192]{1,0:T(8,128)(2,1)}, u32[]{:S(2)}) copy-start(bf16[768,192]{1,0:T(8,128)(2,1)} %get-tuple-element.43) | copy-start | bytes 884740
  55.9 1.2 %copy-start = (f32[1024,192]{1,0:T(8,128)S(1)}, f32[1024,192]{1,0:T(8,128)}, u32[]{:S(2)}) copy-start(f32[1024,192]{1,0:T(8,128)} %copy.99) | copy-start | bytes 2359300
  58.6 5.8 %collective-permute-start.3 = (bf16[3,128,192]{2,1,0:T(8,128)(2,1)S(1)}, bf16[3,128,192]{2,1,0:T(8,128)(2,1)S(1)}, u32[]{:S(2)}, u32[]{:S(2)}) collective-permute-start(bf16[3,128,192]{2,1,0:T(8,128)(2,1)S(1)} %slice_select_fusion), channel_id=1, source_target_pairs={{0,16},{16,0},{1,17},{17,1},{2,18},{18,2},{3,19},{19,3},{4,20},{20... | collective-permute-start | bytes 442376 | tf_op jit(solution)/shard_map/ppermute | solution.py:18
  60.5 10.2 %copy-start.6 = (f32[192,192]{1,0:T(8,128)S(1)}, f32[192,192]{1,0:T(8,128)}, u32[]{:S(2)}) copy-start(f32[192,192]{1,0:T(8,128)} %fusion.38) | copy-start | bytes 442372
  65.1 21.1 %collective-permute-start.4 = (bf16[14,3,192]{2,1,0:T(4,128)(2,1)}, bf16[14,3,192]{2,1,0:T(4,128)(2,1)S(1)}, u32[]{:S(2)}, u32[]{:S(2)}) collective-permute-start(bf16[14,3,192]{2,1,0:T(4,128)(2,1)} %get-tuple-element.38), channel_id=1, source_target_pairs={{0,4},{4,8},{8,12},{1,5},{5,9},{9,13},{2,6},{6,10},{10,14},{3,7},{... | collective-permute-start | bytes 48392 | tf_op jit(solution)/shard_map/ppermute | solution.py:23
  68.6 17.7 %collective-permute-start.5 = (bf16[14,3,192]{2,1,0:T(4,128)(2,1)S(1)}, bf16[14,3,192]{2,1,0:T(4,128)(2,1)S(1)}, u32[]{:S(2)}, u32[]{:S(2)}) collective-permute-start(bf16[14,3,192]{2,1,0:T(4,128)(2,1)S(1)} %get-tuple-element.39), channel_id=1, source_target_pairs={{4,0},{8,4},{12,8},{5,1},{9,5},{13,9},{6,2},{10,6},{14,10},{7,3},{... | collective-permute-start | bytes 48392 | tf_op jit(solution)/shard_map/ppermute | solution.py:24
  73.8 19.0 %collective-permute-start.9 = (f32[42144]{0:T(1024)S(1)}, f32[42144]{0:T(1024)S(1)}, u32[]{:S(2)}, u32[]{:S(2)}) collective-permute-start(f32[42144]{0:T(1024)S(1)} %slice.129), channel_id=1, source_target_pairs={{0,4},{4,0},{8,12},{12,8},{1,5},{5,1},{9,13},{13,9},{2,6},{6,2},{1... | collective-permute-start | bytes 505736 | tf_op jit(solution)/shard_map/ppermute | solution.py:146
  85.6 7.1 %collective-permute-start.6 = (f32[42144]{0:T(1024)S(1)}, f32[42144]{0:T(1024)S(1)}, u32[]{:S(2)}, u32[]{:S(2)}) collective-permute-start(f32[42144]{0:T(1024)S(1)} %slice.124), channel_id=1, source_target_pairs={{0,16},{16,0},{1,17},{17,1},{2,18},{18,2},{3,19},{19,3},{4,20},{20... | collective-permute-start | bytes 505736 | tf_op jit(solution)/shard_map/ppermute | solution.py:146
  92.7 6.8 %collective-permute-start.7 = (f32[42144]{0:T(1024)S(1)}, f32[42144]{0:T(1024)S(1)}, u32[]{:S(2)}, u32[]{:S(2)}) collective-permute-start(f32[42144]{0:T(1024)S(1)} %slice_add_fusion.3), channel_id=1, source_target_pairs={{0,4},{4,0},{8,12},{12,8},{1,5},{5,1},{9,13},{13,9},{2,6},{6,2},{1... | collective-permute-start | bytes 505736 | tf_op jit(solution)/shard_map/ppermute | solution.py:146
  92.9 12.7 %collective-permute-start.10 = (f32[42144]{0:T(1024)S(1)}, f32[42144]{0:T(1024)S(1)}, u32[]{:S(2)}, u32[]{:S(2)}) collective-permute-start(f32[42144]{0:T(1024)S(1)} %slice_add_fusion.2), channel_id=1, source_target_pairs={{0,8},{4,12},{8,0},{12,4},{1,9},{5,13},{9,1},{13,5},{2,10},{6,14},... | collective-permute-start | bytes 505736 | tf_op jit(solution)/shard_map/ppermute | solution.py:146
  99.5 9.1 %collective-permute-start.8 = (f32[42144]{0:T(1024)S(1)}, f32[42144]{0:T(1024)S(1)}, u32[]{:S(2)}, u32[]{:S(2)}) collective-permute-start(f32[42144]{0:T(1024)S(1)} %add.143), channel_id=1, source_target_pairs={{0,8},{4,12},{8,0},{12,4},{1,9},{5,13},{9,1},{13,5},{2,10},{6,14},... | collective-permute-start | bytes 505736 | tf_op jit(solution)/shard_map/ppermute | solution.py:146
  105.7 5.5 %collective-permute-start.11 = (f32[42144]{0:T(1024)S(1)}, f32[42144]{0:T(1024)S(1)}, u32[]{:S(2)}, u32[]{:S(2)}) collective-permute-start(f32[42144]{0:T(1024)S(1)} %add.146), channel_id=1, source_target_pairs={{0,16},{16,0},{1,17},{17,1},{2,18},{18,2},{3,19},{19,3},{4,20},{20... | collective-permute-start | bytes 505736 | tf_op jit(solution)/shard_map/ppermute | solution.py:146
  (3 other events, 3.0 us)

commit v15 on v11

--- a/solution.py
+++ b/solution.py
@@ -246,6 +246,7 @@
     d_pre_own = lax.dynamic_slice_in_dim(d_pre, own * share, share, axis=1)
     grad_w_out = contract(hidden_own, g_out, 0, 0)
     grad_b_in = jnp.sum(d_pre_own, axis=0)
+    grad_b_in, g_pre = lax.optimization_barrier((grad_b_in, g_pre))
     grad_w_in = contract(normalized_output, g_pre_own, 0, 0)
     dn_partials = lax.dot_general(
         g_pre.reshape(pixel_count, blocks, share),

time: 112 us -> 109 us (0.973)
  matrix products: 22.9 us -> 20.1 us
    dot_general x4, matrix products: 9.01 us -> 6.16 us  [contract(): lax.dot_general(left, right, (((dim_left,), (dim_right,)), ((), ())), pre...]
    slice x2, local copies, waits for them, and re-layouts: 0.12 us -> 1.46 us  [butterfly_sum(): part_a, part_b = (flat[:half], flat[half:])]
    reduce_sum x1, other arithmetic: 1.26 us -> 0.12 us  [shards(): grad_b_in = jnp.sum(d_pre_own, axis=0)]
  transfers between devices with their start and end apart: 12 -> 12, of which waited for: 5 -> 5; matrix products, arithmetic and copies ran while one was open for 17% -> 19% of each run, Pallas kernels for 7% -> 7%
where the time goes in v15:
time: 109 us
  starting transfers between devices  21.1 us (19%)
  matrix products  20.1 us (18%)
  local copies, waits for them, and re-layouts  17.7 us (16%)
  waiting for transfers between devices  16.7 us (15%)
  other arithmetic  15.4 us (14%)
  blocking collectives  8.6 us (8%)
  Pallas kernels  7.83 us (7%)
  between operations  1.23 us (1%)
    conv_general_dilated x2, matrix products, depthwise_minor(): lax.conv_general_dilated(padded_t[None], kernel[:, :, None, :], (1, 1), '...  12.6 us
    ppermute x6, waiting for transfers between devices, butterfly_step(): lax.ppermute(flat, axis, [(i, i ^ step) for i in range(devices)])  8.82 us
    all_gather x1, blocking collectives, gathered_weights(): full = lax.all_gather(packed, 'chan', axis=0, tiled=True)  8.6 us
    ppermute x6, starting transfers between devices, butterfly_step(): lax.ppermute(flat, axis, [(i, i ^ step) for i in range(devices)])  7.85 us
    pallas_call x1, Pallas kernels, kernel_grad_minor(): pl.pallas_call(kernel_grad_body, out_shape=jax.ShapeDtypeStruct((side * s...  7.83 us
    ppermute x2, starting transfers between devices, extended(): before = lax.ppermute(last, axis, up)  6.97 us
    dot_general x4, matrix products, contract(): lax.dot_general(left, right, (((dim_left,), (dim_right,)), ((), ())), pre...  6.16 us
    unnamed x36, local copies, waits for them, and re-layouts  4.73 us
  transfers between devices with their start and end apart: 12, of which 5 were waited for; matrix products, arithmetic and copies ran while one was open for 19% of the time, Pallas kernels for 7%

profile of v15, /device:TPU:0, one launch (start us, length us, event | category | flops | bytes accessed | tf_op | source)
XLA Modules:
  0.0 108.7 jit_solution(13987143422635070149)
XLA Ops:
  0.7 1.3 %copy.84 = bf16[192,8,128]{0,2,1:T(8,128)(2,1)S(1)} copy(bf16[192,8,128]{2,1,0:T(8,128)(2,1)} %param.11) | data formatting | bytes 786432 | tf_op args[0]
  2.7 3.0 %collective-permute-start = (bf16[192,3,128]{0,2,1:T(8,128)(2,1)}, bf16[192,3,128]{0,2,1:T(8,128)(2,1)S(1)}, u32[]{:S(2)}, u32[]{:S(2)}) collective-permute-start(bf16[192,3,128]{0,2,1:T(8,128)(2,1)} %slice_select_fusion.1), channel_id=1, source_target_pairs={{0,16},{16,0},{1,17},{17,1},{2,18},{18,2},{3,19},{19,3},{4,20},{20... | collective-permute-start | bytes 442376 | tf_op jit(solution)/shard_map/ppermute | solution.py:18
  8.7 8.6 %all_gather.3 = bf16[768,387]{1,0:T(8,128)(2,1)S(1)} all-gather(bf16[192,387]{1,0:T(8,128)(2,1)S(1)} %concatenate.27), channel_id=1, replica_groups=mesh['row'=2,'col'=4,'chan'=4] {'chan'}, dimensions={0}, use_global_device_ids=true | all-gather | bytes 743040 | tf_op jit(solution)/shard_map/all_gather | solution.py:170
  18.8 3.5 %collective-permute-start.1 = (bf16[192,14,3]{0,2,1:T(4,128)(2,1)S(1)}, bf16[192,14,3]{0,2,1:T(4,128)(2,1)S(1)}, u32[]{:S(2)}, u32[]{:S(2)}) collective-permute-start(bf16[192,14,3]{0,2,1:T(4,128)(2,1)S(1)} %get-tuple-element.44), channel_id=1, source_target_pairs={{0,4},{4,8},{8,12},{1,5},{5,9},{9,13},{2,6},{6,10},{10,14},{3,7},{... | collective-permute-start | bytes 48392 | tf_op jit(solution)/shard_map/ppermute | solution.py:23
  24.1 3.9 %collective-permute-done.2 = bf16[192,14,3]{0,2,1:T(4,128)(2,1)S(1)} collective-permute-done((bf16[192,14,3]{0,2,1:T(4,128)(2,1)S(1)}, bf16[192,14,3]{0,2,1:T(4,128)(2,1)S(1)}, u32[]{:S(2)}, u32[]{:S(2)}) %collective-permute-start.2) | collective-permute-done | bytes 16160 | tf_op jit(solution)/shard_map/ppermute | solution.py:24
  28.0 1.6 %bitcast_convert_fusion = (f32[14,134,192]{2,1,0:T(8,128)}, bf16[1,14,134,192]{3,2,1,0:T(8,128)(2,1)S(1)}) fusion(bf16[192,14,3]{0,2,1:T(4,128)(2,1)S(1)} %collective-permute-done.2, bf16[192,3,128]{0,2,1:T(8,128)(2,1)S(1)} %get-tuple-element.52, bf16[192,8,128]{0,2,1:T(8,128)(2,1)S(1)} %copy.84, bf16[192,3,128]{0,2,1:T(8,128)(2,1)S(1)} %get-tuple-element.51, ...), kind=kLoop, calls=%fused_computation.32 | loop fusion | flops 3962112 | bytes 2881536 | tf_op jit(solution)/shard_map/convert_element_type | solution.py:211
  29.6 8.4 %fusion.6 = f32[1,8,128,192]{3,0,2,1:T(1,128)S(1)} fusion(bf16[1,14,134,192]{3,2,1,0:T(8,128)(2,1)S(1)} %get-tuple-element.41, f32[7,7,1,192]{3,1,0,2:T(8,128)S(1)} %bitcast.130), kind=kOutput, calls=%fused_computation.13 | convolution fusion | flops 115605504 | bytes 1544448 | tf_op jit(solution)/shard_map/conv_general_dilated | solution.py:180
  38.7 1.8 %copy.89 = f32[1,8,128,192]{2,1,3,0:T(8,128)} copy(f32[1,8,128,192]{3,0,2,1:T(1,128)S(1)} %fusion.6) | data formatting | bytes 1572864 | tf_op jit(solution)/shard_map/conv_general_dilated | solution.py:180
  40.9 2.2 %multiply_convert_fusion = (bf16[1024,768]{0,1:T(8,128)(2,1)S(1)}, f32[1024,768]{0,1:T(8,128)S(1)}) fusion(f32[768]{0:T(1024)S(1)} %fusion.35, f32[24,8,8,128]{3,2,1,0:T(8,128)} %bitcast.125, f32[192]{0:T(256)S(1)} %copy-done.13, f32[192]{0:T(256)S(1)} %copy-done.10, f32[1024]{0:T(1024)S(1)} %get-tuple-element.62, f32[1024]{0:T(1024)S(1)} %get-tuple-element.63, ...), kind=kOutput, calls=%fused_computation.9 | convolution fusion | flops 307888128 | bytes 5913600 | tf_op jit(solution)/shard_map/dot_general | solution.py:53
  44.4 3.8 %fusion.31 = (f32[192]{0:T(256)S(1)}, f32[192]{0:T(256)S(1)}, bf16[8,128,192]{1,0,2:T(8,128)(2,1)}) fusion(bf16[192,8,128]{2,1,0:T(8,128)(2,1)S(1)} %copy-done.1, f32[192]{0:T(256)S(1)} %copy-done.11, f32[192]{0:T(256)S(1)} %copy-done.12, f32[24,8,8,128]{3,2,1,0:T(8,128)S(1)} %copy.118, bf16[192,8,128]{2,1,0:T(8,128)(2,1)S(1)} %copy-done.3), kind=kLoop, calls=%fused_computation.47 | loop fusion | flops 1965696 | bytes 1969152 | tf_op jit(solution)/shard_map/reduce_sum | solution.py:239
  48.2 1.6 %fusion.60 = (bf16[1024,768]{0,1:T(8,128)(2,1)S(1)}, f32[1024,768]{0,1:T(8,128)S(1)}) fusion(f32[1024,768]{0,1:T(8,128)S(1)} %get-tuple-element.69, f32[768]{0:T(1024)S(1)} %fusion.35, bf16[1024,192]{0,1:T(8,128)(2,1)S(1)} %fusion.23, bf16[768,387]{1,0:T(8,128)(2,1)S(1)} %all_gather.3), kind=kOutput, calls=%fused_computation.115 | convolution fusion | flops 310640640 | bytes 8654848 | tf_op jit(solution)/shard_map/dot_general | solution.py:53
  52.0 1.3 %copy.99 = f32[1024,192]{1,0:T(8,128)} copy(f32[1024,192]{0,1:T(8,128)S(1)} %get-tuple-element.35) | data formatting | bytes 1572864 | tf_op jit(solution)/shard_map/reduce_sum | solution.py:257
  54.5 1.5 %fusion.57 = (bf16[8,128,192]{2,1,0:T(8,128)(2,1)S(1)}, f32[8,128,192]{2,1,0:T(8,128)}) fusion(f32[8,128]{1,0:T(8,128)S(1)} %broadcast_multiply_fusion, f32[8,128]{1,0:T(8,128)S(1)} %get-tuple-element.64, f32[192]{0:T(256)S(1)} %copy-done.9, f32[1,8,128,192]{3,0,2,1:T(1,128)S(1)} %fusion.6, f32[8,128]{1,0:T(8,128)S(1)} %multiply_bitcast_fusion, ...), kind=kLoop, calls=%fused_computation.113 | loop fusion | flops 1769472 | bytes 2770432 | tf_op jit(solution)/shard_map/convert_element_type | solution.py:293
  57.9 3.9 %collective-permute-done.3 = bf16[3,128,192]{2,1,0:T(8,128)(2,1)S(1)} collective-permute-done((bf16[3,128,192]{2,1,0:T(8,128)(2,1)S(1)}, bf16[3,128,192]{2,1,0:T(8,128)(2,1)S(1)}, u32[]{:S(2)}, u32[]{:S(2)}) %collective-permute-start.3) | collective-permute-done | bytes 147488 | tf_op jit(solution)/shard_map/ppermute | solution.py:18
  61.9 3.5 %collective-permute-start.4 = (bf16[14,3,192]{2,1,0:T(4,128)(2,1)S(1)}, bf16[14,3,192]{2,1,0:T(4,128)(2,1)S(1)}, u32[]{:S(2)}, u32[]{:S(2)}) collective-permute-start(bf16[14,3,192]{2,1,0:T(4,128)(2,1)S(1)} %get-tuple-element.42), channel_id=1, source_target_pairs={{0,4},{4,8},{8,12},{1,5},{5,9},{9,13},{2,6},{6,10},{10,14},{3,7},{... | collective-permute-start | bytes 48392 | tf_op jit(solution)/shard_map/ppermute | solution.py:23
  65.4 1.5 %collective-permute-start.5 = (bf16[14,3,192]{2,1,0:T(4,128)(2,1)S(1)}, bf16[14,3,192]{2,1,0:T(4,128)(2,1)S(1)}, u32[]{:S(2)}, u32[]{:S(2)}) collective-permute-start(bf16[14,3,192]{2,1,0:T(4,128)(2,1)S(1)} %get-tuple-element.43), channel_id=1, source_target_pairs={{4,0},{8,4},{12,8},{5,1},{9,5},{13,9},{6,2},{10,6},{14,10},{7,3},{... | collective-permute-start | bytes 48392 | tf_op jit(solution)/shard_map/ppermute | solution.py:24
  67.6 1.6 %concatenate.31 = f32[74304]{0:T(1024)S(1)} concatenate(f32[36864]{0:T(1024)S(1)} %reshape.302, f32[192]{0:T(256)S(1)} %dynamic-slice_reduce_fusion, f32[36864]{0:T(1024)S(1)} %reshape.303, f32[192]{0:T(256)S(1)} %get-tuple-element.19, f32[192]{0:T(256)S(1)} %get-tuple-element.20), dimensions={0} | concatenate | bytes 594432 | tf_op jit(solution)/shard_map/concatenate | solution.py:116
  70.0 3.7 %collective-permute-start.9 = (f32[42144]{0:T(1024)}, f32[42144]{0:T(1024)S(1)}, u32[]{:S(2)}, u32[]{:S(2)}) collective-permute-start(f32[42144]{0:T(1024)} %slice.129), channel_id=1, source_target_pairs={{0,8},{4,12},{8,0},{12,4},{1,9},{5,13},{9,1},{13,5},{2,10},{6,14},... | collective-permute-start | bytes 505736 | tf_op jit(solution)/shard_map/ppermute | solution.py:146
  73.7 7.8 %shard_map.194 = f32[49,8,192]{2,1,0:T(8,128)} custom-call(f32[8,128,192]{2,1,0:T(8,128)} %get-tuple-element.39.d_ref, f32[14,134,192]{2,1,0:T(8,128)} %get-tuple-element.40.p_ref), custom_call_target="tpu_custom_call" | custom-call | tf_op jit(solution)/shard_map/pallas_call | solution.py:107
  85.2 4.2 %fusion.15 = f32[8,8,17,192]{3,1,2,0:T(8,128)S(1)} fusion(bf16[14,1,7,6,192]{4,2,3,0,1:T(8,128)(2,1)S(1)} %slice.122, bf16[14,1,8,17,192]{4,2,3,0,1:T(8,128)(2,1)S(1)} %copy.105, pred[8,17]{0,1:T(8,128)(4,1)S(1)} %copy-done.14, f32[7,7,1,192]{3,1,0,2:T(8,128)S(1)} %bitcast.131), kind=kOutput, calls=%fused_computation.23 | convolution fusion | flops 126007296 | bytes 1830280 | tf_op jit(solution)/shard_map/conv_general_dilated | solution.py:180
  91.6 1.9 %collective-permute-start.10 = (f32[42144]{0:T(1024)S(1)}, f32[42144]{0:T(1024)S(1)}, u32[]{:S(2)}, u32[]{:S(2)}) collective-permute-start(f32[42144]{0:T(1024)S(1)} %slice_add_fusion.2), channel_id=1, source_target_pairs={{0,4},{4,0},{8,12},{12,8},{1,5},{5,1},{9,13},{13,9},{2,6},{6,2},{1... | collective-permute-start | bytes 505736 | tf_op jit(solution)/shard_map/ppermute | solution.py:146
  93.6 5.6 %collective-permute-done.7 = f32[42144]{0:T(1024)S(1)} collective-permute-done((f32[42144]{0:T(1024)S(1)}, f32[42144]{0:T(1024)S(1)}, u32[]{:S(2)}, u32[]{:S(2)}) %collective-permute-start.7) | collective-permute-done | bytes 168608 | tf_op jit(solution)/shard_map/ppermute | solution.py:146
  100.2 1.6 %collective-permute-start.11 = (f32[42144]{0:T(1024)S(1)}, f32[42144]{0:T(1024)S(1)}, u32[]{:S(2)}, u32[]{:S(2)}) collective-permute-start(f32[42144]{0:T(1024)S(1)} %add.146), channel_id=1, source_target_pairs={{0,16},{16,0},{1,17},{17,1},{2,18},{18,2},{3,19},{19,3},{4,20},{20... | collective-permute-start | bytes 505736 | tf_op jit(solution)/shard_map/ppermute | solution.py:146
  101.8 2.9 %collective-permute-done.8 = f32[42144]{0:T(1024)S(1)} collective-permute-done((f32[42144]{0:T(1024)S(1)}, f32[42144]{0:T(1024)S(1)}, u32[]{:S(2)}, u32[]{:S(2)}) %collective-permute-start.8) | collective-permute-done | bytes 168608 | tf_op jit(solution)/shard_map/ppermute | solution.py:146
  (107 shorter events, 26.8 us)
Async XLA Ops:
  0.6 16.7 %copy-start.1 = (bf16[192,8,128]{2,1,0:T(8,128)(2,1)S(1)}, bf16[192,8,128]{2,1,0:T(8,128)(2,1)}, u32[]{:S(2)}) copy-start(bf16[192,8,128]{2,1,0:T(8,128)(2,1)} %param.21) | copy-start | bytes 1179652
  2.7 16.0 %collective-permute-start = (bf16[192,3,128]{0,2,1:T(8,128)(2,1)}, bf16[192,3,128]{0,2,1:T(8,128)(2,1)S(1)}, u32[]{:S(2)}, u32[]{:S(2)}) collective-permute-start(bf16[192,3,128]{0,2,1:T(8,128)(2,1)} %slice_select_fusion.1), channel_id=1, source_target_pairs={{0,16},{16,0},{1,17},{17,1},{2,18},{18,2},{3,19},{19,3},{4,20},{20... | collective-permute-start | bytes 442376 | tf_op jit(solution)/shard_map/ppermute | solution.py:18
  8.7 9.7 %copy-start.11 = (f32[192]{0:T(256)S(1)}, f32[192]{0:T(256)}, u32[]{:S(2)}) copy-start(f32[192]{0:T(256)} %param.20) | copy-start | bytes 2308
  18.6 5.4 %copy-start.8 = (f32[7,7,192]{2,1,0:T(8,128)S(1)}, f32[7,7,192]{2,1,0:T(8,128)}, u32[]{:S(2)}) copy-start(f32[7,7,192]{2,1,0:T(8,128)} %param.12) | copy-start | bytes 112900
  18.8 5.3 %collective-permute-start.1 = (bf16[192,14,3]{0,2,1:T(4,128)(2,1)S(1)}, bf16[192,14,3]{0,2,1:T(4,128)(2,1)S(1)}, u32[]{:S(2)}, u32[]{:S(2)}) collective-permute-start(bf16[192,14,3]{0,2,1:T(4,128)(2,1)S(1)} %get-tuple-element.44), channel_id=1, source_target_pairs={{0,4},{4,8},{8,12},{1,5},{5,9},{9,13},{2,6},{6,10},{10,14},{3,7},{... | collective-permute-start | bytes 48392 | tf_op jit(solution)/shard_map/ppermute | solution.py:23
  22.3 5.8 %collective-permute-start.2 = (bf16[192,14,3]{0,2,1:T(4,128)(2,1)S(1)}, bf16[192,14,3]{0,2,1:T(4,128)(2,1)S(1)}, u32[]{:S(2)}, u32[]{:S(2)}) collective-permute-start(bf16[192,14,3]{0,2,1:T(4,128)(2,1)S(1)} %get-tuple-element.45), channel_id=1, source_target_pairs={{4,0},{8,4},{12,8},{5,1},{9,5},{13,9},{6,2},{10,6},{14,10},{7,3},{... | collective-permute-start | bytes 48392 | tf_op jit(solution)/shard_map/ppermute | solution.py:24
  38.0 2.5 %copy-start.9 = (f32[192]{0:T(256)S(1)}, f32[192]{0:T(256)}, u32[]{:S(2)}) copy-start(f32[192]{0:T(256)} %param.13) | copy-start | bytes 2308
  38.7 2.2 %copy-start.10 = (f32[192]{0:T(256)S(1)}, f32[192]{0:T(256)}, u32[]{:S(2)}) copy-start(f32[192]{0:T(256)} %param.14) | copy-start | bytes 2308
  38.7 2.2 %copy-start.13 = (f32[192]{0:T(256)S(1)}, f32[192]{0:T(256)}, u32[]{:S(2)}) copy-start(f32[192]{0:T(256)} %param.15) | copy-start | bytes 2308
  40.9 2.2 %copy-start.4 = (bf16[768,192]{1,0:T(8,128)(2,1)S(1)}, bf16[768,192]{1,0:T(8,128)(2,1)}, u32[]{:S(2)}) copy-start(bf16[768,192]{1,0:T(8,128)(2,1)} %get-tuple-element.48) | copy-start | bytes 884740
  43.1 1.3 %copy-start.3 = (bf16[192,8,128]{2,1,0:T(8,128)(2,1)S(1)}, bf16[192,8,128]{2,1,0:T(8,128)(2,1)}, u32[]{:S(2)}) copy-start(bf16[192,8,128]{2,1,0:T(8,128)(2,1)} %param.11) | copy-start | bytes 1179652
  43.1 1.3 %copy-start.12 = (f32[192]{0:T(256)S(1)}, f32[192]{0:T(256)}, u32[]{:S(2)}) copy-start(f32[192]{0:T(256)} %param.19) | copy-start | bytes 2308
  48.2 1.7 %copy-start.5 = (f32[1,8,128,192]{2,1,3,0:T(8,128)S(1)}, f32[1,8,128,192]{2,1,3,0:T(8,128)}, u32[]{:S(2)}) copy-start(f32[1,8,128,192]{2,1,3,0:T(8,128)} %copy.89) | copy-start | bytes 2359300
  49.8 1.2 %copy-start.6 = (bf16[768,192]{1,0:T(8,128)(2,1)S(1)}, bf16[768,192]{1,0:T(8,128)(2,1)}, u32[]{:S(2)}) copy-start(bf16[768,192]{1,0:T(8,128)(2,1)} %get-tuple-element.47) | copy-start | bytes 884740
  56.0 5.8 %collective-permute-start.3 = (bf16[3,128,192]{2,1,0:T(8,128)(2,1)S(1)}, bf16[3,128,192]{2,1,0:T(8,128)(2,1)S(1)}, u32[]{:S(2)}, u32[]{:S(2)}) collective-permute-start(bf16[3,128,192]{2,1,0:T(8,128)(2,1)S(1)} %slice_select_fusion), channel_id=1, source_target_pairs={{0,16},{16,0},{1,17},{17,1},{2,18},{18,2},{3,19},{19,3},{4,20},{20... | collective-permute-start | bytes 442376 | tf_op jit(solution)/shard_map/ppermute | solution.py:18
  57.9 9.6 %copy-start.7 = (f32[192,192]{1,0:T(8,128)S(1)}, f32[192,192]{1,0:T(8,128)}, u32[]{:S(2)}) copy-start(f32[192,192]{1,0:T(8,128)} %fusion.38) | copy-start | bytes 442372
  61.9 22.1 %collective-permute-start.4 = (bf16[14,3,192]{2,1,0:T(4,128)(2,1)S(1)}, bf16[14,3,192]{2,1,0:T(4,128)(2,1)S(1)}, u32[]{:S(2)}, u32[]{:S(2)}) collective-permute-start(bf16[14,3,192]{2,1,0:T(4,128)(2,1)S(1)} %get-tuple-element.42), channel_id=1, source_target_pairs={{0,4},{4,8},{8,12},{1,5},{5,9},{9,13},{2,6},{6,10},{10,14},{3,7},{... | collective-permute-start | bytes 48392 | tf_op jit(solution)/shard_map/ppermute | solution.py:23
  65.4 18.6 %collective-permute-start.5 = (bf16[14,3,192]{2,1,0:T(4,128)(2,1)S(1)}, bf16[14,3,192]{2,1,0:T(4,128)(2,1)S(1)}, u32[]{:S(2)}, u32[]{:S(2)}) collective-permute-start(bf16[14,3,192]{2,1,0:T(4,128)(2,1)S(1)} %get-tuple-element.43), channel_id=1, source_target_pairs={{4,0},{8,4},{12,8},{5,1},{9,5},{13,9},{6,2},{10,6},{14,10},{7,3},{... | collective-permute-start | bytes 48392 | tf_op jit(solution)/shard_map/ppermute | solution.py:24
  70.0 21.5 %collective-permute-start.9 = (f32[42144]{0:T(1024)}, f32[42144]{0:T(1024)S(1)}, u32[]{:S(2)}, u32[]{:S(2)}) collective-permute-start(f32[42144]{0:T(1024)} %slice.129), channel_id=1, source_target_pairs={{0,8},{4,12},{8,0},{12,4},{1,9},{5,13},{9,1},{13,5},{2,10},{6,14},... | collective-permute-start | bytes 505736 | tf_op jit(solution)/shard_map/ppermute | solution.py:146
  83.5 7.0 %collective-permute-start.6 = (f32[42144]{0:T(1024)}, f32[42144]{0:T(1024)}, u32[]{:S(2)}, u32[]{:S(2)}) collective-permute-start(f32[42144]{0:T(1024)} %slice.124), channel_id=1, source_target_pairs={{0,16},{16,0},{1,17},{17,1},{2,18},{18,2},{3,19},{19,3},{4,20},{20... | collective-permute-start | bytes 505736 | tf_op jit(solution)/shard_map/ppermute | solution.py:146
  91.4 7.8 %collective-permute-start.7 = (f32[42144]{0:T(1024)S(1)}, f32[42144]{0:T(1024)S(1)}, u32[]{:S(2)}, u32[]{:S(2)}) collective-permute-start(f32[42144]{0:T(1024)S(1)} %slice_add_fusion.3), channel_id=1, source_target_pairs={{0,8},{4,12},{8,0},{12,4},{1,9},{5,13},{9,1},{13,5},{2,10},{6,14},... | collective-permute-start | bytes 505736 | tf_op jit(solution)/shard_map/ppermute | solution.py:146
  91.6 8.5 %collective-permute-start.10 = (f32[42144]{0:T(1024)S(1)}, f32[42144]{0:T(1024)S(1)}, u32[]{:S(2)}, u32[]{:S(2)}) collective-permute-start(f32[42144]{0:T(1024)S(1)} %slice_add_fusion.2), channel_id=1, source_target_pairs={{0,4},{4,0},{8,12},{12,8},{1,5},{5,1},{9,13},{13,9},{2,6},{6,2},{1... | collective-permute-start | bytes 505736 | tf_op jit(solution)/shard_map/ppermute | solution.py:146
  99.2 5.5 %collective-permute-start.8 = (f32[42144]{0:T(1024)S(1)}, f32[42144]{0:T(1024)S(1)}, u32[]{:S(2)}, u32[]{:S(2)}) collective-permute-start(f32[42144]{0:T(1024)S(1)} %add.143), channel_id=1, source_target_pairs={{0,4},{4,0},{8,12},{12,8},{1,5},{5,1},{9,13},{13,9},{2,6},{6,2},{1... | collective-permute-start | bytes 505736 | tf_op jit(solution)/shard_map/ppermute | solution.py:146
  100.2 5.5 %collective-permute-start.11 = (f32[42144]{0:T(1024)S(1)}, f32[42144]{0:T(1024)S(1)}, u32[]{:S(2)}, u32[]{:S(2)}) collective-permute-start(f32[42144]{0:T(1024)S(1)} %add.146), channel_id=1, source_target_pairs={{0,16},{16,0},{1,17},{17,1},{2,18},{18,2},{3,19},{19,3},{4,20},{20... | collective-permute-start | bytes 505736 | tf_op jit(solution)/shard_map/ppermute | solution.py:146
  (3 other events, 3.1 us)

commit v16 on v15

--- a/solution.py
+++ b/solution.py
@@ -146,12 +146,12 @@
     return flat + lax.ppermute(flat, axis, [(i, i ^ step) for i in range(devices)])
 
 
-def butterfly_sum(values, axes):
+def butterfly_sum(values, axes, late_count):
     flat = flat_pack(values)
     first = butterfly_steps(axes[:1])
     order_a = first + butterfly_steps(axes[1:])[::-1]
     order_b = order_a[len(first) :] + order_a[: len(first)]
-    half = flat.shape[0] // 2
+    half = sum(v.size for v in values[:late_count])
     part_a, part_b = flat[:half], flat[half:]
     for step_a, step_b in zip(order_a, order_b):
         part_a, part_b = butterfly_step(part_a, *step_a), butterfly_step(part_b, *step_b)
@@ -289,6 +289,7 @@
             grad_layer_scale,
         ),
         ("row", "col"),
+        4,
     )
     d_padded = extended(d_t.astype(jnp.bfloat16), (("row", 0), ("col", 1)), 3).astype(jnp.float32)
     grad_feature_t = (

time: 109 us -> 107 us (0.982)
  waiting for transfers between devices: 16.7 us -> 19.7 us
  starting transfers between devices: 21.1 us -> 18.4 us
  other arithmetic: 15.4 us -> 13.8 us
  local copies, waits for them, and re-layouts: 17.7 us -> 16.1 us
    ppermute x6, waiting for transfers between devices: 8.82 us -> 13.1 us  [butterfly_step(): lax.ppermute(flat, axis, [(i, i ^ step) for i in range(devices)])]
    ppermute x2, waiting for transfers between devices: 3.92 us -> 2.03 us  [extended(): got = lax.ppermute(jnp.where(first, last, leading), axis, [(0, 1), (1, 0)])]
    ppermute x6, starting transfers between devices: 7.85 us -> 6.36 us  [butterfly_step(): lax.ppermute(flat, axis, [(i, i ^ step) for i in range(devices)])]
    slice x2 -> x0, local copies, waits for them, and re-layouts: 1.46 us -> none  [butterfly_sum(): part_a, part_b = (flat[:half], flat[half:])]
    ppermute x2, starting transfers between devices: 6.97 us -> 5.85 us  [extended(): before = lax.ppermute(last, axis, up)]
  transfers between devices with their start and end apart: 12 -> 12, of which waited for: 5 -> 8; matrix products, arithmetic and copies ran while one was open for 19% -> 17% of each run, Pallas kernels for 7% -> 0%
where the time goes in v16:
time: 107 us; the launch traced here: 106 us
  matrix products  20.5 us (19%)
  waiting for transfers between devices  19.7 us (18%)
  starting transfers between devices  18.4 us (17%)
  local copies, waits for them, and re-layouts  16.1 us (15%)
  other arithmetic  13.8 us (13%)
  blocking collectives  8.6 us (8%)
  Pallas kernels  8.06 us (8%)
  between operations  1.17 us (1%)
    ppermute x6, waiting for transfers between devices, butterfly_step(): lax.ppermute(flat, axis, [(i, i ^ step) for i in range(devices)])  13.1 us
    conv_general_dilated x2, matrix products, depthwise_minor(): lax.conv_general_dilated(padded_t[None], kernel[:, :, None, :], (1, 1), '...  12.6 us
    all_gather x1, blocking collectives, gathered_weights(): full = lax.all_gather(packed, 'chan', axis=0, tiled=True)  8.6 us
    pallas_call x1, Pallas kernels, kernel_grad_minor(): pl.pallas_call(kernel_grad_body, out_shape=jax.ShapeDtypeStruct((side * s...  8.06 us
    dot_general x4, matrix products, contract(): lax.dot_general(left, right, (((dim_left,), (dim_right,)), ((), ())), pre...  6.49 us
    ppermute x6, starting transfers between devices, butterfly_step(): lax.ppermute(flat, axis, [(i, i ^ step) for i in range(devices)])  6.36 us
    ppermute x2, starting transfers between devices, extended(): before = lax.ppermute(last, axis, up)  5.85 us
    unnamed x36, local copies, waits for them, and re-layouts  4.6 us
  transfers between devices with their start and end apart: 12, of which 8 were waited for; matrix products, arithmetic and copies ran while one was open for 17% of the time, Pallas kernels for 0%

profile of v16, /device:TPU:0, one launch (start us, length us, event | category | flops | bytes accessed | tf_op | source)
XLA Modules:
  0.0 106.3 jit_solution(17663761772442724094)
XLA Ops:
  2.0 3.0 %collective-permute-start = (bf16[192,3,128]{0,2,1:T(8,128)(2,1)S(1)}, bf16[192,3,128]{0,2,1:T(8,128)(2,1)S(1)}, u32[]{:S(2)}, u32[]{:S(2)}) collective-permute-start(bf16[192,3,128]{0,2,1:T(8,128)(2,1)S(1)} %slice_select_fusion.1), channel_id=1, source_target_pairs={{0,16},{16,0},{1,17},{17,1},{2,18},{18,2},{3,19},{19,3},{4,20},{20... | collective-permute-start | bytes 442376 | tf_op jit(solution)/shard_map/ppermute | solution.py:18
  8.1 8.6 %all_gather.3 = bf16[768,387]{1,0:T(8,128)(2,1)S(1)} all-gather(bf16[192,387]{1,0:T(8,128)(2,1)S(1)} %concatenate.24), channel_id=1, replica_groups=mesh['row'=2,'col'=4,'chan'=4] {'chan'}, dimensions={0}, use_global_device_ids=true | all-gather | bytes 743040 | tf_op jit(solution)/shard_map/all_gather | solution.py:170
  18.2 3.5 %collective-permute-start.1 = (bf16[192,14,3]{0,2,1:T(4,128)(2,1)S(1)}, bf16[192,14,3]{0,2,1:T(4,128)(2,1)S(1)}, u32[]{:S(2)}, u32[]{:S(2)}) collective-permute-start(bf16[192,14,3]{0,2,1:T(4,128)(2,1)S(1)} %get-tuple-element.44), channel_id=1, source_target_pairs={{0,4},{4,8},{8,12},{1,5},{5,9},{9,13},{2,6},{6,10},{10,14},{3,7},{... | collective-permute-start | bytes 48392 | tf_op jit(solution)/shard_map/ppermute | solution.py:23
  23.5 3.9 %collective-permute-done.2 = bf16[192,14,3]{0,2,1:T(4,128)(2,1)S(1)} collective-permute-done((bf16[192,14,3]{0,2,1:T(4,128)(2,1)S(1)}, bf16[192,14,3]{0,2,1:T(4,128)(2,1)S(1)}, u32[]{:S(2)}, u32[]{:S(2)}) %collective-permute-start.2) | collective-permute-done | bytes 16160 | tf_op jit(solution)/shard_map/ppermute | solution.py:24
  27.4 1.6 %bitcast_convert_fusion = (f32[14,134,192]{2,1,0:T(8,128)}, bf16[1,14,134,192]{3,2,1,0:T(8,128)(2,1)S(1)}) fusion(bf16[192,14,3]{0,2,1:T(4,128)(2,1)S(1)} %collective-permute-done.2, bf16[192,3,128]{0,2,1:T(8,128)(2,1)S(1)} %get-tuple-element.57, bf16[192,8,128]{0,2,1:T(8,128)(2,1)S(1)} %copy.84, bf16[192,3,128]{0,2,1:T(8,128)(2,1)S(1)} %get-tuple-element.56, ...), kind=kLoop, calls=%fused_computation.32 | loop fusion | flops 3962112 | bytes 2881536 | tf_op jit(solution)/shard_map/convert_element_type | solution.py:211
  29.0 8.4 %fusion.6 = f32[1,8,128,192]{3,0,2,1:T(1,128)S(1)} fusion(bf16[1,14,134,192]{3,2,1,0:T(8,128)(2,1)S(1)} %get-tuple-element.41, f32[7,7,1,192]{3,1,0,2:T(8,128)S(1)} %bitcast.130), kind=kOutput, calls=%fused_computation.13 | convolution fusion | flops 115605504 | bytes 1544448 | tf_op jit(solution)/shard_map/conv_general_dilated | solution.py:180
  38.1 1.9 %copy.89 = f32[1,8,128,192]{2,1,3,0:T(8,128)} copy(f32[1,8,128,192]{3,0,2,1:T(1,128)S(1)} %fusion.6) | data formatting | bytes 1572864 | tf_op jit(solution)/shard_map/conv_general_dilated | solution.py:180
  40.3 2.2 %multiply_convert_fusion = (bf16[1024,768]{0,1:T(8,128)(2,1)S(1)}, f32[1024,768]{0,1:T(8,128)S(1)}) fusion(f32[768]{0:T(1024)S(1)} %fusion.35, f32[24,8,8,128]{3,2,1,0:T(8,128)} %bitcast.125, f32[192]{0:T(256)S(1)} %copy-done.12, f32[192]{0:T(256)S(1)} %copy-done.9, f32[1024]{0:T(1024)S(1)} %get-tuple-element.62, f32[1024]{0:T(1024)S(1)} %get-tuple-element.63, ...), kind=kOutput, calls=%fused_computation.9 | convolution fusion | flops 307888128 | bytes 5913600 | tf_op jit(solution)/shard_map/dot_general | solution.py:53
  43.9 3.8 %fusion.31 = (f32[192]{0:T(256)S(1)}, f32[192]{0:T(256)S(1)}, bf16[8,128,192]{1,0,2:T(8,128)(2,1)}) fusion(bf16[192,8,128]{2,1,0:T(8,128)(2,1)S(1)} %copy-done.1, f32[192]{0:T(256)S(1)} %copy-done.10, f32[192]{0:T(256)S(1)} %copy-done.11, f32[24,8,8,128]{3,2,1,0:T(8,128)S(1)} %copy.118, bf16[192,8,128]{2,1,0:T(8,128)(2,1)S(1)} %copy-done.3), kind=kLoop, calls=%fused_computation.47 | loop fusion | flops 1965696 | bytes 1969152 | tf_op jit(solution)/shard_map/reduce_sum | solution.py:239
  47.6 1.6 %fusion.59 = (bf16[1024,768]{0,1:T(8,128)(2,1)S(1)}, f32[1024,768]{0,1:T(8,128)S(1)}) fusion(f32[1024,768]{0,1:T(8,128)S(1)} %get-tuple-element.69, f32[768]{0:T(1024)S(1)} %fusion.35, bf16[1024,192]{0,1:T(8,128)(2,1)S(1)} %fusion.23, bf16[768,387]{1,0:T(8,128)(2,1)S(1)} %all_gather.3), kind=kOutput, calls=%fused_computation.112 | convolution fusion | flops 310640640 | bytes 8654848 | tf_op jit(solution)/shard_map/dot_general | solution.py:53
  50.6 1.3 %copy.99 = f32[1024,192]{1,0:T(8,128)} copy(f32[1024,192]{0,1:T(8,128)S(1)} %get-tuple-element.35) | data formatting | bytes 1572864 | tf_op jit(solution)/shard_map/reduce_sum | solution.py:257
  53.3 1.5 %fusion.56 = (bf16[8,128,192]{2,1,0:T(8,128)(2,1)S(1)}, f32[8,128,192]{2,1,0:T(8,128)}) fusion(f32[8,128]{1,0:T(8,128)S(1)} %broadcast_multiply_fusion, f32[8,128]{1,0:T(8,128)S(1)} %get-tuple-element.64, f32[192]{0:T(256)S(1)} %copy-done.8, f32[1,8,128,192]{3,0,2,1:T(1,128)S(1)} %fusion.6, f32[8,128]{1,0:T(8,128)S(1)} %multiply_bitcast_fusion, ...), kind=kLoop, calls=%fused_computation.110 | loop fusion | flops 1769472 | bytes 2770432 | tf_op jit(solution)/shard_map/convert_element_type | solution.py:294
  54.8 8.1 %shard_map.194 = f32[49,8,192]{2,1,0:T(8,128)} custom-call(f32[8,128,192]{2,1,0:T(8,128)} %get-tuple-element.39.d_ref, f32[14,134,192]{2,1,0:T(8,128)} %get-tuple-element.40.p_ref), custom_call_target="tpu_custom_call" | custom-call | tf_op jit(solution)/shard_map/pallas_call | solution.py:107
  64.7 1.4 %fusion.38 = f32[192,192]{1,0:T(8,128)S(1)} fusion(bf16[1024,768]{0,1:T(8,128)(2,1)} %copy-done.13, s32[]{:T(128)S(6)} %select_n.42, f32[24,8,8,128]{3,2,1,0:T(8,128)S(1)} %bitcast.126, f32[192]{0:T(256)S(1)} %copy-done.12, f32[192]{0:T(256)S(1)} %copy-done.9, f32[1024]{0:T(1024)S(1)} %get-tuple-element.62, f32[1024]{0:T(1024)S(1)} %get-tuple-element.63, ...), kind=kOutput, calls=%fused_computation.66 | convolution fusion | flops 76677120 | bytes 1337604 | tf_op jit(solution)/shard_map/dot_general | solution.py:53
  66.1 2.1 %collective-permute-done.6 = f32[9984]{0:T(1024)S(1)} collective-permute-done((f32[9984]{0:T(1024)S(1)}, f32[9984]{0:T(1024)S(1)}, u32[]{:S(2)}, u32[]{:S(2)}) %collective-permute-start.6) | collective-permute-done | bytes 39968 | tf_op jit(solution)/shard_map/ppermute | solution.py:146
  68.2 2.6 %collective-permute-start.7 = (f32[9984]{0:T(1024)S(1)}, f32[9984]{0:T(1024)S(1)}, u32[]{:S(2)}, u32[]{:S(2)}) collective-permute-start(f32[9984]{0:T(1024)S(1)} %add.142), channel_id=1, source_target_pairs={{0,8},{4,12},{8,0},{12,4},{1,9},{5,13},{9,1},{13,5},{2,10},{6,14},... | collective-permute-start | bytes 119816 | tf_op jit(solution)/shard_map/ppermute | solution.py:146
  72.3 1.6 %concatenate.28 = f32[74304]{0:T(1024)S(1)} concatenate(f32[36864]{0:T(1024)S(1)} %reshape.310, f32[192]{0:T(256)S(1)} %dynamic-slice_reduce_fusion, f32[36864]{0:T(1024)S(1)} %reshape.311, f32[192]{0:T(256)S(1)} %get-tuple-element.19, f32[192]{0:T(256)S(1)} %get-tuple-element.20), dimensions={0} | concatenate | bytes 594432 | tf_op jit(solution)/shard_map/concatenate | solution.py:116
  74.2 1.6 %collective-permute-start.8 = (f32[9984]{0:T(1024)S(1)}, f32[9984]{0:T(1024)S(1)}, u32[]{:S(2)}, u32[]{:S(2)}) collective-permute-start(f32[9984]{0:T(1024)S(1)} %add.143), channel_id=1, source_target_pairs={{0,4},{4,0},{8,12},{12,8},{1,5},{5,1},{9,13},{13,9},{2,6},{6,2},{1... | collective-permute-start | bytes 119816 | tf_op jit(solution)/shard_map/ppermute | solution.py:146
  76.5 3.1 %collective-permute-done.8 = f32[9984]{0:T(1024)S(1)} collective-permute-done((f32[9984]{0:T(1024)S(1)}, f32[9984]{0:T(1024)S(1)}, u32[]{:S(2)}, u32[]{:S(2)}) %collective-permute-start.8) | collective-permute-done | bytes 39968 | tf_op jit(solution)/shard_map/ppermute | solution.py:146
  79.6 2.0 %collective-permute-done.3 = bf16[3,128,192]{2,1,0:T(8,128)(2,1)S(1)} collective-permute-done((bf16[3,128,192]{2,1,0:T(8,128)(2,1)S(1)}, bf16[3,128,192]{2,1,0:T(8,128)(2,1)S(1)}, u32[]{:S(2)}, u32[]{:S(2)}) %collective-permute-start.3) | collective-permute-done | bytes 147488 | tf_op jit(solution)/shard_map/ppermute | solution.py:18
  81.7 2.4 %collective-permute-start.4 = (bf16[14,3,192]{2,1,0:T(4,128)(2,1)S(1)}, bf16[14,3,192]{2,1,0:T(4,128)(2,1)S(1)}, u32[]{:S(2)}, u32[]{:S(2)}) collective-permute-start(bf16[14,3,192]{2,1,0:T(4,128)(2,1)S(1)} %get-tuple-element.42), channel_id=1, source_target_pairs={{0,4},{4,8},{8,12},{1,5},{5,9},{9,13},{2,6},{6,10},{10,14},{3,7},{... | collective-permute-start | bytes 48392 | tf_op jit(solution)/shard_map/ppermute | solution.py:23
  85.4 2.0 %collective-permute-done.9 = f32[74304]{0:T(1024)S(1)} collective-permute-done((f32[74304]{0:T(1024)S(1)}, f32[74304]{0:T(1024)S(1)}, u32[]{:S(2)}, u32[]{:S(2)}) %collective-permute-start.9) | collective-permute-done | bytes 297248 | tf_op jit(solution)/shard_map/ppermute | solution.py:146
  91.4 4.8 %collective-permute-done.10 = f32[74304]{0:T(1024)S(1)} collective-permute-done((f32[74304]{0:T(1024)S(1)}, f32[74304]{0:T(1024)S(1)}, u32[]{:S(2)}, u32[]{:S(2)}) %collective-permute-start.10) | collective-permute-done | bytes 297248 | tf_op jit(solution)/shard_map/ppermute | solution.py:146
  96.8 4.2 %fusion.15 = f32[8,8,17,192]{3,1,2,0:T(8,128)S(1)} fusion(bf16[14,1,7,6,192]{4,2,3,0,1:T(8,128)(2,1)S(1)} %slice.124, bf16[14,1,8,17,192]{4,2,3,0,1:T(8,128)(2,1)S(1)} %copy.105, pred[8,17]{0,1:T(8,128)(4,1)S(1)} %copy-done.14, f32[7,7,1,192]{3,1,0,2:T(8,128)S(1)} %bitcast.131), kind=kOutput, calls=%fused_computation.23 | convolution fusion | flops 126007296 | bytes 1830280 | tf_op jit(solution)/shard_map/conv_general_dilated | solution.py:180
  (105 shorter events, 27.9 us)
Async XLA Ops:
  0.6 16.1 %copy-start.1 = (bf16[192,8,128]{2,1,0:T(8,128)(2,1)S(1)}, bf16[192,8,128]{2,1,0:T(8,128)(2,1)}, u32[]{:S(2)}) copy-start(bf16[192,8,128]{2,1,0:T(8,128)(2,1)} %param.21) | copy-start | bytes 1179652
  2.0 16.1 %collective-permute-start = (bf16[192,3,128]{0,2,1:T(8,128)(2,1)S(1)}, bf16[192,3,128]{0,2,1:T(8,128)(2,1)S(1)}, u32[]{:S(2)}, u32[]{:S(2)}) collective-permute-start(bf16[192,3,128]{0,2,1:T(8,128)(2,1)S(1)} %slice_select_fusion.1), channel_id=1, source_target_pairs={{0,16},{16,0},{1,17},{17,1},{2,18},{18,2},{3,19},{19,3},{4,20},{20... | collective-permute-start | bytes 442376 | tf_op jit(solution)/shard_map/ppermute | solution.py:18
  8.1 9.7 %copy-start.10 = (f32[192]{0:T(256)S(1)}, f32[192]{0:T(256)}, u32[]{:S(2)}) copy-start(f32[192]{0:T(256)} %param.20) | copy-start | bytes 2308
  18.0 5.4 %copy-start.7 = (f32[7,7,192]{2,1,0:T(8,128)S(1)}, f32[7,7,192]{2,1,0:T(8,128)}, u32[]{:S(2)}) copy-start(f32[7,7,192]{2,1,0:T(8,128)} %param.12) | copy-start | bytes 112900
  18.2 5.3 %collective-permute-start.1 = (bf16[192,14,3]{0,2,1:T(4,128)(2,1)S(1)}, bf16[192,14,3]{0,2,1:T(4,128)(2,1)S(1)}, u32[]{:S(2)}, u32[]{:S(2)}) collective-permute-start(bf16[192,14,3]{0,2,1:T(4,128)(2,1)S(1)} %get-tuple-element.44), channel_id=1, source_target_pairs={{0,4},{4,8},{8,12},{1,5},{5,9},{9,13},{2,6},{6,10},{10,14},{3,7},{... | collective-permute-start | bytes 48392 | tf_op jit(solution)/shard_map/ppermute | solution.py:23
  21.6 5.8 %collective-permute-start.2 = (bf16[192,14,3]{0,2,1:T(4,128)(2,1)S(1)}, bf16[192,14,3]{0,2,1:T(4,128)(2,1)S(1)}, u32[]{:S(2)}, u32[]{:S(2)}) collective-permute-start(bf16[192,14,3]{0,2,1:T(4,128)(2,1)S(1)} %get-tuple-element.45), channel_id=1, source_target_pairs={{4,0},{8,4},{12,8},{5,1},{9,5},{13,9},{6,2},{10,6},{14,10},{7,3},{... | collective-permute-start | bytes 48392 | tf_op jit(solution)/shard_map/ppermute | solution.py:24
  37.4 2.6 %copy-start.8 = (f32[192]{0:T(256)S(1)}, f32[192]{0:T(256)}, u32[]{:S(2)}) copy-start(f32[192]{0:T(256)} %param.13) | copy-start | bytes 2308
  38.1 2.2 %copy-start.9 = (f32[192]{0:T(256)S(1)}, f32[192]{0:T(256)}, u32[]{:S(2)}) copy-start(f32[192]{0:T(256)} %param.14) | copy-start | bytes 2308
  38.1 2.2 %copy-start.12 = (f32[192]{0:T(256)S(1)}, f32[192]{0:T(256)}, u32[]{:S(2)}) copy-start(f32[192]{0:T(256)} %param.15) | copy-start | bytes 2308
  40.3 2.2 %copy-start.4 = (bf16[768,192]{1,0:T(8,128)(2,1)S(1)}, bf16[768,192]{1,0:T(8,128)(2,1)}, u32[]{:S(2)}) copy-start(bf16[768,192]{1,0:T(8,128)(2,1)} %get-tuple-element.48) | copy-start | bytes 884740
  42.5 1.3 %copy-start.3 = (bf16[192,8,128]{2,1,0:T(8,128)(2,1)S(1)}, bf16[192,8,128]{2,1,0:T(8,128)(2,1)}, u32[]{:S(2)}) copy-start(bf16[192,8,128]{2,1,0:T(8,128)(2,1)} %param.11) | copy-start | bytes 1179652
  42.6 1.3 %copy-start.11 = (f32[192]{0:T(256)S(1)}, f32[192]{0:T(256)}, u32[]{:S(2)}) copy-start(f32[192]{0:T(256)} %param.19) | copy-start | bytes 2308
  47.6 1.8 %copy-start.6 = (bf16[768,192]{1,0:T(8,128)(2,1)S(1)}, bf16[768,192]{1,0:T(8,128)(2,1)}, u32[]{:S(2)}) copy-start(bf16[768,192]{1,0:T(8,128)(2,1)} %get-tuple-element.47) | copy-start | bytes 884740
  54.8 9.9 %copy-start.5 = (f32[1,8,128,192]{2,1,3,0:T(8,128)S(1)}, f32[1,8,128,192]{2,1,3,0:T(8,128)}, u32[]{:S(2)}) copy-start(f32[1,8,128,192]{2,1,3,0:T(8,128)} %copy.89) | copy-start | bytes 2359300
  64.2 4.0 %collective-permute-start.6 = (f32[9984]{0:T(1024)S(1)}, f32[9984]{0:T(1024)S(1)}, u32[]{:S(2)}, u32[]{:S(2)}) collective-permute-start(f32[9984]{0:T(1024)S(1)} %concatenate.27), channel_id=1, source_target_pairs={{0,16},{16,0},{1,17},{17,1},{2,18},{18,2},{3,19},{19,3},{4,20},{20... | collective-permute-start | bytes 119816 | tf_op jit(solution)/shard_map/ppermute | solution.py:146
  68.2 6.1 %collective-permute-start.7 = (f32[9984]{0:T(1024)S(1)}, f32[9984]{0:T(1024)S(1)}, u32[]{:S(2)}, u32[]{:S(2)}) collective-permute-start(f32[9984]{0:T(1024)S(1)} %add.142), channel_id=1, source_target_pairs={{0,8},{4,12},{8,0},{12,4},{1,9},{5,13},{9,1},{13,5},{2,10},{6,14},... | collective-permute-start | bytes 119816 | tf_op jit(solution)/shard_map/ppermute | solution.py:146
  73.9 13.6 %collective-permute-start.9 = (f32[74304]{0:T(1024)S(1)}, f32[74304]{0:T(1024)S(1)}, u32[]{:S(2)}, u32[]{:S(2)}) collective-permute-start(f32[74304]{0:T(1024)S(1)} %concatenate.28), channel_id=1, source_target_pairs={{0,8},{4,12},{8,0},{12,4},{1,9},{5,13},{9,1},{13,5},{2,10},{6,14},... | collective-permute-start | bytes 891656 | tf_op jit(solution)/shard_map/ppermute | solution.py:146
  74.2 5.4 %collective-permute-start.8 = (f32[9984]{0:T(1024)S(1)}, f32[9984]{0:T(1024)S(1)}, u32[]{:S(2)}, u32[]{:S(2)}) collective-permute-start(f32[9984]{0:T(1024)S(1)} %add.143), channel_id=1, source_target_pairs={{0,4},{4,0},{8,12},{12,8},{1,5},{5,1},{9,13},{13,9},{2,6},{6,2},{1... | collective-permute-start | bytes 119816 | tf_op jit(solution)/shard_map/ppermute | solution.py:146
  75.9 5.7 %collective-permute-start.3 = (bf16[3,128,192]{2,1,0:T(8,128)(2,1)S(1)}, bf16[3,128,192]{2,1,0:T(8,128)(2,1)S(1)}, u32[]{:S(2)}, u32[]{:S(2)}) collective-permute-start(bf16[3,128,192]{2,1,0:T(8,128)(2,1)S(1)} %slice_select_fusion), channel_id=1, source_target_pairs={{0,16},{16,0},{1,17},{17,1},{2,18},{18,2},{3,19},{19,3},{4,20},{20... | collective-permute-start | bytes 442376 | tf_op jit(solution)/shard_map/ppermute | solution.py:18
  81.7 7.8 %collective-permute-start.4 = (bf16[14,3,192]{2,1,0:T(4,128)(2,1)S(1)}, bf16[14,3,192]{2,1,0:T(4,128)(2,1)S(1)}, u32[]{:S(2)}, u32[]{:S(2)}) collective-permute-start(bf16[14,3,192]{2,1,0:T(4,128)(2,1)S(1)} %get-tuple-element.42), channel_id=1, source_target_pairs={{0,4},{4,8},{8,12},{1,5},{5,9},{9,13},{2,6},{6,10},{10,14},{3,7},{... | collective-permute-start | bytes 48392 | tf_op jit(solution)/shard_map/ppermute | solution.py:23
  84.1 6.1 %collective-permute-start.5 = (bf16[14,3,192]{2,1,0:T(4,128)(2,1)S(1)}, bf16[14,3,192]{2,1,0:T(4,128)(2,1)S(1)}, u32[]{:S(2)}, u32[]{:S(2)}) collective-permute-start(bf16[14,3,192]{2,1,0:T(4,128)(2,1)S(1)} %get-tuple-element.43), channel_id=1, source_target_pairs={{4,0},{8,4},{12,8},{5,1},{9,5},{13,9},{6,2},{10,6},{14,10},{7,3},{... | collective-permute-start | bytes 48392 | tf_op jit(solution)/shard_map/ppermute | solution.py:24
  87.5 8.7 %collective-permute-start.10 = (f32[74304]{0:T(1024)S(1)}, f32[74304]{0:T(1024)S(1)}, u32[]{:S(2)}, u32[]{:S(2)}) collective-permute-start(f32[74304]{0:T(1024)S(1)} %add.145), channel_id=1, source_target_pairs={{0,4},{4,0},{8,12},{12,8},{1,5},{5,1},{9,13},{13,9},{2,6},{6,2},{1... | collective-permute-start | bytes 891656 | tf_op jit(solution)/shard_map/ppermute | solution.py:146
  91.0 5.8 %copy-start.14 = (pred[8,17]{0,1:T(8,128)(4,1)S(1)}, pred[8,17]{0,1:T(8,128)(4,1)}, u32[]{:S(2)}) copy-start(pred[8,17]{0,1:T(8,128)(4,1)} %constant.51) | copy-start | bytes 412
  96.2 7.7 %collective-permute-start.11 = (f32[74304]{0:T(1024)S(1)}, f32[74304]{0:T(1024)S(1)}, u32[]{:S(2)}, u32[]{:S(2)}) collective-permute-start(f32[74304]{0:T(1024)S(1)} %add.146), channel_id=1, source_target_pairs={{0,16},{16,0},{1,17},{17,1},{2,18},{18,2},{3,19},{19,3},{4,20},{20... | collective-permute-start | bytes 891656 | tf_op jit(solution)/shard_map/ppermute | solution.py:146
  (3 other events, 3.5 us)

commit v17 on v16

--- a/solution.py
+++ b/solution.py
@@ -265,6 +265,8 @@
     bias_portion = jnp.sum(normalized_gradient, axis=0)
     grad_conv_bias = jnp.sum(convolved_gradient, axis=0)
     d_t = convolved_gradient.reshape(tile_rows, tile_cols, channel_count)
+    d_padded = extended(d_t.astype(jnp.bfloat16), (("row", 0), ("col", 1)), 3)
+    d_padded, d_t = lax.optimization_barrier((d_padded, d_t))
     grad_kernel = kernel_grad_minor(d_t, padded_t)
     (
         grad_kernel,
@@ -291,7 +293,7 @@
         ("row", "col"),
         4,
     )
-    d_padded = extended(d_t.astype(jnp.bfloat16), (("row", 0), ("col", 1)), 3).astype(jnp.float32)
+    d_padded = d_padded.astype(jnp.float32)
     grad_feature_t = (
         cotangent_t.astype(jnp.float32) + depthwise_minor(d_padded, kernel[::-1, ::-1])
     ).astype(jnp.bfloat16)

time: 107 us -> 111 us (1.037)
  starting transfers between devices: 18.4 us -> 23.1 us
  other arithmetic: 13.8 us -> 18.1 us
  waiting for transfers between devices: 19.7 us -> 15.6 us
    ppermute x6, waiting for transfers between devices: 13.1 us -> 6.6 us  [butterfly_step(): lax.ppermute(flat, axis, [(i, i ^ step) for i in range(devices)])]
    ppermute x2, waiting for transfers between devices: 4.58 us -> 8.97 us  [extended(): after = lax.ppermute(leading, axis, down)]
    ppermute x6, starting transfers between devices: 6.36 us -> 10.2 us  [butterfly_step(): lax.ppermute(flat, axis, [(i, i ^ step) for i in range(devices)])]
    ppermute x2, waiting for transfers between devices: 2.03 us -> 0.01 us  [extended(): got = lax.ppermute(jnp.where(first, last, leading), axis, [(0, 1), (1, 0)])]
    unnamed x36 -> x82, local copies, waits for them, and re-layouts: 4.6 us -> 3.74 us
  transfers between devices with their start and end apart: 12 -> 12, of which waited for: 8 -> 5; matrix products, arithmetic and copies ran while one was open for 17% -> 18% of each run, Pallas kernels for 0% -> 7%
where the time goes in v17:
time: 111 us
  starting transfers between devices  23.1 us (21%)
  matrix products  20.7 us (19%)
  other arithmetic  18.1 us (16%)
  waiting for transfers between devices  15.6 us (14%)
  local copies, waits for them, and re-layouts  15.2 us (14%)
  blocking collectives  8.6 us (8%)
  Pallas kernels  7.82 us (7%)
  between operations  1.47 us (1%)
    conv_general_dilated x2, matrix products, depthwise_minor(): lax.conv_general_dilated(padded_t[None], kernel[:, :, None, :], (1, 1), '...  12.6 us
    ppermute x6, starting transfers between devices, butterfly_step(): lax.ppermute(flat, axis, [(i, i ^ step) for i in range(devices)])  10.2 us
    ppermute x2, waiting for transfers between devices, extended(): after = lax.ppermute(leading, axis, down)  8.97 us
    all_gather x1, blocking collectives, gathered_weights(): full = lax.all_gather(packed, 'chan', axis=0, tiled=True)  8.6 us
    pallas_call x1, Pallas kernels, kernel_grad_minor(): pl.pallas_call(kernel_grad_body, out_shape=jax.ShapeDtypeStruct((side * s...  7.82 us
    ppermute x6, waiting for transfers between devices, butterfly_step(): lax.ppermute(flat, axis, [(i, i ^ step) for i in range(devices)])  6.6 us
    ppermute x2, starting transfers between devices, extended(): before = lax.ppermute(last, axis, up)  6.52 us
    dot_general x4, matrix products, contract(): lax.dot_general(left, right, (((dim_left,), (dim_right,)), ((), ())), pre...  6.19 us
  transfers between devices with their start and end apart: 12, of which 5 were waited for; matrix products, arithmetic and copies ran while one was open for 18% of the time, Pallas kernels for 7%

profile of v17, /device:TPU:0, one launch (start us, length us, event | category | flops | bytes accessed | tf_op | source)
XLA Modules:
  0.0 110.7 jit_solution(4211040126774548379)
XLA Ops:
  2.0 3.0 %collective-permute-start = (bf16[192,3,128]{0,2,1:T(8,128)(2,1)S(1)}, bf16[192,3,128]{0,2,1:T(8,128)(2,1)S(1)}, u32[]{:S(2)}, u32[]{:S(2)}) collective-permute-start(bf16[192,3,128]{0,2,1:T(8,128)(2,1)S(1)} %slice_select_fusion.1), channel_id=1, source_target_pairs={{0,16},{16,0},{1,17},{17,1},{2,18},{18,2},{3,19},{19,3},{4,20},{20... | collective-permute-start | bytes 442376 | tf_op jit(solution)/shard_map/ppermute | solution.py:18
  8.1 8.6 %all_gather.3 = bf16[768,387]{1,0:T(8,128)(2,1)S(1)} all-gather(bf16[192,387]{1,0:T(8,128)(2,1)S(1)} %concatenate.24), channel_id=1, replica_groups=mesh['row'=2,'col'=4,'chan'=4] {'chan'}, dimensions={0}, use_global_device_ids=true | all-gather | bytes 743040 | tf_op jit(solution)/shard_map/all_gather | solution.py:170
  18.1 3.5 %collective-permute-start.1 = (bf16[192,14,3]{0,2,1:T(4,128)(2,1)S(1)}, bf16[192,14,3]{0,2,1:T(4,128)(2,1)S(1)}, u32[]{:S(2)}, u32[]{:S(2)}) collective-permute-start(bf16[192,14,3]{0,2,1:T(4,128)(2,1)S(1)} %get-tuple-element.48), channel_id=1, source_target_pairs={{0,4},{4,8},{8,12},{1,5},{5,9},{9,13},{2,6},{6,10},{10,14},{3,7},{... | collective-permute-start | bytes 48392 | tf_op jit(solution)/shard_map/ppermute | solution.py:23
  23.4 4.0 %collective-permute-done.2 = bf16[192,14,3]{0,2,1:T(4,128)(2,1)S(1)} collective-permute-done((bf16[192,14,3]{0,2,1:T(4,128)(2,1)S(1)}, bf16[192,14,3]{0,2,1:T(4,128)(2,1)S(1)}, u32[]{:S(2)}, u32[]{:S(2)}) %collective-permute-start.2) | collective-permute-done | bytes 16160 | tf_op jit(solution)/shard_map/ppermute | solution.py:24
  27.4 1.6 %bitcast_convert_fusion = (f32[14,134,192]{2,1,0:T(8,128)}, bf16[1,14,134,192]{3,2,1,0:T(8,128)(2,1)S(1)}) fusion(bf16[192,14,3]{0,2,1:T(4,128)(2,1)S(1)} %collective-permute-done.2, bf16[192,3,128]{0,2,1:T(8,128)(2,1)S(1)} %get-tuple-element.61, bf16[192,8,128]{0,2,1:T(8,128)(2,1)S(1)} %copy.84, bf16[192,3,128]{0,2,1:T(8,128)(2,1)S(1)} %get-tuple-element.60, ...), kind=kLoop, calls=%fused_computation.32 | loop fusion | flops 3962112 | bytes 2881536 | tf_op jit(solution)/shard_map/convert_element_type | solution.py:211
  29.0 8.4 %fusion.6 = f32[1,8,128,192]{3,0,2,1:T(1,128)S(1)} fusion(bf16[1,14,134,192]{3,2,1,0:T(8,128)(2,1)S(1)} %get-tuple-element.45, f32[7,7,1,192]{3,1,0,2:T(8,128)S(1)} %bitcast.130), kind=kOutput, calls=%fused_computation.13 | convolution fusion | flops 115605504 | bytes 1544448 | tf_op jit(solution)/shard_map/conv_general_dilated | solution.py:180
  38.1 1.9 %copy.89 = f32[1,8,128,192]{2,1,3,0:T(8,128)} copy(f32[1,8,128,192]{3,0,2,1:T(1,128)S(1)} %fusion.6) | data formatting | bytes 1572864 | tf_op jit(solution)/shard_map/conv_general_dilated | solution.py:180
  41.0 2.2 %multiply_convert_fusion = (bf16[1024,768]{0,1:T(8,128)(2,1)S(1)}, f32[1024,768]{0,1:T(8,128)S(1)}) fusion(f32[768]{0:T(1024)S(1)} %fusion.35, f32[24,8,8,128]{3,2,1,0:T(8,128)} %bitcast.125, f32[192]{0:T(256)S(1)} %copy-done.34, f32[192]{0:T(256)S(1)} %copy-done.22, f32[1024]{0:T(1024)S(1)} %get-tuple-element.66, f32[1024]{0:T(1024)S(1)} %get-tuple-element.67, ...), kind=kOutput, calls=%fused_computation.9 | convolution fusion | flops 307888128 | bytes 5913600 | tf_op jit(solution)/shard_map/dot_general | solution.py:53
  44.2 4.3 %fusion.31 = (f32[192]{0:T(256)}, f32[192]{0:T(256)}, bf16[8,128,192]{1,0,2:T(8,128)(2,1)}) fusion(bf16[192,8,128]{2,1,0:T(8,128)(2,1)S(1)} %copy-done.1, f32[192]{0:T(256)S(1)} %copy-done.31, f32[192]{0:T(256)S(1)} %copy-done.32, f32[24,8,8,128]{3,2,1,0:T(8,128)S(1)} %copy.118, bf16[192,8,128]{2,1,0:T(8,128)(2,1)S(1)} %copy-done.3), kind=kLoop, calls=%fused_computation.47 | loop fusion | flops 1965696 | bytes 1969152 | tf_op jit(solution)/shard_map/reduce_sum | solution.py:239
  49.5 1.6 %fusion.59 = (bf16[1024,768]{0,1:T(8,128)(2,1)S(1)}, f32[1024,768]{0,1:T(8,128)S(1)}) fusion(f32[1024,768]{0,1:T(8,128)S(1)} %get-tuple-element.73, f32[768]{0:T(1024)S(1)} %fusion.35, bf16[1024,192]{0,1:T(8,128)(2,1)S(1)} %fusion.23, bf16[768,387]{1,0:T(8,128)(2,1)S(1)} %all_gather.3), kind=kOutput, calls=%fused_computation.112 | convolution fusion | flops 310640640 | bytes 8654848 | tf_op jit(solution)/shard_map/dot_general | solution.py:53
  56.4 1.5 %fusion.56 = (bf16[8,128,192]{2,1,0:T(8,128)(2,1)S(1)}, f32[8,128,192]{2,1,0:T(8,128)}) fusion(f32[8,128]{1,0:T(8,128)S(1)} %broadcast_multiply_fusion, f32[8,128]{1,0:T(8,128)S(1)} %copy-done.9, f32[192]{0:T(256)S(1)} %copy-done.20, f32[1,8,128,192]{3,0,2,1:T(1,128)S(1)} %fusion.6, f32[8,128]{1,0:T(8,128)S(1)} %multiply_bitcast_fusion, ...), kind=kLoop, calls=%fused_computation.110 | loop fusion | flops 1769472 | bytes 2770432 | tf_op jit(solution)/shard_map/convert_element_type | solution.py:268
  60.2 1.6 %concatenate.28 = f32[74304]{0:T(1024)S(1)} concatenate(f32[36864]{0:T(1024)S(1)} %reshape.310, f32[192]{0:T(256)S(1)} %copy-done.26, f32[36864]{0:T(1024)S(1)} %reshape.311, f32[192]{0:T(256)S(1)} %copy-done.24, f32[192]{0:T(256)S(1)} %copy-done.25), dimensions={0} | concatenate | bytes 594432 | tf_op jit(solution)/shard_map/concatenate | solution.py:116
  61.8 2.6 %collective-permute-start.9 = (f32[74304]{0:T(1024)S(1)}, f32[74304]{0:T(1024)S(1)}, u32[]{:S(2)}, u32[]{:S(2)}) collective-permute-start(f32[74304]{0:T(1024)S(1)} %concatenate.28), channel_id=1, source_target_pairs={{0,8},{4,12},{8,0},{12,4},{1,9},{5,13},{9,1},{13,5},{2,10},{6,14},... | collective-permute-start | bytes 891656 | tf_op jit(solution)/shard_map/ppermute | solution.py:146
  65.4 3.0 %collective-permute-start.4 = (bf16[14,3,192]{2,1,0:T(4,128)(2,1)S(1)}, bf16[14,3,192]{2,1,0:T(4,128)(2,1)S(1)}, u32[]{:S(2)}, u32[]{:S(2)}) collective-permute-start(bf16[14,3,192]{2,1,0:T(4,128)(2,1)S(1)} %get-tuple-element.46), channel_id=1, source_target_pairs={{0,4},{4,8},{8,12},{1,5},{5,9},{9,13},{2,6},{6,10},{10,14},{3,7},{... | collective-permute-start | bytes 48392 | tf_op jit(solution)/shard_map/ppermute | solution.py:23
  68.5 1.5 %collective-permute-start.5 = (bf16[14,3,192]{2,1,0:T(4,128)(2,1)S(1)}, bf16[14,3,192]{2,1,0:T(4,128)(2,1)S(1)}, u32[]{:S(2)}, u32[]{:S(2)}) collective-permute-start(bf16[14,3,192]{2,1,0:T(4,128)(2,1)S(1)} %get-tuple-element.47), channel_id=1, source_target_pairs={{4,0},{8,4},{12,8},{5,1},{9,5},{13,9},{6,2},{10,6},{14,10},{7,3},{... | collective-permute-start | bytes 48392 | tf_op jit(solution)/shard_map/ppermute | solution.py:24
  71.2 4.9 %collective-permute-done.5 = bf16[14,3,192]{2,1,0:T(4,128)(2,1)S(1)} collective-permute-done((bf16[14,3,192]{2,1,0:T(4,128)(2,1)S(1)}, bf16[14,3,192]{2,1,0:T(4,128)(2,1)S(1)}, u32[]{:S(2)}, u32[]{:S(2)}) %collective-permute-start.5) | collective-permute-done | bytes 16160 | tf_op jit(solution)/shard_map/ppermute | solution.py:24
  76.5 7.8 %shard_map.194 = f32[49,8,192]{2,1,0:T(8,128)} custom-call(f32[8,128,192]{2,1,0:T(8,128)} %get-tuple-element.21.d_ref, f32[14,134,192]{2,1,0:T(8,128)} %get-tuple-element.44.p_ref), custom_call_target="tpu_custom_call" | custom-call | tf_op jit(solution)/shard_map/pallas_call | solution.py:107
  85.7 1.5 %collective-permute-start.6 = (f32[9984]{0:T(1024)S(1)}, f32[9984]{0:T(1024)S(1)}, u32[]{:S(2)}, u32[]{:S(2)}) collective-permute-start(f32[9984]{0:T(1024)S(1)} %concatenate.27), channel_id=1, source_target_pairs={{0,16},{16,0},{1,17},{17,1},{2,18},{18,2},{3,19},{19,3},{4,20},{20... | collective-permute-start | bytes 119816 | tf_op jit(solution)/shard_map/ppermute | solution.py:146
  88.1 1.5 %collective-permute-done.6 = f32[9984]{0:T(1024)S(1)} collective-permute-done((f32[9984]{0:T(1024)S(1)}, f32[9984]{0:T(1024)S(1)}, u32[]{:S(2)}, u32[]{:S(2)}) %collective-permute-start.6) | collective-permute-done | bytes 39968 | tf_op jit(solution)/shard_map/ppermute | solution.py:146
  89.7 2.4 %collective-permute-start.7 = (f32[9984]{0:T(1024)S(1)}, f32[9984]{0:T(1024)S(1)}, u32[]{:S(2)}, u32[]{:S(2)}) collective-permute-start(f32[9984]{0:T(1024)S(1)} %add.142), channel_id=1, source_target_pairs={{0,8},{4,12},{8,0},{12,4},{1,9},{5,13},{9,1},{13,5},{2,10},{6,14},... | collective-permute-start | bytes 119816 | tf_op jit(solution)/shard_map/ppermute | solution.py:146
  92.2 4.2 %fusion.15 = f32[8,8,17,192]{3,1,2,0:T(8,128)S(1)} fusion(bf16[14,1,7,6,192]{4,2,3,0,1:T(8,128)(2,1)S(1)} %slice.124, bf16[14,1,8,17,192]{4,2,3,0,1:T(8,128)(2,1)S(1)} %copy.105, pred[8,17]{0,1:T(8,128)(4,1)S(1)} %copy-done.37, f32[7,7,1,192]{3,1,0,2:T(8,128)S(1)} %bitcast.131), kind=kOutput, calls=%fused_computation.23 | convolution fusion | flops 126007296 | bytes 1830280 | tf_op jit(solution)/shard_map/conv_general_dilated | solution.py:180
  97.3 2.1 %collective-permute-start.8 = (f32[9984]{0:T(1024)S(1)}, f32[9984]{0:T(1024)S(1)}, u32[]{:S(2)}, u32[]{:S(2)}) collective-permute-start(f32[9984]{0:T(1024)S(1)} %add.143), channel_id=1, source_target_pairs={{0,4},{4,0},{8,12},{12,8},{1,5},{5,1},{9,13},{13,9},{2,6},{6,2},{1... | collective-permute-start | bytes 119816 | tf_op jit(solution)/shard_map/ppermute | solution.py:146
  101.5 1.6 %collective-permute-start.11 = (f32[74304]{0:T(1024)S(1)}, f32[74304]{0:T(1024)S(1)}, u32[]{:S(2)}, u32[]{:S(2)}) collective-permute-start(f32[74304]{0:T(1024)S(1)} %add.146), channel_id=1, source_target_pairs={{0,16},{16,0},{1,17},{17,1},{2,18},{18,2},{3,19},{19,3},{4,20},{20... | collective-permute-start | bytes 891656 | tf_op jit(solution)/shard_map/ppermute | solution.py:146
  104.4 3.9 %collective-permute-done.11 = f32[74304]{0:T(1024)S(1)} collective-permute-done((f32[74304]{0:T(1024)S(1)}, f32[74304]{0:T(1024)S(1)}, u32[]{:S(2)}, u32[]{:S(2)}) %collective-permute-start.11) | collective-permute-done | bytes 297248 | tf_op jit(solution)/shard_map/ppermute | solution.py:146
  (151 shorter events, 29.9 us)
Async XLA Ops:
  0.6 16.1 %copy-start.1 = (bf16[192,8,128]{2,1,0:T(8,128)(2,1)S(1)}, bf16[192,8,128]{2,1,0:T(8,128)(2,1)}, u32[]{:S(2)}) copy-start(bf16[192,8,128]{2,1,0:T(8,128)(2,1)} %param.21) | copy-start | bytes 1179652
  2.0 16.1 %collective-permute-start = (bf16[192,3,128]{0,2,1:T(8,128)(2,1)S(1)}, bf16[192,3,128]{0,2,1:T(8,128)(2,1)S(1)}, u32[]{:S(2)}, u32[]{:S(2)}) collective-permute-start(bf16[192,3,128]{0,2,1:T(8,128)(2,1)S(1)} %slice_select_fusion.1), channel_id=1, source_target_pairs={{0,16},{16,0},{1,17},{17,1},{2,18},{18,2},{3,19},{19,3},{4,20},{20... | collective-permute-start | bytes 442376 | tf_op jit(solution)/shard_map/ppermute | solution.py:18
  8.1 9.7 %copy-start.31 = (f32[192]{0:T(256)S(1)}, f32[192]{0:T(256)}, u32[]{:S(2)}) copy-start(f32[192]{0:T(256)} %param.20) | copy-start | bytes 2308
  18.1 5.2 %collective-permute-start.1 = (bf16[192,14,3]{0,2,1:T(4,128)(2,1)S(1)}, bf16[192,14,3]{0,2,1:T(4,128)(2,1)S(1)}, u32[]{:S(2)}, u32[]{:S(2)}) collective-permute-start(bf16[192,14,3]{0,2,1:T(4,128)(2,1)S(1)} %get-tuple-element.48), channel_id=1, source_target_pairs={{0,4},{4,8},{8,12},{1,5},{5,9},{9,13},{2,6},{6,10},{10,14},{3,7},{... | collective-permute-start | bytes 48392 | tf_op jit(solution)/shard_map/ppermute | solution.py:23
  21.6 5.8 %collective-permute-start.2 = (bf16[192,14,3]{0,2,1:T(4,128)(2,1)S(1)}, bf16[192,14,3]{0,2,1:T(4,128)(2,1)S(1)}, u32[]{:S(2)}, u32[]{:S(2)}) collective-permute-start(bf16[192,14,3]{0,2,1:T(4,128)(2,1)S(1)} %get-tuple-element.49), channel_id=1, source_target_pairs={{4,0},{8,4},{12,8},{5,1},{9,5},{13,9},{6,2},{10,6},{14,10},{7,3},{... | collective-permute-start | bytes 48392 | tf_op jit(solution)/shard_map/ppermute | solution.py:24
  23.4 5.6 %copy-start.13 = (f32[7,7,192]{2,1,0:T(8,128)S(1)}, f32[7,7,192]{2,1,0:T(8,128)}, u32[]{:S(2)}) copy-start(f32[7,7,192]{2,1,0:T(8,128)} %param.12) | copy-start | bytes 112900
  40.1 3.0 %copy-start.27 = (f32[1024]{0:T(1024)}, f32[1024]{0:T(1024)S(1)}, u32[]{:S(2)}) copy-start(f32[1024]{0:T(1024)S(1)} %get-tuple-element.67) | copy-start | bytes 12292
  58.0 11.9 %copy-start.10 = (f32[8,128]{1,0:T(8,128)S(1)}, f32[8,128]{1,0:T(8,128)}, u32[]{:S(2)}) copy-start(f32[8,128]{1,0:T(8,128)} %copy-done.8) | copy-start | bytes 12292
  58.0 11.9 %copy-start.12 = (f32[8,128]{1,0:T(8,128)S(1)}, f32[8,128]{1,0:T(8,128)}, u32[]{:S(2)}) copy-start(f32[8,128]{1,0:T(8,128)} %get-tuple-element.65) | copy-start | bytes 12292
  58.0 11.9 %copy-start.16 = (f32[8,128]{1,0:T(8,128)S(1)}, f32[8,128]{1,0:T(8,128)}, u32[]{:S(2)}) copy-start(f32[8,128]{1,0:T(8,128)} %copy-done.15) | copy-start | bytes 12292
  58.0 11.9 %copy-start.21 = (f32[192]{0:T(256)S(1)}, f32[192]{0:T(256)}, u32[]{:S(2)}) copy-start(f32[192]{0:T(256)} %param.13) | copy-start | bytes 2308
  58.1 6.4 %collective-permute-start.3 = (bf16[3,128,192]{2,1,0:T(8,128)(2,1)S(1)}, bf16[3,128,192]{2,1,0:T(8,128)(2,1)}, u32[]{:S(2)}, u32[]{:S(2)}) collective-permute-start(bf16[3,128,192]{2,1,0:T(8,128)(2,1)S(1)} %slice_select_fusion), channel_id=1, source_target_pairs={{0,16},{16,0},{1,17},{17,1},{2,18},{18,2},{3,19},{19,3},{4,20},{20... | collective-permute-start | bytes 442376 | tf_op jit(solution)/shard_map/ppermute | solution.py:18
  58.6 11.3 %copy-start.18 = (f32[8,128]{1,0:T(8,128)S(1)}, f32[8,128]{1,0:T(8,128)}, u32[]{:S(2)}) copy-start(f32[8,128]{1,0:T(8,128)} %copy-done.17) | copy-start | bytes 12292
  61.8 30.2 %collective-permute-start.9 = (f32[74304]{0:T(1024)S(1)}, f32[74304]{0:T(1024)S(1)}, u32[]{:S(2)}, u32[]{:S(2)}) collective-permute-start(f32[74304]{0:T(1024)S(1)} %concatenate.28), channel_id=1, source_target_pairs={{0,8},{4,12},{8,0},{12,4},{1,9},{5,13},{9,1},{13,5},{2,10},{6,14},... | collective-permute-start | bytes 891656 | tf_op jit(solution)/shard_map/ppermute | solution.py:146
  65.4 5.8 %collective-permute-start.4 = (bf16[14,3,192]{2,1,0:T(4,128)(2,1)S(1)}, bf16[14,3,192]{2,1,0:T(4,128)(2,1)S(1)}, u32[]{:S(2)}, u32[]{:S(2)}) collective-permute-start(bf16[14,3,192]{2,1,0:T(4,128)(2,1)S(1)} %get-tuple-element.46), channel_id=1, source_target_pairs={{0,4},{4,8},{8,12},{1,5},{5,9},{9,13},{2,6},{6,10},{10,14},{3,7},{... | collective-permute-start | bytes 48392 | tf_op jit(solution)/shard_map/ppermute | solution.py:23
  68.5 7.7 %collective-permute-start.5 = (bf16[14,3,192]{2,1,0:T(4,128)(2,1)S(1)}, bf16[14,3,192]{2,1,0:T(4,128)(2,1)S(1)}, u32[]{:S(2)}, u32[]{:S(2)}) collective-permute-start(bf16[14,3,192]{2,1,0:T(4,128)(2,1)S(1)} %get-tuple-element.47), channel_id=1, source_target_pairs={{4,0},{8,4},{12,8},{5,1},{9,5},{13,9},{6,2},{10,6},{14,10},{7,3},{... | collective-permute-start | bytes 48392 | tf_op jit(solution)/shard_map/ppermute | solution.py:24
  76.5 9.1 %copy-start.33 = (f32[192]{0:T(256)S(1)}, f32[192]{0:T(256)}, u32[]{:S(2)}) copy-start(f32[192]{0:T(256)} %get-tuple-element.38) | copy-start | bytes 2308
  76.5 10.6 %copy-start.14 = (f32[7,7,192]{2,1,0:T(8,128)S(1)}, f32[7,7,192]{2,1,0:T(8,128)}, u32[]{:S(2)}) copy-start(f32[7,7,192]{2,1,0:T(8,128)} %param.12) | copy-start | bytes 112900
  85.7 4.0 %collective-permute-start.6 = (f32[9984]{0:T(1024)S(1)}, f32[9984]{0:T(1024)S(1)}, u32[]{:S(2)}, u32[]{:S(2)}) collective-permute-start(f32[9984]{0:T(1024)S(1)} %concatenate.27), channel_id=1, source_target_pairs={{0,16},{16,0},{1,17},{17,1},{2,18},{18,2},{3,19},{19,3},{4,20},{20... | collective-permute-start | bytes 119816 | tf_op jit(solution)/shard_map/ppermute | solution.py:146
  87.7 4.4 %copy-start.37 = (pred[8,17]{0,1:T(8,128)(4,1)S(1)}, pred[8,17]{0,1:T(8,128)(4,1)}, u32[]{:S(2)}) copy-start(pred[8,17]{0,1:T(8,128)(4,1)} %constant.51) | copy-start | bytes 412
  89.7 7.7 %collective-permute-start.7 = (f32[9984]{0:T(1024)S(1)}, f32[9984]{0:T(1024)S(1)}, u32[]{:S(2)}, u32[]{:S(2)}) collective-permute-start(f32[9984]{0:T(1024)S(1)} %add.142), channel_id=1, source_target_pairs={{0,8},{4,12},{8,0},{12,4},{1,9},{5,13},{9,1},{13,5},{2,10},{6,14},... | collective-permute-start | bytes 119816 | tf_op jit(solution)/shard_map/ppermute | solution.py:146
  92.1 9.4 %collective-permute-start.10 = (f32[74304]{0:T(1024)S(1)}, f32[74304]{0:T(1024)S(1)}, u32[]{:S(2)}, u32[]{:S(2)}) collective-permute-start(f32[74304]{0:T(1024)S(1)} %add.145), channel_id=1, source_target_pairs={{0,4},{4,0},{8,12},{12,8},{1,5},{5,1},{9,13},{13,9},{2,6},{6,2},{1... | collective-permute-start | bytes 891656 | tf_op jit(solution)/shard_map/ppermute | solution.py:146
  97.3 4.1 %collective-permute-start.8 = (f32[9984]{0:T(1024)S(1)}, f32[9984]{0:T(1024)S(1)}, u32[]{:S(2)}, u32[]{:S(2)}) collective-permute-start(f32[9984]{0:T(1024)S(1)} %add.143), channel_id=1, source_target_pairs={{0,4},{4,0},{8,12},{12,8},{1,5},{5,1},{9,13},{13,9},{2,6},{6,2},{1... | collective-permute-start | bytes 119816 | tf_op jit(solution)/shard_map/ppermute | solution.py:146
  101.5 6.8 %collective-permute-start.11 = (f32[74304]{0:T(1024)S(1)}, f32[74304]{0:T(1024)S(1)}, u32[]{:S(2)}, u32[]{:S(2)}) collective-permute-start(f32[74304]{0:T(1024)S(1)} %add.146), channel_id=1, source_target_pairs={{0,16},{16,0},{1,17},{17,1},{2,18},{18,2},{3,19},{19,3},{4,20},{20... | collective-permute-start | bytes 891656 | tf_op jit(solution)/shard_map/ppermute | solution.py:146
  (26 other events, 52.0 us)

commit v18 on v13

--- a/solution.py
+++ b/solution.py
@@ -150,12 +150,12 @@
     return flat + lax.ppermute(flat, axis, [(i, i ^ step) for i in range(devices)])
 
 
-def butterfly_sum(values, axes):
+def butterfly_sum(values, axes, late_count):
     flat = flat_pack(values)
     first = butterfly_steps(axes[:1])
     order_a = first + butterfly_steps(axes[1:])[::-1]
     order_b = order_a[len(first) :] + order_a[: len(first)]
-    half = flat.shape[0] // 2
+    half = sum(v.size for v in values[:late_count])
     part_a, part_b = flat[:half], flat[half:]
     for step_a, step_b in zip(order_a, order_b):
         part_a, part_b = butterfly_step(part_a, *step_a), butterfly_step(part_b, *step_b)
@@ -250,6 +250,7 @@
     d_pre_own = lax.dynamic_slice_in_dim(d_pre, own * share, share, axis=1)
     grad_w_out = contract(hidden_own, g_out, 0, 0)
     grad_b_in = jnp.sum(d_pre_own, axis=0)
+    grad_b_in, g_pre = lax.optimization_barrier((grad_b_in, g_pre))
     grad_w_in = contract(normalized_output, g_pre_own, 0, 0)
     dn_partials = lax.dot_general(
         g_pre.reshape(pixel_count, blocks, share),
@@ -292,6 +293,7 @@
             grad_layer_scale,
         ),
         ("row", "col"),
+        4,
     )
     d_padded = extended(d_t.astype(jnp.bfloat16), (("row", 0), ("col", 1)), 3).astype(jnp.float32)
     grad_feature_t = (

time: 112 us -> 107 us (0.955)
  waiting for transfers between devices: 16.6 us -> 19.8 us
  starting transfers between devices: 21.3 us -> 18.4 us
  matrix products: 23 us -> 20.4 us
  other arithmetic: 14.5 us -> 12.6 us
    ppermute x6, waiting for transfers between devices: 8.82 us -> 13.2 us  [butterfly_step(): lax.ppermute(flat, axis, [(i, i ^ step) for i in range(devices)])]
    dot_general x4, matrix products: 9.02 us -> 6.49 us  [contract(): lax.dot_general(left, right, (((dim_left,), (dim_right,)), ((), ())), pre...]
    ppermute x2, waiting for transfers between devices: 3.9 us -> 2.04 us  [extended(): got = lax.ppermute(jnp.where(first, last, leading), axis, [(0, 1), (1, 0)])]
    ppermute x6, starting transfers between devices: 7.98 us -> 6.35 us  [butterfly_step(): lax.ppermute(flat, axis, [(i, i ^ step) for i in range(devices)])]
    reduce_sum x1, other arithmetic: 1.26 us -> 0.13 us  [shards(): grad_b_in = jnp.sum(d_pre_own, axis=0)]
  transfers between devices with their start and end apart: 12 -> 12, of which waited for: 5 -> 8; matrix products, arithmetic and copies ran while one was open for 17% -> 17% of each run, Pallas kernels for 7% -> 0%
where the time goes in v18:
time: 107 us; the launch traced here: 106 us
  matrix products  20.4 us (19%)
  waiting for transfers between devices  19.8 us (19%)
  starting transfers between devices  18.4 us (17%)
  local copies, waits for them, and re-layouts  16.9 us (16%)
  other arithmetic  12.6 us (12%)
  blocking collectives  8.6 us (8%)
  Pallas kernels  8.49 us (8%)
  between operations  1.17 us (1%)
    ppermute x6, waiting for transfers between devices, butterfly_step(): lax.ppermute(flat, axis, [(i, i ^ step) for i in range(devices)])  13.2 us
    conv_general_dilated x2, matrix products, depthwise_minor(): lax.conv_general_dilated(padded_t[None], kernel[:, :, None, :], (1, 1), '...  12.6 us
    all_gather x1, blocking collectives, gathered_weights(): full = lax.all_gather(packed, 'chan', axis=0, tiled=True)  8.6 us
    pallas_call x1, Pallas kernels, kernel_grad_minor(): pl.pallas_call(kernel_grad_body, out_shape=jax.ShapeDtypeStruct((side * s...  8.49 us
    dot_general x4, matrix products, contract(): lax.dot_general(left, right, (((dim_left,), (dim_right,)), ((), ())), pre...  6.49 us
    ppermute x6, starting transfers between devices, butterfly_step(): lax.ppermute(flat, axis, [(i, i ^ step) for i in range(devices)])  6.35 us
    ppermute x2, starting transfers between devices, extended(): before = lax.ppermute(last, axis, up)  5.85 us
    ppermute x2, waiting for transfers between devices, extended(): after = lax.ppermute(leading, axis, down)  4.58 us
  transfers between devices with their start and end apart: 12, of which 8 were waited for; matrix products, arithmetic and copies ran while one was open for 17% of the time, Pallas kernels for 0%

profile of v18, /device:TPU:0, one launch (start us, length us, event | category | flops | bytes accessed | tf_op | source)
XLA Modules:
  0.0 106.4 jit_solution(11067731508929125886)
XLA Ops:
  2.0 3.0 %collective-permute-start = (bf16[192,3,128]{0,2,1:T(8,128)(2,1)S(1)}, bf16[192,3,128]{0,2,1:T(8,128)(2,1)S(1)}, u32[]{:S(2)}, u32[]{:S(2)}) collective-permute-start(bf16[192,3,128]{0,2,1:T(8,128)(2,1)S(1)} %slice_select_fusion.1), channel_id=1, source_target_pairs={{0,16},{16,0},{1,17},{17,1},{2,18},{18,2},{3,19},{19,3},{4,20},{20... | collective-permute-start | bytes 442376 | tf_op jit(solution)/shard_map/ppermute | solution.py:18
  8.1 8.6 %all_gather.3 = bf16[768,387]{1,0:T(8,128)(2,1)S(1)} all-gather(bf16[192,387]{1,0:T(8,128)(2,1)S(1)} %concatenate.24), channel_id=1, replica_groups=mesh['row'=2,'col'=4,'chan'=4] {'chan'}, dimensions={0}, use_global_device_ids=true | all-gather | bytes 743040 | tf_op jit(solution)/shard_map/all_gather | solution.py:174
  18.2 3.5 %collective-permute-start.1 = (bf16[192,14,3]{0,2,1:T(4,128)(2,1)S(1)}, bf16[192,14,3]{0,2,1:T(4,128)(2,1)S(1)}, u32[]{:S(2)}, u32[]{:S(2)}) collective-permute-start(bf16[192,14,3]{0,2,1:T(4,128)(2,1)S(1)} %get-tuple-element.44), channel_id=1, source_target_pairs={{0,4},{4,8},{8,12},{1,5},{5,9},{9,13},{2,6},{6,10},{10,14},{3,7},{... | collective-permute-start | bytes 48392 | tf_op jit(solution)/shard_map/ppermute | solution.py:23
  23.5 3.9 %collective-permute-done.2 = bf16[192,14,3]{0,2,1:T(4,128)(2,1)S(1)} collective-permute-done((bf16[192,14,3]{0,2,1:T(4,128)(2,1)S(1)}, bf16[192,14,3]{0,2,1:T(4,128)(2,1)S(1)}, u32[]{:S(2)}, u32[]{:S(2)}) %collective-permute-start.2) | collective-permute-done | bytes 16160 | tf_op jit(solution)/shard_map/ppermute | solution.py:24
  27.4 1.6 %bitcast_convert_fusion = (f32[14,134,192]{2,1,0:T(8,128)}, bf16[1,14,134,192]{3,2,1,0:T(8,128)(2,1)S(1)}) fusion(bf16[192,14,3]{0,2,1:T(4,128)(2,1)S(1)} %collective-permute-done.2, bf16[192,3,128]{0,2,1:T(8,128)(2,1)S(1)} %get-tuple-element.57, bf16[192,8,128]{0,2,1:T(8,128)(2,1)S(1)} %copy.84, bf16[192,3,128]{0,2,1:T(8,128)(2,1)S(1)} %get-tuple-element.56, ...), kind=kLoop, calls=%fused_computation.32 | loop fusion | flops 3962112 | bytes 2881536 | tf_op jit(solution)/shard_map/convert_element_type | solution.py:215
  29.0 8.4 %fusion.6 = f32[1,8,128,192]{3,0,2,1:T(1,128)S(1)} fusion(bf16[1,14,134,192]{3,2,1,0:T(8,128)(2,1)S(1)} %get-tuple-element.41, f32[7,7,1,192]{3,1,0,2:T(8,128)S(1)} %bitcast.130), kind=kOutput, calls=%fused_computation.13 | convolution fusion | flops 115605504 | bytes 1544448 | tf_op jit(solution)/shard_map/conv_general_dilated | solution.py:184
  38.1 1.9 %copy.89 = f32[1,8,128,192]{2,1,3,0:T(8,128)} copy(f32[1,8,128,192]{3,0,2,1:T(1,128)S(1)} %fusion.6) | data formatting | bytes 1572864 | tf_op jit(solution)/shard_map/conv_general_dilated | solution.py:184
  40.3 2.2 %multiply_convert_fusion = (bf16[1024,768]{0,1:T(8,128)(2,1)S(1)}, f32[1024,768]{0,1:T(8,128)S(1)}) fusion(f32[768]{0:T(1024)S(1)} %fusion.35, f32[24,8,8,128]{3,2,1,0:T(8,128)} %bitcast.125, f32[192]{0:T(256)S(1)} %copy-done.12, f32[192]{0:T(256)S(1)} %copy-done.9, f32[1024]{0:T(1024)S(1)} %get-tuple-element.62, f32[1024]{0:T(1024)S(1)} %get-tuple-element.63, ...), kind=kOutput, calls=%fused_computation.9 | convolution fusion | flops 307888128 | bytes 5913600 | tf_op jit(solution)/shard_map/dot_general | solution.py:53
  43.9 3.8 %fusion.31 = (f32[192]{0:T(256)S(1)}, f32[192]{0:T(256)S(1)}, bf16[8,128,192]{1,0,2:T(8,128)(2,1)}) fusion(bf16[192,8,128]{2,1,0:T(8,128)(2,1)S(1)} %copy-done.1, f32[192]{0:T(256)S(1)} %copy-done.10, f32[192]{0:T(256)S(1)} %copy-done.11, f32[24,8,8,128]{3,2,1,0:T(8,128)S(1)} %copy.118, bf16[192,8,128]{2,1,0:T(8,128)(2,1)S(1)} %copy-done.3), kind=kLoop, calls=%fused_computation.47 | loop fusion | flops 1965696 | bytes 1969152 | tf_op jit(solution)/shard_map/reduce_sum | solution.py:243
  47.6 1.6 %fusion.59 = (bf16[1024,768]{0,1:T(8,128)(2,1)S(1)}, f32[1024,768]{0,1:T(8,128)S(1)}) fusion(f32[1024,768]{0,1:T(8,128)S(1)} %get-tuple-element.69, f32[768]{0:T(1024)S(1)} %fusion.35, bf16[1024,192]{0,1:T(8,128)(2,1)S(1)} %fusion.23, bf16[768,387]{1,0:T(8,128)(2,1)S(1)} %all_gather.3), kind=kOutput, calls=%fused_computation.112 | convolution fusion | flops 310640640 | bytes 8654848 | tf_op jit(solution)/shard_map/dot_general | solution.py:53
  50.6 1.3 %copy.99 = f32[1024,192]{1,0:T(8,128)} copy(f32[1024,192]{0,1:T(8,128)S(1)} %get-tuple-element.35) | data formatting | bytes 1572864 | tf_op jit(solution)/shard_map/reduce_sum | solution.py:261
  53.3 1.5 %fusion.56 = (bf16[8,128,192]{2,1,0:T(8,128)(2,1)S(1)}, f32[8,128,192]{2,1,0:T(8,128)}) fusion(f32[8,128]{1,0:T(8,128)S(1)} %broadcast_multiply_fusion, f32[8,128]{1,0:T(8,128)S(1)} %get-tuple-element.64, f32[192]{0:T(256)S(1)} %copy-done.8, f32[1,8,128,192]{3,0,2,1:T(1,128)S(1)} %fusion.6, f32[8,128]{1,0:T(8,128)S(1)} %multiply_bitcast_fusion, ...), kind=kLoop, calls=%fused_computation.110 | loop fusion | flops 1769472 | bytes 2770432 | tf_op jit(solution)/shard_map/convert_element_type | solution.py:298
  54.8 8.5 %shard_map.194 = f32[49,192]{1,0:T(8,128)} custom-call(f32[8,128,192]{2,1,0:T(8,128)} %get-tuple-element.39.d_ref, f32[14,134,192]{2,1,0:T(8,128)} %get-tuple-element.40.p_ref), custom_call_target="tpu_custom_call" | custom-call | tf_op jit(solution)/shard_map/pallas_call | solution.py:108
  64.8 1.4 %fusion.38 = f32[192,192]{1,0:T(8,128)S(1)} fusion(bf16[1024,768]{0,1:T(8,128)(2,1)} %copy-done.13, s32[]{:T(128)S(6)} %select_n.42, f32[24,8,8,128]{3,2,1,0:T(8,128)S(1)} %bitcast.126, f32[192]{0:T(256)S(1)} %copy-done.12, f32[192]{0:T(256)S(1)} %copy-done.9, f32[1024]{0:T(1024)S(1)} %get-tuple-element.62, f32[1024]{0:T(1024)S(1)} %get-tuple-element.63, ...), kind=kOutput, calls=%fused_computation.66 | convolution fusion | flops 76677120 | bytes 1337604 | tf_op jit(solution)/shard_map/dot_general | solution.py:53
  66.2 2.1 %collective-permute-done.6 = f32[9984]{0:T(1024)S(1)} collective-permute-done((f32[9984]{0:T(1024)S(1)}, f32[9984]{0:T(1024)S(1)}, u32[]{:S(2)}, u32[]{:S(2)}) %collective-permute-start.6) | collective-permute-done | bytes 39968 | tf_op jit(solution)/shard_map/ppermute | solution.py:150
  68.3 2.6 %collective-permute-start.7 = (f32[9984]{0:T(1024)S(1)}, f32[9984]{0:T(1024)S(1)}, u32[]{:S(2)}, u32[]{:S(2)}) collective-permute-start(f32[9984]{0:T(1024)S(1)} %add.142), channel_id=1, source_target_pairs={{0,8},{4,12},{8,0},{12,4},{1,9},{5,13},{9,1},{13,5},{2,10},{6,14},... | collective-permute-start | bytes 119816 | tf_op jit(solution)/shard_map/ppermute | solution.py:150
  72.4 1.6 %concatenate.28 = f32[74304]{0:T(1024)S(1)} concatenate(f32[36864]{0:T(1024)S(1)} %reshape.310, f32[192]{0:T(256)S(1)} %dynamic-slice_reduce_fusion, f32[36864]{0:T(1024)S(1)} %reshape.311, f32[192]{0:T(256)S(1)} %get-tuple-element.19, f32[192]{0:T(256)S(1)} %get-tuple-element.20), dimensions={0} | concatenate | bytes 594432 | tf_op jit(solution)/shard_map/concatenate | solution.py:120
  74.4 1.6 %collective-permute-start.8 = (f32[9984]{0:T(1024)S(1)}, f32[9984]{0:T(1024)S(1)}, u32[]{:S(2)}, u32[]{:S(2)}) collective-permute-start(f32[9984]{0:T(1024)S(1)} %add.143), channel_id=1, source_target_pairs={{0,4},{4,0},{8,12},{12,8},{1,5},{5,1},{9,13},{13,9},{2,6},{6,2},{1... | collective-permute-start | bytes 119816 | tf_op jit(solution)/shard_map/ppermute | solution.py:150
  76.6 3.1 %collective-permute-done.8 = f32[9984]{0:T(1024)S(1)} collective-permute-done((f32[9984]{0:T(1024)S(1)}, f32[9984]{0:T(1024)S(1)}, u32[]{:S(2)}, u32[]{:S(2)}) %collective-permute-start.8) | collective-permute-done | bytes 39968 | tf_op jit(solution)/shard_map/ppermute | solution.py:150
  79.8 2.0 %collective-permute-done.3 = bf16[3,128,192]{2,1,0:T(8,128)(2,1)S(1)} collective-permute-done((bf16[3,128,192]{2,1,0:T(8,128)(2,1)S(1)}, bf16[3,128,192]{2,1,0:T(8,128)(2,1)S(1)}, u32[]{:S(2)}, u32[]{:S(2)}) %collective-permute-start.3) | collective-permute-done | bytes 147488 | tf_op jit(solution)/shard_map/ppermute | solution.py:18
  81.9 2.4 %collective-permute-start.4 = (bf16[14,3,192]{2,1,0:T(4,128)(2,1)S(1)}, bf16[14,3,192]{2,1,0:T(4,128)(2,1)S(1)}, u32[]{:S(2)}, u32[]{:S(2)}) collective-permute-start(bf16[14,3,192]{2,1,0:T(4,128)(2,1)S(1)} %get-tuple-element.42), channel_id=1, source_target_pairs={{0,4},{4,8},{8,12},{1,5},{5,9},{9,13},{2,6},{6,10},{10,14},{3,7},{... | collective-permute-start | bytes 48392 | tf_op jit(solution)/shard_map/ppermute | solution.py:23
  85.5 2.0 %collective-permute-done.9 = f32[74304]{0:T(1024)S(1)} collective-permute-done((f32[74304]{0:T(1024)S(1)}, f32[74304]{0:T(1024)S(1)}, u32[]{:S(2)}, u32[]{:S(2)}) %collective-permute-start.9) | collective-permute-done | bytes 297248 | tf_op jit(solution)/shard_map/ppermute | solution.py:150
  91.6 4.8 %collective-permute-done.10 = f32[74304]{0:T(1024)S(1)} collective-permute-done((f32[74304]{0:T(1024)S(1)}, f32[74304]{0:T(1024)S(1)}, u32[]{:S(2)}, u32[]{:S(2)}) %collective-permute-start.10) | collective-permute-done | bytes 297248 | tf_op jit(solution)/shard_map/ppermute | solution.py:150
  96.9 4.2 %fusion.15 = f32[8,8,17,192]{3,1,2,0:T(8,128)S(1)} fusion(bf16[14,1,7,6,192]{4,2,3,0,1:T(8,128)(2,1)S(1)} %slice.124, bf16[14,1,8,17,192]{4,2,3,0,1:T(8,128)(2,1)S(1)} %copy.105, pred[8,17]{0,1:T(8,128)(4,1)S(1)} %copy-done.14, f32[7,7,1,192]{3,1,0,2:T(8,128)S(1)} %bitcast.131), kind=kOutput, calls=%fused_computation.23 | convolution fusion | flops 126007296 | bytes 1830280 | tf_op jit(solution)/shard_map/conv_general_dilated | solution.py:184
  (104 shorter events, 27.6 us)
Async XLA Ops:
  0.6 16.1 %copy-start.1 = (bf16[192,8,128]{2,1,0:T(8,128)(2,1)S(1)}, bf16[192,8,128]{2,1,0:T(8,128)(2,1)}, u32[]{:S(2)}) copy-start(bf16[192,8,128]{2,1,0:T(8,128)(2,1)} %param.21) | copy-start | bytes 1179652
  2.0 16.1 %collective-permute-start = (bf16[192,3,128]{0,2,1:T(8,128)(2,1)S(1)}, bf16[192,3,128]{0,2,1:T(8,128)(2,1)S(1)}, u32[]{:S(2)}, u32[]{:S(2)}) collective-permute-start(bf16[192,3,128]{0,2,1:T(8,128)(2,1)S(1)} %slice_select_fusion.1), channel_id=1, source_target_pairs={{0,16},{16,0},{1,17},{17,1},{2,18},{18,2},{3,19},{19,3},{4,20},{20... | collective-permute-start | bytes 442376 | tf_op jit(solution)/shard_map/ppermute | solution.py:18
  8.1 9.7 %copy-start.10 = (f32[192]{0:T(256)S(1)}, f32[192]{0:T(256)}, u32[]{:S(2)}) copy-start(f32[192]{0:T(256)} %param.20) | copy-start | bytes 2308
  18.0 5.4 %copy-start.7 = (f32[7,7,192]{2,1,0:T(8,128)S(1)}, f32[7,7,192]{2,1,0:T(8,128)}, u32[]{:S(2)}) copy-start(f32[7,7,192]{2,1,0:T(8,128)} %param.12) | copy-start | bytes 112900
  18.2 5.3 %collective-permute-start.1 = (bf16[192,14,3]{0,2,1:T(4,128)(2,1)S(1)}, bf16[192,14,3]{0,2,1:T(4,128)(2,1)S(1)}, u32[]{:S(2)}, u32[]{:S(2)}) collective-permute-start(bf16[192,14,3]{0,2,1:T(4,128)(2,1)S(1)} %get-tuple-element.44), channel_id=1, source_target_pairs={{0,4},{4,8},{8,12},{1,5},{5,9},{9,13},{2,6},{6,10},{10,14},{3,7},{... | collective-permute-start | bytes 48392 | tf_op jit(solution)/shard_map/ppermute | solution.py:23
  21.6 5.8 %collective-permute-start.2 = (bf16[192,14,3]{0,2,1:T(4,128)(2,1)S(1)}, bf16[192,14,3]{0,2,1:T(4,128)(2,1)S(1)}, u32[]{:S(2)}, u32[]{:S(2)}) collective-permute-start(bf16[192,14,3]{0,2,1:T(4,128)(2,1)S(1)} %get-tuple-element.45), channel_id=1, source_target_pairs={{4,0},{8,4},{12,8},{5,1},{9,5},{13,9},{6,2},{10,6},{14,10},{7,3},{... | collective-permute-start | bytes 48392 | tf_op jit(solution)/shard_map/ppermute | solution.py:24
  37.4 2.6 %copy-start.8 = (f32[192]{0:T(256)S(1)}, f32[192]{0:T(256)}, u32[]{:S(2)}) copy-start(f32[192]{0:T(256)} %param.13) | copy-start | bytes 2308
  38.1 2.2 %copy-start.9 = (f32[192]{0:T(256)S(1)}, f32[192]{0:T(256)}, u32[]{:S(2)}) copy-start(f32[192]{0:T(256)} %param.14) | copy-start | bytes 2308
  38.1 2.2 %copy-start.12 = (f32[192]{0:T(256)S(1)}, f32[192]{0:T(256)}, u32[]{:S(2)}) copy-start(f32[192]{0:T(256)} %param.15) | copy-start | bytes 2308
  40.3 2.2 %copy-start.4 = (bf16[768,192]{1,0:T(8,128)(2,1)S(1)}, bf16[768,192]{1,0:T(8,128)(2,1)}, u32[]{:S(2)}) copy-start(bf16[768,192]{1,0:T(8,128)(2,1)} %get-tuple-element.48) | copy-start | bytes 884740
  42.5 1.3 %copy-start.3 = (bf16[192,8,128]{2,1,0:T(8,128)(2,1)S(1)}, bf16[192,8,128]{2,1,0:T(8,128)(2,1)}, u32[]{:S(2)}) copy-start(bf16[192,8,128]{2,1,0:T(8,128)(2,1)} %param.11) | copy-start | bytes 1179652
  42.6 1.3 %copy-start.11 = (f32[192]{0:T(256)S(1)}, f32[192]{0:T(256)}, u32[]{:S(2)}) copy-start(f32[192]{0:T(256)} %param.19) | copy-start | bytes 2308
  47.6 1.8 %copy-start.6 = (bf16[768,192]{1,0:T(8,128)(2,1)S(1)}, bf16[768,192]{1,0:T(8,128)(2,1)}, u32[]{:S(2)}) copy-start(bf16[768,192]{1,0:T(8,128)(2,1)} %get-tuple-element.47) | copy-start | bytes 884740
  54.8 10.0 %copy-start.5 = (f32[1,8,128,192]{2,1,3,0:T(8,128)S(1)}, f32[1,8,128,192]{2,1,3,0:T(8,128)}, u32[]{:S(2)}) copy-start(f32[1,8,128,192]{2,1,3,0:T(8,128)} %copy.89) | copy-start | bytes 2359300
  64.3 4.0 %collective-permute-start.6 = (f32[9984]{0:T(1024)S(1)}, f32[9984]{0:T(1024)S(1)}, u32[]{:S(2)}, u32[]{:S(2)}) collective-permute-start(f32[9984]{0:T(1024)S(1)} %concatenate.27), channel_id=1, source_target_pairs={{0,16},{16,0},{1,17},{17,1},{2,18},{18,2},{3,19},{19,3},{4,20},{20... | collective-permute-start | bytes 119816 | tf_op jit(solution)/shard_map/ppermute | solution.py:150
  68.3 6.1 %collective-permute-start.7 = (f32[9984]{0:T(1024)S(1)}, f32[9984]{0:T(1024)S(1)}, u32[]{:S(2)}, u32[]{:S(2)}) collective-permute-start(f32[9984]{0:T(1024)S(1)} %add.142), channel_id=1, source_target_pairs={{0,8},{4,12},{8,0},{12,4},{1,9},{5,13},{9,1},{13,5},{2,10},{6,14},... | collective-permute-start | bytes 119816 | tf_op jit(solution)/shard_map/ppermute | solution.py:150
  74.0 13.6 %collective-permute-start.9 = (f32[74304]{0:T(1024)S(1)}, f32[74304]{0:T(1024)S(1)}, u32[]{:S(2)}, u32[]{:S(2)}) collective-permute-start(f32[74304]{0:T(1024)S(1)} %concatenate.28), channel_id=1, source_target_pairs={{0,8},{4,12},{8,0},{12,4},{1,9},{5,13},{9,1},{13,5},{2,10},{6,14},... | collective-permute-start | bytes 891656 | tf_op jit(solution)/shard_map/ppermute | solution.py:150
  74.4 5.4 %collective-permute-start.8 = (f32[9984]{0:T(1024)S(1)}, f32[9984]{0:T(1024)S(1)}, u32[]{:S(2)}, u32[]{:S(2)}) collective-permute-start(f32[9984]{0:T(1024)S(1)} %add.143), channel_id=1, source_target_pairs={{0,4},{4,0},{8,12},{12,8},{1,5},{5,1},{9,13},{13,9},{2,6},{6,2},{1... | collective-permute-start | bytes 119816 | tf_op jit(solution)/shard_map/ppermute | solution.py:150
  76.1 5.7 %collective-permute-start.3 = (bf16[3,128,192]{2,1,0:T(8,128)(2,1)S(1)}, bf16[3,128,192]{2,1,0:T(8,128)(2,1)S(1)}, u32[]{:S(2)}, u32[]{:S(2)}) collective-permute-start(bf16[3,128,192]{2,1,0:T(8,128)(2,1)S(1)} %slice_select_fusion), channel_id=1, source_target_pairs={{0,16},{16,0},{1,17},{17,1},{2,18},{18,2},{3,19},{19,3},{4,20},{20... | collective-permute-start | bytes 442376 | tf_op jit(solution)/shard_map/ppermute | solution.py:18
  81.9 7.8 %collective-permute-start.4 = (bf16[14,3,192]{2,1,0:T(4,128)(2,1)S(1)}, bf16[14,3,192]{2,1,0:T(4,128)(2,1)S(1)}, u32[]{:S(2)}, u32[]{:S(2)}) collective-permute-start(bf16[14,3,192]{2,1,0:T(4,128)(2,1)S(1)} %get-tuple-element.42), channel_id=1, source_target_pairs={{0,4},{4,8},{8,12},{1,5},{5,9},{9,13},{2,6},{6,10},{10,14},{3,7},{... | collective-permute-start | bytes 48392 | tf_op jit(solution)/shard_map/ppermute | solution.py:23
  84.2 6.1 %collective-permute-start.5 = (bf16[14,3,192]{2,1,0:T(4,128)(2,1)S(1)}, bf16[14,3,192]{2,1,0:T(4,128)(2,1)S(1)}, u32[]{:S(2)}, u32[]{:S(2)}) collective-permute-start(bf16[14,3,192]{2,1,0:T(4,128)(2,1)S(1)} %get-tuple-element.43), channel_id=1, source_target_pairs={{4,0},{8,4},{12,8},{5,1},{9,5},{13,9},{6,2},{10,6},{14,10},{7,3},{... | collective-permute-start | bytes 48392 | tf_op jit(solution)/shard_map/ppermute | solution.py:24
  87.6 8.7 %collective-permute-start.10 = (f32[74304]{0:T(1024)S(1)}, f32[74304]{0:T(1024)S(1)}, u32[]{:S(2)}, u32[]{:S(2)}) collective-permute-start(f32[74304]{0:T(1024)S(1)} %add.145), channel_id=1, source_target_pairs={{0,4},{4,0},{8,12},{12,8},{1,5},{5,1},{9,13},{13,9},{2,6},{6,2},{1... | collective-permute-start | bytes 891656 | tf_op jit(solution)/shard_map/ppermute | solution.py:150
  91.1 5.8 %copy-start.14 = (pred[8,17]{0,1:T(8,128)(4,1)S(1)}, pred[8,17]{0,1:T(8,128)(4,1)}, u32[]{:S(2)}) copy-start(pred[8,17]{0,1:T(8,128)(4,1)} %constant.51) | copy-start | bytes 412
  96.3 7.8 %collective-permute-start.11 = (f32[74304]{0:T(1024)S(1)}, f32[74304]{0:T(1024)S(1)}, u32[]{:S(2)}, u32[]{:S(2)}) collective-permute-start(f32[74304]{0:T(1024)S(1)} %add.146), channel_id=1, source_target_pairs={{0,16},{16,0},{1,17},{17,1},{2,18},{18,2},{3,19},{19,3},{4,20},{20... | collective-permute-start | bytes 891656 | tf_op jit(solution)/shard_map/ppermute | solution.py:150
  (3 other events, 3.5 us)

commit v19 on v16

--- a/solution.py
+++ b/solution.py
@@ -153,7 +153,7 @@
     order_b = order_a[len(first) :] + order_a[: len(first)]
     half = sum(v.size for v in values[:late_count])
     part_a, part_b = flat[:half], flat[half:]
-    for step_a, step_b in zip(order_a, order_b):
+    for step_b, step_a in zip(order_a, order_b):
         part_a, part_b = butterfly_step(part_a, *step_a), butterfly_step(part_b, *step_b)
     return flat_unpack(jnp.concatenate([part_a, part_b]), values)
 

time: 107 us -> 114 us (1.065)
  starting transfers between devices: 18.4 us -> 22.2 us
  waiting for transfers between devices: 19.7 us -> 23 us
    ppermute x6, waiting for transfers between devices: 13.1 us -> 16.9 us  [butterfly_step(): lax.ppermute(flat, axis, [(i, i ^ step) for i in range(devices)])]
    ppermute x6, starting transfers between devices: 6.36 us -> 10.1 us  [butterfly_step(): lax.ppermute(flat, axis, [(i, i ^ step) for i in range(devices)])]
  transfers between devices with their start and end apart: 12 -> 12, of which waited for: 8 -> 6; matrix products, arithmetic and copies ran while one was open for 17% -> 16% of each run, Pallas kernels for 0% -> 0%
where the time goes in v19:
time: 114 us; the launch traced here: 113 us
  waiting for transfers between devices  23 us (20%)
  starting transfers between devices  22.2 us (19%)
  matrix products  20.5 us (18%)
  local copies, waits for them, and re-layouts  16.1 us (14%)
  other arithmetic  13.8 us (12%)
  blocking collectives  8.6 us (8%)
  Pallas kernels  8.06 us (7%)
  between operations  1.17 us (1%)
    ppermute x6, waiting for transfers between devices, butterfly_step(): lax.ppermute(flat, axis, [(i, i ^ step) for i in range(devices)])  16.9 us
    conv_general_dilated x2, matrix products, depthwise_minor(): lax.conv_general_dilated(padded_t[None], kernel[:, :, None, :], (1, 1), '...  12.6 us
    ppermute x6, starting transfers between devices, butterfly_step(): lax.ppermute(flat, axis, [(i, i ^ step) for i in range(devices)])  10.1 us
    all_gather x1, blocking collectives, gathered_weights(): full = lax.all_gather(packed, 'chan', axis=0, tiled=True)  8.6 us
    pallas_call x1, Pallas kernels, kernel_grad_minor(): pl.pallas_call(kernel_grad_body, out_shape=jax.ShapeDtypeStruct((side * s...  8.06 us
    dot_general x4, matrix products, contract(): lax.dot_general(left, right, (((dim_left,), (dim_right,)), ((), ())), pre...  6.49 us
    ppermute x2, starting transfers between devices, extended(): before = lax.ppermute(last, axis, up)  5.9 us
    unnamed x36, local copies, waits for them, and re-layouts  4.6 us
  transfers between devices with their start and end apart: 12, of which 6 were waited for; matrix products, arithmetic and copies ran while one was open for 16% of the time, Pallas kernels for 0%

profile of v19, /device:TPU:0, one launch (start us, length us, event | category | flops | bytes accessed | tf_op | source)
XLA Modules:
  0.0 113.4 jit_solution(17453156876360935377)
XLA Ops:
  2.0 3.0 %collective-permute-start = (bf16[192,3,128]{0,2,1:T(8,128)(2,1)S(1)}, bf16[192,3,128]{0,2,1:T(8,128)(2,1)S(1)}, u32[]{:S(2)}, u32[]{:S(2)}) collective-permute-start(bf16[192,3,128]{0,2,1:T(8,128)(2,1)S(1)} %slice_select_fusion.1), channel_id=1, source_target_pairs={{0,16},{16,0},{1,17},{17,1},{2,18},{18,2},{3,19},{19,3},{4,20},{20... | collective-permute-start | bytes 442376 | tf_op jit(solution)/shard_map/ppermute | solution.py:18
  8.1 8.6 %all_gather.3 = bf16[768,387]{1,0:T(8,128)(2,1)S(1)} all-gather(bf16[192,387]{1,0:T(8,128)(2,1)S(1)} %concatenate.24), channel_id=1, replica_groups=mesh['row'=2,'col'=4,'chan'=4] {'chan'}, dimensions={0}, use_global_device_ids=true | all-gather | bytes 743040 | tf_op jit(solution)/shard_map/all_gather | solution.py:170
  18.2 3.5 %collective-permute-start.1 = (bf16[192,14,3]{0,2,1:T(4,128)(2,1)S(1)}, bf16[192,14,3]{0,2,1:T(4,128)(2,1)S(1)}, u32[]{:S(2)}, u32[]{:S(2)}) collective-permute-start(bf16[192,14,3]{0,2,1:T(4,128)(2,1)S(1)} %get-tuple-element.44), channel_id=1, source_target_pairs={{0,4},{4,8},{8,12},{1,5},{5,9},{9,13},{2,6},{6,10},{10,14},{3,7},{... | collective-permute-start | bytes 48392 | tf_op jit(solution)/shard_map/ppermute | solution.py:23
  23.5 3.9 %collective-permute-done.2 = bf16[192,14,3]{0,2,1:T(4,128)(2,1)S(1)} collective-permute-done((bf16[192,14,3]{0,2,1:T(4,128)(2,1)S(1)}, bf16[192,14,3]{0,2,1:T(4,128)(2,1)S(1)}, u32[]{:S(2)}, u32[]{:S(2)}) %collective-permute-start.2) | collective-permute-done | bytes 16160 | tf_op jit(solution)/shard_map/ppermute | solution.py:24
  27.4 1.6 %bitcast_convert_fusion = (f32[14,134,192]{2,1,0:T(8,128)}, bf16[1,14,134,192]{3,2,1,0:T(8,128)(2,1)S(1)}) fusion(bf16[192,14,3]{0,2,1:T(4,128)(2,1)S(1)} %collective-permute-done.2, bf16[192,3,128]{0,2,1:T(8,128)(2,1)S(1)} %get-tuple-element.57, bf16[192,8,128]{0,2,1:T(8,128)(2,1)S(1)} %copy.84, bf16[192,3,128]{0,2,1:T(8,128)(2,1)S(1)} %get-tuple-element.56, ...), kind=kLoop, calls=%fused_computation.32 | loop fusion | flops 3962112 | bytes 2881536 | tf_op jit(solution)/shard_map/convert_element_type | solution.py:211
  29.0 8.4 %fusion.6 = f32[1,8,128,192]{3,0,2,1:T(1,128)S(1)} fusion(bf16[1,14,134,192]{3,2,1,0:T(8,128)(2,1)S(1)} %get-tuple-element.41, f32[7,7,1,192]{3,1,0,2:T(8,128)S(1)} %bitcast.130), kind=kOutput, calls=%fused_computation.13 | convolution fusion | flops 115605504 | bytes 1544448 | tf_op jit(solution)/shard_map/conv_general_dilated | solution.py:180
  38.1 1.9 %copy.89 = f32[1,8,128,192]{2,1,3,0:T(8,128)} copy(f32[1,8,128,192]{3,0,2,1:T(1,128)S(1)} %fusion.6) | data formatting | bytes 1572864 | tf_op jit(solution)/shard_map/conv_general_dilated | solution.py:180
  40.3 2.2 %multiply_convert_fusion = (bf16[1024,768]{0,1:T(8,128)(2,1)S(1)}, f32[1024,768]{0,1:T(8,128)S(1)}) fusion(f32[768]{0:T(1024)S(1)} %fusion.35, f32[24,8,8,128]{3,2,1,0:T(8,128)} %bitcast.125, f32[192]{0:T(256)S(1)} %copy-done.12, f32[192]{0:T(256)S(1)} %copy-done.9, f32[1024]{0:T(1024)S(1)} %get-tuple-element.62, f32[1024]{0:T(1024)S(1)} %get-tuple-element.63, ...), kind=kOutput, calls=%fused_computation.9 | convolution fusion | flops 307888128 | bytes 5913600 | tf_op jit(solution)/shard_map/dot_general | solution.py:53
  43.9 3.8 %fusion.31 = (f32[192]{0:T(256)S(1)}, f32[192]{0:T(256)S(1)}, bf16[8,128,192]{1,0,2:T(8,128)(2,1)}) fusion(bf16[192,8,128]{2,1,0:T(8,128)(2,1)S(1)} %copy-done.1, f32[192]{0:T(256)S(1)} %copy-done.10, f32[192]{0:T(256)S(1)} %copy-done.11, f32[24,8,8,128]{3,2,1,0:T(8,128)S(1)} %copy.118, bf16[192,8,128]{2,1,0:T(8,128)(2,1)S(1)} %copy-done.3), kind=kLoop, calls=%fused_computation.47 | loop fusion | flops 1965696 | bytes 1969152 | tf_op jit(solution)/shard_map/reduce_sum | solution.py:239
  47.6 1.6 %fusion.59 = (bf16[1024,768]{0,1:T(8,128)(2,1)S(1)}, f32[1024,768]{0,1:T(8,128)S(1)}) fusion(f32[1024,768]{0,1:T(8,128)S(1)} %get-tuple-element.69, f32[768]{0:T(1024)S(1)} %fusion.35, bf16[1024,192]{0,1:T(8,128)(2,1)S(1)} %fusion.23, bf16[768,387]{1,0:T(8,128)(2,1)S(1)} %all_gather.3), kind=kOutput, calls=%fused_computation.112 | convolution fusion | flops 310640640 | bytes 8654848 | tf_op jit(solution)/shard_map/dot_general | solution.py:53
  53.3 1.5 %fusion.56 = (bf16[8,128,192]{2,1,0:T(8,128)(2,1)S(1)}, f32[8,128,192]{2,1,0:T(8,128)}) fusion(f32[8,128]{1,0:T(8,128)S(1)} %broadcast_multiply_fusion, f32[8,128]{1,0:T(8,128)S(1)} %get-tuple-element.64, f32[192]{0:T(256)S(1)} %copy-done.8, f32[1,8,128,192]{3,0,2,1:T(1,128)S(1)} %fusion.6, f32[8,128]{1,0:T(8,128)S(1)} %multiply_bitcast_fusion, ...), kind=kLoop, calls=%fused_computation.110 | loop fusion | flops 1769472 | bytes 2770432 | tf_op jit(solution)/shard_map/convert_element_type | solution.py:294
  54.8 8.1 %shard_map.194 = f32[49,8,192]{2,1,0:T(8,128)} custom-call(f32[8,128,192]{2,1,0:T(8,128)} %get-tuple-element.39.d_ref, f32[14,134,192]{2,1,0:T(8,128)} %get-tuple-element.40.p_ref), custom_call_target="tpu_custom_call" | custom-call | tf_op jit(solution)/shard_map/pallas_call | solution.py:107
  64.2 2.6 %collective-permute-start.6 = (f32[9984]{0:T(1024)S(1)}, f32[9984]{0:T(1024)S(1)}, u32[]{:S(2)}, u32[]{:S(2)}) collective-permute-start(f32[9984]{0:T(1024)S(1)} %concatenate.27), channel_id=1, source_target_pairs={{0,8},{4,12},{8,0},{12,4},{1,9},{5,13},{9,1},{13,5},{2,10},{6,14},... | collective-permute-start | bytes 119816 | tf_op jit(solution)/shard_map/ppermute | solution.py:146
  66.8 1.4 %fusion.38 = f32[192,192]{1,0:T(8,128)S(1)} fusion(bf16[1024,768]{0,1:T(8,128)(2,1)} %copy-done.13, s32[]{:T(128)S(6)} %select_n.42, f32[24,8,8,128]{3,2,1,0:T(8,128)S(1)} %bitcast.126, f32[192]{0:T(256)S(1)} %copy-done.12, f32[192]{0:T(256)S(1)} %copy-done.9, f32[1024]{0:T(1024)S(1)} %get-tuple-element.62, f32[1024]{0:T(1024)S(1)} %get-tuple-element.63, ...), kind=kOutput, calls=%fused_computation.66 | convolution fusion | flops 76677120 | bytes 1337604 | tf_op jit(solution)/shard_map/dot_general | solution.py:53
  69.1 1.6 %collective-permute-start.7 = (f32[9984]{0:T(1024)S(1)}, f32[9984]{0:T(1024)S(1)}, u32[]{:S(2)}, u32[]{:S(2)}) collective-permute-start(f32[9984]{0:T(1024)S(1)} %add.142), channel_id=1, source_target_pairs={{0,4},{4,0},{8,12},{12,8},{1,5},{5,1},{9,13},{13,9},{2,6},{6,2},{1... | collective-permute-start | bytes 119816 | tf_op jit(solution)/shard_map/ppermute | solution.py:146
  72.2 1.6 %concatenate.28 = f32[74304]{0:T(1024)S(1)} concatenate(f32[36864]{0:T(1024)S(1)} %reshape.310, f32[192]{0:T(256)S(1)} %dynamic-slice_reduce_fusion, f32[36864]{0:T(1024)S(1)} %reshape.311, f32[192]{0:T(256)S(1)} %get-tuple-element.19, f32[192]{0:T(256)S(1)} %get-tuple-element.20), dimensions={0} | concatenate | bytes 594432 | tf_op jit(solution)/shard_map/concatenate | solution.py:116
  74.3 1.6 %collective-permute-start.8 = (f32[9984]{0:T(1024)S(1)}, f32[9984]{0:T(1024)S(1)}, u32[]{:S(2)}, u32[]{:S(2)}) collective-permute-start(f32[9984]{0:T(1024)S(1)} %add.143), channel_id=1, source_target_pairs={{0,16},{16,0},{1,17},{17,1},{2,18},{18,2},{3,19},{19,3},{4,20},{20... | collective-permute-start | bytes 119816 | tf_op jit(solution)/shard_map/ppermute | solution.py:146
  76.5 6.8 %collective-permute-done.8 = f32[9984]{0:T(1024)S(1)} collective-permute-done((f32[9984]{0:T(1024)S(1)}, f32[9984]{0:T(1024)S(1)}, u32[]{:S(2)}, u32[]{:S(2)}) %collective-permute-start.8) | collective-permute-done | bytes 39968 | tf_op jit(solution)/shard_map/ppermute | solution.py:146
  83.3 2.1 %collective-permute-done.3 = bf16[3,128,192]{2,1,0:T(8,128)(2,1)S(1)} collective-permute-done((bf16[3,128,192]{2,1,0:T(8,128)(2,1)S(1)}, bf16[3,128,192]{2,1,0:T(8,128)(2,1)S(1)}, u32[]{:S(2)}, u32[]{:S(2)}) %collective-permute-start.3) | collective-permute-done | bytes 147488 | tf_op jit(solution)/shard_map/ppermute | solution.py:18
  85.4 2.4 %collective-permute-start.4 = (bf16[14,3,192]{2,1,0:T(4,128)(2,1)S(1)}, bf16[14,3,192]{2,1,0:T(4,128)(2,1)S(1)}, u32[]{:S(2)}, u32[]{:S(2)}) collective-permute-start(bf16[14,3,192]{2,1,0:T(4,128)(2,1)S(1)} %get-tuple-element.42), channel_id=1, source_target_pairs={{0,4},{4,8},{8,12},{1,5},{5,9},{9,13},{2,6},{6,10},{10,14},{3,7},{... | collective-permute-start | bytes 48392 | tf_op jit(solution)/shard_map/ppermute | solution.py:23
  89.2 3.5 %collective-permute-start.10 = (f32[74304]{0:T(1024)S(1)}, f32[74304]{0:T(1024)S(1)}, u32[]{:S(2)}, u32[]{:S(2)}) collective-permute-start(f32[74304]{0:T(1024)S(1)} %add.145), channel_id=1, source_target_pairs={{0,8},{4,12},{8,0},{12,4},{1,9},{5,13},{9,1},{13,5},{2,10},{6,14},... | collective-permute-start | bytes 891656 | tf_op jit(solution)/shard_map/ppermute | solution.py:146
  95.3 7.8 %collective-permute-done.10 = f32[74304]{0:T(1024)S(1)} collective-permute-done((f32[74304]{0:T(1024)S(1)}, f32[74304]{0:T(1024)S(1)}, u32[]{:S(2)}, u32[]{:S(2)}) %collective-permute-start.10) | collective-permute-done | bytes 297248 | tf_op jit(solution)/shard_map/ppermute | solution.py:146
  103.5 4.2 %fusion.15 = f32[8,8,17,192]{3,1,2,0:T(8,128)S(1)} fusion(bf16[14,1,7,6,192]{4,2,3,0,1:T(8,128)(2,1)S(1)} %slice.124, bf16[14,1,8,17,192]{4,2,3,0,1:T(8,128)(2,1)S(1)} %copy.105, pred[8,17]{0,1:T(8,128)(4,1)S(1)} %copy-done.14, f32[7,7,1,192]{3,1,0,2:T(8,128)S(1)} %bitcast.131), kind=kOutput, calls=%fused_computation.23 | convolution fusion | flops 126007296 | bytes 1830280 | tf_op jit(solution)/shard_map/conv_general_dilated | solution.py:180
  109.6 1.4 %collective-permute-done.11 = f32[74304]{0:T(1024)S(1)} collective-permute-done((f32[74304]{0:T(1024)S(1)}, f32[74304]{0:T(1024)S(1)}, u32[]{:S(2)}, u32[]{:S(2)}) %collective-permute-start.11) | collective-permute-done | bytes 297248 | tf_op jit(solution)/shard_map/ppermute | solution.py:146
  (105 shorter events, 27.2 us)
Async XLA Ops:
  0.6 16.1 %copy-start.1 = (bf16[192,8,128]{2,1,0:T(8,128)(2,1)S(1)}, bf16[192,8,128]{2,1,0:T(8,128)(2,1)}, u32[]{:S(2)}) copy-start(bf16[192,8,128]{2,1,0:T(8,128)(2,1)} %param.21) | copy-start | bytes 1179652
  2.0 16.1 %collective-permute-start = (bf16[192,3,128]{0,2,1:T(8,128)(2,1)S(1)}, bf16[192,3,128]{0,2,1:T(8,128)(2,1)S(1)}, u32[]{:S(2)}, u32[]{:S(2)}) collective-permute-start(bf16[192,3,128]{0,2,1:T(8,128)(2,1)S(1)} %slice_select_fusion.1), channel_id=1, source_target_pairs={{0,16},{16,0},{1,17},{17,1},{2,18},{18,2},{3,19},{19,3},{4,20},{20... | collective-permute-start | bytes 442376 | tf_op jit(solution)/shard_map/ppermute | solution.py:18
  8.1 9.7 %copy-start.10 = (f32[192]{0:T(256)S(1)}, f32[192]{0:T(256)}, u32[]{:S(2)}) copy-start(f32[192]{0:T(256)} %param.20) | copy-start | bytes 2308
  18.0 5.4 %copy-start.7 = (f32[7,7,192]{2,1,0:T(8,128)S(1)}, f32[7,7,192]{2,1,0:T(8,128)}, u32[]{:S(2)}) copy-start(f32[7,7,192]{2,1,0:T(8,128)} %param.12) | copy-start | bytes 112900
  18.2 5.3 %collective-permute-start.1 = (bf16[192,14,3]{0,2,1:T(4,128)(2,1)S(1)}, bf16[192,14,3]{0,2,1:T(4,128)(2,1)S(1)}, u32[]{:S(2)}, u32[]{:S(2)}) collective-permute-start(bf16[192,14,3]{0,2,1:T(4,128)(2,1)S(1)} %get-tuple-element.44), channel_id=1, source_target_pairs={{0,4},{4,8},{8,12},{1,5},{5,9},{9,13},{2,6},{6,10},{10,14},{3,7},{... | collective-permute-start | bytes 48392 | tf_op jit(solution)/shard_map/ppermute | solution.py:23
  21.6 5.8 %collective-permute-start.2 = (bf16[192,14,3]{0,2,1:T(4,128)(2,1)S(1)}, bf16[192,14,3]{0,2,1:T(4,128)(2,1)S(1)}, u32[]{:S(2)}, u32[]{:S(2)}) collective-permute-start(bf16[192,14,3]{0,2,1:T(4,128)(2,1)S(1)} %get-tuple-element.45), channel_id=1, source_target_pairs={{4,0},{8,4},{12,8},{5,1},{9,5},{13,9},{6,2},{10,6},{14,10},{7,3},{... | collective-permute-start | bytes 48392 | tf_op jit(solution)/shard_map/ppermute | solution.py:24
  37.4 2.6 %copy-start.8 = (f32[192]{0:T(256)S(1)}, f32[192]{0:T(256)}, u32[]{:S(2)}) copy-start(f32[192]{0:T(256)} %param.13) | copy-start | bytes 2308
  38.1 2.2 %copy-start.9 = (f32[192]{0:T(256)S(1)}, f32[192]{0:T(256)}, u32[]{:S(2)}) copy-start(f32[192]{0:T(256)} %param.14) | copy-start | bytes 2308
  38.1 2.2 %copy-start.12 = (f32[192]{0:T(256)S(1)}, f32[192]{0:T(256)}, u32[]{:S(2)}) copy-start(f32[192]{0:T(256)} %param.15) | copy-start | bytes 2308
  40.3 2.2 %copy-start.4 = (bf16[768,192]{1,0:T(8,128)(2,1)S(1)}, bf16[768,192]{1,0:T(8,128)(2,1)}, u32[]{:S(2)}) copy-start(bf16[768,192]{1,0:T(8,128)(2,1)} %get-tuple-element.48) | copy-start | bytes 884740
  42.5 1.3 %copy-start.3 = (bf16[192,8,128]{2,1,0:T(8,128)(2,1)S(1)}, bf16[192,8,128]{2,1,0:T(8,128)(2,1)}, u32[]{:S(2)}) copy-start(bf16[192,8,128]{2,1,0:T(8,128)(2,1)} %param.11) | copy-start | bytes 1179652
  42.6 1.3 %copy-start.11 = (f32[192]{0:T(256)S(1)}, f32[192]{0:T(256)}, u32[]{:S(2)}) copy-start(f32[192]{0:T(256)} %param.19) | copy-start | bytes 2308
  47.6 1.8 %copy-start.6 = (bf16[768,192]{1,0:T(8,128)(2,1)S(1)}, bf16[768,192]{1,0:T(8,128)(2,1)}, u32[]{:S(2)}) copy-start(bf16[768,192]{1,0:T(8,128)(2,1)} %get-tuple-element.47) | copy-start | bytes 884740
  54.8 11.9 %copy-start.5 = (f32[1,8,128,192]{2,1,3,0:T(8,128)S(1)}, f32[1,8,128,192]{2,1,3,0:T(8,128)}, u32[]{:S(2)}) copy-start(f32[1,8,128,192]{2,1,3,0:T(8,128)} %copy.89) | copy-start | bytes 2359300
  64.2 4.9 %collective-permute-start.6 = (f32[9984]{0:T(1024)S(1)}, f32[9984]{0:T(1024)S(1)}, u32[]{:S(2)}, u32[]{:S(2)}) collective-permute-start(f32[9984]{0:T(1024)S(1)} %concatenate.27), channel_id=1, source_target_pairs={{0,8},{4,12},{8,0},{12,4},{1,9},{5,13},{9,1},{13,5},{2,10},{6,14},... | collective-permute-start | bytes 119816 | tf_op jit(solution)/shard_map/ppermute | solution.py:146
  69.1 5.2 %collective-permute-start.7 = (f32[9984]{0:T(1024)S(1)}, f32[9984]{0:T(1024)S(1)}, u32[]{:S(2)}, u32[]{:S(2)}) collective-permute-start(f32[9984]{0:T(1024)S(1)} %add.142), channel_id=1, source_target_pairs={{0,4},{4,0},{8,12},{12,8},{1,5},{5,1},{9,13},{13,9},{2,6},{6,2},{1... | collective-permute-start | bytes 119816 | tf_op jit(solution)/shard_map/ppermute | solution.py:146
  73.8 15.4 %collective-permute-start.9 = (f32[74304]{0:T(1024)S(1)}, f32[74304]{0:T(1024)S(1)}, u32[]{:S(2)}, u32[]{:S(2)}) collective-permute-start(f32[74304]{0:T(1024)S(1)} %concatenate.28), channel_id=1, source_target_pairs={{0,16},{16,0},{1,17},{17,1},{2,18},{18,2},{3,19},{19,3},{4,20},{20... | collective-permute-start | bytes 891656 | tf_op jit(solution)/shard_map/ppermute | solution.py:146
  74.3 9.0 %collective-permute-start.8 = (f32[9984]{0:T(1024)S(1)}, f32[9984]{0:T(1024)S(1)}, u32[]{:S(2)}, u32[]{:S(2)}) collective-permute-start(f32[9984]{0:T(1024)S(1)} %add.143), channel_id=1, source_target_pairs={{0,16},{16,0},{1,17},{17,1},{2,18},{18,2},{3,19},{19,3},{4,20},{20... | collective-permute-start | bytes 119816 | tf_op jit(solution)/shard_map/ppermute | solution.py:146
  75.9 9.4 %collective-permute-start.3 = (bf16[3,128,192]{2,1,0:T(8,128)(2,1)S(1)}, bf16[3,128,192]{2,1,0:T(8,128)(2,1)S(1)}, u32[]{:S(2)}, u32[]{:S(2)}) collective-permute-start(bf16[3,128,192]{2,1,0:T(8,128)(2,1)S(1)} %slice_select_fusion), channel_id=1, source_target_pairs={{0,16},{16,0},{1,17},{17,1},{2,18},{18,2},{3,19},{19,3},{4,20},{20... | collective-permute-start | bytes 442376 | tf_op jit(solution)/shard_map/ppermute | solution.py:18
  85.4 8.7 %collective-permute-start.4 = (bf16[14,3,192]{2,1,0:T(4,128)(2,1)S(1)}, bf16[14,3,192]{2,1,0:T(4,128)(2,1)S(1)}, u32[]{:S(2)}, u32[]{:S(2)}) collective-permute-start(bf16[14,3,192]{2,1,0:T(4,128)(2,1)S(1)} %get-tuple-element.42), channel_id=1, source_target_pairs={{0,4},{4,8},{8,12},{1,5},{5,9},{9,13},{2,6},{6,10},{10,14},{3,7},{... | collective-permute-start | bytes 48392 | tf_op jit(solution)/shard_map/ppermute | solution.py:23
  87.8 6.2 %collective-permute-start.5 = (bf16[14,3,192]{2,1,0:T(4,128)(2,1)S(1)}, bf16[14,3,192]{2,1,0:T(4,128)(2,1)S(1)}, u32[]{:S(2)}, u32[]{:S(2)}) collective-permute-start(bf16[14,3,192]{2,1,0:T(4,128)(2,1)S(1)} %get-tuple-element.43), channel_id=1, source_target_pairs={{4,0},{8,4},{12,8},{5,1},{9,5},{13,9},{6,2},{10,6},{14,10},{7,3},{... | collective-permute-start | bytes 48392 | tf_op jit(solution)/shard_map/ppermute | solution.py:24
  89.2 14.0 %collective-permute-start.10 = (f32[74304]{0:T(1024)S(1)}, f32[74304]{0:T(1024)S(1)}, u32[]{:S(2)}, u32[]{:S(2)}) collective-permute-start(f32[74304]{0:T(1024)S(1)} %add.145), channel_id=1, source_target_pairs={{0,8},{4,12},{8,0},{12,4},{1,9},{5,13},{9,1},{13,5},{2,10},{6,14},... | collective-permute-start | bytes 891656 | tf_op jit(solution)/shard_map/ppermute | solution.py:146
  94.9 8.6 %copy-start.14 = (pred[8,17]{0,1:T(8,128)(4,1)S(1)}, pred[8,17]{0,1:T(8,128)(4,1)}, u32[]{:S(2)}) copy-start(pred[8,17]{0,1:T(8,128)(4,1)} %constant.51) | copy-start | bytes 412
  103.2 7.8 %collective-permute-start.11 = (f32[74304]{0:T(1024)S(1)}, f32[74304]{0:T(1024)S(1)}, u32[]{:S(2)}, u32[]{:S(2)}) collective-permute-start(f32[74304]{0:T(1024)S(1)} %add.146), channel_id=1, source_target_pairs={{0,4},{4,0},{8,12},{12,8},{1,5},{5,1},{9,13},{13,9},{2,6},{6,2},{1... | collective-permute-start | bytes 891656 | tf_op jit(solution)/shard_map/ppermute | solution.py:146
  (3 other events, 3.5 us)

commit v20 on v16

--- a/solution.py
+++ b/solution.py
@@ -149,8 +149,9 @@
 def butterfly_sum(values, axes, late_count):
     flat = flat_pack(values)
     first = butterfly_steps(axes[:1])
-    order_a = first + butterfly_steps(axes[1:])[::-1]
-    order_b = order_a[len(first) :] + order_a[: len(first)]
+    rotated = first + butterfly_steps(axes[1:])[::-1]
+    order_a = first + butterfly_steps(axes[1:])
+    order_b = rotated[len(first) :] + rotated[: len(first)]
     half = sum(v.size for v in values[:late_count])
     part_a, part_b = flat[:half], flat[half:]
     for step_a, step_b in zip(order_a, order_b):

time: 107 us -> 112 us (1.047)
  waiting for transfers between devices: 19.7 us -> 23.7 us
    ppermute x6, waiting for transfers between devices: 13.1 us -> 19.1 us  [butterfly_step(): lax.ppermute(flat, axis, [(i, i ^ step) for i in range(devices)])]
    ppermute x2, waiting for transfers between devices: 2.03 us -> 0.01 us  [extended(): got = lax.ppermute(jnp.where(first, last, leading), axis, [(0, 1), (1, 0)])]
    ppermute x6, starting transfers between devices: 6.36 us -> 8.39 us  [butterfly_step(): lax.ppermute(flat, axis, [(i, i ^ step) for i in range(devices)])]
  transfers between devices with their start and end apart: 12 -> 12, of which waited for: 8 -> 6; matrix products, arithmetic and copies ran while one was open for 17% -> 16% of each run, Pallas kernels for 0% -> 0%
where the time goes in v20:
time: 112 us; the launch traced here: 111 us
  waiting for transfers between devices  23.7 us (21%)
  matrix products  20.5 us (18%)
  starting transfers between devices  19.4 us (17%)
  local copies, waits for them, and re-layouts  16.1 us (14%)
  other arithmetic  13.8 us (12%)
  blocking collectives  8.6 us (8%)
  Pallas kernels  8.06 us (7%)
  between operations  1.18 us (1%)
    ppermute x6, waiting for transfers between devices, butterfly_step(): lax.ppermute(flat, axis, [(i, i ^ step) for i in range(devices)])  19.1 us
    conv_general_dilated x2, matrix products, depthwise_minor(): lax.conv_general_dilated(padded_t[None], kernel[:, :, None, :], (1, 1), '...  12.6 us
    all_gather x1, blocking collectives, gathered_weights(): full = lax.all_gather(packed, 'chan', axis=0, tiled=True)  8.6 us
    ppermute x6, starting transfers between devices, butterfly_step(): lax.ppermute(flat, axis, [(i, i ^ step) for i in range(devices)])  8.39 us
    pallas_call x1, Pallas kernels, kernel_grad_minor(): pl.pallas_call(kernel_grad_body, out_shape=jax.ShapeDtypeStruct((side * s...  8.06 us
    dot_general x4, matrix products, contract(): lax.dot_general(left, right, (((dim_left,), (dim_right,)), ((), ())), pre...  6.49 us
    ppermute x2, starting transfers between devices, extended(): before = lax.ppermute(last, axis, up)  4.84 us
    ppermute x2, waiting for transfers between devices, extended(): after = lax.ppermute(leading, axis, down)  4.61 us
  transfers between devices with their start and end apart: 12, of which 6 were waited for; matrix products, arithmetic and copies ran while one was open for 16% of the time, Pallas kernels for 0%

profile of v20, /device:TPU:0, one launch (start us, length us, event | category | flops | bytes accessed | tf_op | source)
XLA Modules:
  0.0 111.4 jit_solution(15523091216646644124)
XLA Ops:
  0.7 1.3 %copy.84 = bf16[192,8,128]{0,2,1:T(8,128)(2,1)S(1)} copy(bf16[192,8,128]{2,1,0:T(8,128)(2,1)} %param.11) | data formatting | bytes 786432 | tf_op args[0]
  2.0 3.0 %collective-permute-start = (bf16[192,3,128]{0,2,1:T(8,128)(2,1)S(1)}, bf16[192,3,128]{0,2,1:T(8,128)(2,1)S(1)}, u32[]{:S(2)}, u32[]{:S(2)}) collective-permute-start(bf16[192,3,128]{0,2,1:T(8,128)(2,1)S(1)} %slice_select_fusion.1), channel_id=1, source_target_pairs={{0,16},{16,0},{1,17},{17,1},{2,18},{18,2},{3,19},{19,3},{4,20},{20... | collective-permute-start | bytes 442376 | tf_op jit(solution)/shard_map/ppermute | solution.py:18
  8.1 8.6 %all_gather.3 = bf16[768,387]{1,0:T(8,128)(2,1)S(1)} all-gather(bf16[192,387]{1,0:T(8,128)(2,1)S(1)} %concatenate.24), channel_id=1, replica_groups=mesh['row'=2,'col'=4,'chan'=4] {'chan'}, dimensions={0}, use_global_device_ids=true | all-gather | bytes 743040 | tf_op jit(solution)/shard_map/all_gather | solution.py:171
  18.2 3.5 %collective-permute-start.1 = (bf16[192,14,3]{0,2,1:T(4,128)(2,1)S(1)}, bf16[192,14,3]{0,2,1:T(4,128)(2,1)S(1)}, u32[]{:S(2)}, u32[]{:S(2)}) collective-permute-start(bf16[192,14,3]{0,2,1:T(4,128)(2,1)S(1)} %get-tuple-element.44), channel_id=1, source_target_pairs={{0,4},{4,8},{8,12},{1,5},{5,9},{9,13},{2,6},{6,10},{10,14},{3,7},{... | collective-permute-start | bytes 48392 | tf_op jit(solution)/shard_map/ppermute | solution.py:23
  23.5 3.9 %collective-permute-done.2 = bf16[192,14,3]{0,2,1:T(4,128)(2,1)S(1)} collective-permute-done((bf16[192,14,3]{0,2,1:T(4,128)(2,1)S(1)}, bf16[192,14,3]{0,2,1:T(4,128)(2,1)S(1)}, u32[]{:S(2)}, u32[]{:S(2)}) %collective-permute-start.2) | collective-permute-done | bytes 16160 | tf_op jit(solution)/shard_map/ppermute | solution.py:24
  27.4 1.6 %bitcast_convert_fusion = (f32[14,134,192]{2,1,0:T(8,128)}, bf16[1,14,134,192]{3,2,1,0:T(8,128)(2,1)S(1)}) fusion(bf16[192,14,3]{0,2,1:T(4,128)(2,1)S(1)} %collective-permute-done.2, bf16[192,3,128]{0,2,1:T(8,128)(2,1)S(1)} %get-tuple-element.57, bf16[192,8,128]{0,2,1:T(8,128)(2,1)S(1)} %copy.84, bf16[192,3,128]{0,2,1:T(8,128)(2,1)S(1)} %get-tuple-element.56, ...), kind=kLoop, calls=%fused_computation.32 | loop fusion | flops 3962112 | bytes 2881536 | tf_op jit(solution)/shard_map/convert_element_type | solution.py:212
  29.0 8.4 %fusion.6 = f32[1,8,128,192]{3,0,2,1:T(1,128)S(1)} fusion(bf16[1,14,134,192]{3,2,1,0:T(8,128)(2,1)S(1)} %get-tuple-element.41, f32[7,7,1,192]{3,1,0,2:T(8,128)S(1)} %bitcast.130), kind=kOutput, calls=%fused_computation.13 | convolution fusion | flops 115605504 | bytes 1544448 | tf_op jit(solution)/shard_map/conv_general_dilated | solution.py:181
  38.1 1.9 %copy.89 = f32[1,8,128,192]{2,1,3,0:T(8,128)} copy(f32[1,8,128,192]{3,0,2,1:T(1,128)S(1)} %fusion.6) | data formatting | bytes 1572864 | tf_op jit(solution)/shard_map/conv_general_dilated | solution.py:181
  40.3 2.2 %multiply_convert_fusion = (bf16[1024,768]{0,1:T(8,128)(2,1)S(1)}, f32[1024,768]{0,1:T(8,128)S(1)}) fusion(f32[768]{0:T(1024)S(1)} %fusion.35, f32[24,8,8,128]{3,2,1,0:T(8,128)} %bitcast.125, f32[192]{0:T(256)S(1)} %copy-done.12, f32[192]{0:T(256)S(1)} %copy-done.9, f32[1024]{0:T(1024)S(1)} %get-tuple-element.62, f32[1024]{0:T(1024)S(1)} %get-tuple-element.63, ...), kind=kOutput, calls=%fused_computation.9 | convolution fusion | flops 307888128 | bytes 5913600 | tf_op jit(solution)/shard_map/dot_general | solution.py:53
  43.9 3.8 %fusion.31 = (f32[192]{0:T(256)S(1)}, f32[192]{0:T(256)S(1)}, bf16[8,128,192]{1,0,2:T(8,128)(2,1)}) fusion(bf16[192,8,128]{2,1,0:T(8,128)(2,1)S(1)} %copy-done.1, f32[192]{0:T(256)S(1)} %copy-done.10, f32[192]{0:T(256)S(1)} %copy-done.11, f32[24,8,8,128]{3,2,1,0:T(8,128)S(1)} %copy.118, bf16[192,8,128]{2,1,0:T(8,128)(2,1)S(1)} %copy-done.3), kind=kLoop, calls=%fused_computation.47 | loop fusion | flops 1965696 | bytes 1969152 | tf_op jit(solution)/shard_map/reduce_sum | solution.py:240
  47.6 1.6 %fusion.59 = (bf16[1024,768]{0,1:T(8,128)(2,1)S(1)}, f32[1024,768]{0,1:T(8,128)S(1)}) fusion(f32[1024,768]{0,1:T(8,128)S(1)} %get-tuple-element.69, f32[768]{0:T(1024)S(1)} %fusion.35, bf16[1024,192]{0,1:T(8,128)(2,1)S(1)} %fusion.23, bf16[768,387]{1,0:T(8,128)(2,1)S(1)} %all_gather.3), kind=kOutput, calls=%fused_computation.112 | convolution fusion | flops 310640640 | bytes 8654848 | tf_op jit(solution)/shard_map/dot_general | solution.py:53
  50.6 1.3 %copy.99 = f32[1024,192]{1,0:T(8,128)} copy(f32[1024,192]{0,1:T(8,128)S(1)} %get-tuple-element.35) | data formatting | bytes 1572864 | tf_op jit(solution)/shard_map/reduce_sum | solution.py:258
  53.3 1.5 %fusion.56 = (bf16[8,128,192]{2,1,0:T(8,128)(2,1)S(1)}, f32[8,128,192]{2,1,0:T(8,128)}) fusion(f32[8,128]{1,0:T(8,128)S(1)} %broadcast_multiply_fusion, f32[8,128]{1,0:T(8,128)S(1)} %get-tuple-element.64, f32[192]{0:T(256)S(1)} %copy-done.8, f32[1,8,128,192]{3,0,2,1:T(1,128)S(1)} %fusion.6, f32[8,128]{1,0:T(8,128)S(1)} %multiply_bitcast_fusion, ...), kind=kLoop, calls=%fused_computation.110 | loop fusion | flops 1769472 | bytes 2770432 | tf_op jit(solution)/shard_map/convert_element_type | solution.py:295
  54.8 8.1 %shard_map.194 = f32[49,8,192]{2,1,0:T(8,128)} custom-call(f32[8,128,192]{2,1,0:T(8,128)} %get-tuple-element.39.d_ref, f32[14,134,192]{2,1,0:T(8,128)} %get-tuple-element.40.p_ref), custom_call_target="tpu_custom_call" | custom-call | tf_op jit(solution)/shard_map/pallas_call | solution.py:107
  64.7 1.4 %fusion.38 = f32[192,192]{1,0:T(8,128)S(1)} fusion(bf16[1024,768]{0,1:T(8,128)(2,1)} %copy-done.13, s32[]{:T(128)S(6)} %select_n.42, f32[24,8,8,128]{3,2,1,0:T(8,128)S(1)} %bitcast.126, f32[192]{0:T(256)S(1)} %copy-done.12, f32[192]{0:T(256)S(1)} %copy-done.9, f32[1024]{0:T(1024)S(1)} %get-tuple-element.62, f32[1024]{0:T(1024)S(1)} %get-tuple-element.63, ...), kind=kOutput, calls=%fused_computation.66 | convolution fusion | flops 76677120 | bytes 1337604 | tf_op jit(solution)/shard_map/dot_general | solution.py:53
  66.1 2.1 %collective-permute-done.6 = f32[9984]{0:T(1024)S(1)} collective-permute-done((f32[9984]{0:T(1024)S(1)}, f32[9984]{0:T(1024)S(1)}, u32[]{:S(2)}, u32[]{:S(2)}) %collective-permute-start.6) | collective-permute-done | bytes 39968 | tf_op jit(solution)/shard_map/ppermute | solution.py:146
  68.2 1.6 %collective-permute-start.7 = (f32[9984]{0:T(1024)S(1)}, f32[9984]{0:T(1024)S(1)}, u32[]{:S(2)}, u32[]{:S(2)}) collective-permute-start(f32[9984]{0:T(1024)S(1)} %add.142), channel_id=1, source_target_pairs={{0,4},{4,0},{8,12},{12,8},{1,5},{5,1},{9,13},{13,9},{2,6},{6,2},{1... | collective-permute-start | bytes 119816 | tf_op jit(solution)/shard_map/ppermute | solution.py:146
  71.3 1.6 %concatenate.28 = f32[74304]{0:T(1024)S(1)} concatenate(f32[36864]{0:T(1024)S(1)} %reshape.310, f32[192]{0:T(256)S(1)} %dynamic-slice_reduce_fusion, f32[36864]{0:T(1024)S(1)} %reshape.311, f32[192]{0:T(256)S(1)} %get-tuple-element.19, f32[192]{0:T(256)S(1)} %get-tuple-element.20), dimensions={0} | concatenate | bytes 594432 | tf_op jit(solution)/shard_map/concatenate | solution.py:116
  73.9 2.0 %collective-permute-start.8 = (f32[9984]{0:T(1024)S(1)}, f32[9984]{0:T(1024)S(1)}, u32[]{:S(2)}, u32[]{:S(2)}) collective-permute-start(f32[9984]{0:T(1024)S(1)} %add.143), channel_id=1, source_target_pairs={{0,8},{4,12},{8,0},{12,4},{1,9},{5,13},{9,1},{13,5},{2,10},{6,14},... | collective-permute-start | bytes 119816 | tf_op jit(solution)/shard_map/ppermute | solution.py:146
  76.5 11.9 %collective-permute-done.8 = f32[9984]{0:T(1024)S(1)} collective-permute-done((f32[9984]{0:T(1024)S(1)}, f32[9984]{0:T(1024)S(1)}, u32[]{:S(2)}, u32[]{:S(2)}) %collective-permute-start.8) | collective-permute-done | bytes 39968 | tf_op jit(solution)/shard_map/ppermute | solution.py:146
  88.5 1.4 %collective-permute-start.4 = (bf16[14,3,192]{2,1,0:T(4,128)(2,1)S(1)}, bf16[14,3,192]{2,1,0:T(4,128)(2,1)S(1)}, u32[]{:S(2)}, u32[]{:S(2)}) collective-permute-start(bf16[14,3,192]{2,1,0:T(4,128)(2,1)S(1)} %get-tuple-element.42), channel_id=1, source_target_pairs={{0,4},{4,8},{8,12},{1,5},{5,9},{9,13},{2,6},{6,10},{10,14},{3,7},{... | collective-permute-start | bytes 48392 | tf_op jit(solution)/shard_map/ppermute | solution.py:23
  91.2 2.7 %collective-permute-start.10 = (f32[74304]{0:T(1024)S(1)}, f32[74304]{0:T(1024)S(1)}, u32[]{:S(2)}, u32[]{:S(2)}) collective-permute-start(f32[74304]{0:T(1024)S(1)} %add.145), channel_id=1, source_target_pairs={{0,4},{4,0},{8,12},{12,8},{1,5},{5,1},{9,13},{13,9},{2,6},{6,2},{1... | collective-permute-start | bytes 891656 | tf_op jit(solution)/shard_map/ppermute | solution.py:146
  97.2 3.9 %collective-permute-done.10 = f32[74304]{0:T(1024)S(1)} collective-permute-done((f32[74304]{0:T(1024)S(1)}, f32[74304]{0:T(1024)S(1)}, u32[]{:S(2)}, u32[]{:S(2)}) %collective-permute-start.10) | collective-permute-done | bytes 297248 | tf_op jit(solution)/shard_map/ppermute | solution.py:146
  101.7 4.2 %fusion.15 = f32[8,8,17,192]{3,1,2,0:T(8,128)S(1)} fusion(bf16[14,1,7,6,192]{4,2,3,0,1:T(8,128)(2,1)S(1)} %slice.124, bf16[14,1,8,17,192]{4,2,3,0,1:T(8,128)(2,1)S(1)} %copy.105, pred[8,17]{0,1:T(8,128)(4,1)S(1)} %copy-done.14, f32[7,7,1,192]{3,1,0,2:T(8,128)S(1)} %bitcast.131), kind=kOutput, calls=%fused_computation.23 | convolution fusion | flops 126007296 | bytes 1830280 | tf_op jit(solution)/shard_map/conv_general_dilated | solution.py:181
  (105 shorter events, 26.8 us)
Async XLA Ops:
  0.6 16.1 %copy-start.1 = (bf16[192,8,128]{2,1,0:T(8,128)(2,1)S(1)}, bf16[192,8,128]{2,1,0:T(8,128)(2,1)}, u32[]{:S(2)}) copy-start(bf16[192,8,128]{2,1,0:T(8,128)(2,1)} %param.21) | copy-start | bytes 1179652
  2.0 16.1 %collective-permute-start = (bf16[192,3,128]{0,2,1:T(8,128)(2,1)S(1)}, bf16[192,3,128]{0,2,1:T(8,128)(2,1)S(1)}, u32[]{:S(2)}, u32[]{:S(2)}) collective-permute-start(bf16[192,3,128]{0,2,1:T(8,128)(2,1)S(1)} %slice_select_fusion.1), channel_id=1, source_target_pairs={{0,16},{16,0},{1,17},{17,1},{2,18},{18,2},{3,19},{19,3},{4,20},{20... | collective-permute-start | bytes 442376 | tf_op jit(solution)/shard_map/ppermute | solution.py:18
  8.1 9.7 %copy-start.10 = (f32[192]{0:T(256)S(1)}, f32[192]{0:T(256)}, u32[]{:S(2)}) copy-start(f32[192]{0:T(256)} %param.20) | copy-start | bytes 2308
  18.0 5.4 %copy-start.7 = (f32[7,7,192]{2,1,0:T(8,128)S(1)}, f32[7,7,192]{2,1,0:T(8,128)}, u32[]{:S(2)}) copy-start(f32[7,7,192]{2,1,0:T(8,128)} %param.12) | copy-start | bytes 112900
  18.2 5.3 %collective-permute-start.1 = (bf16[192,14,3]{0,2,1:T(4,128)(2,1)S(1)}, bf16[192,14,3]{0,2,1:T(4,128)(2,1)S(1)}, u32[]{:S(2)}, u32[]{:S(2)}) collective-permute-start(bf16[192,14,3]{0,2,1:T(4,128)(2,1)S(1)} %get-tuple-element.44), channel_id=1, source_target_pairs={{0,4},{4,8},{8,12},{1,5},{5,9},{9,13},{2,6},{6,10},{10,14},{3,7},{... | collective-permute-start | bytes 48392 | tf_op jit(solution)/shard_map/ppermute | solution.py:23
  21.6 5.8 %collective-permute-start.2 = (bf16[192,14,3]{0,2,1:T(4,128)(2,1)S(1)}, bf16[192,14,3]{0,2,1:T(4,128)(2,1)S(1)}, u32[]{:S(2)}, u32[]{:S(2)}) collective-permute-start(bf16[192,14,3]{0,2,1:T(4,128)(2,1)S(1)} %get-tuple-element.45), channel_id=1, source_target_pairs={{4,0},{8,4},{12,8},{5,1},{9,5},{13,9},{6,2},{10,6},{14,10},{7,3},{... | collective-permute-start | bytes 48392 | tf_op jit(solution)/shard_map/ppermute | solution.py:24
  37.4 2.6 %copy-start.8 = (f32[192]{0:T(256)S(1)}, f32[192]{0:T(256)}, u32[]{:S(2)}) copy-start(f32[192]{0:T(256)} %param.13) | copy-start | bytes 2308
  38.1 2.2 %copy-start.9 = (f32[192]{0:T(256)S(1)}, f32[192]{0:T(256)}, u32[]{:S(2)}) copy-start(f32[192]{0:T(256)} %param.14) | copy-start | bytes 2308
  38.1 2.2 %copy-start.12 = (f32[192]{0:T(256)S(1)}, f32[192]{0:T(256)}, u32[]{:S(2)}) copy-start(f32[192]{0:T(256)} %param.15) | copy-start | bytes 2308
  40.3 2.2 %copy-start.4 = (bf16[768,192]{1,0:T(8,128)(2,1)S(1)}, bf16[768,192]{1,0:T(8,128)(2,1)}, u32[]{:S(2)}) copy-start(bf16[768,192]{1,0:T(8,128)(2,1)} %get-tuple-element.48) | copy-start | bytes 884740
  42.5 1.3 %copy-start.3 = (bf16[192,8,128]{2,1,0:T(8,128)(2,1)S(1)}, bf16[192,8,128]{2,1,0:T(8,128)(2,1)}, u32[]{:S(2)}) copy-start(bf16[192,8,128]{2,1,0:T(8,128)(2,1)} %param.11) | copy-start | bytes 1179652
  42.6 1.3 %copy-start.11 = (f32[192]{0:T(256)S(1)}, f32[192]{0:T(256)}, u32[]{:S(2)}) copy-start(f32[192]{0:T(256)} %param.19) | copy-start | bytes 2308
  47.6 1.8 %copy-start.6 = (bf16[768,192]{1,0:T(8,128)(2,1)S(1)}, bf16[768,192]{1,0:T(8,128)(2,1)}, u32[]{:S(2)}) copy-start(bf16[768,192]{1,0:T(8,128)(2,1)} %get-tuple-element.47) | copy-start | bytes 884740
  54.8 9.9 %copy-start.5 = (f32[1,8,128,192]{2,1,3,0:T(8,128)S(1)}, f32[1,8,128,192]{2,1,3,0:T(8,128)}, u32[]{:S(2)}) copy-start(f32[1,8,128,192]{2,1,3,0:T(8,128)} %copy.89) | copy-start | bytes 2359300
  64.2 4.0 %collective-permute-start.6 = (f32[9984]{0:T(1024)S(1)}, f32[9984]{0:T(1024)S(1)}, u32[]{:S(2)}, u32[]{:S(2)}) collective-permute-start(f32[9984]{0:T(1024)S(1)} %concatenate.27), channel_id=1, source_target_pairs={{0,16},{16,0},{1,17},{17,1},{2,18},{18,2},{3,19},{19,3},{4,20},{20... | collective-permute-start | bytes 119816 | tf_op jit(solution)/shard_map/ppermute | solution.py:146
  68.2 5.7 %collective-permute-start.7 = (f32[9984]{0:T(1024)S(1)}, f32[9984]{0:T(1024)S(1)}, u32[]{:S(2)}, u32[]{:S(2)}) collective-permute-start(f32[9984]{0:T(1024)S(1)} %add.142), channel_id=1, source_target_pairs={{0,4},{4,0},{8,12},{12,8},{1,5},{5,1},{9,13},{13,9},{2,6},{6,2},{1... | collective-permute-start | bytes 119816 | tf_op jit(solution)/shard_map/ppermute | solution.py:146
  72.9 18.3 %collective-permute-start.9 = (f32[74304]{0:T(1024)S(1)}, f32[74304]{0:T(1024)S(1)}, u32[]{:S(2)}, u32[]{:S(2)}) collective-permute-start(f32[74304]{0:T(1024)S(1)} %concatenate.28), channel_id=1, source_target_pairs={{0,8},{4,12},{8,0},{12,4},{1,9},{5,13},{9,1},{13,5},{2,10},{6,14},... | collective-permute-start | bytes 891656 | tf_op jit(solution)/shard_map/ppermute | solution.py:146
  73.9 14.5 %collective-permute-start.8 = (f32[9984]{0:T(1024)S(1)}, f32[9984]{0:T(1024)S(1)}, u32[]{:S(2)}, u32[]{:S(2)}) collective-permute-start(f32[9984]{0:T(1024)S(1)} %add.143), channel_id=1, source_target_pairs={{0,8},{4,12},{8,0},{12,4},{1,9},{5,13},{9,1},{13,5},{2,10},{6,14},... | collective-permute-start | bytes 119816 | tf_op jit(solution)/shard_map/ppermute | solution.py:146
  75.9 12.5 %collective-permute-start.3 = (bf16[3,128,192]{2,1,0:T(8,128)(2,1)S(1)}, bf16[3,128,192]{2,1,0:T(8,128)(2,1)S(1)}, u32[]{:S(2)}, u32[]{:S(2)}) collective-permute-start(bf16[3,128,192]{2,1,0:T(8,128)(2,1)S(1)} %slice_select_fusion), channel_id=1, source_target_pairs={{0,16},{16,0},{1,17},{17,1},{2,18},{18,2},{3,19},{19,3},{4,20},{20... | collective-permute-start | bytes 442376 | tf_op jit(solution)/shard_map/ppermute | solution.py:18
  88.5 6.8 %collective-permute-start.4 = (bf16[14,3,192]{2,1,0:T(4,128)(2,1)S(1)}, bf16[14,3,192]{2,1,0:T(4,128)(2,1)S(1)}, u32[]{:S(2)}, u32[]{:S(2)}) collective-permute-start(bf16[14,3,192]{2,1,0:T(4,128)(2,1)S(1)} %get-tuple-element.42), channel_id=1, source_target_pairs={{0,4},{4,8},{8,12},{1,5},{5,9},{9,13},{2,6},{6,10},{10,14},{3,7},{... | collective-permute-start | bytes 48392 | tf_op jit(solution)/shard_map/ppermute | solution.py:23
  89.8 6.1 %collective-permute-start.5 = (bf16[14,3,192]{2,1,0:T(4,128)(2,1)S(1)}, bf16[14,3,192]{2,1,0:T(4,128)(2,1)S(1)}, u32[]{:S(2)}, u32[]{:S(2)}) collective-permute-start(bf16[14,3,192]{2,1,0:T(4,128)(2,1)S(1)} %get-tuple-element.43), channel_id=1, source_target_pairs={{4,0},{8,4},{12,8},{5,1},{9,5},{13,9},{6,2},{10,6},{14,10},{7,3},{... | collective-permute-start | bytes 48392 | tf_op jit(solution)/shard_map/ppermute | solution.py:24
  91.2 9.9 %collective-permute-start.10 = (f32[74304]{0:T(1024)S(1)}, f32[74304]{0:T(1024)S(1)}, u32[]{:S(2)}, u32[]{:S(2)}) collective-permute-start(f32[74304]{0:T(1024)S(1)} %add.145), channel_id=1, source_target_pairs={{0,4},{4,0},{8,12},{12,8},{1,5},{5,1},{9,13},{13,9},{2,6},{6,2},{1... | collective-permute-start | bytes 891656 | tf_op jit(solution)/shard_map/ppermute | solution.py:146
  96.7 5.0 %copy-start.14 = (pred[8,17]{0,1:T(8,128)(4,1)S(1)}, pred[8,17]{0,1:T(8,128)(4,1)}, u32[]{:S(2)}) copy-start(pred[8,17]{0,1:T(8,128)(4,1)} %constant.51) | copy-start | bytes 412
  101.1 7.9 %collective-permute-start.11 = (f32[74304]{0:T(1024)S(1)}, f32[74304]{0:T(1024)S(1)}, u32[]{:S(2)}, u32[]{:S(2)}) collective-permute-start(f32[74304]{0:T(1024)S(1)} %add.146), channel_id=1, source_target_pairs={{0,16},{16,0},{1,17},{17,1},{2,18},{18,2},{3,19},{19,3},{4,20},{20... | collective-permute-start | bytes 891656 | tf_op jit(solution)/shard_map/ppermute | solution.py:146
  (3 other events, 3.5 us)
